TPU v7x, 32 devices: a whole 2x2x4 slice. The times are simulated.
32 devices in a mesh: groups: 2 (over y), seq: 4 (over x, core), head: 4 (over z).
Axes of the slice: x: 2, y: 2, z: 4, core: 2. Of those that a mesh axis runs over, the one named last changes fastest.
Arguments:
- query_in: bfloat16 [8192, 3072], P(('groups', 'seq', 'head')), parts along dimension 0, may hold values from -4.5 to 4.5
- key_in: bfloat16 [8192, 3072], P(('groups', 'seq', 'head')), parts along dimension 0, may hold values from -4.5 to 4.5
- value_in: bfloat16 [8192, 3072], P(('groups', 'seq', 'head')), parts along dimension 0, may hold values from -6 to 6
- block_lists: int32 [64, 12], P('groups'), parts along dimension 0, may hold values from 0 to 31, as said below
Outputs:
- draft_out: bfloat16 [2048, 3072], P(('groups', 'seq'), 'head'), parts along dimension 0
- sparse_out: bfloat16 [8192, 3072], P(('groups', 'seq', 'head')), parts along dimension 0
There are 2 independent parts, one for each index of `groups`. A program takes and returns all parts, laid end to end along the dimension named above; each array names one. Nothing has to cross between parts.
Inputs may be any that keep to these rules, and one draw needn't show every extreme that they name: block_lists[b] holds 12 distinct block numbers, b among them. Of the 8 blocks b with b // 8 = k, the query blocks with b // 8 = p (p other than k) select at most 2 distinct ones and at least one; in every draw some p selects exactly 2 from every other k.
All inputs are finite; a program needn't handle non-finite values.
Results may differ from a plain program's by a relative error of at most 0.0096.
Values may be sent and summed in bfloat16 or wider, within the bound.
No kernel may reach another device: no remote copies, remote signals or barrier semaphores. Data moves between devices by JAX's collectives and lax.ppermute only.
A program may use at most 128 MiB of HBM per device.

v0:
```python
import math

import jax
import jax.numpy as jnp
from jax import lax
from jax.sharding import PartitionSpec as P

HD = 128
BLOCK = 128
POOL = 4
CAP = 2


NEGATIVE = -1e30


def pool_tokens(matrix):
    grouped = matrix.astype(jnp.float32).reshape(matrix.shape[0] // POOL, POOL, matrix.shape[1])
    return (grouped.sum(axis=1) * POOL ** (-0.5)).astype(jnp.bfloat16)


def smooth_refresh(state_in, logit_values, value_rows, value_form):
    running, totals, weighted = state_in
    newest = jnp.maximum(running, logit_values.max(axis=-1))
    factor = jnp.exp(running - newest)
    weights = jnp.exp(logit_values - newest[..., None])
    totals = totals * factor + weights.sum(axis=-1)
    weighted = weighted * factor[..., None] + jnp.einsum(
        value_form, weights.astype(jnp.bfloat16), value_rows, preferred_element_type=jnp.float32
    )
    return (newest, totals, weighted)


def on_device(query_in, key_in, value_in, block_lists):
    queries, key_rows, value_rows = (
        lax.all_to_all(query_in, "head", split_axis=1, concat_axis=0, tiled=True),
        lax.all_to_all(key_in, "head", split_axis=1, concat_axis=0, tiled=True),
        lax.all_to_all(value_in, "head", split_axis=1, concat_axis=0, tiled=True),
    )
    head_count = queries.shape[1] // HD
    seq_rows = queries.shape[0]
    score_scale = HD ** (-0.5)
    preview_queries = pool_tokens(queries).reshape(seq_rows // POOL, head_count, HD)
    draft_pair = (pool_tokens(key_rows), pool_tokens(value_rows))
    preview_rows = preview_queries.shape[0]
    start_state = (
        jnp.full((preview_rows, head_count), NEGATIVE, jnp.float32),
        jnp.zeros((preview_rows, head_count), jnp.float32),
        jnp.zeros((preview_rows, head_count, HD), jnp.float32),
    )
    piece_keys = lax.all_gather(draft_pair[0], "seq", axis=0, tiled=True)
    piece_values = lax.all_gather(draft_pair[1], "seq", axis=0, tiled=True)
    piece_rows = piece_keys.shape[0]
    block_rows = math.gcd(piece_rows, 512)
    block_count = piece_rows // block_rows
    key_blocks = piece_keys.reshape(block_count, block_rows, head_count, HD)
    value_blocks = piece_values.reshape(block_count, block_rows, head_count, HD)

    def one_block(current_state, block_couple):
        logit_values = (
            jnp.einsum(
                "xfv,tfv->xft", preview_queries, block_couple[0], preferred_element_type=jnp.float32
            )
            * score_scale
        )
        return (smooth_refresh(current_state, logit_values, block_couple[1], "xft,tfo->xfo"), None)

    state_out, ignored = lax.scan(one_block, start_state, (key_blocks, value_blocks))
    running, totals, weighted = state_out
    draft_out = (
        (weighted / totals[..., None]).reshape(preview_rows, head_count * HD).astype(jnp.bfloat16)
    )
    seq_count = lax.axis_size("seq")
    seq_index = lax.axis_index("seq")
    per_dev = seq_rows // BLOCK
    block_total = block_lists.shape[0]
    select_count = block_lists.shape[1]
    block_ids = jnp.arange(block_total, dtype=jnp.int32)
    touched = jnp.any(block_lists[:, :, None] == block_ids[None, None, :], axis=1)
    needed = jnp.any(touched.reshape(seq_count, per_dev, seq_count, per_dev), axis=1)
    slot_rank = jnp.cumsum(needed.astype(jnp.int32), axis=2) - 1
    local_keys = key_rows.reshape(per_dev, BLOCK, head_count, HD)
    local_values = value_rows.reshape(per_dev, BLOCK, head_count, HD)
    local_pair = jnp.stack([local_keys, local_values], axis=0)
    peer_ids = jnp.arange(seq_count, dtype=jnp.int32)
    send_need = lax.dynamic_index_in_dim(
        jnp.take(needed, peer_ids, axis=0), seq_index, axis=1, keepdims=False
    )
    send_rank = lax.dynamic_index_in_dim(
        jnp.take(slot_rank, peer_ids, axis=0), seq_index, axis=1, keepdims=False
    )
    pick_mask = (
        (send_rank[:, None, :] == jnp.arange(CAP, dtype=jnp.int32)[None, :, None])
        & send_need[:, None, :]
        & (peer_ids != seq_index)[:, None, None]
    )
    outgoing = jnp.einsum(
        "tcj,ajrhx->atcrhx",
        pick_mask.astype(jnp.bfloat16),
        local_pair,
        preferred_element_type=jnp.float32,
    ).astype(jnp.bfloat16)
    arrived = lax.all_to_all(outgoing, "seq", split_axis=1, concat_axis=1, tiled=True)
    remote_keys = arrived[0].reshape(seq_count * CAP, BLOCK, head_count, HD)
    remote_values = arrived[1].reshape(seq_count * CAP, BLOCK, head_count, HD)
    own_lists = lax.dynamic_slice_in_dim(block_lists, seq_index * per_dev, per_dev, 0)
    owners = own_lists // per_dev
    within = own_lists % per_dev
    own_rank = lax.dynamic_index_in_dim(slot_rank, seq_index, axis=0, keepdims=False)
    ranks_used = own_rank[owners, within]
    is_local = owners == seq_index
    remote_pos = jnp.where(is_local, 0, owners * CAP + ranks_used)
    joint_pos = jnp.where(is_local, within, per_dev + remote_pos)
    local_pick = jnp.any(
        is_local[:, :, None]
        & (within[:, :, None] == jnp.arange(per_dev, dtype=jnp.int32)[None, None, :]),
        axis=1,
    )
    group_size = math.gcd(per_dev, max(1, 512 // BLOCK))
    group_count = per_dev // group_size
    query_groups = queries.reshape(group_count, group_size, BLOCK, head_count, HD)

    def per_group(table):
        return table.reshape((group_count, group_size) + table.shape[1:])

    all_keys = jnp.concatenate([local_keys, remote_keys], axis=0)
    all_values = jnp.concatenate([local_values, remote_values], axis=0)

    def attend_group(placeholder, group_pack):
        query_block, joint_item, remote_item, local_item, pick_item = group_pack
        current_state = (
            jnp.full((group_size, BLOCK, head_count), NEGATIVE, jnp.float32),
            jnp.zeros((group_size, BLOCK, head_count), jnp.float32),
            jnp.zeros((group_size, BLOCK, head_count, HD), jnp.float32),
        )
        chosen_keys = jnp.take(all_keys, joint_item.reshape(-1), axis=0).reshape(
            group_size, select_count * BLOCK, head_count, HD
        )
        chosen_values = jnp.take(all_values, joint_item.reshape(-1), axis=0).reshape(
            group_size, select_count * BLOCK, head_count, HD
        )
        logit_values = (
            jnp.einsum(
                "bnhd,bmhd->bnhm", query_block, chosen_keys, preferred_element_type=jnp.float32
            )
            * score_scale
        )
        current_state = smooth_refresh(
            current_state, logit_values, chosen_values, "bnhm,bmhd->bnhd"
        )
        running_now, totals_now, weighted_now = current_state
        return (placeholder, (weighted_now / totals_now[..., None]).astype(jnp.bfloat16))

    group_pack = (
        query_groups,
        per_group(joint_pos),
        per_group(remote_pos),
        per_group(is_local),
        per_group(local_pick),
    )
    placeholder, results = lax.scan(attend_group, jnp.zeros((), jnp.int32), group_pack)
    sparse_rows = results.reshape(seq_rows, head_count * HD)
    sparse_out = lax.all_to_all(sparse_rows, "head", split_axis=0, concat_axis=1, tiled=True)
    return (draft_out, sparse_out)


def solution(mesh):
    return jax.shard_map(
        on_device,
        mesh=mesh,
        in_specs=(
            P(("groups", "seq", "head"), None),
            P(("groups", "seq", "head"), None),
            P(("groups", "seq", "head"), None),
            P("groups", None),
        ),
        out_specs=(P(("groups", "seq"), "head"), P(("groups", "seq", "head"), None)),
        check_vma=False,
    )
```

profile of v0, /device:TPU:0, one launch (start us, length us, event | category | flops | bytes accessed | tf_op | source)
XLA Modules:
  0.0 410.1 jit_solution(8338828075649173384)
XLA Ops:
  9.9 6.3 %all-to-all-start = ((bf16[256,4,768]{0,2,1:T(8,128)(2,1)}), bf16[256,4,768]{0,2,1:T(8,128)(2,1)S(1)}, u32[]{:S(2)}, u32[]{:S(2)}) async-start(bf16[256,4,768]{0,2,1:T(8,128)(2,1)} %bitcast.6), calls=%async_computation | async-start | bytes 3145728 | tf_op jit(solution)/shard_map/all_to_all | solution.py:37
  17.7 35.4 %all-to-all-done = bf16[256,4,768]{0,2,1:T(8,128)(2,1)S(1)} async-done(((bf16[256,4,768]{0,2,1:T(8,128)(2,1)}), bf16[256,4,768]{0,2,1:T(8,128)(2,1)S(1)}, u32[]{:S(2)}, u32[]{:S(2)}) %all-to-all-start) | async-done | bytes 1572896 | tf_op jit(solution)/shard_map/all_to_all | solution.py:37
  62.2 4.9 %reshape.111 = f32[256,4,768]{2,1,0:T(4,128)} reshape(f32[4,256,768]{2,1,0:T(8,128)} %copy.109) | data formatting | bytes 6291456 | tf_op jit(solution)/shard_map/convert_element_type | solution.py:18
  76.3 16.8 %all-to-all-done.2 = bf16[256,4,768]{0,2,1:T(8,128)(2,1)S(1)} async-done(((bf16[256,4,768]{0,2,1:T(8,128)(2,1)}), bf16[256,4,768]{0,2,1:T(8,128)(2,1)S(1)}, u32[]{:S(2)}, u32[]{:S(2)}) %all-to-all-start.2) | async-done | bytes 1572896 | tf_op jit(solution)/shard_map/all_to_all | solution.py:38
  107.4 4.9 %reshape.113 = f32[256,4,768]{2,1,0:T(4,128)} reshape(f32[4,256,768]{2,1,0:T(8,128)} %copy.115) | data formatting | bytes 6291456 | tf_op jit(solution)/shard_map/convert_element_type | solution.py:18
  193.3 4.9 %fusion.65 = (bf16[1,4,2,128,6,128]{5,2,4,3,0,1:T(2,128)(2,1)}, bf16[1,4,2,128,6,128]{5,2,4,3,0,1:T(2,128)(2,1)S(1)}) fusion(bf16[2,4,2,128,6,128]{5,2,4,3,0,1:T(2,128)(2,1)} %all-to-all-done.3), kind=kLoop, calls=%fused_computation.105 | loop fusion | bytes 6291456 | tf_op jit(solution)/shard_map/slice | solution.py:105
  204.4 6.0 %copy.134 = bf16[16,128,6,128]{3,2,1,0:T(8,128)(2,1)} copy(bf16[16,128,6,128]{1,0,3,2:T(8,128)(2,1)} %pad_maximum_fusion) | data formatting | bytes 6291456 | tf_op jit(solution)/shard_map/while | solution.py:161
  218.1 5.8 %copy.136 = bf16[16,128,6,128]{3,2,1,0:T(8,128)(2,1)} copy(bf16[16,128,6,128]{1,0,3,2:T(8,128)(2,1)} %pad_maximum_fusion.1) | data formatting | bytes 6291456 | tf_op jit(solution)/shard_map/while | solution.py:161
  223.9 129.4 %while.25 = (s32[]{:T(128)}, bf16[2,4,128,6,128]{2,1,0,4,3:T(4,128)(2,1)}, s32[2,4,12]{2,1,0:T(4,128)S(1)}, bf16[16,128,6,128]{3,2,1,0:T(8,128)(2,1)}, bf16[2,4,...) while((s32[]{:T(128)}, bf16[2,4,128,6,128]{2,1,0,4,3:T(4,128)(2,1)}, ...), condition=%wide.region_13.15_spmd, body=%wide.region_10.14_spmd.sunk | while | flops 2464295424 | bytes 170023056 | solution.py:161
  224.9 8.5 %gather_fusion = bf16[48,128,6,128]{3,2,1,0:T(8,128)(2,1)} fusion(bf16[16,128,6,128]{3,2,1,0:T(8,128)(2,1)} %get-tuple-element.344, s32[1024]{0:T(1024)S(1)} %pad_clamp_fusion.3), kind=kCustom, calls=%fused_computation.1.clone.clone.1 | custom fusion | bytes 18874560 | tf_op jit(solution)/shard_map/while/body/eval_jaxpr/jit(_take)/gather | solution.py:139
  233.4 8.5 %gather_fusion.1 = bf16[48,128,6,128]{3,2,1,0:T(8,128)(2,1)} fusion(bf16[16,128,6,128]{3,2,1,0:T(8,128)(2,1)} %get-tuple-element.342, s32[1024]{0:T(1024)S(1)} %pad_clamp_fusion.3), kind=kCustom, calls=%fused_computation.clone.clone.1 | custom fusion | bytes 18874560 | tf_op jit(solution)/shard_map/while/body/eval_jaxpr/jit(_take)/gather | solution.py:136
  241.9 14.2 %broadcast_select_fusion.4 = (bf16[48,128,6,128]{3,2,1,0:T(8,128)(2,1)}, bf16[48,128,6,128]{3,2,1,0:T(8,128)(2,1)S(1)}) fusion(bf16[48,128,6,128]{3,2,1,0:T(8,128)(2,1)} %gather_fusion, pred[48]{0:T(512)(128)(4,1)S(1)} %compare_and_fusion.2, bf16[48,128,6,128]{3,2,1,0:T(8,128)(2,1)} %gather_fusion.1), kind=kLoop, calls=%fused_computation.33.clone.1 | loop fusion | flops 9437184 | bytes 37748784 | tf_op jit(solution)/shard_map/while/body/eval_jaxpr/jit(_take)/select_n | solution.py:139
  256.1 7.9 %bitcast_reduce_fusion.4 = (f32[4,128,6]{1,2,0:T(8,128)S(1)}, f32[4,6,1536,128]{3,2,1,0:T(8,128)}) fusion(bf16[1,4,128,6,128]{4,2,3,1,0:T(8,128)(2,1)S(1)} %copy.177, bf16[4,1536,6,128]{3,2,1,0:T(8,128)(2,1)S(1)} %bitcast.137), kind=kOutput, calls=%fused_computation.29.clone.1 | convolution fusion | flops 1217393664 | bytes 29110272 | tf_op jit(solution)/shard_map/while/body/eval_jaxpr/bnhd,bmhd->bnhm/dot_general | solution.py:143
  263.9 9.5 %fusion.79 = f32[4,128,6]{1,2,0:T(8,128)S(1)} fusion(f32[4,6,1536,128]{3,2,1,0:T(8,128)} %get-tuple-element.282, f32[4,128,6]{1,2,0:T(8,128)S(1)} %broadcast_maximum_fusion.2), kind=kLoop, calls=%fused_computation.31.clone.1 | loop fusion | flops 14152704 | bytes 18898944 | tf_op jit(solution)/shard_map/while/body/eval_jaxpr/reduce_sum | solution.py:27
  273.4 13.0 %fusion.80 = bf16[1,4,128,6,128]{2,4,3,1,0:T(8,128)(2,1)S(1)} fusion(f32[4,6,1536,128]{3,2,1,0:T(8,128)} %get-tuple-element.282, f32[4,128,6]{1,2,0:T(8,128)S(1)} %broadcast_maximum_fusion.2, bf16[4,1536,6,128]{3,2,1,0:T(8,128)(2,1)} %bitcast.138, f32[4,128,6]{1,2,0:T(8,128)S(1)} %get-tuple-element.285, f32[4,128,6]{1,2,0:T(8,128)S(1)} %get-tuple-element.286), kind=kOutput, calls=%fused_computation.44.clone.1 | convolution fusion | flops 1223294976 | bytes 29134848 | tf_op jit(solution)/shard_map/while/body/eval_jaxpr/bnhm,bmhd->bnhd/dot_general | solution.py:28
  289.6 8.6 %gather_fusion = bf16[48,128,6,128]{3,2,1,0:T(8,128)(2,1)} fusion(bf16[16,128,6,128]{3,2,1,0:T(8,128)(2,1)} %get-tuple-element.344, s32[1024]{0:T(1024)S(1)} %pad_clamp_fusion.3), kind=kCustom, calls=%fused_computation.1.clone.clone.1 | custom fusion | bytes 18874560 | tf_op jit(solution)/shard_map/while/body/eval_jaxpr/jit(_take)/gather | solution.py:139
  298.1 8.5 %gather_fusion.1 = bf16[48,128,6,128]{3,2,1,0:T(8,128)(2,1)} fusion(bf16[16,128,6,128]{3,2,1,0:T(8,128)(2,1)} %get-tuple-element.342, s32[1024]{0:T(1024)S(1)} %pad_clamp_fusion.3), kind=kCustom, calls=%fused_computation.clone.clone.1 | custom fusion | bytes 18874560 | tf_op jit(solution)/shard_map/while/body/eval_jaxpr/jit(_take)/gather | solution.py:136
  306.7 14.2 %broadcast_select_fusion.4 = (bf16[48,128,6,128]{3,2,1,0:T(8,128)(2,1)}, bf16[48,128,6,128]{3,2,1,0:T(8,128)(2,1)S(1)}) fusion(bf16[48,128,6,128]{3,2,1,0:T(8,128)(2,1)} %gather_fusion, pred[48]{0:T(512)(128)(4,1)S(1)} %compare_and_fusion.2, bf16[48,128,6,128]{3,2,1,0:T(8,128)(2,1)} %gather_fusion.1), kind=kLoop, calls=%fused_computation.33.clone.1 | loop fusion | flops 9437184 | bytes 37748784 | tf_op jit(solution)/shard_map/while/body/eval_jaxpr/jit(_take)/select_n | solution.py:139
  320.8 7.9 %bitcast_reduce_fusion.4 = (f32[4,128,6]{1,2,0:T(8,128)S(1)}, f32[4,6,1536,128]{3,2,1,0:T(8,128)}) fusion(bf16[1,4,128,6,128]{4,2,3,1,0:T(8,128)(2,1)S(1)} %copy.177, bf16[4,1536,6,128]{3,2,1,0:T(8,128)(2,1)S(1)} %bitcast.137), kind=kOutput, calls=%fused_computation.29.clone.1 | convolution fusion | flops 1217393664 | bytes 29110272 | tf_op jit(solution)/shard_map/while/body/eval_jaxpr/bnhd,bmhd->bnhm/dot_general | solution.py:143
  328.7 9.5 %fusion.79 = f32[4,128,6]{1,2,0:T(8,128)S(1)} fusion(f32[4,6,1536,128]{3,2,1,0:T(8,128)} %get-tuple-element.282, f32[4,128,6]{1,2,0:T(8,128)S(1)} %broadcast_maximum_fusion.2), kind=kLoop, calls=%fused_computation.31.clone.1 | loop fusion | flops 14152704 | bytes 18898944 | tf_op jit(solution)/shard_map/while/body/eval_jaxpr/reduce_sum | solution.py:27
  338.2 13.0 %fusion.80 = bf16[1,4,128,6,128]{2,4,3,1,0:T(8,128)(2,1)S(1)} fusion(f32[4,6,1536,128]{3,2,1,0:T(8,128)} %get-tuple-element.282, f32[4,128,6]{1,2,0:T(8,128)S(1)} %broadcast_maximum_fusion.2, bf16[4,1536,6,128]{3,2,1,0:T(8,128)(2,1)} %bitcast.138, f32[4,128,6]{1,2,0:T(8,128)S(1)} %get-tuple-element.285, f32[4,128,6]{1,2,0:T(8,128)S(1)} %get-tuple-element.286), kind=kOutput, calls=%fused_computation.44.clone.1 | convolution fusion | flops 1223294976 | bytes 29134848 | tf_op jit(solution)/shard_map/while/body/eval_jaxpr/bnhm,bmhd->bnhd/dot_general | solution.py:28
  357.7 5.0 %all-to-all-start.4 = ((bf16[4,256,768]{1,2,0:T(8,128)(2,1)}), bf16[4,256,768]{1,2,0:T(8,128)(2,1)}, u32[]{:S(2)}, u32[]{:S(2)}) async-start(bf16[4,256,768]{1,2,0:T(8,128)(2,1)} %copy.138), calls=%async_computation.4 | async-start | bytes 3145728 | tf_op jit(solution)/shard_map/all_to_all | solution.py:163
  362.7 10.4 %while.26 = (s32[]{:T(128)}, f32[256,6]{0,1:T(8,128)S(1)}, f32[256,6]{0,1:T(8,128)}, f32[256,6,128]{0,2,1:T(8,128)}, bf16[2,512,6,128]{3,1,2,0:T(8,128)(2,1)}, /...) while((s32[]{:T(128)}, f32[256,6]{0,1:T(8,128)S(1)}, ...), condition=%wide.region_6.7_spmd.clone, body=%wide.region_3.6_spmd.clone.sunk | while | flops 409542144 | bytes 25710852 | solution.py:68
  375.2 25.2 %all-to-all-done.4 = bf16[4,256,768]{1,2,0:T(8,128)(2,1)} async-done(((bf16[4,256,768]{1,2,0:T(8,128)(2,1)}), bf16[4,256,768]{1,2,0:T(8,128)(2,1)}, u32[]{:S(2)}, u32[]{:S(2)}) %all-to-all-start.4) | async-done | bytes 1572896 | tf_op jit(solution)/shard_map/all_to_all | solution.py:163
  (155 shorter events, 156.8 us)
Async XLA Ops:
  7.2 9.0 %copy-start.6 = (bf16[256,3072]{1,0:T(8,128)(2,1)S(1)}, bf16[256,3072]{1,0:T(8,128)(2,1)}, u32[]{:S(2)}) copy-start(bf16[256,3072]{1,0:T(8,128)(2,1)} %param.12) | copy-start | bytes 4718596
  9.9 43.3 %all-to-all-start = ((bf16[256,4,768]{0,2,1:T(8,128)(2,1)}), bf16[256,4,768]{0,2,1:T(8,128)(2,1)S(1)}, u32[]{:S(2)}, u32[]{:S(2)}) async-start(bf16[256,4,768]{0,2,1:T(8,128)(2,1)} %bitcast.6), calls=%async_computation | async-start | bytes 3145728 | tf_op jit(solution)/shard_map/all_to_all | solution.py:37
  53.1 40.0 %all-to-all-start.2 = ((bf16[256,4,768]{0,2,1:T(8,128)(2,1)}), bf16[256,4,768]{0,2,1:T(8,128)(2,1)S(1)}, u32[]{:S(2)}, u32[]{:S(2)}) async-start(bf16[256,4,768]{0,2,1:T(8,128)(2,1)} %bitcast.143), calls=%async_computation.2 | async-start | bytes 3145728 | tf_op jit(solution)/shard_map/all_to_all | solution.py:38
  56.7 120.7 %all-gather.3.cloned.1.call-start = ((), (), s32[]{:S(2)}) async-start(), calls=%async_computation.5 | async-start | bytes 1966080 | tf_op jit(solution)/shard_map/all_gather | solution.py:51
  73.7 24.4 %copy-start.12 = (s32[32,12]{0,1:T(8,128)S(1)}, s32[32,12]{0,1:T(8,128)}, u32[]{:S(2)}) copy-start(s32[32,12]{0,1:T(8,128)} %param.13) | copy-start | bytes 4612
  93.2 1.1 copy-start.4
  94.3 50.6 %all-to-all-start.1 = ((bf16[256,4,768]{0,2,1:T(8,128)(2,1)}), bf16[256,4,768]{0,2,1:T(8,128)(2,1)S(1)}, u32[]{:S(2)}, u32[]{:S(2)}) async-start(bf16[256,4,768]{0,2,1:T(8,128)(2,1)} %bitcast.142), calls=%async_computation.1 | async-start | bytes 3145728 | tf_op jit(solution)/shard_map/all_to_all | solution.py:36
  97.9 86.9 %all-gather.5.cloned.1.call-start = ((), (), s32[]{:S(2)}) async-start(), calls=%async_computation.6 | async-start | bytes 1966080 | tf_op jit(solution)/shard_map/all_gather | solution.py:52
  144.9 48.3 %all-to-all-start.3 = ((bf16[2,4,2,128,6,128]{5,2,4,3,0,1:T(2,128)(2,1)}), bf16[2,4,2,128,6,128]{5,2,4,3,0,1:T(2,128)(2,1)}, u32[]{:S(2)}, u32[]{:S(2)}) async-start(bf16[2,4,2,128,6,128]{5,2,4,3,0,1:T(2,128)(2,1)} %copy.127), calls=%async_computation.3 | async-start | bytes 6291456 | tf_op jit(solution)/shard_map/all_to_all | solution.py:103
  149.9 5.3 %copy-start.5 = (bf16[4,256,768]{1,0,2:T(4,128)(2,1)S(1)}, bf16[4,256,768]{1,0,2:T(4,128)(2,1)}, u32[]{:S(2)}) copy-start(bf16[4,256,768]{1,0,2:T(4,128)(2,1)} %copy.124) | copy-start | bytes 4718596
  273.4 13.1 %copy-start.7 = (bf16[2,4,128,6,128]{2,1,0,4,3:T(4,128)(2,1)S(1)}, bf16[2,4,128,6,128]{2,1,0,4,3:T(4,128)(2,1)}, u32[]{:S(2)}) copy-start(bf16[2,4,128,6,128]{2,1,0,4,3:T(4,128)(2,1)} %get-tuple-element.333) | copy-start | bytes 4718596 | tf_op jit(solution)/shard_map/while
  287.4 1.2 copy-start.8
  338.2 13.1 %copy-start.7 = (bf16[2,4,128,6,128]{2,1,0,4,3:T(4,128)(2,1)S(1)}, bf16[2,4,128,6,128]{2,1,0,4,3:T(4,128)(2,1)}, u32[]{:S(2)}) copy-start(bf16[2,4,128,6,128]{2,1,0,4,3:T(4,128)(2,1)} %get-tuple-element.333) | copy-start | bytes 4718596 | tf_op jit(solution)/shard_map/while
  352.1 1.2 copy-start.8
  356.3 6.4 %copy-start.3 = (bf16[256,6,128]{2,0,1:T(8,128)(2,1)S(1)}, bf16[256,6,128]{2,0,1:T(8,128)(2,1)}, u32[]{:S(2)}) copy-start(bf16[256,6,128]{2,0,1:T(8,128)(2,1)} %copy.118) | copy-start | bytes 1179652
  356.3 6.4 %copy-start.9 = (f32[256,6]{0,1:T(8,128)S(1)}, f32[256,6]{0,1:T(8,128)}, u32[]{:S(2)}) copy-start(f32[256,6]{0,1:T(8,128)} %custom-call.2) | copy-start | bytes 18436
  357.7 42.8 %all-to-all-start.4 = ((bf16[4,256,768]{1,2,0:T(8,128)(2,1)}), bf16[4,256,768]{1,2,0:T(8,128)(2,1)}, u32[]{:S(2)}, u32[]{:S(2)}) async-start(bf16[4,256,768]{1,2,0:T(8,128)(2,1)} %copy.138), calls=%async_computation.4 | async-start | bytes 3145728 | tf_op jit(solution)/shard_map/all_to_all | solution.py:163
  364.4 1.1 copy-start
  364.4 1.7 copy-start.2
  365.1 1.9 copy-start.11
  367.0 0.9 copy-start.1
  369.6 1.1 copy-start
  369.6 1.7 copy-start.2
  370.3 1.9 copy-start.11
  (3 other events, 2.3 us)
Sparse Core Ops, SparseCore 0:
  73.8 21.0 all-gather.2
  137.2 25.1 all-gather.4
where the time goes:
time: 416 us; the launch traced here: 410 us
  local copies, waits for them, and re-layouts  161 us (39%)
  other arithmetic  83 us (20%)
  waiting for transfers between devices  77.6 us (19%)
  matrix products  50.7 us (12%)
  starting transfers between devices  23.4 us (6%)
  between operations  14.5 us (3%)
    all_to_all x1, waiting for transfers between devices, on_device(): lax.all_to_all(key_in, 'head', split_axis=1, concat_axis=0, tiled=True)  35.4 us
    select_n x2, other arithmetic, attend_group(): jnp.take(all_values, joint_item.reshape(-1), axis=0)  28.3 us
    dot_general x4, matrix products, smooth_refresh(): jnp.einsum(value_form, weights.astype(jnp.bfloat16), value_rows, preferre...  27.9 us
    convert_element_type x6, local copies, waits for them, and re-layouts, pool_tokens(): matrix.astype(jnp.float32)  25.3 us
    all_to_all x1, waiting for transfers between devices, on_device(): lax.all_to_all(sparse_rows, 'head', split_axis=0, concat_axis=1, tiled=True)  25.2 us
    unnamed x24, local copies, waits for them, and re-layouts  21.8 us
    reduce_sum x4, other arithmetic, smooth_refresh(): totals = totals * factor + weights.sum(axis=-1)  20 us
    gather x2, local copies, waits for them, and re-layouts, attend_group(): jnp.take(all_values, joint_item.reshape(-1), axis=0)  17.1 us
  transfers between devices with their start and end apart: 7, of which 3 were waited for; matrix products, arithmetic and copies ran while one was open for 29% of the time, Pallas kernels for 0%

commit v1 on v0

v1 whole, which is shorter than its diff:
```python
import jax
import jax.numpy as jnp
from jax import lax
from jax.experimental import pallas as pl
from jax.experimental.pallas import tpu as pltpu
from jax.sharding import PartitionSpec as P

HD = 128
BLOCK = 128
POOL = 4
CAP = 2
SCALE = HD ** (-0.5)
DRAFT_ROWS = 128


def pool_tokens(matrix):
    grouped = matrix.astype(jnp.float32).reshape(matrix.shape[0] // POOL, POOL, matrix.shape[1])
    return (grouped.sum(axis=1) * POOL ** (-0.5)).astype(jnp.bfloat16)


def _scores(q, k):
    return lax.dot_general(
        q, k, (((1,), (1,)), ((), ())), preferred_element_type=jnp.float32
    ) * SCALE


def sparse_kernel(tbl_ref, q_ref, k_ref, v_ref, o_ref, s_ref):
    per_dev = q_ref.shape[0] // BLOCK
    sel = s_ref.shape[1] // BLOCK

    def body(i, carry):
        row = pl.multiple_of(i * BLOCK, BLOCK)
        q = q_ref[pl.ds(row, BLOCK), :]
        for j in range(sel):
            idx = tbl_ref[i * sel + j]
            k = k_ref[pl.ds(pl.multiple_of(idx * BLOCK, BLOCK), BLOCK), :]
            s_ref[:, j * BLOCK:(j + 1) * BLOCK] = _scores(q, k)
        s = s_ref[...]
        running = jnp.max(s, axis=1, keepdims=True)
        weights = jnp.exp(s - running)
        totals = jnp.sum(weights, axis=1, keepdims=True)
        rounded = weights.astype(jnp.bfloat16)
        acc = jnp.zeros((BLOCK, HD), jnp.float32)
        for j in range(sel):
            idx = tbl_ref[i * sel + j]
            v = v_ref[pl.ds(pl.multiple_of(idx * BLOCK, BLOCK), BLOCK), :]
            acc = acc + jnp.dot(
                rounded[:, j * BLOCK:(j + 1) * BLOCK], v, preferred_element_type=jnp.float32
            )
        o_ref[pl.ds(row, BLOCK), :] = (acc / totals).astype(o_ref.dtype)
        return carry

    lax.fori_loop(0, per_dev, body, 0)


def sparse_attention(tbl, queries, keys, values, sel):
    rows, width = queries.shape
    heads = width // HD
    key_rows = keys.shape[0]
    return pl.pallas_call(
        sparse_kernel,
        out_shape=jax.ShapeDtypeStruct((rows, width), jnp.bfloat16),
        grid_spec=pltpu.PrefetchScalarGridSpec(
            num_scalar_prefetch=1,
            grid=(heads,),
            in_specs=[
                pl.BlockSpec((rows, HD), lambda h, t: (0, h)),
                pl.BlockSpec((key_rows, HD), lambda h, t: (0, h)),
                pl.BlockSpec((key_rows, HD), lambda h, t: (0, h)),
            ],
            out_specs=pl.BlockSpec((rows, HD), lambda h, t: (0, h)),
            scratch_shapes=[pltpu.VMEM((BLOCK, sel * BLOCK), jnp.float32)],
        ),
    )(tbl, queries, keys, values)


def draft_kernel(q_ref, k_ref, v_ref, o_ref):
    s = _scores(q_ref[...], k_ref[...])
    running = jnp.max(s, axis=1, keepdims=True)
    weights = jnp.exp(s - running)
    totals = jnp.sum(weights, axis=1, keepdims=True)
    weighted = jnp.dot(weights.astype(jnp.bfloat16), v_ref[...], preferred_element_type=jnp.float32)
    o_ref[...] = (weighted / totals).astype(o_ref.dtype)


def draft_attention(queries, keys, values):
    rows, width = queries.shape
    heads = width // HD
    key_rows = keys.shape[0]
    tile = min(DRAFT_ROWS, rows)
    return pl.pallas_call(
        draft_kernel,
        out_shape=jax.ShapeDtypeStruct((rows, width), jnp.bfloat16),
        grid=(heads, rows // tile),
        in_specs=[
            pl.BlockSpec((tile, HD), lambda h, r: (r, h)),
            pl.BlockSpec((key_rows, HD), lambda h, r: (0, h)),
            pl.BlockSpec((key_rows, HD), lambda h, r: (0, h)),
        ],
        out_specs=pl.BlockSpec((tile, HD), lambda h, r: (r, h)),
    )(queries, keys, values)


def on_device(query_in, key_in, value_in, block_lists):
    key_rows = lax.all_to_all(key_in, "head", split_axis=1, concat_axis=0, tiled=True)
    value_rows = lax.all_to_all(value_in, "head", split_axis=1, concat_axis=0, tiled=True)
    queries = lax.all_to_all(query_in, "head", split_axis=1, concat_axis=0, tiled=True)
    seq_rows, width = queries.shape

    draft_keys = lax.all_gather(pool_tokens(key_rows), "seq", axis=0, tiled=True)
    draft_values = lax.all_gather(pool_tokens(value_rows), "seq", axis=0, tiled=True)

    seq_count = lax.axis_size("seq")
    seq_index = lax.axis_index("seq")
    per_dev = seq_rows // BLOCK
    block_total, select_count = block_lists.shape
    block_ids = jnp.arange(block_total, dtype=jnp.int32)
    touched = jnp.any(block_lists[:, :, None] == block_ids[None, None, :], axis=1)
    needed = jnp.any(touched.reshape(seq_count, per_dev, seq_count, per_dev), axis=1)
    slot_rank = jnp.cumsum(needed.astype(jnp.int32), axis=2) - 1
    send_need = lax.dynamic_index_in_dim(needed, seq_index, axis=1, keepdims=False)
    send_rank = lax.dynamic_index_in_dim(slot_rank, seq_index, axis=1, keepdims=False)
    slot_hit = send_need[:, None, :] & (
        send_rank[:, None, :] == jnp.arange(CAP, dtype=jnp.int32)[None, :, None]
    )
    send_idx = jnp.sum(
        jnp.where(slot_hit, jnp.arange(per_dev, dtype=jnp.int32)[None, None, :], 0), axis=2
    ).reshape(-1)
    key_blocks = key_rows.reshape(per_dev, BLOCK, width)
    value_blocks = value_rows.reshape(per_dev, BLOCK, width)
    outgoing = jnp.stack(
        [jnp.take(key_blocks, send_idx, axis=0), jnp.take(value_blocks, send_idx, axis=0)], axis=1
    ).reshape(seq_count, CAP, 2, BLOCK, width)
    arrived = lax.all_to_all(outgoing, "seq", split_axis=0, concat_axis=0, tiled=True)
    remote_keys = arrived[:, :, 0].reshape(seq_count * CAP * BLOCK, width)
    remote_values = arrived[:, :, 1].reshape(seq_count * CAP * BLOCK, width)
    all_keys = jnp.concatenate([key_rows, remote_keys], axis=0)
    all_values = jnp.concatenate([value_rows, remote_values], axis=0)

    own_lists = lax.dynamic_slice_in_dim(block_lists, seq_index * per_dev, per_dev, 0)
    owners = own_lists // per_dev
    within = own_lists % per_dev
    own_rank = lax.dynamic_index_in_dim(slot_rank, seq_index, axis=0, keepdims=False)
    ranks_used = jnp.clip(own_rank[owners, within], 0, CAP - 1)
    joint_pos = jnp.where(owners == seq_index, within, per_dev + owners * CAP + ranks_used)
    table = jnp.clip(joint_pos, 0, per_dev + seq_count * CAP - 1).reshape(-1).astype(jnp.int32)

    sparse_rows = sparse_attention(table, queries, all_keys, all_values, select_count)
    sparse_out = lax.all_to_all(sparse_rows, "head", split_axis=0, concat_axis=1, tiled=True)

    draft_out = draft_attention(pool_tokens(queries), draft_keys, draft_values)
    return (draft_out, sparse_out)


def solution(mesh):
    return jax.shard_map(
        on_device,
        mesh=mesh,
        in_specs=(
            P(("groups", "seq", "head"), None),
            P(("groups", "seq", "head"), None),
            P(("groups", "seq", "head"), None),
            P("groups", None),
        ),
        out_specs=(P(("groups", "seq"), "head"), P(("groups", "seq", "head"), None)),
        check_vma=False,
    )
```

time: 416 us -> 292 us (0.70); the launches traced: 410 us -> 290 us
  local copies, waits for them, and re-layouts: 161 us -> 30.7 us
  Pallas kernels: 0 us -> 59.8 us
  matrix products: 50.7 us -> 0 us
  waiting for transfers between devices: 77.6 us -> 128 us
  other arithmetic: 83 us -> 33.6 us
    pallas_call x0 -> x2, Pallas kernels: none -> 59.8 us  [the longest x1 49 us: sparse_attention(): pl.pallas_call(sparse_kernel, out_shape=jax.ShapeDtypeStruct((rows, width...]
    dot_general x9 -> x0, matrix products: 50.7 us -> none  [the longest x4 27.9 us: smooth_refresh(): jnp.einsum(value_form, weights.astype(jnp.bfloat16), value_rows, preferre...]
    gather x8 -> x3, local copies, waits for them, and re-layouts: 36.8 us -> 5.12 us  [the longest x1 1.8 us: on_device(): jnp.take(value_blocks, send_idx, axis=0)]
    all_to_all x1, waiting for transfers between devices: 0.01 us -> 29.3 us  [on_device(): lax.all_to_all(outgoing, 'seq', split_axis=0, concat_axis=0, tiled=True)]
    select_n x7 -> x2, other arithmetic: 28.5 us -> 2.23 us  [on_device(): jnp.take(key_blocks, send_idx, axis=0)]
    unnamed x24 -> x6, local copies, waits for them, and re-layouts: 21.8 us -> 0.1 us
    reduce_sum x4 -> x1, other arithmetic: 20 us -> 0.14 us  [on_device(): jnp.sum(jnp.where(slot_hit, jnp.arange(per_dev, dtype=jnp.int32)[None, No...]
    while x32 -> x0, local copies, waits for them, and re-layouts: 18.1 us -> none  [the longest x2 11.8 us: on_device(): lax.scan(attend_group, jnp.zeros((), jnp.int32), group_pack)]
  transfers between devices with their start and end apart: 7 -> 7, of which waited for: 3 -> 5; matrix products, arithmetic and copies ran while one was open for 29% -> 18% of each run, Pallas kernels for 0% -> 21%
where the time goes in v1:
time: 292 us; the launch traced here: 290 us
  waiting for transfers between devices  128 us (44%)
  Pallas kernels  59.8 us (20%)
  other arithmetic  33.6 us (12%)
  local copies, waits for them, and re-layouts  30.7 us (11%)
  starting transfers between devices  23.8 us (8%)
  between operations  14.2 us (5%)
    pallas_call x1, Pallas kernels, sparse_attention(): pl.pallas_call(sparse_kernel, out_shape=jax.ShapeDtypeStruct((rows, width...  49 us
    all_to_all x1, waiting for transfers between devices, on_device(): lax.all_to_all(key_in, 'head', split_axis=1, concat_axis=0, tiled=True)  35.7 us
    all_to_all x1, waiting for transfers between devices, on_device(): lax.all_to_all(value_in, 'head', split_axis=1, concat_axis=0, tiled=True)  33.2 us
    all_to_all x1, waiting for transfers between devices, on_device(): lax.all_to_all(outgoing, 'seq', split_axis=0, concat_axis=0, tiled=True)  29.3 us
    all_to_all x1, waiting for transfers between devices, on_device(): lax.all_to_all(query_in, 'head', split_axis=1, concat_axis=0, tiled=True)  15.9 us
    all_to_all x1, waiting for transfers between devices, on_device(): lax.all_to_all(sparse_rows, 'head', split_axis=0, concat_axis=1, tiled=True)  14.2 us
    convert_element_type x3, local copies, waits for them, and re-layouts, pool_tokens(): matrix.astype(jnp.float32)  12.8 us
    reduce_sum x3, other arithmetic, pool_tokens(): return (grouped.sum(axis=1) * POOL ** (-0.5)).astype(jnp.bfloat16)  12.2 us
  transfers between devices with their start and end apart: 7, of which 5 were waited for; matrix products, arithmetic and copies ran while one was open for 18% of the time, Pallas kernels for 21%

profile of v1, /device:TPU:0, one launch (start us, length us, event | category | flops | bytes accessed | tf_op | source)
XLA Modules:
  0.0 290.4 jit_solution(10245101671541912426)
XLA Ops:
  7.2 2.7 copy.50
  9.8 6.4 %all-to-all-start.1 = ((bf16[256,4,768]{2,0,1:T(8,128)(2,1)}), bf16[256,4,768]{2,0,1:T(8,128)(2,1)S(1)}, u32[]{:S(2)}, u32[]{:S(2)}) async-start(bf16[256,4,768]{2,0,1:T(8,128)(2,1)} %bitcast.39), calls=%async_computation.1 | async-start | bytes 3145728 | tf_op jit(solution)/shard_map/all_to_all | solution.py:105
  17.5 35.7 %all-to-all-done.1 = bf16[256,4,768]{2,0,1:T(8,128)(2,1)S(1)} async-done(((bf16[256,4,768]{2,0,1:T(8,128)(2,1)}), bf16[256,4,768]{2,0,1:T(8,128)(2,1)S(1)}, u32[]{:S(2)}, u32[]{:S(2)}) %all-to-all-start.1) | async-done | bytes 1572896 | tf_op jit(solution)/shard_map/all_to_all | solution.py:105
  53.2 3.7 %all-to-all-start.2 = ((bf16[256,4,768]{2,0,1:T(8,128)(2,1)}), bf16[256,4,768]{2,0,1:T(8,128)(2,1)S(1)}, u32[]{:S(2)}, u32[]{:S(2)}) async-start(bf16[256,4,768]{2,0,1:T(8,128)(2,1)} %bitcast.47), calls=%async_computation.2 | async-start | bytes 3145728 | tf_op jit(solution)/shard_map/all_to_all | solution.py:106
  60.1 33.2 %all-to-all-done.2 = bf16[256,4,768]{2,0,1:T(8,128)(2,1)S(1)} async-done(((bf16[256,4,768]{2,0,1:T(8,128)(2,1)}), bf16[256,4,768]{2,0,1:T(8,128)(2,1)S(1)}, u32[]{:S(2)}, u32[]{:S(2)}) %all-to-all-start.2) | async-done | bytes 1572896 | tf_op jit(solution)/shard_map/all_to_all | solution.py:106
  95.2 2.2 broadcast_select_fusion.1
  99.4 4.6 %all-to-all-start.3 = ((bf16[4,2,2,128,768]{4,3,1,2,0:T(8,128)(2,1)}), bf16[4,2,2,128,768]{4,3,1,2,0:T(8,128)(2,1)}, u32[]{:S(2)}, u32[]{:S(2)}) async-start(bf16[4,2,2,128,768]{4,3,1,2,0:T(8,128)(2,1)} %pad_maximum_fusion), calls=%async_computation.3 | async-start | bytes 6291456 | tf_op jit(solution)/shard_map/all_to_all | solution.py:134
  106.0 4.8 %reshape.62 = f32[256,4,768]{2,1,0:T(4,128)} reshape(f32[4,256,768]{2,1,0:T(8,128)} %bitcast_convert_fusion.1) | data formatting | bytes 6291456 | tf_op jit(solution)/shard_map/convert_element_type | solution.py:17
  110.9 4.6 %reduce_sum.37 = f32[256,768]{1,0:T(8,128)} reduce(f32[256,4,768]{2,1,0:T(4,128)} %reshape.62, f32[]{:T(128)} %constant.47.clone.1), dimensions={1}, to_apply=%region_1.0 | reduce | flops 589824 | bytes 3932164 | tf_op jit(solution)/shard_map/reduce_sum | solution.py:18
  117.5 2.7 copy.51
  120.1 29.3 %all-to-all-done.3 = bf16[4,2,2,128,768]{4,3,1,2,0:T(8,128)(2,1)} async-done(((bf16[4,2,2,128,768]{4,3,1,2,0:T(8,128)(2,1)}), bf16[4,2,2,128,768]{4,3,1,2,0:T(8,128)(2,1)}, u32[]{:S(2)}, u32[]{:S(2)}) %all-to-all-start.3) | async-done | bytes 3145760 | tf_op jit(solution)/shard_map/all_to_all | solution.py:134
  149.5 4.4 %all-to-all-start = ((bf16[256,4,768]{2,0,1:T(8,128)(2,1)}), bf16[256,4,768]{2,0,1:T(8,128)(2,1)}, u32[]{:S(2)}, u32[]{:S(2)}) async-start(bf16[256,4,768]{2,0,1:T(8,128)(2,1)} %bitcast.46), calls=%async_computation | async-start | bytes 3145728 | tf_op jit(solution)/shard_map/all_to_all | solution.py:107
  158.4 4.9 %reshape.63 = f32[256,4,768]{2,1,0:T(4,128)} reshape(f32[4,256,768]{2,1,0:T(8,128)} %bitcast_convert_fusion) | data formatting | bytes 6291456 | tf_op jit(solution)/shard_map/convert_element_type | solution.py:17
  163.2 4.6 %reduce_sum.38 = f32[256,768]{1,0:T(8,128)} reduce(f32[256,4,768]{2,1,0:T(4,128)} %reshape.63, f32[]{:T(128)} %constant.47.clone.1), dimensions={1}, to_apply=%region_2.0 | reduce | flops 589824 | bytes 3932164 | tf_op jit(solution)/shard_map/reduce_sum | solution.py:18
  172.0 3.0 %pad_maximum_fusion.1 = (bf16[2048,768]{1,0:T(8,128)(2,1)}, bf16[2048,768]{1,0:T(8,128)(2,1)}) fusion(bf16[1024,768]{1,0:T(8,128)(2,1)S(1)} %bitcast.50, bf16[1024,768]{1,0:T(8,128)(2,1)S(1)} %bitcast.43, bf16[1024,768]{1,0:T(8,128)(2,1)S(1)} %bitcast.49, bf16[1024,768]{1,0:T(8,128)(2,1)S(1)} %bitcast.45), kind=kLoop, calls=%fused_computation.4 | loop fusion | flops 12582912 | bytes 12582912 | tf_op jit(solution)/shard_map/concatenate | solution.py:137
  175.0 15.9 %all-to-all-done = bf16[256,4,768]{2,0,1:T(8,128)(2,1)} async-done(((bf16[256,4,768]{2,0,1:T(8,128)(2,1)}), bf16[256,4,768]{2,0,1:T(8,128)(2,1)}, u32[]{:S(2)}, u32[]{:S(2)}) %all-to-all-start) | async-done | bytes 1572896 | tf_op jit(solution)/shard_map/all_to_all | solution.py:107
  190.9 49.0 %shard_map.60 = bf16[1024,768]{1,0:T(8,128)(2,1)} custom-call(s32[96]{0:T(128)} %reshape.57.tbl_ref, bf16[1024,768]{1,0:T(8,128)(2,1)} %bitcast.4.q_ref, bf16[2048,768]{1,0:T(8,128)(2,1)} %get-tuple-element.7.k_ref, bf16[2048,768]{1,0:T(8,128)(2,1)} %get-tuple-element.8.v_ref), custom_call_target="tpu_custom_call" | custom-call | tf_op jit(solution)/shard_map/pallas_call | solution.py:60
  239.9 4.5 %all-to-all-start.4 = ((bf16[4,256,768]{2,1,0:T(8,128)(2,1)}), bf16[4,256,768]{2,1,0:T(8,128)(2,1)}, u32[]{:S(2)}, u32[]{:S(2)}) async-start(bf16[4,256,768]{2,1,0:T(8,128)(2,1)} %bitcast.48), calls=%async_computation.4 | async-start | bytes 3145728 | tf_op jit(solution)/shard_map/all_to_all | solution.py:149
  244.5 3.3 %bitcast_convert_fusion.2 = f32[4,256,768]{2,1,0:T(8,128)} fusion(bf16[256,4,768]{2,0,1:T(8,128)(2,1)} %all-to-all-done), kind=kLoop, calls=%fused_computation.11 | loop fusion | flops 786432 | bytes 4718592 | tf_op jit(solution)/shard_map/convert_element_type | solution.py:17
  247.8 3.1 %reshape.61 = f32[256,4,768]{2,1,0:T(4,128)S(1)} reshape(f32[4,256,768]{2,1,0:T(8,128)} %bitcast_convert_fusion.2) | data formatting | bytes 6291456 | tf_op jit(solution)/shard_map/convert_element_type | solution.py:17
  250.9 3.0 %reduce_sum.36 = f32[256,768]{1,0:T(8,128)} reduce(f32[256,4,768]{2,1,0:T(4,128)S(1)} %reshape.61, f32[]{:T(128)} %constant.47.clone.1), dimensions={1}, to_apply=%region_0.0 | reduce | flops 589824 | bytes 3932164 | tf_op jit(solution)/shard_map/reduce_sum | solution.py:18
  255.8 10.8 %shard_map.59 = bf16[256,768]{1,0:T(8,128)(2,1)} custom-call(bf16[256,768]{1,0:T(8,128)(2,1)} %multiply_convert_fusion.2.q_ref, bf16[1024,768]{1,0:T(8,128)(2,1)} %all-gather.3.cloned.1.call-done.k_ref, bf16[1024,768]{1,0:T(8,128)(2,1)} %all-gather.5.cloned.1.call-done.v_ref), custom_call_target="tpu_custom_call" | custom-call | tf_op jit(solution)/shard_map/pallas_call | solution.py:91
  266.7 14.2 %all-to-all-done.4 = bf16[4,256,768]{2,1,0:T(8,128)(2,1)} async-done(((bf16[4,256,768]{2,1,0:T(8,128)(2,1)}), bf16[4,256,768]{2,1,0:T(8,128)(2,1)}, u32[]{:S(2)}, u32[]{:S(2)}) %all-to-all-start.4) | async-done | bytes 1572896 | tf_op jit(solution)/shard_map/all_to_all | solution.py:149
  280.8 2.7 copy.44
  (45 shorter events, 22.7 us)
Async XLA Ops:
  9.8 6.5 %copy-start = (bf16[256,3072]{1,0:T(8,128)(2,1)S(1)}, bf16[256,3072]{1,0:T(8,128)(2,1)}, u32[]{:S(2)}) copy-start(bf16[256,3072]{1,0:T(8,128)(2,1)} %param.8) | copy-start | bytes 4718596
  9.8 43.4 %all-to-all-start.1 = ((bf16[256,4,768]{2,0,1:T(8,128)(2,1)}), bf16[256,4,768]{2,0,1:T(8,128)(2,1)S(1)}, u32[]{:S(2)}, u32[]{:S(2)}) async-start(bf16[256,4,768]{2,0,1:T(8,128)(2,1)} %bitcast.39), calls=%async_computation.1 | async-start | bytes 3145728 | tf_op jit(solution)/shard_map/all_to_all | solution.py:105
  53.2 3.7 %copy-start.1 = (s32[32,12]{0,1:T(8,128)S(1)}, s32[32,12]{0,1:T(8,128)}, u32[]{:S(2)}) copy-start(s32[32,12]{0,1:T(8,128)} %param.9) | copy-start | bytes 4612
  53.2 40.1 %all-to-all-start.2 = ((bf16[256,4,768]{2,0,1:T(8,128)(2,1)}), bf16[256,4,768]{2,0,1:T(8,128)(2,1)S(1)}, u32[]{:S(2)}, u32[]{:S(2)}) async-start(bf16[256,4,768]{2,0,1:T(8,128)(2,1)} %bitcast.47), calls=%async_computation.2 | async-start | bytes 3145728 | tf_op jit(solution)/shard_map/all_to_all | solution.py:106
  99.4 50.1 %all-to-all-start.3 = ((bf16[4,2,2,128,768]{4,3,1,2,0:T(8,128)(2,1)}), bf16[4,2,2,128,768]{4,3,1,2,0:T(8,128)(2,1)}, u32[]{:S(2)}, u32[]{:S(2)}) async-start(bf16[4,2,2,128,768]{4,3,1,2,0:T(8,128)(2,1)} %pad_maximum_fusion), calls=%async_computation.3 | async-start | bytes 6291456 | tf_op jit(solution)/shard_map/all_to_all | solution.py:134
  104.0 151.8 %all-gather.3.cloned.1.call-start = ((), (), s32[]{:S(2)}) async-start(), calls=%async_computation.5 | async-start | bytes 1966080 | tf_op jit(solution)/shard_map/all_gather | solution.py:110
  149.5 41.5 %all-to-all-start = ((bf16[256,4,768]{2,0,1:T(8,128)(2,1)}), bf16[256,4,768]{2,0,1:T(8,128)(2,1)}, u32[]{:S(2)}, u32[]{:S(2)}) async-start(bf16[256,4,768]{2,0,1:T(8,128)(2,1)} %bitcast.46), calls=%async_computation | async-start | bytes 3145728 | tf_op jit(solution)/shard_map/all_to_all | solution.py:107
  153.8 102.0 %all-gather.5.cloned.1.call-start = ((), (), s32[]{:S(2)}) async-start(), calls=%async_computation.6 | async-start | bytes 1966080 | tf_op jit(solution)/shard_map/all_gather | solution.py:111
  239.9 40.9 %all-to-all-start.4 = ((bf16[4,256,768]{2,1,0:T(8,128)(2,1)}), bf16[4,256,768]{2,1,0:T(8,128)(2,1)}, u32[]{:S(2)}, u32[]{:S(2)}) async-start(bf16[4,256,768]{2,1,0:T(8,128)(2,1)} %bitcast.48), calls=%async_computation.4 | async-start | bytes 3145728 | tf_op jit(solution)/shard_map/all_to_all | solution.py:149
Sparse Core Ops, SparseCore 0:
  117.6 27.7 all-gather.2
  170.0 20.0 all-gather.4

commit v2 on v1

--- a/solution.py
+++ b/solution.py
@@ -24,30 +24,24 @@
     ) * SCALE
 
 
-def sparse_kernel(tbl_ref, q_ref, k_ref, v_ref, o_ref, s_ref):
+def sparse_kernel(tbl_ref, q_ref, k_ref, v_ref, o_ref, ks_ref, vs_ref):
     per_dev = q_ref.shape[0] // BLOCK
-    sel = s_ref.shape[1] // BLOCK
+    sel = ks_ref.shape[0] // BLOCK
 
     def body(i, carry):
         row = pl.multiple_of(i * BLOCK, BLOCK)
-        q = q_ref[pl.ds(row, BLOCK), :]
         for j in range(sel):
-            idx = tbl_ref[i * sel + j]
-            k = k_ref[pl.ds(pl.multiple_of(idx * BLOCK, BLOCK), BLOCK), :]
-            s_ref[:, j * BLOCK:(j + 1) * BLOCK] = _scores(q, k)
-        s = s_ref[...]
+            start = pl.multiple_of(tbl_ref[i * sel + j] * BLOCK, BLOCK)
+            ks_ref[j * BLOCK:(j + 1) * BLOCK, :] = k_ref[pl.ds(start, BLOCK), :]
+            vs_ref[j * BLOCK:(j + 1) * BLOCK, :] = v_ref[pl.ds(start, BLOCK), :]
+        s = _scores(q_ref[pl.ds(row, BLOCK), :], ks_ref[...])
         running = jnp.max(s, axis=1, keepdims=True)
         weights = jnp.exp(s - running)
         totals = jnp.sum(weights, axis=1, keepdims=True)
-        rounded = weights.astype(jnp.bfloat16)
-        acc = jnp.zeros((BLOCK, HD), jnp.float32)
-        for j in range(sel):
-            idx = tbl_ref[i * sel + j]
-            v = v_ref[pl.ds(pl.multiple_of(idx * BLOCK, BLOCK), BLOCK), :]
-            acc = acc + jnp.dot(
-                rounded[:, j * BLOCK:(j + 1) * BLOCK], v, preferred_element_type=jnp.float32
-            )
-        o_ref[pl.ds(row, BLOCK), :] = (acc / totals).astype(o_ref.dtype)
+        weighted = jnp.dot(
+            weights.astype(jnp.bfloat16), vs_ref[...], preferred_element_type=jnp.float32
+        )
+        o_ref[pl.ds(row, BLOCK), :] = (weighted / totals).astype(o_ref.dtype)
         return carry
 
     lax.fori_loop(0, per_dev, body, 0)
@@ -69,7 +63,10 @@
                 pl.BlockSpec((key_rows, HD), lambda h, t: (0, h)),
             ],
             out_specs=pl.BlockSpec((rows, HD), lambda h, t: (0, h)),
-            scratch_shapes=[pltpu.VMEM((BLOCK, sel * BLOCK), jnp.float32)],
+            scratch_shapes=[
+                pltpu.VMEM((sel * BLOCK, HD), jnp.bfloat16),
+                pltpu.VMEM((sel * BLOCK, HD), jnp.bfloat16),
+            ],
         ),
     )(tbl, queries, keys, values)
 

time: 292 us -> 277 us (0.949)
  Pallas kernels: 59.8 us -> 45.2 us
    pallas_call x1, Pallas kernels: 49 us -> 34.4 us  [sparse_attention(): pl.pallas_call(sparse_kernel, out_shape=jax.ShapeDtypeStruct((rows, width...]
  transfers between devices with their start and end apart: 7 -> 7, of which waited for: 5 -> 5; matrix products, arithmetic and copies ran while one was open for 18% -> 19% of each run, Pallas kernels for 21% -> 16%
where the time goes in v2:
time: 277 us; the launch traced here: 276 us
  waiting for transfers between devices  128 us (46%)
  Pallas kernels  45.2 us (16%)
  other arithmetic  33.6 us (12%)
  local copies, waits for them, and re-layouts  30.7 us (11%)
  starting transfers between devices  23.8 us (9%)
  between operations  14.2 us (5%)
    all_to_all x1, waiting for transfers between devices, on_device(): lax.all_to_all(key_in, 'head', split_axis=1, concat_axis=0, tiled=True)  35.7 us
    pallas_call x1, Pallas kernels, sparse_attention(): pl.pallas_call(sparse_kernel, out_shape=jax.ShapeDtypeStruct((rows, width...  34.4 us
    all_to_all x1, waiting for transfers between devices, on_device(): lax.all_to_all(value_in, 'head', split_axis=1, concat_axis=0, tiled=True)  33.2 us
    all_to_all x1, waiting for transfers between devices, on_device(): lax.all_to_all(outgoing, 'seq', split_axis=0, concat_axis=0, tiled=True)  29.3 us
    all_to_all x1, waiting for transfers between devices, on_device(): lax.all_to_all(query_in, 'head', split_axis=1, concat_axis=0, tiled=True)  15.9 us
    all_to_all x1, waiting for transfers between devices, on_device(): lax.all_to_all(sparse_rows, 'head', split_axis=0, concat_axis=1, tiled=True)  14.2 us
    convert_element_type x3, local copies, waits for them, and re-layouts, pool_tokens(): matrix.astype(jnp.float32)  12.8 us
    reduce_sum x3, other arithmetic, pool_tokens(): return (grouped.sum(axis=1) * POOL ** (-0.5)).astype(jnp.bfloat16)  12.2 us
  transfers between devices with their start and end apart: 7, of which 5 were waited for; matrix products, arithmetic and copies ran while one was open for 19% of the time, Pallas kernels for 16%

profile of v2, /device:TPU:0, one launch (start us, length us, event | category | flops | bytes accessed | tf_op | source)
XLA Modules:
  0.0 275.8 jit_solution(600061140351018414)
XLA Ops:
  7.2 2.7 copy.50
  9.8 6.4 %all-to-all-start.1 = ((bf16[256,4,768]{2,0,1:T(8,128)(2,1)}), bf16[256,4,768]{2,0,1:T(8,128)(2,1)S(1)}, u32[]{:S(2)}, u32[]{:S(2)}) async-start(bf16[256,4,768]{2,0,1:T(8,128)(2,1)} %bitcast.39), calls=%async_computation.1 | async-start | bytes 3145728 | tf_op jit(solution)/shard_map/all_to_all | solution.py:102
  17.5 35.7 %all-to-all-done.1 = bf16[256,4,768]{2,0,1:T(8,128)(2,1)S(1)} async-done(((bf16[256,4,768]{2,0,1:T(8,128)(2,1)}), bf16[256,4,768]{2,0,1:T(8,128)(2,1)S(1)}, u32[]{:S(2)}, u32[]{:S(2)}) %all-to-all-start.1) | async-done | bytes 1572896 | tf_op jit(solution)/shard_map/all_to_all | solution.py:102
  53.2 3.7 %all-to-all-start.2 = ((bf16[256,4,768]{2,0,1:T(8,128)(2,1)}), bf16[256,4,768]{2,0,1:T(8,128)(2,1)S(1)}, u32[]{:S(2)}, u32[]{:S(2)}) async-start(bf16[256,4,768]{2,0,1:T(8,128)(2,1)} %bitcast.47), calls=%async_computation.2 | async-start | bytes 3145728 | tf_op jit(solution)/shard_map/all_to_all | solution.py:103
  60.1 33.2 %all-to-all-done.2 = bf16[256,4,768]{2,0,1:T(8,128)(2,1)S(1)} async-done(((bf16[256,4,768]{2,0,1:T(8,128)(2,1)}), bf16[256,4,768]{2,0,1:T(8,128)(2,1)S(1)}, u32[]{:S(2)}, u32[]{:S(2)}) %all-to-all-start.2) | async-done | bytes 1572896 | tf_op jit(solution)/shard_map/all_to_all | solution.py:103
  95.2 2.2 broadcast_select_fusion.1
  99.4 4.6 %all-to-all-start.3 = ((bf16[4,2,2,128,768]{4,3,1,2,0:T(8,128)(2,1)}), bf16[4,2,2,128,768]{4,3,1,2,0:T(8,128)(2,1)}, u32[]{:S(2)}, u32[]{:S(2)}) async-start(bf16[4,2,2,128,768]{4,3,1,2,0:T(8,128)(2,1)} %pad_maximum_fusion), calls=%async_computation.3 | async-start | bytes 6291456 | tf_op jit(solution)/shard_map/all_to_all | solution.py:131
  106.0 4.8 %reshape.62 = f32[256,4,768]{2,1,0:T(4,128)} reshape(f32[4,256,768]{2,1,0:T(8,128)} %bitcast_convert_fusion.1) | data formatting | bytes 6291456 | tf_op jit(solution)/shard_map/convert_element_type | solution.py:17
  110.9 4.6 %reduce_sum.37 = f32[256,768]{1,0:T(8,128)} reduce(f32[256,4,768]{2,1,0:T(4,128)} %reshape.62, f32[]{:T(128)} %constant.47.clone.1), dimensions={1}, to_apply=%region_1.0 | reduce | flops 589824 | bytes 3932164 | tf_op jit(solution)/shard_map/reduce_sum | solution.py:18
  117.5 2.7 copy.51
  120.1 29.3 %all-to-all-done.3 = bf16[4,2,2,128,768]{4,3,1,2,0:T(8,128)(2,1)} async-done(((bf16[4,2,2,128,768]{4,3,1,2,0:T(8,128)(2,1)}), bf16[4,2,2,128,768]{4,3,1,2,0:T(8,128)(2,1)}, u32[]{:S(2)}, u32[]{:S(2)}) %all-to-all-start.3) | async-done | bytes 3145760 | tf_op jit(solution)/shard_map/all_to_all | solution.py:131
  149.5 4.4 %all-to-all-start = ((bf16[256,4,768]{2,0,1:T(8,128)(2,1)}), bf16[256,4,768]{2,0,1:T(8,128)(2,1)}, u32[]{:S(2)}, u32[]{:S(2)}) async-start(bf16[256,4,768]{2,0,1:T(8,128)(2,1)} %bitcast.46), calls=%async_computation | async-start | bytes 3145728 | tf_op jit(solution)/shard_map/all_to_all | solution.py:104
  158.4 4.9 %reshape.63 = f32[256,4,768]{2,1,0:T(4,128)} reshape(f32[4,256,768]{2,1,0:T(8,128)} %bitcast_convert_fusion) | data formatting | bytes 6291456 | tf_op jit(solution)/shard_map/convert_element_type | solution.py:17
  163.2 4.6 %reduce_sum.38 = f32[256,768]{1,0:T(8,128)} reduce(f32[256,4,768]{2,1,0:T(4,128)} %reshape.63, f32[]{:T(128)} %constant.47.clone.1), dimensions={1}, to_apply=%region_2.0 | reduce | flops 589824 | bytes 3932164 | tf_op jit(solution)/shard_map/reduce_sum | solution.py:18
  172.0 3.0 %pad_maximum_fusion.1 = (bf16[2048,768]{1,0:T(8,128)(2,1)}, bf16[2048,768]{1,0:T(8,128)(2,1)}) fusion(bf16[1024,768]{1,0:T(8,128)(2,1)S(1)} %bitcast.50, bf16[1024,768]{1,0:T(8,128)(2,1)S(1)} %bitcast.43, bf16[1024,768]{1,0:T(8,128)(2,1)S(1)} %bitcast.49, bf16[1024,768]{1,0:T(8,128)(2,1)S(1)} %bitcast.45), kind=kLoop, calls=%fused_computation.4 | loop fusion | flops 12582912 | bytes 12582912 | tf_op jit(solution)/shard_map/concatenate | solution.py:134
  175.0 15.9 %all-to-all-done = bf16[256,4,768]{2,0,1:T(8,128)(2,1)} async-done(((bf16[256,4,768]{2,0,1:T(8,128)(2,1)}), bf16[256,4,768]{2,0,1:T(8,128)(2,1)}, u32[]{:S(2)}, u32[]{:S(2)}) %all-to-all-start) | async-done | bytes 1572896 | tf_op jit(solution)/shard_map/all_to_all | solution.py:104
  190.9 34.4 %shard_map.60 = bf16[1024,768]{1,0:T(8,128)(2,1)} custom-call(s32[96]{0:T(128)} %reshape.57.tbl_ref, bf16[1024,768]{1,0:T(8,128)(2,1)} %bitcast.4.q_ref, bf16[2048,768]{1,0:T(8,128)(2,1)} %get-tuple-element.7.k_ref, bf16[2048,768]{1,0:T(8,128)(2,1)} %get-tuple-element.8.v_ref), custom_call_target="tpu_custom_call" | custom-call | tf_op jit(solution)/shard_map/pallas_call | solution.py:54
  225.3 4.5 %all-to-all-start.4 = ((bf16[4,256,768]{2,1,0:T(8,128)(2,1)}), bf16[4,256,768]{2,1,0:T(8,128)(2,1)}, u32[]{:S(2)}, u32[]{:S(2)}) async-start(bf16[4,256,768]{2,1,0:T(8,128)(2,1)} %bitcast.48), calls=%async_computation.4 | async-start | bytes 3145728 | tf_op jit(solution)/shard_map/all_to_all | solution.py:146
  229.8 3.3 %bitcast_convert_fusion.2 = f32[4,256,768]{2,1,0:T(8,128)} fusion(bf16[256,4,768]{2,0,1:T(8,128)(2,1)} %all-to-all-done), kind=kLoop, calls=%fused_computation.11 | loop fusion | flops 786432 | bytes 4718592 | tf_op jit(solution)/shard_map/convert_element_type | solution.py:17
  233.2 3.1 %reshape.61 = f32[256,4,768]{2,1,0:T(4,128)S(1)} reshape(f32[4,256,768]{2,1,0:T(8,128)} %bitcast_convert_fusion.2) | data formatting | bytes 6291456 | tf_op jit(solution)/shard_map/convert_element_type | solution.py:17
  236.3 3.0 %reduce_sum.36 = f32[256,768]{1,0:T(8,128)} reduce(f32[256,4,768]{2,1,0:T(4,128)S(1)} %reshape.61, f32[]{:T(128)} %constant.47.clone.1), dimensions={1}, to_apply=%region_0.0 | reduce | flops 589824 | bytes 3932164 | tf_op jit(solution)/shard_map/reduce_sum | solution.py:18
  241.2 10.8 %shard_map.59 = bf16[256,768]{1,0:T(8,128)(2,1)} custom-call(bf16[256,768]{1,0:T(8,128)(2,1)} %multiply_convert_fusion.2.q_ref, bf16[1024,768]{1,0:T(8,128)(2,1)} %all-gather.3.cloned.1.call-done.k_ref, bf16[1024,768]{1,0:T(8,128)(2,1)} %all-gather.5.cloned.1.call-done.v_ref), custom_call_target="tpu_custom_call" | custom-call | tf_op jit(solution)/shard_map/pallas_call | solution.py:88
  252.0 14.2 %all-to-all-done.4 = bf16[4,256,768]{2,1,0:T(8,128)(2,1)} async-done(((bf16[4,256,768]{2,1,0:T(8,128)(2,1)}), bf16[4,256,768]{2,1,0:T(8,128)(2,1)}, u32[]{:S(2)}, u32[]{:S(2)}) %all-to-all-start.4) | async-done | bytes 1572896 | tf_op jit(solution)/shard_map/all_to_all | solution.py:146
  266.2 2.7 copy.44
  (45 shorter events, 22.7 us)
Async XLA Ops:
  9.8 6.5 %copy-start = (bf16[256,3072]{1,0:T(8,128)(2,1)S(1)}, bf16[256,3072]{1,0:T(8,128)(2,1)}, u32[]{:S(2)}) copy-start(bf16[256,3072]{1,0:T(8,128)(2,1)} %param.8) | copy-start | bytes 4718596
  9.8 43.4 %all-to-all-start.1 = ((bf16[256,4,768]{2,0,1:T(8,128)(2,1)}), bf16[256,4,768]{2,0,1:T(8,128)(2,1)S(1)}, u32[]{:S(2)}, u32[]{:S(2)}) async-start(bf16[256,4,768]{2,0,1:T(8,128)(2,1)} %bitcast.39), calls=%async_computation.1 | async-start | bytes 3145728 | tf_op jit(solution)/shard_map/all_to_all | solution.py:102
  53.2 3.7 %copy-start.1 = (s32[32,12]{0,1:T(8,128)S(1)}, s32[32,12]{0,1:T(8,128)}, u32[]{:S(2)}) copy-start(s32[32,12]{0,1:T(8,128)} %param.9) | copy-start | bytes 4612
  53.2 40.1 %all-to-all-start.2 = ((bf16[256,4,768]{2,0,1:T(8,128)(2,1)}), bf16[256,4,768]{2,0,1:T(8,128)(2,1)S(1)}, u32[]{:S(2)}, u32[]{:S(2)}) async-start(bf16[256,4,768]{2,0,1:T(8,128)(2,1)} %bitcast.47), calls=%async_computation.2 | async-start | bytes 3145728 | tf_op jit(solution)/shard_map/all_to_all | solution.py:103
  99.4 50.1 %all-to-all-start.3 = ((bf16[4,2,2,128,768]{4,3,1,2,0:T(8,128)(2,1)}), bf16[4,2,2,128,768]{4,3,1,2,0:T(8,128)(2,1)}, u32[]{:S(2)}, u32[]{:S(2)}) async-start(bf16[4,2,2,128,768]{4,3,1,2,0:T(8,128)(2,1)} %pad_maximum_fusion), calls=%async_computation.3 | async-start | bytes 6291456 | tf_op jit(solution)/shard_map/all_to_all | solution.py:131
  104.0 137.2 %all-gather.3.cloned.1.call-start = ((), (), s32[]{:S(2)}) async-start(), calls=%async_computation.5 | async-start | bytes 1966080 | tf_op jit(solution)/shard_map/all_gather | solution.py:107
  149.5 41.5 %all-to-all-start = ((bf16[256,4,768]{2,0,1:T(8,128)(2,1)}), bf16[256,4,768]{2,0,1:T(8,128)(2,1)}, u32[]{:S(2)}, u32[]{:S(2)}) async-start(bf16[256,4,768]{2,0,1:T(8,128)(2,1)} %bitcast.46), calls=%async_computation | async-start | bytes 3145728 | tf_op jit(solution)/shard_map/all_to_all | solution.py:104
  153.8 87.4 %all-gather.5.cloned.1.call-start = ((), (), s32[]{:S(2)}) async-start(), calls=%async_computation.6 | async-start | bytes 1966080 | tf_op jit(solution)/shard_map/all_gather | solution.py:108
  225.3 40.9 %all-to-all-start.4 = ((bf16[4,256,768]{2,1,0:T(8,128)(2,1)}), bf16[4,256,768]{2,1,0:T(8,128)(2,1)}, u32[]{:S(2)}, u32[]{:S(2)}) async-start(bf16[4,256,768]{2,1,0:T(8,128)(2,1)} %bitcast.48), calls=%async_computation.4 | async-start | bytes 3145728 | tf_op jit(solution)/shard_map/all_to_all | solution.py:146
Sparse Core Ops, SparseCore 0:
  117.6 27.7 all-gather.2
  170.0 20.0 all-gather.4

commit v3 on v2

--- a/solution.py
+++ b/solution.py
@@ -128,9 +128,19 @@
     outgoing = jnp.stack(
         [jnp.take(key_blocks, send_idx, axis=0), jnp.take(value_blocks, send_idx, axis=0)], axis=1
     ).reshape(seq_count, CAP, 2, BLOCK, width)
-    arrived = lax.all_to_all(outgoing, "seq", split_axis=0, concat_axis=0, tiled=True)
-    remote_keys = arrived[:, :, 0].reshape(seq_count * CAP * BLOCK, width)
-    remote_values = arrived[:, :, 1].reshape(seq_count * CAP * BLOCK, width)
+    arrivals = []
+    for shift in range(1, seq_count):
+        parcel = lax.dynamic_index_in_dim(
+            outgoing, (seq_index + shift) % seq_count, axis=0, keepdims=False
+        )
+        arrivals.append(
+            lax.ppermute(
+                parcel, "seq", [(i, (i + shift) % seq_count) for i in range(seq_count)]
+            )
+        )
+    arrived = jnp.stack(arrivals, axis=0)
+    remote_keys = arrived[:, :, 0].reshape((seq_count - 1) * CAP * BLOCK, width)
+    remote_values = arrived[:, :, 1].reshape((seq_count - 1) * CAP * BLOCK, width)
     all_keys = jnp.concatenate([key_rows, remote_keys], axis=0)
     all_values = jnp.concatenate([value_rows, remote_values], axis=0)
 
@@ -139,8 +149,9 @@
     within = own_lists % per_dev
     own_rank = lax.dynamic_index_in_dim(slot_rank, seq_index, axis=0, keepdims=False)
     ranks_used = jnp.clip(own_rank[owners, within], 0, CAP - 1)
-    joint_pos = jnp.where(owners == seq_index, within, per_dev + owners * CAP + ranks_used)
-    table = jnp.clip(joint_pos, 0, per_dev + seq_count * CAP - 1).reshape(-1).astype(jnp.int32)
+    distance = (seq_index - owners) % seq_count
+    joint_pos = jnp.where(distance == 0, within, per_dev + (distance - 1) * CAP + ranks_used)
+    table = jnp.clip(joint_pos, 0, per_dev + (seq_count - 1) * CAP - 1).reshape(-1).astype(jnp.int32)
 
     sparse_rows = sparse_attention(table, queries, all_keys, all_values, select_count)
     sparse_out = lax.all_to_all(sparse_rows, "head", split_axis=0, concat_axis=1, tiled=True)

time: 277 us -> 243 us (0.88)
  waiting for transfers between devices: 128 us -> 96 us
    all_to_all x1 -> x0, waiting for transfers between devices: 29.3 us -> none  [on_device(): lax.all_to_all(outgoing, 'seq', split_axis=0, concat_axis=0, tiled=True)]
    ppermute x0 -> x3, waiting for transfers between devices: none -> 27.4 us  [on_device(): lax.ppermute(parcel, 'seq', [(i, (i + shift) % seq_count) for i in range(...]
    all_to_all x1, waiting for transfers between devices: 33.2 us -> 17.1 us  [on_device(): lax.all_to_all(value_in, 'head', split_axis=1, concat_axis=0, tiled=True)]
    all_to_all x1, waiting for transfers between devices: 15.9 us -> 0.01 us  [on_device(): lax.all_to_all(query_in, 'head', split_axis=1, concat_axis=0, tiled=True)]
    all_to_all x1 -> x0, starting transfers between devices: 4.64 us -> none  [on_device(): lax.all_to_all(outgoing, 'seq', split_axis=0, concat_axis=0, tiled=True)]
    ppermute x0 -> x3, starting transfers between devices: none -> 2.96 us  [on_device(): lax.ppermute(parcel, 'seq', [(i, (i + shift) % seq_count) for i in range(...]
  transfers between devices with their start and end apart: 7 -> 9, of which waited for: 5 -> 6; matrix products, arithmetic and copies ran while one was open for 19% -> 24% of each run, Pallas kernels for 16% -> 19%
where the time goes in v3:
time: 243 us; the launch traced here: 241 us
  waiting for transfers between devices  96 us (40%)
  Pallas kernels  45.2 us (19%)
  other arithmetic  34.7 us (14%)
  local copies, waits for them, and re-layouts  28.8 us (12%)
  starting transfers between devices  22.5 us (9%)
  between operations  14.2 us (6%)
    all_to_all x1, waiting for transfers between devices, on_device(): lax.all_to_all(key_in, 'head', split_axis=1, concat_axis=0, tiled=True)  35.6 us
    pallas_call x1, Pallas kernels, sparse_attention(): pl.pallas_call(sparse_kernel, out_shape=jax.ShapeDtypeStruct((rows, width...  34.3 us
    ppermute x3, waiting for transfers between devices, on_device(): lax.ppermute(parcel, 'seq', [(i, (i + shift) % seq_count) for i in range(...  27.4 us
    all_to_all x1, waiting for transfers between devices, on_device(): lax.all_to_all(value_in, 'head', split_axis=1, concat_axis=0, tiled=True)  17.1 us
    all_to_all x1, waiting for transfers between devices, on_device(): lax.all_to_all(sparse_rows, 'head', split_axis=0, concat_axis=1, tiled=True)  15.9 us
    convert_element_type x3, local copies, waits for them, and re-layouts, pool_tokens(): matrix.astype(jnp.float32)  12.8 us
    reduce_sum x3, other arithmetic, pool_tokens(): return (grouped.sum(axis=1) * POOL ** (-0.5)).astype(jnp.bfloat16)  12.3 us
    pallas_call x1, Pallas kernels, draft_attention(): pl.pallas_call(draft_kernel, out_shape=jax.ShapeDtypeStruct((rows, width)...  10.8 us
  transfers between devices with their start and end apart: 9, of which 6 were waited for; matrix products, arithmetic and copies ran while one was open for 24% of the time, Pallas kernels for 19%

profile of v3, /device:TPU:0, one launch (start us, length us, event | category | flops | bytes accessed | tf_op | source)
XLA Modules:
  0.0 241.4 jit_solution(2222250770719966432)
XLA Ops:
  7.2 2.7 %copy.44 = bf16[32,4,8,768]{3,2,0,1:T(8,128)(2,1)} copy(bf16[32,4,8,768]{3,2,1,0:T(8,128)(2,1)} %bitcast.62) | data formatting | bytes 3145728 | tf_op jit(solution)/shard_map/all_to_all | solution.py:102
  9.8 6.4 %all-to-all-start.1 = ((bf16[256,4,768]{2,0,1:T(8,128)(2,1)}), bf16[256,4,768]{2,0,1:T(8,128)(2,1)S(1)}, u32[]{:S(2)}, u32[]{:S(2)}) async-start(bf16[256,4,768]{2,0,1:T(8,128)(2,1)} %bitcast.48), calls=%async_computation.1 | async-start | bytes 3145728 | tf_op jit(solution)/shard_map/all_to_all | solution.py:102
  17.6 35.6 %all-to-all-done.1 = bf16[256,4,768]{2,0,1:T(8,128)(2,1)S(1)} async-done(((bf16[256,4,768]{2,0,1:T(8,128)(2,1)}), bf16[256,4,768]{2,0,1:T(8,128)(2,1)S(1)}, u32[]{:S(2)}, u32[]{:S(2)}) %all-to-all-start.1) | async-done | bytes 1572896 | tf_op jit(solution)/shard_map/all_to_all | solution.py:102
  53.2 3.7 %all-to-all-start.2 = ((bf16[256,4,768]{2,0,1:T(8,128)(2,1)}), bf16[256,4,768]{2,0,1:T(8,128)(2,1)S(1)}, u32[]{:S(2)}, u32[]{:S(2)}) async-start(bf16[256,4,768]{2,0,1:T(8,128)(2,1)} %bitcast.56), calls=%async_computation.2 | async-start | bytes 3145728 | tf_op jit(solution)/shard_map/all_to_all | solution.py:103
  60.1 4.9 %reshape.62 = f32[256,4,768]{2,1,0:T(4,128)} reshape(f32[4,256,768]{2,1,0:T(8,128)} %bitcast_convert_fusion.1) | data formatting | bytes 6291456 | tf_op jit(solution)/shard_map/convert_element_type | solution.py:17
  65.0 4.6 %reduce_sum.37 = f32[256,768]{1,0:T(8,128)} reduce(f32[256,4,768]{2,1,0:T(4,128)} %reshape.62, f32[]{:T(128)} %constant.98.clone.1), dimensions={1}, to_apply=%region_1.0 | reduce | flops 589824 | bytes 3932164 | tf_op jit(solution)/shard_map/reduce_sum | solution.py:18
  73.6 2.7 %copy.45 = bf16[32,4,8,768]{3,2,0,1:T(8,128)(2,1)} copy(bf16[32,4,8,768]{3,2,1,0:T(8,128)(2,1)} %bitcast.64) | data formatting | bytes 3145728 | tf_op jit(solution)/shard_map/all_to_all | solution.py:104
  76.3 17.1 %all-to-all-done.2 = bf16[256,4,768]{2,0,1:T(8,128)(2,1)S(1)} async-done(((bf16[256,4,768]{2,0,1:T(8,128)(2,1)}), bf16[256,4,768]{2,0,1:T(8,128)(2,1)S(1)}, u32[]{:S(2)}, u32[]{:S(2)}) %all-to-all-start.2) | async-done | bytes 1572896 | tf_op jit(solution)/shard_map/all_to_all | solution.py:103
  93.4 4.3 %all-to-all-start = ((bf16[256,4,768]{2,0,1:T(8,128)(2,1)}), bf16[256,4,768]{2,0,1:T(8,128)(2,1)}, u32[]{:S(2)}, u32[]{:S(2)}) async-start(bf16[256,4,768]{2,0,1:T(8,128)(2,1)} %bitcast.55), calls=%async_computation | async-start | bytes 3145728 | tf_op jit(solution)/shard_map/all_to_all | solution.py:104
  101.4 2.2 broadcast_select_fusion
  110.7 4.9 %reshape.63 = f32[256,4,768]{2,1,0:T(4,128)} reshape(f32[4,256,768]{2,1,0:T(8,128)} %bitcast_convert_fusion) | data formatting | bytes 6291456 | tf_op jit(solution)/shard_map/convert_element_type | solution.py:17
  115.6 4.6 %reduce_sum.38 = f32[256,768]{1,0:T(8,128)} reduce(f32[256,4,768]{2,1,0:T(4,128)} %reshape.63, f32[]{:T(128)} %constant.98.clone.1), dimensions={1}, to_apply=%region_2.0 | reduce | flops 589824 | bytes 3932164 | tf_op jit(solution)/shard_map/reduce_sum | solution.py:18
  120.2 2.0 multiply_convert_fusion
  122.2 2.6 %collective-permute-done = bf16[2,2,128,768]{3,2,0,1:T(8,128)(2,1)} collective-permute-done((bf16[2,2,128,768]{3,2,0,1:T(8,128)(2,1)}, bf16[2,2,128,768]{3,2,0,1:T(8,128)(2,1)}, u32[]{:S(2)}, u32[]{:S(2)}) %collective-permute-start) | collective-permute-done | bytes 786464 | tf_op jit(solution)/shard_map/ppermute | solution.py:137
  125.9 23.7 %collective-permute-done.2 = bf16[2,2,128,768]{3,2,0,1:T(8,128)(2,1)} collective-permute-done((bf16[2,2,128,768]{3,2,0,1:T(8,128)(2,1)}, bf16[2,2,128,768]{3,2,0,1:T(8,128)(2,1)}, u32[]{:S(2)}, u32[]{:S(2)}) %collective-permute-start.2) | collective-permute-done | bytes 786464 | tf_op jit(solution)/shard_map/ppermute | solution.py:137
  151.7 2.7 %pad_maximum_fusion = (bf16[1792,768]{1,0:T(8,128)(2,1)}, bf16[1792,768]{1,0:T(8,128)(2,1)}) fusion(bf16[768,768]{1,0:T(8,128)(2,1)S(1)} %bitcast.61, bf16[1024,768]{1,0:T(8,128)(2,1)S(1)} %bitcast.52, bf16[768,768]{1,0:T(8,128)(2,1)S(1)} %bitcast.60, bf16[1024,768]{1,0:T(8,128)(2,1)S(1)} %bitcast.54), kind=kLoop, calls=%fused_computation.9 | loop fusion | flops 11010048 | bytes 11010048 | tf_op jit(solution)/shard_map/concatenate | solution.py:144
  154.4 34.3 %shard_map.60 = bf16[1024,768]{1,0:T(8,128)(2,1)} custom-call(s32[96]{0:T(128)} %reshape.57.tbl_ref, bf16[1024,768]{1,0:T(8,128)(2,1)} %bitcast.4.q_ref, bf16[1792,768]{1,0:T(8,128)(2,1)} %get-tuple-element.10.k_ref, bf16[1792,768]{1,0:T(8,128)(2,1)} %get-tuple-element.11.v_ref), custom_call_target="tpu_custom_call" | custom-call | tf_op jit(solution)/shard_map/pallas_call | solution.py:54
  188.8 5.0 %all-to-all-start.3 = ((bf16[4,256,768]{2,1,0:T(8,128)(2,1)}), bf16[4,256,768]{2,1,0:T(8,128)(2,1)}, u32[]{:S(2)}, u32[]{:S(2)}) async-start(bf16[4,256,768]{2,1,0:T(8,128)(2,1)} %bitcast.59), calls=%async_computation.3 | async-start | bytes 3145728 | tf_op jit(solution)/shard_map/all_to_all | solution.py:157
  193.7 3.3 %bitcast_convert_fusion.2 = f32[4,256,768]{2,1,0:T(8,128)} fusion(bf16[256,4,768]{2,0,1:T(8,128)(2,1)} %all-to-all-done), kind=kLoop, calls=%fused_computation.17 | loop fusion | flops 786432 | bytes 4718592 | tf_op jit(solution)/shard_map/convert_element_type | solution.py:17
  197.1 3.1 %reshape.61 = f32[256,4,768]{2,1,0:T(4,128)S(1)} reshape(f32[4,256,768]{2,1,0:T(8,128)} %bitcast_convert_fusion.2) | data formatting | bytes 6291456 | tf_op jit(solution)/shard_map/convert_element_type | solution.py:17
  200.2 3.0 %reduce_sum.36 = f32[256,768]{1,0:T(8,128)} reduce(f32[256,4,768]{2,1,0:T(4,128)S(1)} %reshape.61, f32[]{:T(128)} %constant.98.clone.1), dimensions={1}, to_apply=%region_0.0 | reduce | flops 589824 | bytes 3932164 | tf_op jit(solution)/shard_map/reduce_sum | solution.py:18
  205.1 10.8 %shard_map.59 = bf16[256,768]{1,0:T(8,128)(2,1)} custom-call(bf16[256,768]{1,0:T(8,128)(2,1)} %multiply_convert_fusion.2.q_ref, bf16[1024,768]{1,0:T(8,128)(2,1)} %all-gather.3.cloned.1.call-done.k_ref, bf16[1024,768]{1,0:T(8,128)(2,1)} %all-gather.5.cloned.1.call-done.v_ref), custom_call_target="tpu_custom_call" | custom-call | tf_op jit(solution)/shard_map/pallas_call | solution.py:88
  215.9 15.9 %all-to-all-done.3 = bf16[4,256,768]{2,1,0:T(8,128)(2,1)} async-done(((bf16[4,256,768]{2,1,0:T(8,128)(2,1)}), bf16[4,256,768]{2,1,0:T(8,128)(2,1)}, u32[]{:S(2)}, u32[]{:S(2)}) %all-to-all-start.3) | async-done | bytes 1572896 | tf_op jit(solution)/shard_map/all_to_all | solution.py:157
  231.8 2.7 %copy.38 = bf16[4,32,8,768]{3,2,0,1:T(8,128)(2,1)} copy(bf16[4,32,8,768]{3,2,1,0:T(8,128)(2,1)} %bitcast.34) | data formatting | bytes 3145728 | tf_op jit(solution)/shard_map/all_to_all | solution.py:157
  (50 shorter events, 24.3 us)
Async XLA Ops:
  9.8 6.5 %copy-start = (bf16[256,3072]{1,0:T(8,128)(2,1)S(1)}, bf16[256,3072]{1,0:T(8,128)(2,1)}, u32[]{:S(2)}) copy-start(bf16[256,3072]{1,0:T(8,128)(2,1)} %param.8) | copy-start | bytes 4718596
  9.8 43.4 %all-to-all-start.1 = ((bf16[256,4,768]{2,0,1:T(8,128)(2,1)}), bf16[256,4,768]{2,0,1:T(8,128)(2,1)S(1)}, u32[]{:S(2)}, u32[]{:S(2)}) async-start(bf16[256,4,768]{2,0,1:T(8,128)(2,1)} %bitcast.48), calls=%async_computation.1 | async-start | bytes 3145728 | tf_op jit(solution)/shard_map/all_to_all | solution.py:102
  53.2 3.8 %copy-start.1 = (s32[32,12]{0,1:T(8,128)S(1)}, s32[32,12]{0,1:T(8,128)}, u32[]{:S(2)}) copy-start(s32[32,12]{0,1:T(8,128)} %param.9) | copy-start | bytes 4612
  53.2 40.1 %all-to-all-start.2 = ((bf16[256,4,768]{2,0,1:T(8,128)(2,1)}), bf16[256,4,768]{2,0,1:T(8,128)(2,1)S(1)}, u32[]{:S(2)}, u32[]{:S(2)}) async-start(bf16[256,4,768]{2,0,1:T(8,128)(2,1)} %bitcast.56), calls=%async_computation.2 | async-start | bytes 3145728 | tf_op jit(solution)/shard_map/all_to_all | solution.py:103
  56.9 148.2 %all-gather.3.cloned.1.call-start = ((), (), s32[]{:S(2)}) async-start(), calls=%async_computation.4 | async-start | bytes 1966080 | tf_op jit(solution)/shard_map/all_gather | solution.py:107
  93.4 61.1 %all-to-all-start = ((bf16[256,4,768]{2,0,1:T(8,128)(2,1)}), bf16[256,4,768]{2,0,1:T(8,128)(2,1)}, u32[]{:S(2)}, u32[]{:S(2)}) async-start(bf16[256,4,768]{2,0,1:T(8,128)(2,1)} %bitcast.55), calls=%async_computation | async-start | bytes 3145728 | tf_op jit(solution)/shard_map/all_to_all | solution.py:104
  97.7 107.4 %all-gather.5.cloned.1.call-start = ((), (), s32[]{:S(2)}) async-start(), calls=%async_computation.5 | async-start | bytes 1966080 | tf_op jit(solution)/shard_map/all_gather | solution.py:108
  105.2 19.6 %collective-permute-start = (bf16[2,2,128,768]{3,2,0,1:T(8,128)(2,1)}, bf16[2,2,128,768]{3,2,0,1:T(8,128)(2,1)}, u32[]{:S(2)}, u32[]{:S(2)}) collective-permute-start(bf16[2,2,128,768]{3,2,0,1:T(8,128)(2,1)} %get-tuple-element.3), channel_id=1, source_target_pairs={{0,4},{4,8},{8,12},{12,0},{1,5},{5,9},{9,13},{13,1},{2,6},{6,10},{... | collective-permute-start | bytes 2359304 | tf_op jit(solution)/shard_map/ppermute | solution.py:137
  105.2 20.7 %collective-permute-start.1 = (bf16[2,2,128,768]{3,2,0,1:T(8,128)(2,1)}, bf16[2,2,128,768]{3,2,0,1:T(8,128)(2,1)}, u32[]{:S(2)}, u32[]{:S(2)}) collective-permute-start(bf16[2,2,128,768]{3,2,0,1:T(8,128)(2,1)} %get-tuple-element.4), channel_id=1, source_target_pairs={{0,8},{4,12},{8,0},{12,4},{1,9},{5,13},{9,1},{13,5},{2,10},{6,14},... | collective-permute-start | bytes 2359304 | tf_op jit(solution)/shard_map/ppermute | solution.py:137
  106.7 42.9 %collective-permute-start.2 = (bf16[2,2,128,768]{3,2,0,1:T(8,128)(2,1)}, bf16[2,2,128,768]{3,2,0,1:T(8,128)(2,1)}, u32[]{:S(2)}, u32[]{:S(2)}) collective-permute-start(bf16[2,2,128,768]{3,2,0,1:T(8,128)(2,1)} %get-tuple-element.5), channel_id=1, source_target_pairs={{0,12},{4,0},{8,4},{12,8},{1,13},{5,1},{9,5},{13,9},{2,14},{6,2},{... | collective-permute-start | bytes 2359304 | tf_op jit(solution)/shard_map/ppermute | solution.py:137
  188.8 43.0 %all-to-all-start.3 = ((bf16[4,256,768]{2,1,0:T(8,128)(2,1)}), bf16[4,256,768]{2,1,0:T(8,128)(2,1)}, u32[]{:S(2)}, u32[]{:S(2)}) async-start(bf16[4,256,768]{2,1,0:T(8,128)(2,1)} %bitcast.59), calls=%async_computation.3 | async-start | bytes 3145728 | tf_op jit(solution)/shard_map/all_to_all | solution.py:157
Sparse Core Ops, SparseCore 0:
  71.7 21.0 all-gather.2
  122.3 28.6 all-gather.4

commit v4 on v3

--- a/solution.py
+++ b/solution.py
@@ -24,16 +24,30 @@
     ) * SCALE
 
 
-def sparse_kernel(tbl_ref, q_ref, k_ref, v_ref, o_ref, ks_ref, vs_ref):
+def sparse_kernel(tbl_ref, q_ref, k_ref, v_ref, kr_ref, vr_ref, o_ref, ks_ref, vs_ref):
     per_dev = q_ref.shape[0] // BLOCK
     sel = ks_ref.shape[0] // BLOCK
+    remote_count = kr_ref.shape[0] // BLOCK
 
     def body(i, carry):
         row = pl.multiple_of(i * BLOCK, BLOCK)
         for j in range(sel):
-            start = pl.multiple_of(tbl_ref[i * sel + j] * BLOCK, BLOCK)
-            ks_ref[j * BLOCK:(j + 1) * BLOCK, :] = k_ref[pl.ds(start, BLOCK), :]
-            vs_ref[j * BLOCK:(j + 1) * BLOCK, :] = v_ref[pl.ds(start, BLOCK), :]
+            idx = tbl_ref[i * sel + j]
+            dest = slice(j * BLOCK, (j + 1) * BLOCK)
+
+            @pl.when(idx < per_dev)
+            def _():
+                start = pl.multiple_of(jnp.minimum(idx, per_dev - 1) * BLOCK, BLOCK)
+                ks_ref[dest, :] = k_ref[pl.ds(start, BLOCK), :]
+                vs_ref[dest, :] = v_ref[pl.ds(start, BLOCK), :]
+
+            @pl.when(idx >= per_dev)
+            def _():
+                far = jnp.clip(idx - per_dev, 0, remote_count - 1)
+                start = pl.multiple_of(far * BLOCK, BLOCK)
+                ks_ref[dest, :] = kr_ref[pl.ds(start, BLOCK), :]
+                vs_ref[dest, :] = vr_ref[pl.ds(start, BLOCK), :]
+
         s = _scores(q_ref[pl.ds(row, BLOCK), :], ks_ref[...])
         running = jnp.max(s, axis=1, keepdims=True)
         weights = jnp.exp(s - running)
@@ -47,20 +61,26 @@
     lax.fori_loop(0, per_dev, body, 0)
 
 
-def sparse_attention(tbl, queries, keys, values, sel):
-    rows, width = queries.shape
-    heads = width // HD
-    key_rows = keys.shape[0]
+def sparse_attention(tbl, queries, keys, values, far_keys, far_values, sel, head_lo, heads):
+    rows = queries.shape[0]
+    near_rows = keys.shape[0]
+    far_rows = far_keys.shape[0]
+
+    def column(h, t):
+        return (0, h + head_lo)
+
     return pl.pallas_call(
         sparse_kernel,
-        out_shape=jax.ShapeDtypeStruct((rows, width), jnp.bfloat16),
+        out_shape=jax.ShapeDtypeStruct((rows, heads * HD), jnp.bfloat16),
         grid_spec=pltpu.PrefetchScalarGridSpec(
             num_scalar_prefetch=1,
             grid=(heads,),
             in_specs=[
-                pl.BlockSpec((rows, HD), lambda h, t: (0, h)),
-                pl.BlockSpec((key_rows, HD), lambda h, t: (0, h)),
-                pl.BlockSpec((key_rows, HD), lambda h, t: (0, h)),
+                pl.BlockSpec((rows, HD), column),
+                pl.BlockSpec((near_rows, HD), column),
+                pl.BlockSpec((near_rows, HD), column),
+                pl.BlockSpec((far_rows, HD), column),
+                pl.BlockSpec((far_rows, HD), column),
             ],
             out_specs=pl.BlockSpec((rows, HD), lambda h, t: (0, h)),
             scratch_shapes=[
@@ -68,7 +88,7 @@
                 pltpu.VMEM((sel * BLOCK, HD), jnp.bfloat16),
             ],
         ),
-    )(tbl, queries, keys, values)
+    )(tbl, queries, keys, values, far_keys, far_values)
 
 
 def draft_kernel(q_ref, k_ref, v_ref, o_ref):
@@ -99,8 +119,10 @@
 
 
 def on_device(query_in, key_in, value_in, block_lists):
-    key_rows = lax.all_to_all(key_in, "head", split_axis=1, concat_axis=0, tiled=True)
-    value_rows = lax.all_to_all(value_in, "head", split_axis=1, concat_axis=0, tiled=True)
+    pair_rows = lax.all_to_all(
+        jnp.stack([key_in, value_in], axis=0), "head", split_axis=2, concat_axis=1, tiled=True
+    )
+    key_rows, value_rows = pair_rows[0], pair_rows[1]
     queries = lax.all_to_all(query_in, "head", split_axis=1, concat_axis=0, tiled=True)
     seq_rows, width = queries.shape
 
@@ -141,8 +163,6 @@
     arrived = jnp.stack(arrivals, axis=0)
     remote_keys = arrived[:, :, 0].reshape((seq_count - 1) * CAP * BLOCK, width)
     remote_values = arrived[:, :, 1].reshape((seq_count - 1) * CAP * BLOCK, width)
-    all_keys = jnp.concatenate([key_rows, remote_keys], axis=0)
-    all_values = jnp.concatenate([value_rows, remote_values], axis=0)
 
     own_lists = lax.dynamic_slice_in_dim(block_lists, seq_index * per_dev, per_dev, 0)
     owners = own_lists // per_dev
@@ -153,8 +173,19 @@
     joint_pos = jnp.where(distance == 0, within, per_dev + (distance - 1) * CAP + ranks_used)
     table = jnp.clip(joint_pos, 0, per_dev + (seq_count - 1) * CAP - 1).reshape(-1).astype(jnp.int32)
 
-    sparse_rows = sparse_attention(table, queries, all_keys, all_values, select_count)
-    sparse_out = lax.all_to_all(sparse_rows, "head", split_axis=0, concat_axis=1, tiled=True)
+    heads = width // HD
+    first = max(1, heads // 2)
+    pieces = []
+    for head_lo, count in ((0, first), (first, heads - first)):
+        if count == 0:
+            continue
+        rows_part = sparse_attention(
+            table, queries, key_rows, value_rows, remote_keys, remote_values,
+            select_count, head_lo, count,
+        )
+        back = lax.all_to_all(rows_part, "head", split_axis=0, concat_axis=1, tiled=True)
+        pieces.append(back.reshape(back.shape[0], -1, count * HD))
+    sparse_out = jnp.concatenate(pieces, axis=2).reshape(pieces[0].shape[0], -1)
 
     draft_out = draft_attention(pool_tokens(queries), draft_keys, draft_values)
     return (draft_out, sparse_out)

time: 243 us -> 273 us (1.12)
  Pallas kernels: 45.2 us -> 57.8 us
  waiting for transfers between devices: 96 us -> 108 us
  local copies, waits for them, and re-layouts: 28.8 us -> 35 us
    pallas_call x1 -> x2, Pallas kernels: 34.3 us -> 47 us  [sparse_attention(): pl.pallas_call(sparse_kernel, out_shape=jax.ShapeDtypeStruct((rows, heads...]
    ppermute x3, waiting for transfers between devices: 27.4 us -> 35.1 us  [on_device(): lax.ppermute(parcel, 'seq', [(i, (i + shift) % seq_count) for i in range(...]
    another operation x0 -> x1, local copies, waits for them, and re-layouts: none -> 5.63 us  [on_device(): jnp.stack([key_in, value_in], axis=0)]
    slice x0 -> x1, other arithmetic: none -> 5.24 us  [on_device(): key_rows, value_rows = (pair_rows[0], pair_rows[1])]
    all_to_all x3, waiting for transfers between devices: 68.6 us -> 73.2 us  [the longest x1 66.6 us: on_device(): lax.all_to_all(jnp.stack([key_in, value_in], axis=0), 'head', split_axis=...]
    convert_element_type x3 -> x1, other arithmetic: 7.18 us -> 3.32 us  [pool_tokens(): matrix.astype(jnp.float32)]
    concatenate x1 -> x0, other arithmetic: 2.74 us -> none  [on_device(): all_keys = jnp.concatenate([key_rows, remote_keys], axis=0)]
    all_to_all x3 -> x1, local copies, waits for them, and re-layouts: 6.74 us -> 5.75 us  [on_device(): lax.all_to_all(jnp.stack([key_in, value_in], axis=0), 'head', split_axis=...]
  transfers between devices with their start and end apart: 9 -> 9, of which waited for: 6 -> 5; matrix products, arithmetic and copies ran while one was open for 24% -> 22% of each run, Pallas kernels for 19% -> 17%
where the time goes in v4:
time: 273 us; the launch traced here: 272 us
  waiting for transfers between devices  108 us (40%)
  Pallas kernels  57.8 us (21%)
  local copies, waits for them, and re-layouts  35 us (13%)
  other arithmetic  33.5 us (12%)
  starting transfers between devices  22.7 us (8%)
  between operations  14.2 us (5%)
    all_to_all x1, waiting for transfers between devices, on_device(): lax.all_to_all(jnp.stack([key_in, value_in], axis=0), 'head', split_axis=...  66.6 us
    pallas_call x2, Pallas kernels, sparse_attention(): pl.pallas_call(sparse_kernel, out_shape=jax.ShapeDtypeStruct((rows, heads...  47 us
    ppermute x3, waiting for transfers between devices, on_device(): lax.ppermute(parcel, 'seq', [(i, (i + shift) % seq_count) for i in range(...  35.1 us
    convert_element_type x3, local copies, waits for them, and re-layouts, pool_tokens(): matrix.astype(jnp.float32)  11.7 us
    pallas_call x1, Pallas kernels, draft_attention(): pl.pallas_call(draft_kernel, out_shape=jax.ShapeDtypeStruct((rows, width)...  10.8 us
    reduce_sum x3, other arithmetic, pool_tokens(): return (grouped.sum(axis=1) * POOL ** (-0.5)).astype(jnp.bfloat16)  10.6 us
    all_to_all x2, starting transfers between devices, on_device(): lax.all_to_all(rows_part, 'head', split_axis=0, concat_axis=1, tiled=True)  10.2 us
    all_to_all x2, waiting for transfers between devices, on_device(): lax.all_to_all(rows_part, 'head', split_axis=0, concat_axis=1, tiled=True)  6.61 us
  transfers between devices with their start and end apart: 9, of which 5 were waited for; matrix products, arithmetic and copies ran while one was open for 22% of the time, Pallas kernels for 17%

profile of v4, /device:TPU:0, one launch (start us, length us, event | category | flops | bytes accessed | tf_op | source)
XLA Modules:
  0.0 271.6 jit_solution(11978510764705199490)
XLA Ops:
  7.2 2.2 pad_maximum_fusion
  9.3 5.6 %copy.37 = bf16[2,256,3072]{1,0,2:T(2,128)(2,1)} copy(bf16[2,256,3072]{2,1,0:T(8,128)(2,1)S(1)} %pad_maximum_fusion) | data formatting | bytes 6291456 | tf_op jit(solution)/shard_map/stack | solution.py:123
  15.0 6.3 %all-to-all-start.1 = ((bf16[2,256,3072]{1,0,2:T(2,128)(2,1)}), bf16[2,256,3072]{1,0,2:T(2,128)(2,1)S(1)}, u32[]{:S(2)}, u32[]{:S(2)}) async-start(bf16[2,256,3072]{1,0,2:T(2,128)(2,1)} %copy.37), calls=%async_computation.1 | async-start | bytes 6291456 | tf_op jit(solution)/shard_map/all_to_all | solution.py:122
  21.3 2.7 copy.50
  25.3 66.6 %all-to-all-done.1 = bf16[2,256,3072]{1,0,2:T(2,128)(2,1)S(1)} async-done(((bf16[2,256,3072]{1,0,2:T(2,128)(2,1)}), bf16[2,256,3072]{1,0,2:T(2,128)(2,1)S(1)}, u32[]{:S(2)}, u32[]{:S(2)}) %all-to-all-start.1) | async-done | bytes 3145760 | tf_op jit(solution)/shard_map/all_to_all | solution.py:122
  92.0 4.4 %all-to-all-start = ((bf16[256,4,768]{2,0,1:T(8,128)(2,1)}), bf16[256,4,768]{2,0,1:T(8,128)(2,1)}, u32[]{:S(2)}, u32[]{:S(2)}) async-start(bf16[256,4,768]{2,0,1:T(8,128)(2,1)} %bitcast.58), calls=%async_computation | async-start | bytes 3145728 | tf_op jit(solution)/shard_map/all_to_all | solution.py:126
  96.4 5.8 %copy.38 = bf16[2,256,4,768]{3,1,2,0:T(8,128)(2,1)} copy(bf16[2,256,4,768]{1,0,3,2:T(2,128)(2,1)S(1)} %bitcast.52) | data formatting | bytes 6291456 | tf_op jit(solution)/shard_map/all_to_all | solution.py:122
  102.1 5.2 %fusion.17 = (bf16[1,4,256,768]{3,2,1,0:T(8,128)(2,1)S(1)}, f32[1,4,256,768]{3,2,1,0:T(8,128)}, f32[1,4,256,768]{3,2,1,0:T(8,128)}, bf16[1,4,256,768]{3,2,1,0:T(8,128)(2,1)S(1)}) fusion(bf16[2,4,256,768]{3,2,1,0:T(8,128)(2,1)} %bitcast.53), kind=kLoop, calls=%fused_computation.63 | loop fusion | flops 1572864 | bytes 12582912 | tf_op jit(solution)/shard_map/slice | solution.py:125
  107.4 5.4 %reshape.63 = f32[256,4,768]{2,1,0:T(4,128)} reshape(f32[1,4,256,768]{3,2,1,0:T(8,128)} %get-tuple-element.7) | data formatting | bytes 6291456 | tf_op jit(solution)/shard_map/convert_element_type | solution.py:17
  112.8 4.6 %reduce_sum.37 = f32[256,768]{1,0:T(8,128)} reduce(f32[256,4,768]{2,1,0:T(4,128)} %reshape.63, f32[]{:T(128)} %constant.98.clone.1), dimensions={1}, to_apply=%region_1.0 | reduce | flops 589824 | bytes 3932164 | tf_op jit(solution)/shard_map/reduce_sum | solution.py:18
  130.6 3.1 %reshape.64 = f32[256,4,768]{2,1,0:T(4,128)S(1)} reshape(f32[1,4,256,768]{3,2,1,0:T(8,128)} %get-tuple-element.8) | data formatting | bytes 6291456 | tf_op jit(solution)/shard_map/convert_element_type | solution.py:17
  133.7 3.0 %reduce_sum.38 = f32[256,768]{1,0:T(8,128)} reduce(f32[256,4,768]{2,1,0:T(4,128)S(1)} %reshape.64, f32[]{:T(128)} %constant.98.clone.1), dimensions={1}, to_apply=%region_2.0 | reduce | flops 589824 | bytes 3932164 | tf_op jit(solution)/shard_map/reduce_sum | solution.py:18
  136.6 15.8 %collective-permute-done.2 = bf16[2,2,128,768]{3,2,0,1:T(8,128)(2,1)} collective-permute-done((bf16[2,2,128,768]{3,2,0,1:T(8,128)(2,1)}, bf16[2,2,128,768]{3,2,0,1:T(8,128)(2,1)}, u32[]{:S(2)}, u32[]{:S(2)}) %collective-permute-start.2) | collective-permute-done | bytes 786464 | tf_op jit(solution)/shard_map/ppermute | solution.py:159
  152.5 19.2 %collective-permute-done.1 = bf16[2,2,128,768]{3,2,0,1:T(8,128)(2,1)} collective-permute-done((bf16[2,2,128,768]{3,2,0,1:T(8,128)(2,1)}, bf16[2,2,128,768]{3,2,0,1:T(8,128)(2,1)}, u32[]{:S(2)}, u32[]{:S(2)}) %collective-permute-start.1) | collective-permute-done | bytes 786464 | tf_op jit(solution)/shard_map/ppermute | solution.py:159
  175.2 23.5 %shard_map.61 = bf16[1024,384]{1,0:T(8,128)(2,1)} custom-call(s32[96]{0:T(128)} %reshape.59.tbl_ref, bf16[1024,768]{1,0:T(8,128)(2,1)} %bitcast.6.q_ref, bf16[1024,768]{1,0:T(8,128)(2,1)} %bitcast.50, bf16[1024,768]{1,0:T(8,128)(2,1)} %bitcast.47, bf16[768,768]{1,0:T(8,128)(2,1)} %bitcast.56, bf16[768,768]{1,0:T(8,128)(2,1)} %bitcast.54), custom_call_target="tpu_custom_call" | custom-call | tf_op jit(solution)/shard_map/pallas_call | solution.py:72
  198.7 5.1 %all-to-all-start.3 = ((bf16[4,256,384]{2,1,0:T(8,128)(2,1)}), bf16[4,256,384]{2,1,0:T(8,128)(2,1)S(1)}, u32[]{:S(2)}, u32[]{:S(2)}) async-start(bf16[4,256,384]{2,1,0:T(8,128)(2,1)} %bitcast.63), calls=%async_computation.3 | async-start | bytes 1572864 | tf_op jit(solution)/shard_map/all_to_all | solution.py:186
  204.7 23.5 %shard_map.60 = bf16[1024,384]{1,0:T(8,128)(2,1)} custom-call(s32[96]{0:T(128)} %reshape.59.tbl_ref, bf16[1024,768]{1,0:T(8,128)(2,1)} %bitcast.6.q_ref, bf16[1024,768]{1,0:T(8,128)(2,1)} %bitcast.51, bf16[1024,768]{1,0:T(8,128)(2,1)} %bitcast.48, bf16[768,768]{1,0:T(8,128)(2,1)} %bitcast.57, bf16[768,768]{1,0:T(8,128)(2,1)} %bitcast.55), custom_call_target="tpu_custom_call" | custom-call | tf_op jit(solution)/shard_map/pallas_call | solution.py:72
  228.2 5.1 %all-to-all-start.2 = ((bf16[4,256,384]{2,1,0:T(8,128)(2,1)}), bf16[4,256,384]{2,1,0:T(8,128)(2,1)}, u32[]{:S(2)}, u32[]{:S(2)}) async-start(bf16[4,256,384]{2,1,0:T(8,128)(2,1)} %bitcast.62), calls=%async_computation.2 | async-start | bytes 1572864 | tf_op jit(solution)/shard_map/all_to_all | solution.py:186
  233.4 3.3 %bitcast_convert_fusion = f32[4,256,768]{2,1,0:T(8,128)} fusion(bf16[256,4,768]{2,0,1:T(8,128)(2,1)} %all-to-all-done), kind=kLoop, calls=%fused_computation.13 | loop fusion | flops 786432 | bytes 4718592 | tf_op jit(solution)/shard_map/convert_element_type | solution.py:17
  236.7 3.1 %reshape.62 = f32[256,4,768]{2,1,0:T(4,128)S(1)} reshape(f32[4,256,768]{2,1,0:T(8,128)} %bitcast_convert_fusion) | data formatting | bytes 6291456 | tf_op jit(solution)/shard_map/convert_element_type | solution.py:17
  239.8 3.0 %reduce_sum.36 = f32[256,768]{1,0:T(8,128)} reduce(f32[256,4,768]{2,1,0:T(4,128)S(1)} %reshape.62, f32[]{:T(128)} %constant.98.clone.1), dimensions={1}, to_apply=%region_0.0 | reduce | flops 589824 | bytes 3932164 | tf_op jit(solution)/shard_map/reduce_sum | solution.py:18
  242.8 2.0 multiply_convert_fusion.2.q_ref
  244.8 6.6 %all-to-all-done.2 = bf16[4,256,384]{2,1,0:T(8,128)(2,1)} async-done(((bf16[4,256,384]{2,1,0:T(8,128)(2,1)}), bf16[4,256,384]{2,1,0:T(8,128)(2,1)}, u32[]{:S(2)}, u32[]{:S(2)}) %all-to-all-start.2) | async-done | bytes 786464 | tf_op jit(solution)/shard_map/all_to_all | solution.py:186
  254.0 10.8 %shard_map.59 = bf16[256,768]{1,0:T(8,128)(2,1)} custom-call(bf16[256,768]{1,0:T(8,128)(2,1)} %multiply_convert_fusion.2.q_ref, bf16[1024,768]{1,0:T(8,128)(2,1)} %all-gather.3.cloned.1.call-done.k_ref, bf16[1024,768]{1,0:T(8,128)(2,1)} %all-gather.5.cloned.1.call-done.v_ref), custom_call_target="tpu_custom_call" | custom-call | tf_op jit(solution)/shard_map/pallas_call | solution.py:108
  (61 shorter events, 21.4 us)
Async XLA Ops:
  15.0 77.0 %all-to-all-start.1 = ((bf16[2,256,3072]{1,0,2:T(2,128)(2,1)}), bf16[2,256,3072]{1,0,2:T(2,128)(2,1)S(1)}, u32[]{:S(2)}, u32[]{:S(2)}) async-start(bf16[2,256,3072]{1,0,2:T(2,128)(2,1)} %copy.37), calls=%async_computation.1 | async-start | bytes 6291456 | tf_op jit(solution)/shard_map/all_to_all | solution.py:122
  21.3 2.7 copy-start.6
  92.0 83.3 %all-to-all-start = ((bf16[256,4,768]{2,0,1:T(8,128)(2,1)}), bf16[256,4,768]{2,0,1:T(8,128)(2,1)}, u32[]{:S(2)}, u32[]{:S(2)}) async-start(bf16[256,4,768]{2,0,1:T(8,128)(2,1)} %bitcast.58), calls=%async_computation | async-start | bytes 3145728 | tf_op jit(solution)/shard_map/all_to_all | solution.py:126
  96.3 157.7 %all-gather.3.cloned.1.call-start = ((), (), s32[]{:S(2)}) async-start(), calls=%async_computation.4 | async-start | bytes 1966080 | tf_op jit(solution)/shard_map/all_gather | solution.py:129
  107.4 12.1 %copy-start = (bf16[1,4,256,768]{3,2,1,0:T(8,128)(2,1)}, bf16[1,4,256,768]{3,2,1,0:T(8,128)(2,1)S(1)}, u32[]{:S(2)}) copy-start(bf16[1,4,256,768]{3,2,1,0:T(8,128)(2,1)S(1)} %get-tuple-element.6) | copy-start | bytes 4718596
  107.4 13.9 %copy-start.1 = (bf16[1,4,256,768]{3,2,1,0:T(8,128)(2,1)}, bf16[1,4,256,768]{3,2,1,0:T(8,128)(2,1)S(1)}, u32[]{:S(2)}) copy-start(bf16[1,4,256,768]{3,2,1,0:T(8,128)(2,1)S(1)} %get-tuple-element.9) | copy-start | bytes 4718596
  121.3 1.8 copy-start.2
  126.3 26.2 %collective-permute-start.2 = (bf16[2,2,128,768]{3,2,0,1:T(8,128)(2,1)}, bf16[2,2,128,768]{3,2,0,1:T(8,128)(2,1)}, u32[]{:S(2)}, u32[]{:S(2)}) collective-permute-start(bf16[2,2,128,768]{3,2,0,1:T(8,128)(2,1)} %get-tuple-element.5), channel_id=1, source_target_pairs={{0,12},{4,0},{8,4},{12,8},{1,13},{5,1},{9,5},{13,9},{2,14},{6,2},{... | collective-permute-start | bytes 2359304 | tf_op jit(solution)/shard_map/ppermute | solution.py:159
  126.5 45.2 %collective-permute-start.1 = (bf16[2,2,128,768]{3,2,0,1:T(8,128)(2,1)}, bf16[2,2,128,768]{3,2,0,1:T(8,128)(2,1)}, u32[]{:S(2)}, u32[]{:S(2)}) collective-permute-start(bf16[2,2,128,768]{3,2,0,1:T(8,128)(2,1)} %get-tuple-element.4), channel_id=1, source_target_pairs={{0,8},{4,12},{8,0},{12,4},{1,9},{5,13},{9,1},{13,5},{2,10},{6,14},... | collective-permute-start | bytes 2359304 | tf_op jit(solution)/shard_map/ppermute | solution.py:159
  127.8 44.0 %collective-permute-start = (bf16[2,2,128,768]{3,2,0,1:T(8,128)(2,1)}, bf16[2,2,128,768]{3,2,0,1:T(8,128)(2,1)}, u32[]{:S(2)}, u32[]{:S(2)}) collective-permute-start(bf16[2,2,128,768]{3,2,0,1:T(8,128)(2,1)} %get-tuple-element.3), channel_id=1, source_target_pairs={{0,4},{4,8},{8,12},{12,0},{1,5},{5,9},{9,13},{13,1},{2,6},{6,10},{... | collective-permute-start | bytes 2359304 | tf_op jit(solution)/shard_map/ppermute | solution.py:159
  198.7 5.1 %copy-start.5 = (f32[256,768]{1,0:T(8,128)S(1)}, f32[256,768]{1,0:T(8,128)}, u32[]{:S(2)}) copy-start(f32[256,768]{1,0:T(8,128)} %reduce_sum.38) | copy-start | bytes 2359300
  198.7 29.5 %all-to-all-start.3 = ((bf16[4,256,384]{2,1,0:T(8,128)(2,1)}), bf16[4,256,384]{2,1,0:T(8,128)(2,1)S(1)}, u32[]{:S(2)}, u32[]{:S(2)}) async-start(bf16[4,256,384]{2,1,0:T(8,128)(2,1)} %bitcast.63), calls=%async_computation.3 | async-start | bytes 1572864 | tf_op jit(solution)/shard_map/all_to_all | solution.py:186
  203.9 50.1 %all-gather.5.cloned.1.call-start = ((), (), s32[]{:S(2)}) async-start(), calls=%async_computation.5 | async-start | bytes 1966080 | tf_op jit(solution)/shard_map/all_gather | solution.py:130
  228.2 5.1 %copy-start.3 = (bf16[4,256,384]{2,1,0:T(8,128)(2,1)}, bf16[4,256,384]{2,1,0:T(8,128)(2,1)S(1)}, u32[]{:S(2)}) copy-start(bf16[4,256,384]{2,1,0:T(8,128)(2,1)S(1)} %all-to-all-done.3) | copy-start | bytes 2359300
  228.2 23.1 %all-to-all-start.2 = ((bf16[4,256,384]{2,1,0:T(8,128)(2,1)}), bf16[4,256,384]{2,1,0:T(8,128)(2,1)}, u32[]{:S(2)}, u32[]{:S(2)}) async-start(bf16[4,256,384]{2,1,0:T(8,128)(2,1)} %bitcast.62), calls=%async_computation.2 | async-start | bytes 1572864 | tf_op jit(solution)/shard_map/all_to_all | solution.py:186
  242.8 8.6 %copy-start.4 = (bf16[4,256,384]{2,1,0:T(8,128)(2,1)S(1)}, bf16[4,256,384]{2,1,0:T(8,128)(2,1)}, u32[]{:S(2)}) copy-start(bf16[4,256,384]{2,1,0:T(8,128)(2,1)} %copy-done.3) | copy-start | bytes 2359300
Sparse Core Ops, SparseCore 0:
  119.5 29.4 all-gather.2
  206.2 20.2 all-gather.4

commit v5 on v4

--- a/solution.py
+++ b/solution.py
@@ -33,21 +33,15 @@
         row = pl.multiple_of(i * BLOCK, BLOCK)
         for j in range(sel):
             idx = tbl_ref[i * sel + j]
-            dest = slice(j * BLOCK, (j + 1) * BLOCK)
-
-            @pl.when(idx < per_dev)
-            def _():
-                start = pl.multiple_of(jnp.minimum(idx, per_dev - 1) * BLOCK, BLOCK)
-                ks_ref[dest, :] = k_ref[pl.ds(start, BLOCK), :]
-                vs_ref[dest, :] = v_ref[pl.ds(start, BLOCK), :]
-
-            @pl.when(idx >= per_dev)
-            def _():
-                far = jnp.clip(idx - per_dev, 0, remote_count - 1)
-                start = pl.multiple_of(far * BLOCK, BLOCK)
-                ks_ref[dest, :] = kr_ref[pl.ds(start, BLOCK), :]
-                vs_ref[dest, :] = vr_ref[pl.ds(start, BLOCK), :]
-
+            near = pl.multiple_of(jnp.minimum(idx, per_dev - 1) * BLOCK, BLOCK)
+            far = pl.multiple_of(jnp.clip(idx - per_dev, 0, remote_count - 1) * BLOCK, BLOCK)
+            is_near = idx < per_dev
+            ks_ref[j * BLOCK:(j + 1) * BLOCK, :] = jnp.where(
+                is_near, k_ref[pl.ds(near, BLOCK), :], kr_ref[pl.ds(far, BLOCK), :]
+            )
+            vs_ref[j * BLOCK:(j + 1) * BLOCK, :] = jnp.where(
+                is_near, v_ref[pl.ds(near, BLOCK), :], vr_ref[pl.ds(far, BLOCK), :]
+            )
         s = _scores(q_ref[pl.ds(row, BLOCK), :], ks_ref[...])
         running = jnp.max(s, axis=1, keepdims=True)
         weights = jnp.exp(s - running)
@@ -119,10 +113,8 @@
 
 
 def on_device(query_in, key_in, value_in, block_lists):
-    pair_rows = lax.all_to_all(
-        jnp.stack([key_in, value_in], axis=0), "head", split_axis=2, concat_axis=1, tiled=True
-    )
-    key_rows, value_rows = pair_rows[0], pair_rows[1]
+    key_rows = lax.all_to_all(key_in, "head", split_axis=1, concat_axis=0, tiled=True)
+    value_rows = lax.all_to_all(value_in, "head", split_axis=1, concat_axis=0, tiled=True)
     queries = lax.all_to_all(query_in, "head", split_axis=1, concat_axis=0, tiled=True)
     seq_rows, width = queries.shape
 
@@ -145,24 +137,23 @@
     send_idx = jnp.sum(
         jnp.where(slot_hit, jnp.arange(per_dev, dtype=jnp.int32)[None, None, :], 0), axis=2
     ).reshape(-1)
-    key_blocks = key_rows.reshape(per_dev, BLOCK, width)
-    value_blocks = value_rows.reshape(per_dev, BLOCK, width)
-    outgoing = jnp.stack(
-        [jnp.take(key_blocks, send_idx, axis=0), jnp.take(value_blocks, send_idx, axis=0)], axis=1
-    ).reshape(seq_count, CAP, 2, BLOCK, width)
-    arrivals = []
-    for shift in range(1, seq_count):
-        parcel = lax.dynamic_index_in_dim(
-            outgoing, (seq_index + shift) % seq_count, axis=0, keepdims=False
-        )
-        arrivals.append(
-            lax.ppermute(
-                parcel, "seq", [(i, (i + shift) % seq_count) for i in range(seq_count)]
+    def exchange(rows):
+        blocks = jnp.take(rows.reshape(per_dev, BLOCK, width), send_idx, axis=0)
+        outgoing = blocks.reshape(seq_count, CAP, BLOCK, width)
+        arrivals = []
+        for shift in range(1, seq_count):
+            parcel = lax.dynamic_index_in_dim(
+                outgoing, (seq_index + shift) % seq_count, axis=0, keepdims=False
             )
-        )
-    arrived = jnp.stack(arrivals, axis=0)
-    remote_keys = arrived[:, :, 0].reshape((seq_count - 1) * CAP * BLOCK, width)
-    remote_values = arrived[:, :, 1].reshape((seq_count - 1) * CAP * BLOCK, width)
+            arrivals.append(
+                lax.ppermute(
+                    parcel, "seq", [(i, (i + shift) % seq_count) for i in range(seq_count)]
+                )
+            )
+        return jnp.stack(arrivals, axis=0).reshape((seq_count - 1) * CAP * BLOCK, width)
+
+    remote_keys = exchange(key_rows)
+    remote_values = exchange(value_rows)
 
     own_lists = lax.dynamic_slice_in_dim(block_lists, seq_index * per_dev, per_dev, 0)
     owners = own_lists // per_dev

time: 273 us -> 249 us (0.912)
  waiting for transfers between devices: 108 us -> 91.5 us
  local copies, waits for them, and re-layouts: 35 us -> 27.5 us
  starting transfers between devices: 22.7 us -> 30 us
  Pallas kernels: 57.8 us -> 52.9 us
    all_to_all x1 -> x2, waiting for transfers between devices: 66.6 us -> 56.4 us  [the longest x1 35.6 us: on_device(): lax.all_to_all(value_in, 'head', split_axis=1, concat_axis=0, tiled=True)]
    ppermute x3 -> x6, waiting for transfers between devices: 35.1 us -> 27.5 us  [exchange(): lax.ppermute(parcel, 'seq', [(i, (i + shift) % seq_count) for i in range(...]
    another operation x1 -> x0, local copies, waits for them, and re-layouts: 5.63 us -> none  [on_device(): jnp.stack([key_in, value_in], axis=0)]
    slice x1 -> x0, other arithmetic: 5.24 us -> none  [on_device(): key_rows, value_rows = (pair_rows[0], pair_rows[1])]
    pallas_call x2, Pallas kernels: 47 us -> 42.1 us  [sparse_attention(): pl.pallas_call(sparse_kernel, out_shape=jax.ShapeDtypeStruct((rows, heads...]
    ppermute x3 -> x6, starting transfers between devices: 1.72 us -> 5.62 us  [exchange(): lax.ppermute(parcel, 'seq', [(i, (i + shift) % seq_count) for i in range(...]
    all_to_all x1 -> x2, starting transfers between devices: 6.32 us -> 10.1 us  [the longest x1 6.45 us: on_device(): lax.all_to_all(value_in, 'head', split_axis=1, concat_axis=0, tiled=True)]
    convert_element_type x1 -> x3, other arithmetic: 3.32 us -> 7.13 us  [pool_tokens(): matrix.astype(jnp.float32)]
  transfers between devices with their start and end apart: 9 -> 13, of which waited for: 5 -> 7; matrix products, arithmetic and copies ran while one was open for 22% -> 23% of each run, Pallas kernels for 17% -> 17%
where the time goes in v5:
time: 249 us; the launch traced here: 248 us
  waiting for transfers between devices  91.5 us (37%)
  Pallas kernels  52.9 us (21%)
  other arithmetic  31.8 us (13%)
  starting transfers between devices  30 us (12%)
  local copies, waits for them, and re-layouts  27.5 us (11%)
  between operations  14.2 us (6%)
    pallas_call x2, Pallas kernels, sparse_attention(): pl.pallas_call(sparse_kernel, out_shape=jax.ShapeDtypeStruct((rows, heads...  42.1 us
    all_to_all x1, waiting for transfers between devices, on_device(): lax.all_to_all(value_in, 'head', split_axis=1, concat_axis=0, tiled=True)  35.6 us
    ppermute x6, waiting for transfers between devices, exchange(): lax.ppermute(parcel, 'seq', [(i, (i + shift) % seq_count) for i in range(...  27.5 us
    all_to_all x1, waiting for transfers between devices, on_device(): lax.all_to_all(key_in, 'head', split_axis=1, concat_axis=0, tiled=True)  20.8 us
    convert_element_type x3, local copies, waits for them, and re-layouts, pool_tokens(): matrix.astype(jnp.float32)  11.1 us
    pallas_call x1, Pallas kernels, draft_attention(): pl.pallas_call(draft_kernel, out_shape=jax.ShapeDtypeStruct((rows, width)...  10.8 us
    reduce_sum x3, other arithmetic, pool_tokens(): return (grouped.sum(axis=1) * POOL ** (-0.5)).astype(jnp.bfloat16)  10.6 us
    all_to_all x2, starting transfers between devices, on_device(): lax.all_to_all(rows_part, 'head', split_axis=0, concat_axis=1, tiled=True)  9.83 us
  transfers between devices with their start and end apart: 13, of which 7 were waited for; matrix products, arithmetic and copies ran while one was open for 23% of the time, Pallas kernels for 17%

profile of v5, /device:TPU:0, one launch (start us, length us, event | category | flops | bytes accessed | tf_op | source)
XLA Modules:
  0.0 248.0 jit_solution(1767278123275394175)
XLA Ops:
  7.2 2.7 %copy.43 = bf16[32,4,8,768]{3,2,0,1:T(8,128)(2,1)} copy(bf16[32,4,8,768]{3,2,1,0:T(8,128)(2,1)} %bitcast.80) | data formatting | bytes 3145728 | tf_op jit(solution)/shard_map/all_to_all | solution.py:117
  9.8 6.4 %all-to-all-start.2 = ((bf16[256,4,768]{2,0,1:T(8,128)(2,1)}), bf16[256,4,768]{2,0,1:T(8,128)(2,1)S(1)}, u32[]{:S(2)}, u32[]{:S(2)}) async-start(bf16[256,4,768]{2,0,1:T(8,128)(2,1)} %bitcast.59), calls=%async_computation.2 | async-start | bytes 3145728 | tf_op jit(solution)/shard_map/all_to_all | solution.py:117
  17.6 35.6 %all-to-all-done.2 = bf16[256,4,768]{2,0,1:T(8,128)(2,1)S(1)} async-done(((bf16[256,4,768]{2,0,1:T(8,128)(2,1)}), bf16[256,4,768]{2,0,1:T(8,128)(2,1)S(1)}, u32[]{:S(2)}, u32[]{:S(2)}) %all-to-all-start.2) | async-done | bytes 1572896 | tf_op jit(solution)/shard_map/all_to_all | solution.py:117
  53.2 3.7 %all-to-all-start.1 = ((bf16[256,4,768]{2,0,1:T(8,128)(2,1)}), bf16[256,4,768]{2,0,1:T(8,128)(2,1)S(1)}, u32[]{:S(2)}, u32[]{:S(2)}) async-start(bf16[256,4,768]{2,0,1:T(8,128)(2,1)} %bitcast.74), calls=%async_computation.1 | async-start | bytes 3145728 | tf_op jit(solution)/shard_map/all_to_all | solution.py:116
  58.5 2.7 %copy.45 = bf16[32,4,8,768]{3,2,0,1:T(8,128)(2,1)} copy(bf16[32,4,8,768]{3,2,1,0:T(8,128)(2,1)} %bitcast.82) | data formatting | bytes 3145728 | tf_op jit(solution)/shard_map/all_to_all | solution.py:118
  63.1 4.8 %reshape.85 = f32[256,4,768]{2,1,0:T(4,128)} reshape(f32[4,256,768]{2,1,0:T(8,128)} %bitcast_convert_fusion) | data formatting | bytes 6291456 | tf_op jit(solution)/shard_map/convert_element_type | solution.py:17
  67.9 4.6 %reduce_sum.38 = f32[256,768]{1,0:T(8,128)} reduce(f32[256,4,768]{2,1,0:T(4,128)} %reshape.85, f32[]{:T(128)} %constant.110.clone.1), dimensions={1}, to_apply=%region_2.0 | reduce | flops 589824 | bytes 3932164 | tf_op jit(solution)/shard_map/reduce_sum | solution.py:18
  72.6 20.8 %all-to-all-done.1 = bf16[256,4,768]{2,0,1:T(8,128)(2,1)S(1)} async-done(((bf16[256,4,768]{2,0,1:T(8,128)(2,1)}), bf16[256,4,768]{2,0,1:T(8,128)(2,1)S(1)}, u32[]{:S(2)}, u32[]{:S(2)}) %all-to-all-start.1) | async-done | bytes 1572896 | tf_op jit(solution)/shard_map/all_to_all | solution.py:116
  93.4 4.4 %all-to-all-start = ((bf16[256,4,768]{2,0,1:T(8,128)(2,1)}), bf16[256,4,768]{2,0,1:T(8,128)(2,1)}, u32[]{:S(2)}, u32[]{:S(2)}) async-start(bf16[256,4,768]{2,0,1:T(8,128)(2,1)} %bitcast.73), calls=%async_computation | async-start | bytes 3145728 | tf_op jit(solution)/shard_map/all_to_all | solution.py:118
  115.0 12.3 %collective-permute-done = bf16[2,128,768]{2,1,0:T(8,128)(2,1)} collective-permute-done((bf16[2,128,768]{2,1,0:T(8,128)(2,1)}, bf16[2,128,768]{2,1,0:T(8,128)(2,1)}, u32[]{:S(2)}, u32[]{:S(2)}) %collective-permute-start) | collective-permute-done | bytes 393248 | tf_op jit(solution)/shard_map/ppermute | solution.py:149
  129.9 3.1 %reshape.84 = f32[256,4,768]{2,1,0:T(4,128)S(1)} reshape(f32[4,256,768]{2,1,0:T(8,128)} %bitcast_convert_fusion.1) | data formatting | bytes 6291456 | tf_op jit(solution)/shard_map/convert_element_type | solution.py:17
  133.0 3.0 %reduce_sum.37 = f32[256,768]{1,0:T(8,128)} reduce(f32[256,4,768]{2,1,0:T(4,128)S(1)} %reshape.84, f32[]{:T(128)} %constant.110.clone.1), dimensions={1}, to_apply=%region_1.0 | reduce | flops 589824 | bytes 3932164 | tf_op jit(solution)/shard_map/reduce_sum | solution.py:18
  139.9 4.3 %collective-permute-done.3 = bf16[2,128,768]{2,1,0:T(8,128)(2,1)} collective-permute-done((bf16[2,128,768]{2,1,0:T(8,128)(2,1)}, bf16[2,128,768]{2,1,0:T(8,128)(2,1)}, u32[]{:S(2)}, u32[]{:S(2)}) %collective-permute-start.3) | collective-permute-done | bytes 393248 | tf_op jit(solution)/shard_map/ppermute | solution.py:149
  144.2 9.3 %collective-permute-done.4 = bf16[2,128,768]{2,1,0:T(8,128)(2,1)} collective-permute-done((bf16[2,128,768]{2,1,0:T(8,128)(2,1)}, bf16[2,128,768]{2,1,0:T(8,128)(2,1)}, u32[]{:S(2)}, u32[]{:S(2)}) %collective-permute-start.4) | collective-permute-done | bytes 393248 | tf_op jit(solution)/shard_map/ppermute | solution.py:149
  153.5 2.4 pad_maximum_fusion.1
  155.9 21.0 %shard_map.61 = bf16[1024,384]{1,0:T(8,128)(2,1)} custom-call(s32[96]{0:T(128)} %reshape.74.tbl_ref, bf16[1024,768]{1,0:T(8,128)(2,1)} %bitcast.4.q_ref, bf16[1024,768]{1,0:T(8,128)(2,1)} %bitcast.67, bf16[1024,768]{1,0:T(8,128)(2,1)} %bitcast.64, bf16[768,768]{1,0:T(8,128)(2,1)} %bitcast.69, bf16[768,768]{1,0:T(8,128)(2,1)} %bitcast.71), custom_call_target="tpu_custom_call" | custom-call | tf_op jit(solution)/shard_map/pallas_call | solution.py:66
  177.0 4.7 %all-to-all-start.4 = ((bf16[4,256,384]{2,1,0:T(8,128)(2,1)}), bf16[4,256,384]{2,1,0:T(8,128)(2,1)S(1)}, u32[]{:S(2)}, u32[]{:S(2)}) async-start(bf16[4,256,384]{2,1,0:T(8,128)(2,1)} %bitcast.79), calls=%async_computation.4 | async-start | bytes 1572864 | tf_op jit(solution)/shard_map/all_to_all | solution.py:177
  182.5 21.1 %shard_map.60 = bf16[1024,384]{1,0:T(8,128)(2,1)} custom-call(s32[96]{0:T(128)} %reshape.74.tbl_ref, bf16[1024,768]{1,0:T(8,128)(2,1)} %bitcast.4.q_ref, bf16[1024,768]{1,0:T(8,128)(2,1)} %bitcast.68, bf16[1024,768]{1,0:T(8,128)(2,1)} %bitcast.65, bf16[768,768]{1,0:T(8,128)(2,1)} %bitcast.70, bf16[768,768]{1,0:T(8,128)(2,1)} %bitcast.72), custom_call_target="tpu_custom_call" | custom-call | tf_op jit(solution)/shard_map/pallas_call | solution.py:66
  203.6 5.1 %all-to-all-start.3 = ((bf16[4,256,384]{2,1,0:T(8,128)(2,1)}), bf16[4,256,384]{2,1,0:T(8,128)(2,1)}, u32[]{:S(2)}, u32[]{:S(2)}) async-start(bf16[4,256,384]{2,1,0:T(8,128)(2,1)} %bitcast.78), calls=%async_computation.3 | async-start | bytes 1572864 | tf_op jit(solution)/shard_map/all_to_all | solution.py:177
  208.7 3.3 %bitcast_convert_fusion.2 = f32[4,256,768]{2,1,0:T(8,128)} fusion(bf16[256,4,768]{2,0,1:T(8,128)(2,1)} %all-to-all-done), kind=kLoop, calls=%fused_computation.9 | loop fusion | flops 786432 | bytes 4718592 | tf_op jit(solution)/shard_map/convert_element_type | solution.py:17
  212.0 3.1 %reshape.83 = f32[256,4,768]{2,1,0:T(4,128)S(1)} reshape(f32[4,256,768]{2,1,0:T(8,128)} %bitcast_convert_fusion.2) | data formatting | bytes 6291456 | tf_op jit(solution)/shard_map/convert_element_type | solution.py:17
  215.1 3.0 %reduce_sum.36 = f32[256,768]{1,0:T(8,128)} reduce(f32[256,4,768]{2,1,0:T(4,128)S(1)} %reshape.83, f32[]{:T(128)} %constant.110.clone.1), dimensions={1}, to_apply=%region_0.0 | reduce | flops 589824 | bytes 3932164 | tf_op jit(solution)/shard_map/reduce_sum | solution.py:18
  220.1 7.6 %all-to-all-done.3 = bf16[4,256,384]{2,1,0:T(8,128)(2,1)} async-done(((bf16[4,256,384]{2,1,0:T(8,128)(2,1)}), bf16[4,256,384]{2,1,0:T(8,128)(2,1)}, u32[]{:S(2)}, u32[]{:S(2)}) %all-to-all-start.3) | async-done | bytes 786464 | tf_op jit(solution)/shard_map/all_to_all | solution.py:177
  230.3 10.8 %shard_map.59 = bf16[256,768]{1,0:T(8,128)(2,1)} custom-call(bf16[256,768]{1,0:T(8,128)(2,1)} %multiply_convert_fusion.2.q_ref, bf16[1024,768]{1,0:T(8,128)(2,1)} %all-gather.3.cloned.1.call-done.k_ref, bf16[1024,768]{1,0:T(8,128)(2,1)} %all-gather.5.cloned.1.call-done.v_ref), custom_call_target="tpu_custom_call" | custom-call | tf_op jit(solution)/shard_map/pallas_call | solution.py:102
  (70 shorter events, 33.9 us)
Async XLA Ops:
  9.8 6.5 %copy-start.5 = (bf16[256,3072]{1,0:T(8,128)(2,1)S(1)}, bf16[256,3072]{1,0:T(8,128)(2,1)}, u32[]{:S(2)}) copy-start(bf16[256,3072]{1,0:T(8,128)(2,1)} %param.7) | copy-start | bytes 4718596
  9.8 43.4 %all-to-all-start.2 = ((bf16[256,4,768]{2,0,1:T(8,128)(2,1)}), bf16[256,4,768]{2,0,1:T(8,128)(2,1)S(1)}, u32[]{:S(2)}, u32[]{:S(2)}) async-start(bf16[256,4,768]{2,0,1:T(8,128)(2,1)} %bitcast.59), calls=%async_computation.2 | async-start | bytes 3145728 | tf_op jit(solution)/shard_map/all_to_all | solution.py:117
  53.2 50.0 %copy-start = (bf16[256,4,768]{2,0,1:T(8,128)(2,1)}, bf16[256,4,768]{2,0,1:T(8,128)(2,1)S(1)}, u32[]{:S(2)}) copy-start(bf16[256,4,768]{2,0,1:T(8,128)(2,1)S(1)} %all-to-all-done.2) | copy-start | bytes 4718596
  53.2 3.7 %copy-start.6 = (s32[32,12]{0,1:T(8,128)S(1)}, s32[32,12]{0,1:T(8,128)}, u32[]{:S(2)}) copy-start(s32[32,12]{0,1:T(8,128)} %param.9) | copy-start | bytes 4612
  53.2 40.1 %all-to-all-start.1 = ((bf16[256,4,768]{2,0,1:T(8,128)(2,1)}), bf16[256,4,768]{2,0,1:T(8,128)(2,1)S(1)}, u32[]{:S(2)}, u32[]{:S(2)}) async-start(bf16[256,4,768]{2,0,1:T(8,128)(2,1)} %bitcast.74), calls=%async_computation.1 | async-start | bytes 3145728 | tf_op jit(solution)/shard_map/all_to_all | solution.py:116
  93.4 34.6 %copy-start.1 = (bf16[256,4,768]{2,0,1:T(8,128)(2,1)}, bf16[256,4,768]{2,0,1:T(8,128)(2,1)S(1)}, u32[]{:S(2)}) copy-start(bf16[256,4,768]{2,0,1:T(8,128)(2,1)S(1)} %all-to-all-done.1) | copy-start | bytes 4718596
  93.4 62.6 %all-to-all-start = ((bf16[256,4,768]{2,0,1:T(8,128)(2,1)}), bf16[256,4,768]{2,0,1:T(8,128)(2,1)}, u32[]{:S(2)}, u32[]{:S(2)}) async-start(bf16[256,4,768]{2,0,1:T(8,128)(2,1)} %bitcast.73), calls=%async_computation | async-start | bytes 3145728 | tf_op jit(solution)/shard_map/all_to_all | solution.py:118
  97.7 132.6 %all-gather.5.cloned.1.call-start = ((), (), s32[]{:S(2)}) async-start(), calls=%async_computation.6 | async-start | bytes 1966080 | tf_op jit(solution)/shard_map/all_gather | solution.py:122
  108.2 19.1 %collective-permute-start = (bf16[2,128,768]{2,1,0:T(8,128)(2,1)}, bf16[2,128,768]{2,1,0:T(8,128)(2,1)}, u32[]{:S(2)}, u32[]{:S(2)}) collective-permute-start(bf16[2,128,768]{2,1,0:T(8,128)(2,1)} %get-tuple-element.6), channel_id=1, source_target_pairs={{0,4},{4,8},{8,12},{12,0},{1,5},{5,9},{9,13},{13,1},{2,6},{6,10},{... | collective-permute-start | bytes 1179656 | tf_op jit(solution)/shard_map/ppermute | solution.py:149
  109.0 27.0 %collective-permute-start.2 = (bf16[2,128,768]{2,1,0:T(8,128)(2,1)}, bf16[2,128,768]{2,1,0:T(8,128)(2,1)}, u32[]{:S(2)}, u32[]{:S(2)}) collective-permute-start(bf16[2,128,768]{2,1,0:T(8,128)(2,1)} %get-tuple-element.7), channel_id=1, source_target_pairs={{0,12},{4,0},{8,4},{12,8},{1,13},{5,1},{9,5},{13,9},{2,14},{6,2},{... | collective-permute-start | bytes 1179656 | tf_op jit(solution)/shard_map/ppermute | solution.py:149
  110.7 26.9 %collective-permute-start.1 = (bf16[2,128,768]{2,1,0:T(8,128)(2,1)S(1)}, bf16[2,128,768]{2,1,0:T(8,128)(2,1)}, u32[]{:S(2)}, u32[]{:S(2)}) collective-permute-start(bf16[2,128,768]{2,1,0:T(8,128)(2,1)S(1)} %get-tuple-element.8), channel_id=1, source_target_pairs={{0,8},{4,12},{8,0},{12,4},{1,9},{5,13},{9,1},{13,5},{2,10},{6,14},... | collective-permute-start | bytes 1179656 | tf_op jit(solution)/shard_map/ppermute | solution.py:149
  113.3 31.0 %collective-permute-start.3 = (bf16[2,128,768]{2,1,0:T(8,128)(2,1)}, bf16[2,128,768]{2,1,0:T(8,128)(2,1)}, u32[]{:S(2)}, u32[]{:S(2)}) collective-permute-start(bf16[2,128,768]{2,1,0:T(8,128)(2,1)} %get-tuple-element.3), channel_id=1, source_target_pairs={{0,4},{4,8},{8,12},{12,0},{1,5},{5,9},{9,13},{13,1},{2,6},{6,10},{... | collective-permute-start | bytes 1179656 | tf_op jit(solution)/shard_map/ppermute | solution.py:149
  113.3 31.0 %collective-permute-start.5 = (bf16[2,128,768]{2,1,0:T(8,128)(2,1)}, bf16[2,128,768]{2,1,0:T(8,128)(2,1)}, u32[]{:S(2)}, u32[]{:S(2)}) collective-permute-start(bf16[2,128,768]{2,1,0:T(8,128)(2,1)} %get-tuple-element.4), channel_id=1, source_target_pairs={{0,12},{4,0},{8,4},{12,8},{1,13},{5,1},{9,5},{13,9},{2,14},{6,2},{... | collective-permute-start | bytes 1179656 | tf_op jit(solution)/shard_map/ppermute | solution.py:149
  127.4 26.2 %collective-permute-start.4 = (bf16[2,128,768]{2,1,0:T(8,128)(2,1)}, bf16[2,128,768]{2,1,0:T(8,128)(2,1)}, u32[]{:S(2)}, u32[]{:S(2)}) collective-permute-start(bf16[2,128,768]{2,1,0:T(8,128)(2,1)} %get-tuple-element.5), channel_id=1, source_target_pairs={{0,8},{4,12},{8,0},{12,4},{1,9},{5,13},{9,1},{13,5},{2,10},{6,14},... | collective-permute-start | bytes 1179656 | tf_op jit(solution)/shard_map/ppermute | solution.py:149
  177.0 4.7 %copy-start.4 = (f32[256,768]{1,0:T(8,128)S(1)}, f32[256,768]{1,0:T(8,128)}, u32[]{:S(2)}) copy-start(f32[256,768]{1,0:T(8,128)} %reduce_sum.37) | copy-start | bytes 2359300
  177.0 26.6 %all-to-all-start.4 = ((bf16[4,256,384]{2,1,0:T(8,128)(2,1)}), bf16[4,256,384]{2,1,0:T(8,128)(2,1)S(1)}, u32[]{:S(2)}, u32[]{:S(2)}) async-start(bf16[4,256,384]{2,1,0:T(8,128)(2,1)} %bitcast.79), calls=%async_computation.4 | async-start | bytes 1572864 | tf_op jit(solution)/shard_map/all_to_all | solution.py:177
  181.7 48.6 %all-gather.3.cloned.1.call-start = ((), (), s32[]{:S(2)}) async-start(), calls=%async_computation.5 | async-start | bytes 1966080 | tf_op jit(solution)/shard_map/all_gather | solution.py:121
  203.6 5.1 %copy-start.2 = (bf16[4,256,384]{2,1,0:T(8,128)(2,1)}, bf16[4,256,384]{2,1,0:T(8,128)(2,1)S(1)}, u32[]{:S(2)}) copy-start(bf16[4,256,384]{2,1,0:T(8,128)(2,1)S(1)} %all-to-all-done.4) | copy-start | bytes 2359300
  203.6 24.1 %all-to-all-start.3 = ((bf16[4,256,384]{2,1,0:T(8,128)(2,1)}), bf16[4,256,384]{2,1,0:T(8,128)(2,1)}, u32[]{:S(2)}, u32[]{:S(2)}) async-start(bf16[4,256,384]{2,1,0:T(8,128)(2,1)} %bitcast.78), calls=%async_computation.3 | async-start | bytes 1572864 | tf_op jit(solution)/shard_map/all_to_all | solution.py:177
  218.1 9.6 %copy-start.3 = (bf16[4,256,384]{2,1,0:T(8,128)(2,1)S(1)}, bf16[4,256,384]{2,1,0:T(8,128)(2,1)}, u32[]{:S(2)}) copy-start(bf16[4,256,384]{2,1,0:T(8,128)(2,1)} %copy-done.2) | copy-start | bytes 2359300
Sparse Core Ops, SparseCore 0:
  100.1 28.6 all-gather.4
  184.7 20.1 all-gather.2

commit v6 on v5

--- a/solution.py
+++ b/solution.py
@@ -11,6 +11,8 @@
 CAP = 2
 SCALE = HD ** (-0.5)
 DRAFT_ROWS = 128
+PAIR = 2
+EXP2_SCALE = SCALE * 1.4426950408889634
 
 
 def pool_tokens(matrix):
@@ -18,77 +20,85 @@
     return (grouped.sum(axis=1) * POOL ** (-0.5)).astype(jnp.bfloat16)
 
 
-def _scores(q, k):
-    return lax.dot_general(
-        q, k, (((1,), (1,)), ((), ())), preferred_element_type=jnp.float32
-    ) * SCALE
-
-
-def sparse_kernel(tbl_ref, q_ref, k_ref, v_ref, kr_ref, vr_ref, o_ref, ks_ref, vs_ref):
+def sparse_kernel(tbl_ref, q_ref, *refs):
+    near_k, near_v = refs[0], refs[1]
+    far_count = (len(refs) - 5) // 2
+    far_k = refs[2:2 + far_count]
+    far_v = refs[2 + far_count:2 + 2 * far_count]
+    o_ref, kall_ref, vall_ref = refs[2 + 2 * far_count:]
     per_dev = q_ref.shape[0] // BLOCK
-    sel = ks_ref.shape[0] // BLOCK
-    remote_count = kr_ref.shape[0] // BLOCK
-
-    def body(i, carry):
+    sel = tbl_ref.shape[0] // per_dev
+    near_rows = near_k.shape[0]
+    kall_ref[0:near_rows, :] = near_k[...]
+    vall_ref[0:near_rows, :] = near_v[...]
+    offset = near_rows
+    for kr, vr in zip(far_k, far_v):
+        kall_ref[offset:offset + kr.shape[0], :] = kr[...]
+        vall_ref[offset:offset + vr.shape[0], :] = vr[...]
+        offset += kr.shape[0]
+    last = offset // BLOCK - 1
+
+    def one_block(i):
         row = pl.multiple_of(i * BLOCK, BLOCK)
+        keys = []
+        values = []
         for j in range(sel):
-            idx = tbl_ref[i * sel + j]
-            near = pl.multiple_of(jnp.minimum(idx, per_dev - 1) * BLOCK, BLOCK)
-            far = pl.multiple_of(jnp.clip(idx - per_dev, 0, remote_count - 1) * BLOCK, BLOCK)
-            is_near = idx < per_dev
-            ks_ref[j * BLOCK:(j + 1) * BLOCK, :] = jnp.where(
-                is_near, k_ref[pl.ds(near, BLOCK), :], kr_ref[pl.ds(far, BLOCK), :]
-            )
-            vs_ref[j * BLOCK:(j + 1) * BLOCK, :] = jnp.where(
-                is_near, v_ref[pl.ds(near, BLOCK), :], vr_ref[pl.ds(far, BLOCK), :]
-            )
-        s = _scores(q_ref[pl.ds(row, BLOCK), :], ks_ref[...])
-        running = jnp.max(s, axis=1, keepdims=True)
-        weights = jnp.exp(s - running)
+            start = pl.multiple_of(jnp.clip(tbl_ref[i * sel + j], 0, last) * BLOCK, BLOCK)
+            keys.append(kall_ref[pl.ds(start, BLOCK), :])
+            values.append(vall_ref[pl.ds(start, BLOCK), :])
+        raw = lax.dot_general(
+            q_ref[pl.ds(row, BLOCK), :], jnp.concatenate(keys, axis=0),
+            (((1,), (1,)), ((), ())), preferred_element_type=jnp.float32,
+        )
+        running = jnp.max(raw, axis=1, keepdims=True)
+        weights = jnp.exp2((raw - running) * EXP2_SCALE)
         totals = jnp.sum(weights, axis=1, keepdims=True)
         weighted = jnp.dot(
-            weights.astype(jnp.bfloat16), vs_ref[...], preferred_element_type=jnp.float32
+            weights.astype(jnp.bfloat16), jnp.concatenate(values, axis=0),
+            preferred_element_type=jnp.float32,
         )
         o_ref[pl.ds(row, BLOCK), :] = (weighted / totals).astype(o_ref.dtype)
+
+    def body(i, carry):
+        for lane in range(PAIR):
+            one_block(i * PAIR + lane)
         return carry
 
-    lax.fori_loop(0, per_dev, body, 0)
-
-
-def sparse_attention(tbl, queries, keys, values, far_keys, far_values, sel, head_lo, heads):
+    lax.fori_loop(0, per_dev // PAIR, body, 0)
+    for i in range(per_dev - per_dev % PAIR, per_dev):
+        one_block(i)
+
+
+def sparse_attention(tbl, queries, keys, values, far_keys, far_values, head_lo, heads):
     rows = queries.shape[0]
-    near_rows = keys.shape[0]
-    far_rows = far_keys.shape[0]
 
     def column(h, t):
         return (0, h + head_lo)
 
+    operands = [queries, keys, values] + list(far_keys) + list(far_values)
+    total_rows = keys.shape[0] + sum(k.shape[0] for k in far_keys)
     return pl.pallas_call(
         sparse_kernel,
         out_shape=jax.ShapeDtypeStruct((rows, heads * HD), jnp.bfloat16),
         grid_spec=pltpu.PrefetchScalarGridSpec(
             num_scalar_prefetch=1,
             grid=(heads,),
-            in_specs=[
-                pl.BlockSpec((rows, HD), column),
-                pl.BlockSpec((near_rows, HD), column),
-                pl.BlockSpec((near_rows, HD), column),
-                pl.BlockSpec((far_rows, HD), column),
-                pl.BlockSpec((far_rows, HD), column),
-            ],
+            in_specs=[pl.BlockSpec((x.shape[0], HD), column) for x in operands],
             out_specs=pl.BlockSpec((rows, HD), lambda h, t: (0, h)),
             scratch_shapes=[
-                pltpu.VMEM((sel * BLOCK, HD), jnp.bfloat16),
-                pltpu.VMEM((sel * BLOCK, HD), jnp.bfloat16),
+                pltpu.VMEM((total_rows, HD), jnp.bfloat16),
+                pltpu.VMEM((total_rows, HD), jnp.bfloat16),
             ],
         ),
-    )(tbl, queries, keys, values, far_keys, far_values)
+    )(tbl, *operands)
 
 
 def draft_kernel(q_ref, k_ref, v_ref, o_ref):
-    s = _scores(q_ref[...], k_ref[...])
-    running = jnp.max(s, axis=1, keepdims=True)
-    weights = jnp.exp(s - running)
+    raw = lax.dot_general(
+        q_ref[...], k_ref[...], (((1,), (1,)), ((), ())), preferred_element_type=jnp.float32
+    )
+    running = jnp.max(raw, axis=1, keepdims=True)
+    weights = jnp.exp2((raw - running) * EXP2_SCALE)
     totals = jnp.sum(weights, axis=1, keepdims=True)
     weighted = jnp.dot(weights.astype(jnp.bfloat16), v_ref[...], preferred_element_type=jnp.float32)
     o_ref[...] = (weighted / totals).astype(o_ref.dtype)
@@ -150,7 +160,7 @@
                     parcel, "seq", [(i, (i + shift) % seq_count) for i in range(seq_count)]
                 )
             )
-        return jnp.stack(arrivals, axis=0).reshape((seq_count - 1) * CAP * BLOCK, width)
+        return [a.reshape(CAP * BLOCK, width) for a in arrivals]
 
     remote_keys = exchange(key_rows)
     remote_values = exchange(value_rows)
@@ -164,6 +174,8 @@
     joint_pos = jnp.where(distance == 0, within, per_dev + (distance - 1) * CAP + ranks_used)
     table = jnp.clip(joint_pos, 0, per_dev + (seq_count - 1) * CAP - 1).reshape(-1).astype(jnp.int32)
 
+    draft_out = draft_attention(pool_tokens(queries), draft_keys, draft_values)
+    queries, draft_out = lax.optimization_barrier((queries, draft_out))
     heads = width // HD
     first = max(1, heads // 2)
     pieces = []
@@ -171,14 +183,11 @@
         if count == 0:
             continue
         rows_part = sparse_attention(
-            table, queries, key_rows, value_rows, remote_keys, remote_values,
-            select_count, head_lo, count,
+            table, queries, key_rows, value_rows, remote_keys, remote_values, head_lo, count,
         )
         back = lax.all_to_all(rows_part, "head", split_axis=0, concat_axis=1, tiled=True)
         pieces.append(back.reshape(back.shape[0], -1, count * HD))
     sparse_out = jnp.concatenate(pieces, axis=2).reshape(pieces[0].shape[0], -1)
-
-    draft_out = draft_attention(pool_tokens(queries), draft_keys, draft_values)
     return (draft_out, sparse_out)
 
 

time: 249 us -> 238 us (0.956)
  blocking collectives: 0 us -> 24.3 us
  waiting for transfers between devices: 91.5 us -> 75.9 us
  Pallas kernels: 52.9 us -> 41.4 us
  starting transfers between devices: 30 us -> 22.8 us
  other arithmetic: 31.8 us -> 28.3 us
    all_to_all x0 -> x1, blocking collectives: none -> 24.3 us  [on_device(): lax.all_to_all(rows_part, 'head', split_axis=0, concat_axis=1, tiled=True)]
    all_to_all x1, waiting for transfers between devices: 35.6 us -> 18.7 us  [on_device(): lax.all_to_all(value_in, 'head', split_axis=1, concat_axis=0, tiled=True)]
    all_to_all x1, waiting for transfers between devices: 20.8 us -> 35.6 us  [on_device(): lax.all_to_all(key_in, 'head', split_axis=1, concat_axis=0, tiled=True)]
    ppermute x6, waiting for transfers between devices: 27.5 us -> 15.8 us  [exchange(): lax.ppermute(parcel, 'seq', [(i, (i + shift) % seq_count) for i in range(...]
    pallas_call x2, Pallas kernels: 42.1 us -> 30.7 us  [sparse_attention(): pl.pallas_call(sparse_kernel, out_shape=jax.ShapeDtypeStruct((rows, heads...]
    all_to_all x2 -> x1, starting transfers between devices: 9.83 us -> 4.84 us  [on_device(): lax.all_to_all(rows_part, 'head', split_axis=0, concat_axis=1, tiled=True)]
    another operation x2 -> x0, other arithmetic: 4.76 us -> none  [exchange(): jnp.stack(arrivals, axis=0).reshape((seq_count - 1) * CAP * BLOCK, width)]
    all_to_all x1, starting transfers between devices: 6.45 us -> 3.56 us  [on_device(): lax.all_to_all(value_in, 'head', split_axis=1, concat_axis=0, tiled=True)]
  transfers between devices with their start and end apart: 13 -> 12, of which waited for: 7 -> 5; matrix products, arithmetic and copies ran while one was open for 23% -> 23% of each run, Pallas kernels for 17% -> 11%
where the time goes in v6:
time: 238 us; the launch traced here: 236 us
  waiting for transfers between devices  75.9 us (32%)
  Pallas kernels  41.4 us (17%)
  local copies, waits for them, and re-layouts  29.3 us (12%)
  other arithmetic  28.3 us (12%)
  blocking collectives  24.3 us (10%)
  starting transfers between devices  22.8 us (10%)
  between operations  14.3 us (6%)
    all_to_all x1, waiting for transfers between devices, on_device(): lax.all_to_all(key_in, 'head', split_axis=1, concat_axis=0, tiled=True)  35.6 us
    pallas_call x2, Pallas kernels, sparse_attention(): pl.pallas_call(sparse_kernel, out_shape=jax.ShapeDtypeStruct((rows, heads...  30.7 us
    all_to_all x1, blocking collectives, on_device(): lax.all_to_all(rows_part, 'head', split_axis=0, concat_axis=1, tiled=True)  24.3 us
    all_to_all x1, waiting for transfers between devices, on_device(): lax.all_to_all(value_in, 'head', split_axis=1, concat_axis=0, tiled=True)  18.7 us
    ppermute x6, waiting for transfers between devices, exchange(): lax.ppermute(parcel, 'seq', [(i, (i + shift) % seq_count) for i in range(...  15.8 us
    convert_element_type x3, local copies, waits for them, and re-layouts, pool_tokens(): matrix.astype(jnp.float32)  12.8 us
    reduce_sum x3, other arithmetic, pool_tokens(): return (grouped.sum(axis=1) * POOL ** (-0.5)).astype(jnp.bfloat16)  12.2 us
    pallas_call x1, Pallas kernels, draft_attention(): pl.pallas_call(draft_kernel, out_shape=jax.ShapeDtypeStruct((rows, width)...  10.7 us
  transfers between devices with their start and end apart: 12, of which 5 were waited for; matrix products, arithmetic and copies ran while one was open for 23% of the time, Pallas kernels for 11%

profile of v6, /device:TPU:0, one launch (start us, length us, event | category | flops | bytes accessed | tf_op | source)
XLA Modules:
  0.0 236.3 jit_solution(1028032357440700776)
XLA Ops:
  7.2 2.7 %copy.44 = bf16[32,4,8,768]{3,2,0,1:T(8,128)(2,1)} copy(bf16[32,4,8,768]{3,2,1,0:T(8,128)(2,1)} %bitcast.77) | data formatting | bytes 3145728 | tf_op jit(solution)/shard_map/all_to_all | solution.py:126
  9.8 6.4 %all-to-all-start.1 = ((bf16[256,4,768]{2,0,1:T(8,128)(2,1)}), bf16[256,4,768]{2,0,1:T(8,128)(2,1)S(1)}, u32[]{:S(2)}, u32[]{:S(2)}) async-start(bf16[256,4,768]{2,0,1:T(8,128)(2,1)} %bitcast.58), calls=%async_computation.1 | async-start | bytes 3145728 | tf_op jit(solution)/shard_map/all_to_all | solution.py:126
  17.6 35.6 %all-to-all-done.1 = bf16[256,4,768]{2,0,1:T(8,128)(2,1)S(1)} async-done(((bf16[256,4,768]{2,0,1:T(8,128)(2,1)}), bf16[256,4,768]{2,0,1:T(8,128)(2,1)S(1)}, u32[]{:S(2)}, u32[]{:S(2)}) %all-to-all-start.1) | async-done | bytes 1572896 | tf_op jit(solution)/shard_map/all_to_all | solution.py:126
  53.2 3.6 %all-to-all-start.2 = ((bf16[256,4,768]{2,0,1:T(8,128)(2,1)}), bf16[256,4,768]{2,0,1:T(8,128)(2,1)S(1)}, u32[]{:S(2)}, u32[]{:S(2)}) async-start(bf16[256,4,768]{2,0,1:T(8,128)(2,1)} %bitcast.67), calls=%async_computation.2 | async-start | bytes 3145728 | tf_op jit(solution)/shard_map/all_to_all | solution.py:127
  58.8 4.9 %reshape.100 = f32[256,4,768]{2,1,0:T(4,128)} reshape(f32[4,256,768]{2,1,0:T(8,128)} %bitcast_convert_fusion.1) | data formatting | bytes 6291456 | tf_op jit(solution)/shard_map/convert_element_type | solution.py:19
  63.6 4.6 %reduce_sum.37 = f32[256,768]{1,0:T(8,128)} reduce(f32[256,4,768]{2,1,0:T(4,128)} %reshape.100, f32[]{:T(128)} %constant.110.clone.1), dimensions={1}, to_apply=%region_1.0 | reduce | flops 589824 | bytes 3932164 | tf_op jit(solution)/shard_map/reduce_sum | solution.py:20
  70.3 2.7 %copy.45 = bf16[32,4,8,768]{3,2,0,1:T(8,128)(2,1)} copy(bf16[32,4,8,768]{3,2,1,0:T(8,128)(2,1)} %bitcast.79) | data formatting | bytes 3145728 | tf_op jit(solution)/shard_map/all_to_all | solution.py:128
  74.6 18.7 %all-to-all-done.2 = bf16[256,4,768]{2,0,1:T(8,128)(2,1)S(1)} async-done(((bf16[256,4,768]{2,0,1:T(8,128)(2,1)}), bf16[256,4,768]{2,0,1:T(8,128)(2,1)S(1)}, u32[]{:S(2)}, u32[]{:S(2)}) %all-to-all-start.2) | async-done | bytes 1572896 | tf_op jit(solution)/shard_map/all_to_all | solution.py:127
  93.2 4.4 %all-to-all-start = ((bf16[256,4,768]{2,0,1:T(8,128)(2,1)}), bf16[256,4,768]{2,0,1:T(8,128)(2,1)}, u32[]{:S(2)}, u32[]{:S(2)}) async-start(bf16[256,4,768]{2,0,1:T(8,128)(2,1)} %bitcast.68), calls=%async_computation | async-start | bytes 3145728 | tf_op jit(solution)/shard_map/all_to_all | solution.py:128
  97.7 2.0 bitcast_convert_fusion
  99.6 4.8 %reshape.101 = f32[256,4,768]{2,1,0:T(4,128)} reshape(f32[4,256,768]{2,1,0:T(8,128)} %bitcast_convert_fusion) | data formatting | bytes 6291456 | tf_op jit(solution)/shard_map/convert_element_type | solution.py:19
  104.5 4.6 %reduce_sum.38 = f32[256,768]{1,0:T(8,128)} reduce(f32[256,4,768]{2,1,0:T(4,128)} %reshape.101, f32[]{:T(128)} %constant.110.clone.1), dimensions={1}, to_apply=%region_2.0 | reduce | flops 589824 | bytes 3932164 | tf_op jit(solution)/shard_map/reduce_sum | solution.py:20
  109.1 1.9 multiply_convert_fusion
  124.4 13.2 %collective-permute-done = bf16[2,128,768]{2,1,0:T(8,128)(2,1)S(1)} collective-permute-done((bf16[2,128,768]{2,1,0:T(8,128)(2,1)S(1)}, bf16[2,128,768]{2,1,0:T(8,128)(2,1)S(1)}, u32[]{:S(2)}, u32[]{:S(2)}) %collective-permute-start) | collective-permute-done | bytes 393248 | tf_op jit(solution)/shard_map/ppermute | solution.py:159
  137.6 3.5 %bitcast_convert_fusion.2 = f32[4,256,768]{2,1,0:T(8,128)} fusion(bf16[256,4,768]{2,0,1:T(8,128)(2,1)} %all-to-all-done), kind=kLoop, calls=%fused_computation.9 | loop fusion | flops 786432 | bytes 4718592 | tf_op jit(solution)/shard_map/convert_element_type | solution.py:19
  141.1 3.1 %reshape.99 = f32[256,4,768]{2,1,0:T(4,128)S(1)} reshape(f32[4,256,768]{2,1,0:T(8,128)} %bitcast_convert_fusion.2) | data formatting | bytes 6291456 | tf_op jit(solution)/shard_map/convert_element_type | solution.py:19
  144.2 3.0 %reduce_sum.36 = f32[256,768]{1,0:T(8,128)} reduce(f32[256,4,768]{2,1,0:T(4,128)S(1)} %reshape.99, f32[]{:T(128)} %constant.110.clone.1), dimensions={1}, to_apply=%region_0.0 | reduce | flops 589824 | bytes 3932164 | tf_op jit(solution)/shard_map/reduce_sum | solution.py:20
  149.1 10.7 %shard_map.59 = bf16[256,768]{1,0:T(8,128)(2,1)} custom-call(bf16[256,768]{1,0:T(8,128)(2,1)} %multiply_convert_fusion.2.q_ref, bf16[1024,768]{1,0:T(8,128)(2,1)} %all-gather.3.cloned.1.call-done.k_ref, bf16[1024,768]{1,0:T(8,128)(2,1)} %all-gather.5.cloned.1.call-done.v_ref), custom_call_target="tpu_custom_call" | custom-call | tf_op jit(solution)/shard_map/pallas_call | solution.py:112
  159.9 2.5 %collective-permute-done.5 = bf16[2,128,768]{2,1,0:T(8,128)(2,1)} collective-permute-done((bf16[2,128,768]{2,1,0:T(8,128)(2,1)}, bf16[2,128,768]{2,1,0:T(8,128)(2,1)}, u32[]{:S(2)}, u32[]{:S(2)}) %collective-permute-start.5) | collective-permute-done | bytes 393248 | tf_op jit(solution)/shard_map/ppermute | solution.py:159
  162.4 15.4 %shard_map.61 = bf16[1024,384]{1,0:T(8,128)(2,1)} custom-call(s32[96]{0:T(128)} %reshape.86.tbl_ref, bf16[1024,768]{1,0:T(8,128)(2,1)} %bitcast.1.q_ref, bf16[1024,768]{1,0:T(8,128)(2,1)} %bitcast.62, bf16[1024,768]{1,0:T(8,128)(2,1)} %bitcast.65, bf16[256,768]{1,0:T(8,128)(2,1)} %bitcast.75, bf16[256,768]{1,0:T(8,128)(2,1)} %bitcast.13.refs_3_, ...), custom_call_target="tpu_custom_call" | custom-call | tf_op jit(solution)/shard_map/pallas_call | solution.py:80
  177.8 4.8 %all-to-all-start.4 = ((bf16[4,256,384]{2,1,0:T(8,128)(2,1)}), bf16[4,256,384]{2,1,0:T(8,128)(2,1)S(1)}, u32[]{:S(2)}, u32[]{:S(2)}) async-start(bf16[4,256,384]{2,1,0:T(8,128)(2,1)} %bitcast.73), calls=%async_computation.4 | async-start | bytes 1572864 | tf_op jit(solution)/shard_map/all_to_all | solution.py:188
  182.6 15.4 %shard_map.60 = bf16[1024,384]{1,0:T(8,128)(2,1)} custom-call(s32[96]{0:T(128)} %reshape.86.tbl_ref, bf16[1024,768]{1,0:T(8,128)(2,1)} %bitcast.1.q_ref, bf16[1024,768]{1,0:T(8,128)(2,1)} %bitcast.63, bf16[1024,768]{1,0:T(8,128)(2,1)} %bitcast.66, bf16[256,768]{1,0:T(8,128)(2,1)} %bitcast.76, bf16[256,768]{1,0:T(8,128)(2,1)} %bitcast.13.refs_3_, ...), custom_call_target="tpu_custom_call" | custom-call | tf_op jit(solution)/shard_map/pallas_call | solution.py:80
  198.0 5.7 %all-to-all-done.4 = bf16[4,256,384]{2,1,0:T(8,128)(2,1)S(1)} async-done(((bf16[4,256,384]{2,1,0:T(8,128)(2,1)}), bf16[4,256,384]{2,1,0:T(8,128)(2,1)S(1)}, u32[]{:S(2)}, u32[]{:S(2)}) %all-to-all-start.4) | async-done | bytes 786464 | tf_op jit(solution)/shard_map/all_to_all | solution.py:188
  203.7 24.3 %all_to_all.89 = bf16[4,256,384]{2,1,0:T(8,128)(2,1)S(1)} all-to-all(bf16[4,256,384]{2,1,0:T(8,128)(2,1)} %bitcast.74), channel_id=1, replica_groups=mesh['groups'=2,'seq'=4,'head'=4] {'head'}, dimensions={0} | all-to-all | bytes 1572864 | tf_op jit(solution)/shard_map/all_to_all | solution.py:188
  (65 shorter events, 23.5 us)
Async XLA Ops:
  9.8 6.5 %copy-start.4 = (bf16[256,3072]{1,0:T(8,128)(2,1)S(1)}, bf16[256,3072]{1,0:T(8,128)(2,1)}, u32[]{:S(2)}) copy-start(bf16[256,3072]{1,0:T(8,128)(2,1)} %param.8) | copy-start | bytes 4718596
  9.8 43.4 %all-to-all-start.1 = ((bf16[256,4,768]{2,0,1:T(8,128)(2,1)}), bf16[256,4,768]{2,0,1:T(8,128)(2,1)S(1)}, u32[]{:S(2)}, u32[]{:S(2)}) async-start(bf16[256,4,768]{2,0,1:T(8,128)(2,1)} %bitcast.58), calls=%async_computation.1 | async-start | bytes 3145728 | tf_op jit(solution)/shard_map/all_to_all | solution.py:126
  53.2 61.3 %copy-start = (bf16[256,4,768]{2,0,1:T(8,128)(2,1)}, bf16[256,4,768]{2,0,1:T(8,128)(2,1)S(1)}, u32[]{:S(2)}) copy-start(bf16[256,4,768]{2,0,1:T(8,128)(2,1)S(1)} %all-to-all-done.1) | copy-start | bytes 4718596
  53.2 40.0 %all-to-all-start.2 = ((bf16[256,4,768]{2,0,1:T(8,128)(2,1)}), bf16[256,4,768]{2,0,1:T(8,128)(2,1)S(1)}, u32[]{:S(2)}, u32[]{:S(2)}) async-start(bf16[256,4,768]{2,0,1:T(8,128)(2,1)} %bitcast.67), calls=%async_computation.2 | async-start | bytes 3145728 | tf_op jit(solution)/shard_map/all_to_all | solution.py:127
  56.8 92.3 %all-gather.3.cloned.1.call-start = ((), (), s32[]{:S(2)}) async-start(), calls=%async_computation.5 | async-start | bytes 1966080 | tf_op jit(solution)/shard_map/all_gather | solution.py:131
  70.3 2.7 %copy-start.5 = (s32[32,12]{0,1:T(8,128)S(1)}, s32[32,12]{0,1:T(8,128)}, u32[]{:S(2)}) copy-start(s32[32,12]{0,1:T(8,128)} %param.9) | copy-start | bytes 4612
  93.2 19.4 %copy-start.1 = (bf16[256,4,768]{2,0,1:T(8,128)(2,1)}, bf16[256,4,768]{2,0,1:T(8,128)(2,1)S(1)}, u32[]{:S(2)}) copy-start(bf16[256,4,768]{2,0,1:T(8,128)(2,1)S(1)} %all-to-all-done.2) | copy-start | bytes 4718596
  93.2 44.4 %all-to-all-start = ((bf16[256,4,768]{2,0,1:T(8,128)(2,1)}), bf16[256,4,768]{2,0,1:T(8,128)(2,1)}, u32[]{:S(2)}, u32[]{:S(2)}) async-start(bf16[256,4,768]{2,0,1:T(8,128)(2,1)} %bitcast.68), calls=%async_computation | async-start | bytes 3145728 | tf_op jit(solution)/shard_map/all_to_all | solution.py:128
  97.6 51.5 %all-gather.5.cloned.1.call-start = ((), (), s32[]{:S(2)}) async-start(), calls=%async_computation.6 | async-start | bytes 1966080 | tf_op jit(solution)/shard_map/all_gather | solution.py:132
  114.5 1.8 copy-start.2
  119.0 18.6 %collective-permute-start = (bf16[2,128,768]{2,1,0:T(8,128)(2,1)S(1)}, bf16[2,128,768]{2,1,0:T(8,128)(2,1)S(1)}, u32[]{:S(2)}, u32[]{:S(2)}) collective-permute-start(bf16[2,128,768]{2,1,0:T(8,128)(2,1)S(1)} %get-tuple-element.12), channel_id=1, source_target_pairs={{0,4},{4,8},{8,12},{12,0},{1,5},{5,9},{9,13},{13,1},{2,6},{6,10},{... | collective-permute-start | bytes 1179656 | tf_op jit(solution)/shard_map/ppermute | solution.py:159
  119.8 40.1 %collective-permute-start.1 = (bf16[2,128,768]{2,1,0:T(8,128)(2,1)}, bf16[2,128,768]{2,1,0:T(8,128)(2,1)}, u32[]{:S(2)}, u32[]{:S(2)}) collective-permute-start(bf16[2,128,768]{2,1,0:T(8,128)(2,1)} %get-tuple-element.11), channel_id=1, source_target_pairs={{0,8},{4,12},{8,0},{12,4},{1,9},{5,13},{9,1},{13,5},{2,10},{6,14},... | collective-permute-start | bytes 1179656 | tf_op jit(solution)/shard_map/ppermute | solution.py:159
  121.3 38.6 %collective-permute-start.2 = (bf16[2,128,768]{2,1,0:T(8,128)(2,1)}, bf16[2,128,768]{2,1,0:T(8,128)(2,1)}, u32[]{:S(2)}, u32[]{:S(2)}) collective-permute-start(bf16[2,128,768]{2,1,0:T(8,128)(2,1)} %get-tuple-element.10), channel_id=1, source_target_pairs={{0,12},{4,0},{8,4},{12,8},{1,13},{5,1},{9,5},{13,9},{2,14},{6,2},{... | collective-permute-start | bytes 1179656 | tf_op jit(solution)/shard_map/ppermute | solution.py:159
  123.8 36.0 %collective-permute-start.3 = (bf16[2,128,768]{2,1,0:T(8,128)(2,1)}, bf16[2,128,768]{2,1,0:T(8,128)(2,1)}, u32[]{:S(2)}, u32[]{:S(2)}) collective-permute-start(bf16[2,128,768]{2,1,0:T(8,128)(2,1)} %get-tuple-element.9), channel_id=1, source_target_pairs={{0,4},{4,8},{8,12},{12,0},{1,5},{5,9},{9,13},{13,1},{2,6},{6,10},{... | collective-permute-start | bytes 1179656 | tf_op jit(solution)/shard_map/ppermute | solution.py:159
  123.8 36.0 %collective-permute-start.4 = (bf16[2,128,768]{2,1,0:T(8,128)(2,1)}, bf16[2,128,768]{2,1,0:T(8,128)(2,1)}, u32[]{:S(2)}, u32[]{:S(2)}) collective-permute-start(bf16[2,128,768]{2,1,0:T(8,128)(2,1)} %get-tuple-element.8), channel_id=1, source_target_pairs={{0,8},{4,12},{8,0},{12,4},{1,9},{5,13},{9,1},{13,5},{2,10},{6,14},... | collective-permute-start | bytes 1179656 | tf_op jit(solution)/shard_map/ppermute | solution.py:159
  137.6 3.5 %copy-start.3 = (bf16[2,128,768]{2,1,0:T(8,128)(2,1)}, bf16[2,128,768]{2,1,0:T(8,128)(2,1)S(1)}, u32[]{:S(2)}) copy-start(bf16[2,128,768]{2,1,0:T(8,128)(2,1)S(1)} %collective-permute-done) | copy-start | bytes 1179652
  137.6 24.8 %collective-permute-start.5 = (bf16[2,128,768]{2,1,0:T(8,128)(2,1)}, bf16[2,128,768]{2,1,0:T(8,128)(2,1)}, u32[]{:S(2)}, u32[]{:S(2)}) collective-permute-start(bf16[2,128,768]{2,1,0:T(8,128)(2,1)} %get-tuple-element.7), channel_id=1, source_target_pairs={{0,12},{4,0},{8,4},{12,8},{1,13},{5,1},{9,5},{13,9},{2,14},{6,2},{... | collective-permute-start | bytes 1179656 | tf_op jit(solution)/shard_map/ppermute | solution.py:159
  177.8 25.9 %all-to-all-start.4 = ((bf16[4,256,384]{2,1,0:T(8,128)(2,1)}), bf16[4,256,384]{2,1,0:T(8,128)(2,1)S(1)}, u32[]{:S(2)}, u32[]{:S(2)}) async-start(bf16[4,256,384]{2,1,0:T(8,128)(2,1)} %bitcast.73), calls=%async_computation.4 | async-start | bytes 1572864 | tf_op jit(solution)/shard_map/all_to_all | solution.py:188
Sparse Core Ops, SparseCore 0:
  70.3 21.0 all-gather.2
  111.2 29.2 all-gather.4

commit v7 on v6

--- a/solution.py
+++ b/solution.py
@@ -75,22 +75,30 @@
     def column(h, t):
         return (0, h + head_lo)
 
-    operands = [queries, keys, values] + list(far_keys) + list(far_values)
+    operands = [keys, values] + list(far_keys) + list(far_values)
     total_rows = keys.shape[0] + sum(k.shape[0] for k in far_keys)
+    sel = tbl.shape[0] * BLOCK // rows
+    cost = pl.CostEstimate(
+        flops=4 * rows * sel * BLOCK * HD * heads,
+        transcendentals=rows * sel * BLOCK * heads,
+        bytes_accessed=2 * HD * heads * (2 * rows + 2 * total_rows),
+    )
     return pl.pallas_call(
         sparse_kernel,
         out_shape=jax.ShapeDtypeStruct((rows, heads * HD), jnp.bfloat16),
+        cost_estimate=cost,
         grid_spec=pltpu.PrefetchScalarGridSpec(
             num_scalar_prefetch=1,
             grid=(heads,),
-            in_specs=[pl.BlockSpec((x.shape[0], HD), column) for x in operands],
+            in_specs=[pl.BlockSpec((rows, HD), lambda h, t: (0, h))]
+            + [pl.BlockSpec((x.shape[0], HD), column) for x in operands],
             out_specs=pl.BlockSpec((rows, HD), lambda h, t: (0, h)),
             scratch_shapes=[
                 pltpu.VMEM((total_rows, HD), jnp.bfloat16),
                 pltpu.VMEM((total_rows, HD), jnp.bfloat16),
             ],
         ),
-    )(tbl, *operands)
+    )(tbl, queries, *operands)
 
 
 def draft_kernel(q_ref, k_ref, v_ref, o_ref):
@@ -109,9 +117,15 @@
     heads = width // HD
     key_rows = keys.shape[0]
     tile = min(DRAFT_ROWS, rows)
+    cost = pl.CostEstimate(
+        flops=4 * rows * key_rows * HD * heads,
+        transcendentals=rows * key_rows * heads,
+        bytes_accessed=2 * HD * heads * (2 * rows + 2 * key_rows),
+    )
     return pl.pallas_call(
         draft_kernel,
         out_shape=jax.ShapeDtypeStruct((rows, width), jnp.bfloat16),
+        cost_estimate=cost,
         grid=(heads, rows // tile),
         in_specs=[
             pl.BlockSpec((tile, HD), lambda h, r: (r, h)),
@@ -125,8 +139,19 @@
 def on_device(query_in, key_in, value_in, block_lists):
     key_rows = lax.all_to_all(key_in, "head", split_axis=1, concat_axis=0, tiled=True)
     value_rows = lax.all_to_all(value_in, "head", split_axis=1, concat_axis=0, tiled=True)
-    queries = lax.all_to_all(query_in, "head", split_axis=1, concat_axis=0, tiled=True)
-    seq_rows, width = queries.shape
+    seq_rows, width = key_rows.shape
+    head_count = lax.axis_size("head")
+    heads = width // HD
+    first = max(1, heads // 2)
+    spans = [(lo, n) for lo, n in ((0, first), (first, heads - first)) if n > 0]
+    grouped_q = query_in.reshape(query_in.shape[0], head_count, width)
+    query_parts = [
+        lax.all_to_all(
+            grouped_q[:, :, lo * HD:(lo + n) * HD].reshape(query_in.shape[0], -1),
+            "head", split_axis=1, concat_axis=0, tiled=True,
+        )
+        for lo, n in spans
+    ]
 
     draft_keys = lax.all_gather(pool_tokens(key_rows), "seq", axis=0, tiled=True)
     draft_values = lax.all_gather(pool_tokens(value_rows), "seq", axis=0, tiled=True)
@@ -174,20 +199,21 @@
     joint_pos = jnp.where(distance == 0, within, per_dev + (distance - 1) * CAP + ranks_used)
     table = jnp.clip(joint_pos, 0, per_dev + (seq_count - 1) * CAP - 1).reshape(-1).astype(jnp.int32)
 
-    draft_out = draft_attention(pool_tokens(queries), draft_keys, draft_values)
-    queries, draft_out = lax.optimization_barrier((queries, draft_out))
-    heads = width // HD
-    first = max(1, heads // 2)
+    pooled = None
     pieces = []
-    for head_lo, count in ((0, first), (first, heads - first)):
-        if count == 0:
-            continue
+    for index, ((head_lo, count), queries) in enumerate(zip(spans, query_parts)):
         rows_part = sparse_attention(
             table, queries, key_rows, value_rows, remote_keys, remote_values, head_lo, count,
         )
+        if index == len(spans) - 1:
+            pooled = jnp.concatenate([pool_tokens(q) for q in query_parts], axis=1)
+            rows_part, pooled, draft_keys, draft_values = lax.optimization_barrier(
+                (rows_part, pooled, draft_keys, draft_values)
+            )
         back = lax.all_to_all(rows_part, "head", split_axis=0, concat_axis=1, tiled=True)
         pieces.append(back.reshape(back.shape[0], -1, count * HD))
     sparse_out = jnp.concatenate(pieces, axis=2).reshape(pieces[0].shape[0], -1)
+    draft_out = draft_attention(pooled, draft_keys, draft_values)
     return (draft_out, sparse_out)
 
 

time: 238 us -> 241 us (1.013)
  blocking collectives: 24.3 us -> 0 us
  waiting for transfers between devices: 75.9 us -> 94.4 us
  starting transfers between devices: 22.8 us -> 31.7 us
  local copies, waits for them, and re-layouts: 29.3 us -> 32.7 us
  other arithmetic: 28.3 us -> 25.1 us
    all_to_all x1 -> x0, blocking collectives: 24.3 us -> none  [on_device(): lax.all_to_all(rows_part, 'head', split_axis=0, concat_axis=1, tiled=True)]
    all_to_all x1, waiting for transfers between devices: 35.6 us -> 13.3 us  [on_device(): lax.all_to_all(key_in, 'head', split_axis=1, concat_axis=0, tiled=True)]
    ppermute x6, waiting for transfers between devices: 15.8 us -> 33.9 us  [exchange(): lax.ppermute(parcel, 'seq', [(i, (i + shift) % seq_count) for i in range(...]
    all_to_all x1, waiting for transfers between devices: 18.7 us -> 35.6 us  [on_device(): lax.all_to_all(value_in, 'head', split_axis=1, concat_axis=0, tiled=True)]
    all_to_all x1 -> x2, starting transfers between devices: 4.84 us -> 9.83 us  [on_device(): lax.all_to_all(rows_part, 'head', split_axis=0, concat_axis=1, tiled=True)]
    reshape x0 -> x1, local copies, waits for them, and re-layouts: none -> 4.25 us  [on_device(): grouped_q = query_in.reshape(query_in.shape[0], head_count, width)]
    convert_element_type x3 -> x4, local copies, waits for them, and re-layouts: 12.8 us -> 8.91 us  [pool_tokens(): matrix.astype(jnp.float32)]
    unnamed x14 -> x26, local copies, waits for them, and re-layouts: 0.11 us -> 3.76 us
  transfers between devices with their start and end apart: 12 -> 14, of which waited for: 5 -> 9; matrix products, arithmetic and copies ran while one was open for 23% -> 21% of each run, Pallas kernels for 11% -> 17%
where the time goes in v7:
time: 241 us; the launch traced here: 240 us
  waiting for transfers between devices  94.4 us (39%)
  Pallas kernels  41.4 us (17%)
  local copies, waits for them, and re-layouts  32.7 us (14%)
  starting transfers between devices  31.7 us (13%)
  other arithmetic  25.1 us (10%)
  between operations  14.4 us (6%)
    all_to_all x1, waiting for transfers between devices, on_device(): lax.all_to_all(value_in, 'head', split_axis=1, concat_axis=0, tiled=True)  35.6 us
    ppermute x6, waiting for transfers between devices, exchange(): lax.ppermute(parcel, 'seq', [(i, (i + shift) % seq_count) for i in range(...  33.9 us
    pallas_call x2, Pallas kernels, sparse_attention(): pl.pallas_call(sparse_kernel, out_shape=jax.ShapeDtypeStruct((rows, heads...  30.7 us
    all_to_all x1, waiting for transfers between devices, on_device(): lax.all_to_all(key_in, 'head', split_axis=1, concat_axis=0, tiled=True)  13.3 us
    pallas_call x1, Pallas kernels, draft_attention(): pl.pallas_call(draft_kernel, out_shape=jax.ShapeDtypeStruct((rows, width)...  10.7 us
    all_to_all x2, starting transfers between devices, on_device(): lax.all_to_all(rows_part, 'head', split_axis=0, concat_axis=1, tiled=True)  9.83 us
    reduce_sum x4, other arithmetic, pool_tokens(): return (grouped.sum(axis=1) * POOL ** (-0.5)).astype(jnp.bfloat16)  9.48 us
    convert_element_type x4, local copies, waits for them, and re-layouts, pool_tokens(): matrix.astype(jnp.float32)  8.91 us
  transfers between devices with their start and end apart: 14, of which 9 were waited for; matrix products, arithmetic and copies ran while one was open for 21% of the time, Pallas kernels for 17%

profile of v7, /device:TPU:0, one launch (start us, length us, event | category | flops | bytes accessed | tf_op | source)
XLA Modules:
  0.0 239.7 jit_solution(15886825192364082904)
XLA Ops:
  7.2 2.7 %copy.47 = bf16[32,4,8,768]{3,2,0,1:T(8,128)(2,1)} copy(bf16[32,4,8,768]{3,2,1,0:T(8,128)(2,1)} %bitcast.72) | data formatting | bytes 3145728 | tf_op jit(solution)/shard_map/all_to_all | solution.py:141
  9.8 6.4 %all-to-all-start.2 = ((bf16[256,4,768]{2,0,1:T(8,128)(2,1)}), bf16[256,4,768]{2,0,1:T(8,128)(2,1)S(1)}, u32[]{:S(2)}, u32[]{:S(2)}) async-start(bf16[256,4,768]{2,0,1:T(8,128)(2,1)} %bitcast.58), calls=%async_computation.2 | async-start | bytes 3145728 | tf_op jit(solution)/shard_map/all_to_all | solution.py:141
  17.6 35.6 %all-to-all-done.2 = bf16[256,4,768]{2,0,1:T(8,128)(2,1)S(1)} async-done(((bf16[256,4,768]{2,0,1:T(8,128)(2,1)}), bf16[256,4,768]{2,0,1:T(8,128)(2,1)S(1)}, u32[]{:S(2)}, u32[]{:S(2)}) %all-to-all-start.2) | async-done | bytes 1572896 | tf_op jit(solution)/shard_map/all_to_all | solution.py:141
  53.2 3.7 %all-to-all-start.1 = ((bf16[256,4,768]{2,0,1:T(8,128)(2,1)}), bf16[256,4,768]{2,0,1:T(8,128)(2,1)S(1)}, u32[]{:S(2)}, u32[]{:S(2)}) async-start(bf16[256,4,768]{2,0,1:T(8,128)(2,1)} %bitcast.67), calls=%async_computation.1 | async-start | bytes 3145728 | tf_op jit(solution)/shard_map/all_to_all | solution.py:140
  60.1 4.9 %reshape.117 = f32[256,4,768]{2,1,0:T(4,128)} reshape(f32[4,256,768]{2,1,0:T(8,128)} %bitcast_convert_fusion) | data formatting | bytes 6291456 | tf_op jit(solution)/shard_map/convert_element_type | solution.py:19
  65.0 4.6 %reduce_sum.49 = f32[256,768]{1,0:T(8,128)} reduce(f32[256,4,768]{2,1,0:T(4,128)} %reshape.117, f32[]{:T(128)} %constant.124.clone.1), dimensions={1}, to_apply=%region_7.9 | reduce | flops 589824 | bytes 3932164 | tf_op jit(solution)/shard_map/reduce_sum | solution.py:20
  71.9 4.3 %reshape.101 = bf16[256,4,768]{2,1,0:T(4,128)(2,1)} reshape(bf16[256,3072]{1,0:T(8,128)(2,1)} %param.6) | data formatting | bytes 3145728 | tf_op jit(solution)/shard_map/reshape | solution.py:147
  80.0 13.3 %all-to-all-done.1 = bf16[256,4,768]{2,0,1:T(8,128)(2,1)S(1)} async-done(((bf16[256,4,768]{2,0,1:T(8,128)(2,1)}), bf16[256,4,768]{2,0,1:T(8,128)(2,1)S(1)}, u32[]{:S(2)}, u32[]{:S(2)}) %all-to-all-start.1) | async-done | bytes 1572896 | tf_op jit(solution)/shard_map/all_to_all | solution.py:140
  93.4 4.2 %all-to-all-start.3 = ((bf16[256,4,384]{2,0,1:T(8,128)(2,1)}), bf16[256,4,384]{2,0,1:T(8,128)(2,1)}, u32[]{:S(2)}, u32[]{:S(2)}) async-start(bf16[256,4,384]{2,0,1:T(8,128)(2,1)} %copy.40), calls=%async_computation.3 | async-start | bytes 1572864 | tf_op jit(solution)/shard_map/all_to_all | solution.py:149
  101.3 3.5 %broadcast_select_fusion = (bf16[8,128,768]{2,1,0:T(8,128)(2,1)}, bf16[8,128,768]{2,1,0:T(8,128)(2,1)S(1)}) fusion(bf16[8,128,768]{2,1,0:T(8,128)(2,1)} %gather_fusion.2, pred[8]{0:T(512)(128)(4,1)S(1)} %compare_and_fusion, bf16[8,128,768]{2,1,0:T(8,128)(2,1)} %gather_fusion.1), kind=kLoop, calls=%fused_computation.8 | loop fusion | flops 1572864 | bytes 6291464 | tf_op jit(solution)/shard_map/jit(_take)/select_n | solution.py:176
  107.9 3.1 %reshape.116 = f32[256,4,768]{2,1,0:T(4,128)S(1)} reshape(f32[4,256,768]{2,1,0:T(8,128)} %bitcast_convert_fusion.1) | data formatting | bytes 6291456 | tf_op jit(solution)/shard_map/convert_element_type | solution.py:19
  111.0 3.0 %reduce_sum.48 = f32[256,768]{1,0:T(8,128)} reduce(f32[256,4,768]{2,1,0:T(4,128)S(1)} %reshape.116, f32[]{:T(128)} %constant.124.clone.1), dimensions={1}, to_apply=%region_6.8 | reduce | flops 589824 | bytes 3932164 | tf_op jit(solution)/shard_map/reduce_sum | solution.py:20
  114.0 3.2 %all-to-all-done.3 = bf16[256,4,384]{2,0,1:T(8,128)(2,1)} async-done(((bf16[256,4,384]{2,0,1:T(8,128)(2,1)}), bf16[256,4,384]{2,0,1:T(8,128)(2,1)}, u32[]{:S(2)}, u32[]{:S(2)}) %all-to-all-start.3) | async-done | bytes 786464 | tf_op jit(solution)/shard_map/all_to_all | solution.py:149
  117.2 3.5 %all-to-all-start = ((bf16[256,4,384]{2,0,1:T(8,128)(2,1)}), bf16[256,4,384]{2,0,1:T(8,128)(2,1)S(1)}, u32[]{:S(2)}, u32[]{:S(2)}) async-start(bf16[256,4,384]{2,0,1:T(8,128)(2,1)} %copy.39), calls=%async_computation | async-start | bytes 1572864 | tf_op jit(solution)/shard_map/all_to_all | solution.py:149
  128.9 7.0 %collective-permute-done.1 = bf16[2,128,768]{2,1,0:T(8,128)(2,1)} collective-permute-done((bf16[2,128,768]{2,1,0:T(8,128)(2,1)S(1)}, bf16[2,128,768]{2,1,0:T(8,128)(2,1)}, u32[]{:S(2)}, u32[]{:S(2)}) %collective-permute-start.1) | collective-permute-done | bytes 393248 | tf_op jit(solution)/shard_map/ppermute | solution.py:184
  135.9 8.8 %collective-permute-done = bf16[2,128,768]{2,1,0:T(8,128)(2,1)} collective-permute-done((bf16[2,128,768]{2,1,0:T(8,128)(2,1)S(1)}, bf16[2,128,768]{2,1,0:T(8,128)(2,1)}, u32[]{:S(2)}, u32[]{:S(2)}) %collective-permute-start) | collective-permute-done | bytes 393248 | tf_op jit(solution)/shard_map/ppermute | solution.py:184
  144.7 6.6 %collective-permute-done.5 = bf16[2,128,768]{2,1,0:T(8,128)(2,1)S(1)} collective-permute-done((bf16[2,128,768]{2,1,0:T(8,128)(2,1)}, bf16[2,128,768]{2,1,0:T(8,128)(2,1)S(1)}, u32[]{:S(2)}, u32[]{:S(2)}) %collective-permute-start.5) | collective-permute-done | bytes 393248 | tf_op jit(solution)/shard_map/ppermute | solution.py:184
  151.4 9.3 %collective-permute-done.4 = bf16[2,128,768]{2,1,0:T(8,128)(2,1)S(1)} collective-permute-done((bf16[2,128,768]{2,1,0:T(8,128)(2,1)}, bf16[2,128,768]{2,1,0:T(8,128)(2,1)S(1)}, u32[]{:S(2)}, u32[]{:S(2)}) %collective-permute-start.4) | collective-permute-done | bytes 393248 | tf_op jit(solution)/shard_map/ppermute | solution.py:184
  163.7 15.4 %shard_map.61 = bf16[1024,384]{1,0:T(8,128)(2,1)} custom-call(s32[96]{0:T(128)} %reshape.100.tbl_ref, bf16[1024,384]{1,0:T(8,128)(2,1)} %bitcast.25.q_ref, bf16[1024,768]{1,0:T(8,128)(2,1)} %bitcast.65, bf16[1024,768]{1,0:T(8,128)(2,1)} %bitcast.62, bf16[256,768]{1,0:T(8,128)(2,1)} %bitcast.11.refs_2_, bf16[256,768]{1,0:T(8,128)(2,1)} %bitcast.13.refs_3_, ...), custom_call_target="tpu_custom_call" | custom-call | flops 2415919104 | bytes 4325376 | tf_op jit(solution)/shard_map/pallas_call | solution.py:86
  179.9 4.7 %all-to-all-start.4 = ((bf16[4,256,384]{2,1,0:T(8,128)(2,1)}), bf16[4,256,384]{2,1,0:T(8,128)(2,1)}, u32[]{:S(2)}, u32[]{:S(2)}) async-start(bf16[4,256,384]{2,1,0:T(8,128)(2,1)} %bitcast.75), calls=%async_computation.4 | async-start | bytes 1572864 | tf_op jit(solution)/shard_map/all_to_all | solution.py:213
  190.8 15.3 %shard_map.59 = bf16[1024,384]{1,0:T(8,128)(2,1)} custom-call(s32[96]{0:T(128)} %reshape.100.tbl_ref, bf16[1024,384]{1,0:T(8,128)(2,1)} %bitcast.70, bf16[1024,768]{1,0:T(8,128)(2,1)} %bitcast.66, bf16[1024,768]{1,0:T(8,128)(2,1)} %bitcast.63, bf16[256,768]{1,0:T(8,128)(2,1)} %bitcast.11.refs_2_, bf16[256,768]{1,0:T(8,128)(2,1)} %bitcast.13.refs_3_, ...), custom_call_target="tpu_custom_call" | custom-call | flops 2415919104 | bytes 4325376 | tf_op jit(solution)/shard_map/pallas_call | solution.py:86
  206.2 5.1 %all-to-all-start.5 = ((bf16[4,256,384]{2,1,0:T(8,128)(2,1)}), bf16[4,256,384]{2,1,0:T(8,128)(2,1)S(1)}, u32[]{:S(2)}, u32[]{:S(2)}) async-start(bf16[4,256,384]{2,1,0:T(8,128)(2,1)} %bitcast.76), calls=%async_computation.5 | async-start | bytes 1572864 | tf_op jit(solution)/shard_map/all_to_all | solution.py:213
  211.3 10.7 %shard_map.60 = bf16[256,768]{1,0:T(8,128)(2,1)} custom-call(bf16[256,768]{1,0:T(8,128)(2,1)} %pad_maximum_fusion.q_ref, bf16[1024,768]{1,0:T(8,128)(2,1)} %all-gather.3.cloned.1.call-done.k_ref, bf16[1024,768]{1,0:T(8,128)(2,1)} %all-gather.5.cloned.1.call-done.v_ref), custom_call_target="tpu_custom_call" | custom-call | flops 805306368 | bytes 3932160 | tf_op jit(solution)/shard_map/pallas_call | solution.py:125
  222.0 8.2 %all-to-all-done.5 = bf16[4,256,384]{2,1,0:T(8,128)(2,1)S(1)} async-done(((bf16[4,256,384]{2,1,0:T(8,128)(2,1)}), bf16[4,256,384]{2,1,0:T(8,128)(2,1)S(1)}, u32[]{:S(2)}, u32[]{:S(2)}) %all-to-all-start.5) | async-done | bytes 786464 | tf_op jit(solution)/shard_map/all_to_all | solution.py:213
  (86 shorter events, 38.2 us)
Async XLA Ops:
  9.8 6.5 %copy-start.5 = (bf16[256,3072]{1,0:T(8,128)(2,1)S(1)}, bf16[256,3072]{1,0:T(8,128)(2,1)}, u32[]{:S(2)}) copy-start(bf16[256,3072]{1,0:T(8,128)(2,1)} %param.7) | copy-start | bytes 4718596
  9.8 43.4 %all-to-all-start.2 = ((bf16[256,4,768]{2,0,1:T(8,128)(2,1)}), bf16[256,4,768]{2,0,1:T(8,128)(2,1)S(1)}, u32[]{:S(2)}, u32[]{:S(2)}) async-start(bf16[256,4,768]{2,0,1:T(8,128)(2,1)} %bitcast.58), calls=%async_computation.2 | async-start | bytes 3145728 | tf_op jit(solution)/shard_map/all_to_all | solution.py:141
  53.2 46.2 %copy-start = (bf16[256,4,768]{2,0,1:T(8,128)(2,1)}, bf16[256,4,768]{2,0,1:T(8,128)(2,1)S(1)}, u32[]{:S(2)}) copy-start(bf16[256,4,768]{2,0,1:T(8,128)(2,1)S(1)} %all-to-all-done.2) | copy-start | bytes 4718596
  53.2 3.8 %copy-start.7 = (s32[32,12]{0,1:T(8,128)S(1)}, s32[32,12]{0,1:T(8,128)}, u32[]{:S(2)}) copy-start(s32[32,12]{0,1:T(8,128)} %param.9) | copy-start | bytes 4612
  53.2 40.1 %all-to-all-start.1 = ((bf16[256,4,768]{2,0,1:T(8,128)(2,1)}), bf16[256,4,768]{2,0,1:T(8,128)(2,1)S(1)}, u32[]{:S(2)}, u32[]{:S(2)}) async-start(bf16[256,4,768]{2,0,1:T(8,128)(2,1)} %bitcast.67), calls=%async_computation.1 | async-start | bytes 3145728 | tf_op jit(solution)/shard_map/all_to_all | solution.py:140
  56.9 149.2 %all-gather.5.cloned.1.call-start = ((), (), s32[]{:S(2)}) async-start(), calls=%async_computation.7 | async-start | bytes 1966080 | tf_op jit(solution)/shard_map/all_gather | solution.py:157
  93.4 12.6 %copy-start.1 = (bf16[256,4,768]{2,0,1:T(8,128)(2,1)}, bf16[256,4,768]{2,0,1:T(8,128)(2,1)S(1)}, u32[]{:S(2)}) copy-start(bf16[256,4,768]{2,0,1:T(8,128)(2,1)S(1)} %all-to-all-done.1) | copy-start | bytes 4718596
  93.4 23.9 %all-to-all-start.3 = ((bf16[256,4,384]{2,0,1:T(8,128)(2,1)}), bf16[256,4,384]{2,0,1:T(8,128)(2,1)}, u32[]{:S(2)}, u32[]{:S(2)}) async-start(bf16[256,4,384]{2,0,1:T(8,128)(2,1)} %copy.40), calls=%async_computation.3 | async-start | bytes 1572864 | tf_op jit(solution)/shard_map/all_to_all | solution.py:149
  105.8 22.3 %collective-permute-start.2 = (bf16[2,128,768]{2,1,0:T(8,128)(2,1)}, bf16[2,128,768]{2,1,0:T(8,128)(2,1)}, u32[]{:S(2)}, u32[]{:S(2)}) collective-permute-start(bf16[2,128,768]{2,1,0:T(8,128)(2,1)} %get-tuple-element.16), channel_id=1, source_target_pairs={{0,12},{4,0},{8,4},{12,8},{1,13},{5,1},{9,5},{13,9},{2,14},{6,2},{... | collective-permute-start | bytes 1179656 | tf_op jit(solution)/shard_map/ppermute | solution.py:184
  114.0 6.8 %copy-start.4 = (f32[256,768]{1,0:T(8,128)S(1)}, f32[256,768]{1,0:T(8,128)}, u32[]{:S(2)}) copy-start(f32[256,768]{1,0:T(8,128)} %reduce_sum.48) | copy-start | bytes 2359300
  117.2 61.8 %all-to-all-start = ((bf16[256,4,384]{2,0,1:T(8,128)(2,1)}), bf16[256,4,384]{2,0,1:T(8,128)(2,1)S(1)}, u32[]{:S(2)}, u32[]{:S(2)}) async-start(bf16[256,4,384]{2,0,1:T(8,128)(2,1)} %copy.39), calls=%async_computation | async-start | bytes 1572864 | tf_op jit(solution)/shard_map/all_to_all | solution.py:149
  120.7 85.4 %all-gather.3.cloned.1.call-start = ((), (), s32[]{:S(2)}) async-start(), calls=%async_computation.6 | async-start | bytes 1966080 | tf_op jit(solution)/shard_map/all_gather | solution.py:156
  121.7 1.5 copy-start.6
  121.7 3.1 %copy-start.2 = (bf16[8,128,768]{2,1,0:T(8,128)(2,1)S(1)}, bf16[8,128,768]{2,1,0:T(8,128)(2,1)}, u32[]{:S(2)}) copy-start(bf16[8,128,768]{2,1,0:T(8,128)(2,1)} %get-tuple-element.19) | copy-start | bytes 4718596
  123.3 12.7 %collective-permute-start.1 = (bf16[2,128,768]{2,1,0:T(8,128)(2,1)S(1)}, bf16[2,128,768]{2,1,0:T(8,128)(2,1)}, u32[]{:S(2)}, u32[]{:S(2)}) collective-permute-start(bf16[2,128,768]{2,1,0:T(8,128)(2,1)S(1)} %copy-done.6), channel_id=1, source_target_pairs={{0,8},{4,12},{8,0},{12,4},{1,9},{5,13},{9,1},{13,5},{2,10},{6,14},... | collective-permute-start | bytes 1179656 | tf_op jit(solution)/shard_map/ppermute | solution.py:184
  124.8 19.9 %collective-permute-start = (bf16[2,128,768]{2,1,0:T(8,128)(2,1)S(1)}, bf16[2,128,768]{2,1,0:T(8,128)(2,1)}, u32[]{:S(2)}, u32[]{:S(2)}) collective-permute-start(bf16[2,128,768]{2,1,0:T(8,128)(2,1)S(1)} %get-tuple-element.18), channel_id=1, source_target_pairs={{0,4},{4,8},{8,12},{12,0},{1,5},{5,9},{9,13},{13,1},{2,6},{6,10},{... | collective-permute-start | bytes 1179656 | tf_op jit(solution)/shard_map/ppermute | solution.py:184
  125.9 25.5 %collective-permute-start.5 = (bf16[2,128,768]{2,1,0:T(8,128)(2,1)}, bf16[2,128,768]{2,1,0:T(8,128)(2,1)S(1)}, u32[]{:S(2)}, u32[]{:S(2)}) collective-permute-start(bf16[2,128,768]{2,1,0:T(8,128)(2,1)} %get-tuple-element.13), channel_id=1, source_target_pairs={{0,12},{4,0},{8,4},{12,8},{1,13},{5,1},{9,5},{13,9},{2,14},{6,2},{... | collective-permute-start | bytes 1179656 | tf_op jit(solution)/shard_map/ppermute | solution.py:184
  127.6 33.1 %collective-permute-start.4 = (bf16[2,128,768]{2,1,0:T(8,128)(2,1)}, bf16[2,128,768]{2,1,0:T(8,128)(2,1)S(1)}, u32[]{:S(2)}, u32[]{:S(2)}) collective-permute-start(bf16[2,128,768]{2,1,0:T(8,128)(2,1)} %get-tuple-element.14), channel_id=1, source_target_pairs={{0,8},{4,12},{8,0},{12,4},{1,9},{5,13},{9,1},{13,5},{2,10},{6,14},... | collective-permute-start | bytes 1179656 | tf_op jit(solution)/shard_map/ppermute | solution.py:184
  128.1 34.7 %collective-permute-start.3 = (bf16[2,128,768]{2,1,0:T(8,128)(2,1)}, bf16[2,128,768]{2,1,0:T(8,128)(2,1)S(1)}, u32[]{:S(2)}, u32[]{:S(2)}) collective-permute-start(bf16[2,128,768]{2,1,0:T(8,128)(2,1)} %get-tuple-element.15), channel_id=1, source_target_pairs={{0,4},{4,8},{8,12},{12,0},{1,5},{5,9},{9,13},{13,1},{2,6},{6,10},{... | collective-permute-start | bytes 1179656 | tf_op jit(solution)/shard_map/ppermute | solution.py:184
  151.3 11.5 %copy-start.8 = (bf16[2,128,768]{2,1,0:T(8,128)(2,1)}, bf16[2,128,768]{2,1,0:T(8,128)(2,1)S(1)}, u32[]{:S(2)}) copy-start(bf16[2,128,768]{2,1,0:T(8,128)(2,1)S(1)} %collective-permute-done.5) | copy-start | bytes 1179652
  160.7 2.2 copy-start.9
  179.0 0.9 copy-start.3
  179.9 26.2 %all-to-all-start.4 = ((bf16[4,256,384]{2,1,0:T(8,128)(2,1)}), bf16[4,256,384]{2,1,0:T(8,128)(2,1)}, u32[]{:S(2)}, u32[]{:S(2)}) async-start(bf16[4,256,384]{2,1,0:T(8,128)(2,1)} %bitcast.75), calls=%async_computation.4 | async-start | bytes 1572864 | tf_op jit(solution)/shard_map/all_to_all | solution.py:213
  206.2 24.1 %all-to-all-start.5 = ((bf16[4,256,384]{2,1,0:T(8,128)(2,1)}), bf16[4,256,384]{2,1,0:T(8,128)(2,1)S(1)}, u32[]{:S(2)}, u32[]{:S(2)}) async-start(bf16[4,256,384]{2,1,0:T(8,128)(2,1)} %bitcast.76), calls=%async_computation.5 | async-start | bytes 1572864 | tf_op jit(solution)/shard_map/all_to_all | solution.py:213
  (1 other events, 0.8 us)
Sparse Core Ops, SparseCore 0:
  71.7 20.9 all-gather.4
  123.7 29.6 all-gather.2

commit v8 on v7

--- a/solution.py
+++ b/solution.py
@@ -145,13 +145,12 @@
     first = max(1, heads // 2)
     spans = [(lo, n) for lo, n in ((0, first), (first, heads - first)) if n > 0]
     grouped_q = query_in.reshape(query_in.shape[0], head_count, width)
-    query_parts = [
-        lax.all_to_all(
-            grouped_q[:, :, lo * HD:(lo + n) * HD].reshape(query_in.shape[0], -1),
-            "head", split_axis=1, concat_axis=0, tiled=True,
-        )
-        for lo, n in spans
+    query_slices = [
+        grouped_q[:, :, lo * HD:(lo + n) * HD].reshape(query_in.shape[0], -1) for lo, n in spans
     ]
+
+    def query_a2a(piece):
+        return lax.all_to_all(piece, "head", split_axis=1, concat_axis=0, tiled=True)
 
     draft_keys = lax.all_gather(pool_tokens(key_rows), "seq", axis=0, tiled=True)
     draft_values = lax.all_gather(pool_tokens(value_rows), "seq", axis=0, tiled=True)
@@ -189,6 +188,11 @@
 
     remote_keys = exchange(key_rows)
     remote_values = exchange(value_rows)
+    query_parts = [query_a2a(query_slices[0])]
+    later, remote_keys, remote_values = lax.optimization_barrier(
+        (query_slices[1:], remote_keys, remote_values)
+    )
+    query_parts += [query_a2a(piece) for piece in later]
 
     own_lists = lax.dynamic_slice_in_dim(block_lists, seq_index * per_dev, per_dev, 0)
     owners = own_lists // per_dev

time: 241 us -> 231 us (0.959)
  waiting for transfers between devices: 94.4 us -> 73 us
  local copies, waits for them, and re-layouts: 32.7 us -> 39.7 us
  starting transfers between devices: 31.7 us -> 36.3 us
    ppermute x6, waiting for transfers between devices: 33.9 us -> 16.5 us  [exchange(): lax.ppermute(parcel, 'seq', [(i, (i + shift) % seq_count) for i in range(...]
    convert_element_type x4 -> x5, local copies, waits for them, and re-layouts: 8.91 us -> 14.7 us  [pool_tokens(): matrix.astype(jnp.float32)]
    all_to_all x2, waiting for transfers between devices: 3.24 us -> 0.01 us  [query_a2a(): lax.all_to_all(piece, 'head', split_axis=1, concat_axis=0, tiled=True)]
    ppermute x6, starting transfers between devices: 3.98 us -> 6.63 us  [exchange(): lax.ppermute(parcel, 'seq', [(i, (i + shift) % seq_count) for i in range(...]
  transfers between devices with their start and end apart: 14 -> 14, of which waited for: 9 -> 7; matrix products, arithmetic and copies ran while one was open for 21% -> 26% of each run, Pallas kernels for 17% -> 18%
where the time goes in v8:
time: 231 us; the launch traced here: 230 us
  waiting for transfers between devices  73 us (32%)
  Pallas kernels  41.4 us (18%)
  local copies, waits for them, and re-layouts  39.7 us (17%)
  starting transfers between devices  36.3 us (16%)
  other arithmetic  25 us (11%)
  between operations  14.3 us (6%)
    all_to_all x1, waiting for transfers between devices, on_device(): lax.all_to_all(value_in, 'head', split_axis=1, concat_axis=0, tiled=True)  35.7 us
    pallas_call x2, Pallas kernels, sparse_attention(): pl.pallas_call(sparse_kernel, out_shape=jax.ShapeDtypeStruct((rows, heads...  30.7 us
    ppermute x6, waiting for transfers between devices, exchange(): lax.ppermute(parcel, 'seq', [(i, (i + shift) % seq_count) for i in range(...  16.5 us
    convert_element_type x5, local copies, waits for them, and re-layouts, pool_tokens(): matrix.astype(jnp.float32)  14.7 us
    all_to_all x1, waiting for transfers between devices, on_device(): lax.all_to_all(key_in, 'head', split_axis=1, concat_axis=0, tiled=True)  13.5 us
    reduce_sum x4, other arithmetic, pool_tokens(): return (grouped.sum(axis=1) * POOL ** (-0.5)).astype(jnp.bfloat16)  11.7 us
    pallas_call x1, Pallas kernels, draft_attention(): pl.pallas_call(draft_kernel, out_shape=jax.ShapeDtypeStruct((rows, width)...  10.7 us
    all_to_all x2, starting transfers between devices, on_device(): lax.all_to_all(rows_part, 'head', split_axis=0, concat_axis=1, tiled=True)  10.2 us
  transfers between devices with their start and end apart: 14, of which 7 were waited for; matrix products, arithmetic and copies ran while one was open for 26% of the time, Pallas kernels for 18%

profile of v8, /device:TPU:0, one launch (start us, length us, event | category | flops | bytes accessed | tf_op | source)
XLA Modules:
  0.0 229.7 jit_solution(3729105852504382589)
XLA Ops:
  7.2 2.7 %copy.60 = bf16[32,4,8,768]{3,2,0,1:T(8,128)(2,1)} copy(bf16[32,4,8,768]{3,2,1,0:T(8,128)(2,1)} %bitcast.73) | data formatting | bytes 3145728 | tf_op jit(solution)/shard_map/all_to_all | solution.py:141
  9.8 6.4 %all-to-all-start.1 = ((bf16[256,4,768]{2,0,1:T(8,128)(2,1)}), bf16[256,4,768]{2,0,1:T(8,128)(2,1)S(1)}, u32[]{:S(2)}, u32[]{:S(2)}) async-start(bf16[256,4,768]{2,0,1:T(8,128)(2,1)} %bitcast.59), calls=%async_computation.1 | async-start | bytes 3145728 | tf_op jit(solution)/shard_map/all_to_all | solution.py:141
  17.5 35.7 %all-to-all-done.1 = bf16[256,4,768]{2,0,1:T(8,128)(2,1)S(1)} async-done(((bf16[256,4,768]{2,0,1:T(8,128)(2,1)}), bf16[256,4,768]{2,0,1:T(8,128)(2,1)S(1)}, u32[]{:S(2)}, u32[]{:S(2)}) %all-to-all-start.1) | async-done | bytes 1572896 | tf_op jit(solution)/shard_map/all_to_all | solution.py:141
  53.2 3.7 %all-to-all-start = ((bf16[256,4,768]{2,0,1:T(8,128)(2,1)}), bf16[256,4,768]{2,0,1:T(8,128)(2,1)S(1)}, u32[]{:S(2)}, u32[]{:S(2)}) async-start(bf16[256,4,768]{2,0,1:T(8,128)(2,1)} %bitcast.69), calls=%async_computation | async-start | bytes 3145728 | tf_op jit(solution)/shard_map/all_to_all | solution.py:140
  58.4 4.3 %reshape.102 = bf16[256,4,768]{2,1,0:T(4,128)(2,1)} reshape(bf16[256,3072]{1,0:T(8,128)(2,1)} %param.6) | data formatting | bytes 3145728 | tf_op jit(solution)/shard_map/reshape | solution.py:147
  64.6 4.8 %reshape.119 = f32[256,4,768]{2,1,0:T(4,128)} reshape(f32[4,256,768]{2,1,0:T(8,128)} %bitcast_convert_fusion) | data formatting | bytes 6291456 | tf_op jit(solution)/shard_map/convert_element_type | solution.py:19
  69.5 4.6 %reduce_sum.49 = f32[256,768]{1,0:T(8,128)} reduce(f32[256,4,768]{2,1,0:T(4,128)} %reshape.119, f32[]{:T(128)} %constant.124.clone.1), dimensions={1}, to_apply=%region_7.9 | reduce | flops 589824 | bytes 3932164 | tf_op jit(solution)/shard_map/reduce_sum | solution.py:20
  76.1 2.8 %fusion.11 = (bf16[256,4,384]{2,1,0:T(4,128)(2,1)S(1)}, bf16[256,4,384]{2,1,0:T(4,128)(2,1)}) fusion(bf16[256,4,768]{2,1,0:T(4,128)(2,1)} %reshape.102), kind=kLoop, calls=%fused_computation.59 | loop fusion | bytes 3145728 | tf_op jit(solution)/shard_map/slice | solution.py:149
  79.9 13.5 %all-to-all-done = bf16[256,4,768]{2,0,1:T(8,128)(2,1)S(1)} async-done(((bf16[256,4,768]{2,0,1:T(8,128)(2,1)}), bf16[256,4,768]{2,0,1:T(8,128)(2,1)S(1)}, u32[]{:S(2)}, u32[]{:S(2)}) %all-to-all-start) | async-done | bytes 1572896 | tf_op jit(solution)/shard_map/all_to_all | solution.py:140
  93.4 4.2 %all-to-all-start.3 = ((bf16[256,4,384]{2,0,1:T(8,128)(2,1)}), bf16[256,4,384]{2,0,1:T(8,128)(2,1)}, u32[]{:S(2)}, u32[]{:S(2)}) async-start(bf16[256,4,384]{2,0,1:T(8,128)(2,1)} %copy.53), calls=%async_computation.3 | async-start | bytes 1572864 | tf_op jit(solution)/shard_map/all_to_all | solution.py:153
  101.2 2.2 broadcast_select_fusion
  109.4 4.1 %collective-permute-done.2 = bf16[2,128,768]{2,1,0:T(8,128)(2,1)} collective-permute-done((bf16[2,128,768]{2,1,0:T(8,128)(2,1)}, bf16[2,128,768]{2,1,0:T(8,128)(2,1)}, u32[]{:S(2)}, u32[]{:S(2)}) %collective-permute-start.2) | collective-permute-done | bytes 393248 | tf_op jit(solution)/shard_map/ppermute | solution.py:183
  113.5 2.7 %collective-permute-start.3 = (bf16[2,128,768]{2,1,0:T(8,128)(2,1)}, bf16[2,128,768]{2,1,0:T(8,128)(2,1)}, u32[]{:S(2)}, u32[]{:S(2)}) collective-permute-start(bf16[2,128,768]{2,1,0:T(8,128)(2,1)} %get-tuple-element.29), channel_id=1, source_target_pairs={{0,4},{4,8},{8,12},{12,0},{1,5},{5,9},{9,13},{13,1},{2,6},{6,10},{... | collective-permute-start | bytes 1179656 | tf_op jit(solution)/shard_map/ppermute | solution.py:183
  120.4 4.9 %reshape.118 = f32[256,4,768]{2,1,0:T(4,128)} reshape(f32[4,256,768]{2,1,0:T(8,128)} %bitcast_convert_fusion.1) | data formatting | bytes 6291456 | tf_op jit(solution)/shard_map/convert_element_type | solution.py:19
  125.3 3.8 %reduce_sum.48 = f32[256,768]{1,0:T(8,128)S(1)} reduce(f32[256,4,768]{2,1,0:T(4,128)} %reshape.118, f32[]{:T(128)} %constant.124.clone.1), dimensions={1}, to_apply=%region_6.8 | reduce | flops 589824 | bytes 3932164 | tf_op jit(solution)/shard_map/reduce_sum | solution.py:20
  130.3 11.0 %collective-permute-done.4 = bf16[2,128,768]{2,1,0:T(8,128)(2,1)} collective-permute-done((bf16[2,128,768]{2,1,0:T(8,128)(2,1)}, bf16[2,128,768]{2,1,0:T(8,128)(2,1)}, u32[]{:S(2)}, u32[]{:S(2)}) %collective-permute-start.4) | collective-permute-done | bytes 393248 | tf_op jit(solution)/shard_map/ppermute | solution.py:183
  141.4 5.0 %all-to-all-start.2 = ((bf16[256,4,384]{0,2,1:T(8,128)(2,1)}), bf16[256,4,384]{0,2,1:T(8,128)(2,1)S(1)}, u32[]{:S(2)}, u32[]{:S(2)}) async-start(bf16[256,4,384]{0,2,1:T(8,128)(2,1)} %bitcast.21), calls=%async_computation.2 | async-start | bytes 1572864 | tf_op jit(solution)/shard_map/all_to_all | solution.py:153
  149.7 15.3 %shard_map.61 = bf16[1024,384]{1,0:T(8,128)(2,1)} custom-call(s32[96]{0:T(128)} %reshape.101.tbl_ref, bf16[1024,384]{1,0:T(8,128)(2,1)} %bitcast.27.q_ref, bf16[1024,768]{1,0:T(8,128)(2,1)} %bitcast.66, bf16[1024,768]{1,0:T(8,128)(2,1)} %bitcast.63, bf16[256,768]{1,0:T(8,128)(2,1)} %bitcast.7.refs_2_, bf16[256,768]{1,0:T(8,128)(2,1)} %bitcast.9.refs_3_, ...), custom_call_target="tpu_custom_call" | custom-call | flops 2415919104 | bytes 4325376 | tf_op jit(solution)/shard_map/pallas_call | solution.py:86
  165.0 5.1 %all-to-all-start.4 = ((bf16[4,256,384]{2,1,0:T(8,128)(2,1)}), bf16[4,256,384]{2,1,0:T(8,128)(2,1)}, u32[]{:S(2)}, u32[]{:S(2)}) async-start(bf16[4,256,384]{2,1,0:T(8,128)(2,1)} %bitcast.76), calls=%async_computation.4 | async-start | bytes 1572864 | tf_op jit(solution)/shard_map/all_to_all | solution.py:217
  173.0 2.3 %reduce_sum.46 = f32[256,384]{1,0:T(8,128)S(1)} reduce(f32[256,4,384]{2,1,0:T(4,128)} %reshape.116, f32[]{:T(128)} %constant.124.clone.1), dimensions={1}, to_apply=%region_4.6 | reduce | flops 294912 | bytes 1966084 | tf_op jit(solution)/shard_map/reduce_sum | solution.py:20
  181.8 15.3 %shard_map.59 = bf16[1024,384]{1,0:T(8,128)(2,1)} custom-call(s32[96]{0:T(128)} %reshape.101.tbl_ref, bf16[1024,384]{1,0:T(8,128)(2,1)} %bitcast.78, bf16[1024,768]{1,0:T(8,128)(2,1)} %bitcast.67, bf16[1024,768]{1,0:T(8,128)(2,1)} %bitcast.64, bf16[256,768]{1,0:T(8,128)(2,1)} %bitcast.7.refs_2_, bf16[256,768]{1,0:T(8,128)(2,1)} %bitcast.9.refs_3_, ...), custom_call_target="tpu_custom_call" | custom-call | flops 2415919104 | bytes 4325376 | tf_op jit(solution)/shard_map/pallas_call | solution.py:86
  197.2 5.1 %all-to-all-start.5 = ((bf16[4,256,384]{2,1,0:T(8,128)(2,1)}), bf16[4,256,384]{2,1,0:T(8,128)(2,1)S(1)}, u32[]{:S(2)}, u32[]{:S(2)}) async-start(bf16[4,256,384]{2,1,0:T(8,128)(2,1)} %bitcast.77), calls=%async_computation.5 | async-start | bytes 1572864 | tf_op jit(solution)/shard_map/all_to_all | solution.py:217
  202.3 10.7 %shard_map.60 = bf16[256,768]{1,0:T(8,128)(2,1)} custom-call(bf16[256,768]{1,0:T(8,128)(2,1)} %pad_maximum_fusion.q_ref, bf16[1024,768]{1,0:T(8,128)(2,1)} %all-gather.3.cloned.1.call-done.k_ref, bf16[1024,768]{1,0:T(8,128)(2,1)} %all-gather.5.cloned.1.call-done.v_ref), custom_call_target="tpu_custom_call" | custom-call | flops 805306368 | bytes 3932160 | tf_op jit(solution)/shard_map/pallas_call | solution.py:125
  213.0 7.3 %all-to-all-done.5 = bf16[4,256,384]{2,1,0:T(8,128)(2,1)S(1)} async-done(((bf16[4,256,384]{2,1,0:T(8,128)(2,1)}), bf16[4,256,384]{2,1,0:T(8,128)(2,1)S(1)}, u32[]{:S(2)}, u32[]{:S(2)}) %all-to-all-start.5) | async-done | bytes 786464 | tf_op jit(solution)/shard_map/all_to_all | solution.py:217
  (76 shorter events, 37.8 us)
Async XLA Ops:
  9.8 6.5 %copy-start.2 = (bf16[256,3072]{1,0:T(8,128)(2,1)S(1)}, bf16[256,3072]{1,0:T(8,128)(2,1)}, u32[]{:S(2)}) copy-start(bf16[256,3072]{1,0:T(8,128)(2,1)} %param.7) | copy-start | bytes 4718596
  9.8 43.4 %all-to-all-start.1 = ((bf16[256,4,768]{2,0,1:T(8,128)(2,1)}), bf16[256,4,768]{2,0,1:T(8,128)(2,1)S(1)}, u32[]{:S(2)}, u32[]{:S(2)}) async-start(bf16[256,4,768]{2,0,1:T(8,128)(2,1)} %bitcast.59), calls=%async_computation.1 | async-start | bytes 3145728 | tf_op jit(solution)/shard_map/all_to_all | solution.py:141
  53.2 46.1 %copy-start = (bf16[256,4,768]{2,0,1:T(8,128)(2,1)}, bf16[256,4,768]{2,0,1:T(8,128)(2,1)S(1)}, u32[]{:S(2)}) copy-start(bf16[256,4,768]{2,0,1:T(8,128)(2,1)S(1)} %all-to-all-done.1) | copy-start | bytes 4718596
  53.2 3.8 %copy-start.3 = (s32[32,12]{0,1:T(8,128)S(1)}, s32[32,12]{0,1:T(8,128)}, u32[]{:S(2)}) copy-start(s32[32,12]{0,1:T(8,128)} %param.9) | copy-start | bytes 4612
  53.2 40.1 %all-to-all-start = ((bf16[256,4,768]{2,0,1:T(8,128)(2,1)}), bf16[256,4,768]{2,0,1:T(8,128)(2,1)S(1)}, u32[]{:S(2)}, u32[]{:S(2)}) async-start(bf16[256,4,768]{2,0,1:T(8,128)(2,1)} %bitcast.69), calls=%async_computation | async-start | bytes 3145728 | tf_op jit(solution)/shard_map/all_to_all | solution.py:140
  56.9 140.2 %all-gather.5.cloned.1.call-start = ((), (), s32[]{:S(2)}) async-start(), calls=%async_computation.7 | async-start | bytes 1966080 | tf_op jit(solution)/shard_map/all_gather | solution.py:156
  93.4 25.1 %copy-start.1 = (bf16[256,4,768]{2,0,1:T(8,128)(2,1)}, bf16[256,4,768]{2,0,1:T(8,128)(2,1)S(1)}, u32[]{:S(2)}) copy-start(bf16[256,4,768]{2,0,1:T(8,128)(2,1)S(1)} %all-to-all-done) | copy-start | bytes 4718596
  93.4 48.1 %all-to-all-start.3 = ((bf16[256,4,384]{2,0,1:T(8,128)(2,1)}), bf16[256,4,384]{2,0,1:T(8,128)(2,1)}, u32[]{:S(2)}, u32[]{:S(2)}) async-start(bf16[256,4,384]{2,0,1:T(8,128)(2,1)} %copy.53), calls=%async_computation.3 | async-start | bytes 1572864 | tf_op jit(solution)/shard_map/all_to_all | solution.py:153
  104.4 9.1 %collective-permute-start.2 = (bf16[2,128,768]{2,1,0:T(8,128)(2,1)}, bf16[2,128,768]{2,1,0:T(8,128)(2,1)}, u32[]{:S(2)}, u32[]{:S(2)}) collective-permute-start(bf16[2,128,768]{2,1,0:T(8,128)(2,1)} %get-tuple-element.30), channel_id=1, source_target_pairs={{0,12},{4,0},{8,4},{12,8},{1,13},{5,1},{9,5},{13,9},{2,14},{6,2},{... | collective-permute-start | bytes 1179656 | tf_op jit(solution)/shard_map/ppermute | solution.py:183
  104.5 24.5 %collective-permute-start.1 = (bf16[2,128,768]{2,1,0:T(8,128)(2,1)}, bf16[2,128,768]{2,1,0:T(8,128)(2,1)}, u32[]{:S(2)}, u32[]{:S(2)}) collective-permute-start(bf16[2,128,768]{2,1,0:T(8,128)(2,1)} %get-tuple-element.31), channel_id=1, source_target_pairs={{0,8},{4,12},{8,0},{12,4},{1,9},{5,13},{9,1},{13,5},{2,10},{6,14},... | collective-permute-start | bytes 1179656 | tf_op jit(solution)/shard_map/ppermute | solution.py:183
  105.9 23.2 %collective-permute-start = (bf16[2,128,768]{2,1,0:T(8,128)(2,1)S(1)}, bf16[2,128,768]{2,1,0:T(8,128)(2,1)}, u32[]{:S(2)}, u32[]{:S(2)}) collective-permute-start(bf16[2,128,768]{2,1,0:T(8,128)(2,1)S(1)} %get-tuple-element.32), channel_id=1, source_target_pairs={{0,4},{4,8},{8,12},{12,0},{1,5},{5,9},{9,13},{13,1},{2,6},{6,10},{... | collective-permute-start | bytes 1179656 | tf_op jit(solution)/shard_map/ppermute | solution.py:183
  107.2 23.1 %collective-permute-start.5 = (bf16[2,128,768]{2,1,0:T(8,128)(2,1)}, bf16[2,128,768]{2,1,0:T(8,128)(2,1)S(1)}, u32[]{:S(2)}, u32[]{:S(2)}) collective-permute-start(bf16[2,128,768]{2,1,0:T(8,128)(2,1)} %get-tuple-element.27), channel_id=1, source_target_pairs={{0,12},{4,0},{8,4},{12,8},{1,13},{5,1},{9,5},{13,9},{2,14},{6,2},{... | collective-permute-start | bytes 1179656 | tf_op jit(solution)/shard_map/ppermute | solution.py:183
  108.7 32.6 %collective-permute-start.4 = (bf16[2,128,768]{2,1,0:T(8,128)(2,1)}, bf16[2,128,768]{2,1,0:T(8,128)(2,1)}, u32[]{:S(2)}, u32[]{:S(2)}) collective-permute-start(bf16[2,128,768]{2,1,0:T(8,128)(2,1)} %get-tuple-element.28), channel_id=1, source_target_pairs={{0,8},{4,12},{8,0},{12,4},{1,9},{5,13},{9,1},{13,5},{2,10},{6,14},... | collective-permute-start | bytes 1179656 | tf_op jit(solution)/shard_map/ppermute | solution.py:183
  113.5 28.0 %collective-permute-start.3 = (bf16[2,128,768]{2,1,0:T(8,128)(2,1)}, bf16[2,128,768]{2,1,0:T(8,128)(2,1)}, u32[]{:S(2)}, u32[]{:S(2)}) collective-permute-start(bf16[2,128,768]{2,1,0:T(8,128)(2,1)} %get-tuple-element.29), channel_id=1, source_target_pairs={{0,4},{4,8},{8,12},{12,0},{1,5},{5,9},{9,13},{13,1},{2,6},{6,10},{... | collective-permute-start | bytes 1179656 | tf_op jit(solution)/shard_map/ppermute | solution.py:183
  130.3 17.0 %copy-start.4 = (bf16[2,128,768]{2,1,0:T(8,128)(2,1)}, bf16[2,128,768]{2,1,0:T(8,128)(2,1)S(1)}, u32[]{:S(2)}) copy-start(bf16[2,128,768]{2,1,0:T(8,128)(2,1)S(1)} %collective-permute-done.5) | copy-start | bytes 1179652
  141.4 23.6 %all-to-all-start.2 = ((bf16[256,4,384]{0,2,1:T(8,128)(2,1)}), bf16[256,4,384]{0,2,1:T(8,128)(2,1)S(1)}, u32[]{:S(2)}, u32[]{:S(2)}) async-start(bf16[256,4,384]{0,2,1:T(8,128)(2,1)} %bitcast.21), calls=%async_computation.2 | async-start | bytes 1572864 | tf_op jit(solution)/shard_map/all_to_all | solution.py:153
  146.5 50.7 %all-gather.3.cloned.1.call-start = ((), (), s32[]{:S(2)}) async-start(), calls=%async_computation.6 | async-start | bytes 1966080 | tf_op jit(solution)/shard_map/all_gather | solution.py:155
  165.0 32.1 %all-to-all-start.4 = ((bf16[4,256,384]{2,1,0:T(8,128)(2,1)}), bf16[4,256,384]{2,1,0:T(8,128)(2,1)}, u32[]{:S(2)}, u32[]{:S(2)}) async-start(bf16[4,256,384]{2,1,0:T(8,128)(2,1)} %bitcast.76), calls=%async_computation.4 | async-start | bytes 1572864 | tf_op jit(solution)/shard_map/all_to_all | solution.py:217
  197.2 23.1 %all-to-all-start.5 = ((bf16[4,256,384]{2,1,0:T(8,128)(2,1)}), bf16[4,256,384]{2,1,0:T(8,128)(2,1)S(1)}, u32[]{:S(2)}, u32[]{:S(2)}) async-start(bf16[4,256,384]{2,1,0:T(8,128)(2,1)} %bitcast.77), calls=%async_computation.5 | async-start | bytes 1572864 | tf_op jit(solution)/shard_map/all_to_all | solution.py:217
Sparse Core Ops, SparseCore 0:
  76.2 20.9 all-gather.4
  149.4 20.2 all-gather.2

commit v9 on v8

--- a/solution.py
+++ b/solution.py
@@ -102,8 +102,13 @@
 
 
 def draft_kernel(q_ref, k_ref, v_ref, o_ref):
+    tile = o_ref.shape[0]
+    token = lax.broadcasted_iota(jnp.int32, (tile, tile * POOL), 1)
+    draft = lax.broadcasted_iota(jnp.int32, (tile, tile * POOL), 0)
+    pooling = jnp.where(token // POOL == draft, POOL ** (-0.5), 0.0).astype(jnp.bfloat16)
+    pooled = jnp.dot(pooling, q_ref[...], preferred_element_type=jnp.float32).astype(jnp.bfloat16)
     raw = lax.dot_general(
-        q_ref[...], k_ref[...], (((1,), (1,)), ((), ())), preferred_element_type=jnp.float32
+        pooled, k_ref[...], (((1,), (1,)), ((), ())), preferred_element_type=jnp.float32
     )
     running = jnp.max(raw, axis=1, keepdims=True)
     weights = jnp.exp2((raw - running) * EXP2_SCALE)
@@ -112,15 +117,16 @@
     o_ref[...] = (weighted / totals).astype(o_ref.dtype)
 
 
-def draft_attention(queries, keys, values):
-    rows, width = queries.shape
+def draft_attention(queries, keys, values, head_lo):
+    token_rows, width = queries.shape
+    rows = token_rows // POOL
     heads = width // HD
     key_rows = keys.shape[0]
     tile = min(DRAFT_ROWS, rows)
     cost = pl.CostEstimate(
-        flops=4 * rows * key_rows * HD * heads,
+        flops=4 * rows * key_rows * HD * heads + 2 * rows * tile * POOL * HD * heads,
         transcendentals=rows * key_rows * heads,
-        bytes_accessed=2 * HD * heads * (2 * rows + 2 * key_rows),
+        bytes_accessed=2 * HD * heads * (token_rows + rows + 2 * key_rows),
     )
     return pl.pallas_call(
         draft_kernel,
@@ -128,9 +134,9 @@
         cost_estimate=cost,
         grid=(heads, rows // tile),
         in_specs=[
-            pl.BlockSpec((tile, HD), lambda h, r: (r, h)),
-            pl.BlockSpec((key_rows, HD), lambda h, r: (0, h)),
-            pl.BlockSpec((key_rows, HD), lambda h, r: (0, h)),
+            pl.BlockSpec((tile * POOL, HD), lambda h, r: (r, h)),
+            pl.BlockSpec((key_rows, HD), lambda h, r: (0, h + head_lo)),
+            pl.BlockSpec((key_rows, HD), lambda h, r: (0, h + head_lo)),
         ],
         out_specs=pl.BlockSpec((tile, HD), lambda h, r: (r, h)),
     )(queries, keys, values)
@@ -203,21 +209,25 @@
     joint_pos = jnp.where(distance == 0, within, per_dev + (distance - 1) * CAP + ranks_used)
     table = jnp.clip(joint_pos, 0, per_dev + (seq_count - 1) * CAP - 1).reshape(-1).astype(jnp.int32)
 
-    pooled = None
     pieces = []
     for index, ((head_lo, count), queries) in enumerate(zip(spans, query_parts)):
         rows_part = sparse_attention(
             table, queries, key_rows, value_rows, remote_keys, remote_values, head_lo, count,
         )
         if index == len(spans) - 1:
-            pooled = jnp.concatenate([pool_tokens(q) for q in query_parts], axis=1)
-            rows_part, pooled, draft_keys, draft_values = lax.optimization_barrier(
-                (rows_part, pooled, draft_keys, draft_values)
+            rows_part, draft_keys, draft_values = lax.optimization_barrier(
+                (rows_part, draft_keys, draft_values)
             )
         back = lax.all_to_all(rows_part, "head", split_axis=0, concat_axis=1, tiled=True)
         pieces.append(back.reshape(back.shape[0], -1, count * HD))
     sparse_out = jnp.concatenate(pieces, axis=2).reshape(pieces[0].shape[0], -1)
-    draft_out = draft_attention(pooled, draft_keys, draft_values)
+    draft_out = jnp.concatenate(
+        [
+            draft_attention(queries, draft_keys, draft_values, head_lo)
+            for (head_lo, count), queries in zip(spans, query_parts)
+        ],
+        axis=1,
+    )
     return (draft_out, sparse_out)
 
 

time: 231 us -> 229 us (level)
  waiting for transfers between devices: 73 us -> 80.5 us
  local copies, waits for them, and re-layouts: 39.7 us -> 34 us
  other arithmetic: 25 us -> 20.6 us
  Pallas kernels: 41.4 us -> 43.9 us
    ppermute x6, waiting for transfers between devices: 16.5 us -> 26.3 us  [exchange(): lax.ppermute(parcel, 'seq', [(i, (i + shift) % seq_count) for i in range(...]
    convert_element_type x5 -> x2, local copies, waits for them, and re-layouts: 14.7 us -> 7.94 us  [pool_tokens(): matrix.astype(jnp.float32)]
    reduce_sum x4 -> x2, other arithmetic: 11.7 us -> 7.65 us  [pool_tokens(): return (grouped.sum(axis=1) * POOL ** (-0.5)).astype(jnp.bfloat16)]
    pallas_call x1 -> x2, Pallas kernels: 10.7 us -> 13.1 us  [draft_attention(): pl.pallas_call(draft_kernel, out_shape=jax.ShapeDtypeStruct((rows, width)...]
    convert_element_type x4 -> x2, other arithmetic: 5.22 us -> 3.87 us  [pool_tokens(): matrix.astype(jnp.float32)]
  transfers between devices with their start and end apart: 14 -> 14, of which waited for: 7 -> 8; matrix products, arithmetic and copies ran while one was open for 26% -> 22% of each run, Pallas kernels for 18% -> 19%
where the time goes in v9:
time: 229 us; the launch traced here: 227 us
  waiting for transfers between devices  80.5 us (35%)
  Pallas kernels  43.9 us (19%)
  starting transfers between devices  34.2 us (15%)
  local copies, waits for them, and re-layouts  34 us (15%)
  other arithmetic  20.6 us (9%)
  between operations  14.2 us (6%)
    all_to_all x1, waiting for transfers between devices, on_device(): lax.all_to_all(value_in, 'head', split_axis=1, concat_axis=0, tiled=True)  35.6 us
    pallas_call x2, Pallas kernels, sparse_attention(): pl.pallas_call(sparse_kernel, out_shape=jax.ShapeDtypeStruct((rows, heads...  30.8 us
    ppermute x6, waiting for transfers between devices, exchange(): lax.ppermute(parcel, 'seq', [(i, (i + shift) % seq_count) for i in range(...  26.3 us
    all_to_all x1, waiting for transfers between devices, on_device(): lax.all_to_all(key_in, 'head', split_axis=1, concat_axis=0, tiled=True)  13.5 us
    pallas_call x2, Pallas kernels, draft_attention(): pl.pallas_call(draft_kernel, out_shape=jax.ShapeDtypeStruct((rows, width)...  13.1 us
    all_to_all x2, starting transfers between devices, query_a2a(): lax.all_to_all(piece, 'head', split_axis=1, concat_axis=0, tiled=True)  9.22 us
    all_to_all x2, starting transfers between devices, on_device(): lax.all_to_all(rows_part, 'head', split_axis=0, concat_axis=1, tiled=True)  8.98 us
    convert_element_type x2, local copies, waits for them, and re-layouts, pool_tokens(): matrix.astype(jnp.float32)  7.94 us
  transfers between devices with their start and end apart: 14, of which 8 were waited for; matrix products, arithmetic and copies ran while one was open for 22% of the time, Pallas kernels for 19%

profile of v9, /device:TPU:0, one launch (start us, length us, event | category | flops | bytes accessed | tf_op | source)
XLA Modules:
  0.0 227.4 jit_solution(11453982513965456265)
XLA Ops:
  7.2 2.7 %copy.49 = bf16[32,4,8,768]{3,2,0,1:T(8,128)(2,1)} copy(bf16[32,4,8,768]{3,2,1,0:T(8,128)(2,1)} %bitcast.74) | data formatting | bytes 3145728 | tf_op jit(solution)/shard_map/all_to_all | solution.py:147
  9.8 6.4 %all-to-all-start.2 = ((bf16[256,4,768]{2,0,1:T(8,128)(2,1)}), bf16[256,4,768]{2,0,1:T(8,128)(2,1)S(1)}, u32[]{:S(2)}, u32[]{:S(2)}) async-start(bf16[256,4,768]{2,0,1:T(8,128)(2,1)} %bitcast.57), calls=%async_computation.2 | async-start | bytes 3145728 | tf_op jit(solution)/shard_map/all_to_all | solution.py:147
  17.6 35.6 %all-to-all-done.2 = bf16[256,4,768]{2,0,1:T(8,128)(2,1)S(1)} async-done(((bf16[256,4,768]{2,0,1:T(8,128)(2,1)}), bf16[256,4,768]{2,0,1:T(8,128)(2,1)S(1)}, u32[]{:S(2)}, u32[]{:S(2)}) %all-to-all-start.2) | async-done | bytes 1572896 | tf_op jit(solution)/shard_map/all_to_all | solution.py:147
  53.2 3.7 %all-to-all-start.1 = ((bf16[256,4,768]{2,0,1:T(8,128)(2,1)}), bf16[256,4,768]{2,0,1:T(8,128)(2,1)S(1)}, u32[]{:S(2)}, u32[]{:S(2)}) async-start(bf16[256,4,768]{2,0,1:T(8,128)(2,1)} %bitcast.66), calls=%async_computation.1 | async-start | bytes 3145728 | tf_op jit(solution)/shard_map/all_to_all | solution.py:146
  58.4 4.3 %reshape.92 = bf16[256,4,768]{2,1,0:T(4,128)(2,1)} reshape(bf16[256,3072]{1,0:T(8,128)(2,1)} %param.6) | data formatting | bytes 3145728 | tf_op jit(solution)/shard_map/reshape | solution.py:153
  64.6 4.8 %reshape.109 = f32[256,4,768]{2,1,0:T(4,128)} reshape(f32[4,256,768]{2,1,0:T(8,128)} %bitcast_convert_fusion) | data formatting | bytes 6291456 | tf_op jit(solution)/shard_map/convert_element_type | solution.py:19
  69.4 4.7 %reduce_sum.29 = f32[256,768]{1,0:T(8,128)} reduce(f32[256,4,768]{2,1,0:T(4,128)} %reshape.109, f32[]{:T(128)} %constant.123.clone.1), dimensions={1}, to_apply=%region_5.7 | reduce | flops 589824 | bytes 3932164 | tf_op jit(solution)/shard_map/reduce_sum | solution.py:20
  76.1 2.8 %fusion.11 = (bf16[256,4,384]{2,1,0:T(4,128)(2,1)S(1)}, bf16[256,4,384]{2,1,0:T(4,128)(2,1)}) fusion(bf16[256,4,768]{2,1,0:T(4,128)(2,1)} %reshape.92), kind=kLoop, calls=%fused_computation.55 | loop fusion | bytes 3145728 | tf_op jit(solution)/shard_map/slice | solution.py:155
  79.9 13.5 %all-to-all-done.1 = bf16[256,4,768]{2,0,1:T(8,128)(2,1)S(1)} async-done(((bf16[256,4,768]{2,0,1:T(8,128)(2,1)}), bf16[256,4,768]{2,0,1:T(8,128)(2,1)S(1)}, u32[]{:S(2)}, u32[]{:S(2)}) %all-to-all-start.1) | async-done | bytes 1572896 | tf_op jit(solution)/shard_map/all_to_all | solution.py:146
  93.4 4.2 %all-to-all-start = ((bf16[256,4,384]{2,0,1:T(8,128)(2,1)}), bf16[256,4,384]{2,0,1:T(8,128)(2,1)}, u32[]{:S(2)}, u32[]{:S(2)}) async-start(bf16[256,4,384]{2,0,1:T(8,128)(2,1)} %copy.40), calls=%async_computation | async-start | bytes 1572864 | tf_op jit(solution)/shard_map/all_to_all | solution.py:159
  104.7 2.3 %copy.42 = bf16[256,4,384]{0,2,1:T(8,128)(2,1)} copy(bf16[256,4,384]{2,1,0:T(4,128)(2,1)} %get-tuple-element.24) | data formatting | bytes 1572864
  115.6 3.1 %reshape.108 = f32[256,4,768]{2,1,0:T(4,128)S(1)} reshape(f32[4,256,768]{2,1,0:T(8,128)} %bitcast_convert_fusion.1) | data formatting | bytes 6291456 | tf_op jit(solution)/shard_map/convert_element_type | solution.py:19
  118.7 3.0 %reduce_sum.28 = f32[256,768]{1,0:T(8,128)} reduce(f32[256,4,768]{2,1,0:T(4,128)S(1)} %reshape.108, f32[]{:T(128)} %constant.123.clone.1), dimensions={1}, to_apply=%region_4.6 | reduce | flops 589824 | bytes 3932164 | tf_op jit(solution)/shard_map/reduce_sum | solution.py:20
  123.7 3.5 %collective-permute-done = bf16[2,128,768]{2,1,0:T(8,128)(2,1)} collective-permute-done((bf16[2,128,768]{2,1,0:T(8,128)(2,1)S(1)}, bf16[2,128,768]{2,1,0:T(8,128)(2,1)}, u32[]{:S(2)}, u32[]{:S(2)}) %collective-permute-start) | collective-permute-done | bytes 393248 | tf_op jit(solution)/shard_map/ppermute | solution.py:189
  128.1 15.6 %collective-permute-done.4 = bf16[2,128,768]{2,1,0:T(8,128)(2,1)} collective-permute-done((bf16[2,128,768]{2,1,0:T(8,128)(2,1)}, bf16[2,128,768]{2,1,0:T(8,128)(2,1)}, u32[]{:S(2)}, u32[]{:S(2)}) %collective-permute-start.4) | collective-permute-done | bytes 393248 | tf_op jit(solution)/shard_map/ppermute | solution.py:189
  143.7 6.3 %collective-permute-done.3 = bf16[2,128,768]{2,1,0:T(8,128)(2,1)} collective-permute-done((bf16[2,128,768]{2,1,0:T(8,128)(2,1)}, bf16[2,128,768]{2,1,0:T(8,128)(2,1)}, u32[]{:S(2)}, u32[]{:S(2)}) %collective-permute-start.3) | collective-permute-done | bytes 393248 | tf_op jit(solution)/shard_map/ppermute | solution.py:189
  150.0 5.0 %all-to-all-start.3 = ((bf16[256,4,384]{0,2,1:T(8,128)(2,1)}), bf16[256,4,384]{0,2,1:T(8,128)(2,1)S(1)}, u32[]{:S(2)}, u32[]{:S(2)}) async-start(bf16[256,4,384]{0,2,1:T(8,128)(2,1)} %bitcast.23), calls=%async_computation.3 | async-start | bytes 1572864 | tf_op jit(solution)/shard_map/all_to_all | solution.py:159
  158.3 15.4 %shard_map.62 = bf16[1024,384]{1,0:T(8,128)(2,1)} custom-call(s32[96]{0:T(128)} %reshape.94.tbl_ref, bf16[1024,384]{1,0:T(8,128)(2,1)} %bitcast.1.q_ref, bf16[1024,768]{1,0:T(8,128)(2,1)} %bitcast.64, bf16[1024,768]{1,0:T(8,128)(2,1)} %bitcast.61, bf16[256,768]{1,0:T(8,128)(2,1)} %bitcast.9.refs_2_, bf16[256,768]{1,0:T(8,128)(2,1)} %bitcast.11.refs_3_, ...), custom_call_target="tpu_custom_call" | custom-call | flops 2415919104 | bytes 4325376 | tf_op jit(solution)/shard_map/pallas_call | solution.py:86
  173.7 5.1 %all-to-all-start.4 = ((bf16[4,256,384]{2,1,0:T(8,128)(2,1)}), bf16[4,256,384]{2,1,0:T(8,128)(2,1)S(1)}, u32[]{:S(2)}, u32[]{:S(2)}) async-start(bf16[4,256,384]{2,1,0:T(8,128)(2,1)} %bitcast.78), calls=%async_computation.4 | async-start | bytes 1572864 | tf_op jit(solution)/shard_map/all_to_all | solution.py:221
  179.9 15.4 %shard_map.59 = bf16[1024,384]{1,0:T(8,128)(2,1)} custom-call(s32[96]{0:T(128)} %reshape.94.tbl_ref, bf16[1024,384]{1,0:T(8,128)(2,1)} %bitcast.72, bf16[1024,768]{1,0:T(8,128)(2,1)} %bitcast.65, bf16[1024,768]{1,0:T(8,128)(2,1)} %bitcast.62, bf16[256,768]{1,0:T(8,128)(2,1)} %bitcast.9.refs_2_, bf16[256,768]{1,0:T(8,128)(2,1)} %bitcast.11.refs_3_, ...), custom_call_target="tpu_custom_call" | custom-call | flops 2415919104 | bytes 4325376 | tf_op jit(solution)/shard_map/pallas_call | solution.py:86
  196.6 3.9 %all-to-all-start.5 = ((bf16[4,256,384]{2,1,0:T(8,128)(2,1)}), bf16[4,256,384]{2,1,0:T(8,128)(2,1)S(1)}, u32[]{:S(2)}, u32[]{:S(2)}) async-start(bf16[4,256,384]{2,1,0:T(8,128)(2,1)} %bitcast.77), calls=%async_computation.5 | async-start | bytes 1572864 | tf_op jit(solution)/shard_map/all_to_all | solution.py:221
  200.5 6.5 %shard_map.61 = bf16[256,384]{1,0:T(8,128)(2,1)} custom-call(bf16[1024,384]{1,0:T(8,128)(2,1)} %bitcast.73, bf16[1024,768]{1,0:T(8,128)(2,1)} %all-gather.3.cloned.1.call-done.k_ref, bf16[1024,768]{1,0:T(8,128)(2,1)} %all-gather.5.cloned.1.call-done.v_ref), custom_call_target="tpu_custom_call" | custom-call | flops 503316480 | bytes 2555904 | tf_op jit(solution)/shard_map/pallas_call | solution.py:131
  207.0 6.6 %shard_map.60 = bf16[256,384]{1,0:T(8,128)(2,1)} custom-call(bf16[1024,384]{1,0:T(8,128)(2,1)} %bitcast.1.q_ref, bf16[1024,768]{1,0:T(8,128)(2,1)} %all-gather.3.cloned.1.call-done.k_ref, bf16[1024,768]{1,0:T(8,128)(2,1)} %all-gather.5.cloned.1.call-done.v_ref), custom_call_target="tpu_custom_call" | custom-call | flops 503316480 | bytes 2555904 | tf_op jit(solution)/shard_map/pallas_call | solution.py:131
  215.3 3.8 %all-to-all-done.5 = bf16[4,256,384]{2,1,0:T(8,128)(2,1)S(1)} async-done(((bf16[4,256,384]{2,1,0:T(8,128)(2,1)}), bf16[4,256,384]{2,1,0:T(8,128)(2,1)S(1)}, u32[]{:S(2)}, u32[]{:S(2)}) %all-to-all-start.5) | async-done | bytes 786464 | tf_op jit(solution)/shard_map/all_to_all | solution.py:221
  (70 shorter events, 35.1 us)
Async XLA Ops:
  9.8 6.5 %copy-start.2 = (bf16[256,3072]{1,0:T(8,128)(2,1)S(1)}, bf16[256,3072]{1,0:T(8,128)(2,1)}, u32[]{:S(2)}) copy-start(bf16[256,3072]{1,0:T(8,128)(2,1)} %param.7) | copy-start | bytes 4718596
  9.8 43.4 %all-to-all-start.2 = ((bf16[256,4,768]{2,0,1:T(8,128)(2,1)}), bf16[256,4,768]{2,0,1:T(8,128)(2,1)S(1)}, u32[]{:S(2)}, u32[]{:S(2)}) async-start(bf16[256,4,768]{2,0,1:T(8,128)(2,1)} %bitcast.57), calls=%async_computation.2 | async-start | bytes 3145728 | tf_op jit(solution)/shard_map/all_to_all | solution.py:147
  53.2 46.2 %copy-start = (bf16[256,4,768]{2,0,1:T(8,128)(2,1)}, bf16[256,4,768]{2,0,1:T(8,128)(2,1)S(1)}, u32[]{:S(2)}) copy-start(bf16[256,4,768]{2,0,1:T(8,128)(2,1)S(1)} %all-to-all-done.2) | copy-start | bytes 4718596
  53.2 3.8 %copy-start.4 = (s32[32,12]{0,1:T(8,128)S(1)}, s32[32,12]{0,1:T(8,128)}, u32[]{:S(2)}) copy-start(s32[32,12]{0,1:T(8,128)} %param.9) | copy-start | bytes 4612
  53.2 40.1 %all-to-all-start.1 = ((bf16[256,4,768]{2,0,1:T(8,128)(2,1)}), bf16[256,4,768]{2,0,1:T(8,128)(2,1)S(1)}, u32[]{:S(2)}, u32[]{:S(2)}) async-start(bf16[256,4,768]{2,0,1:T(8,128)(2,1)} %bitcast.66), calls=%async_computation.1 | async-start | bytes 3145728 | tf_op jit(solution)/shard_map/all_to_all | solution.py:146
  56.9 138.4 %all-gather.5.cloned.1.call-start = ((), (), s32[]{:S(2)}) async-start(), calls=%async_computation.7 | async-start | bytes 1966080 | tf_op jit(solution)/shard_map/all_gather | solution.py:162
  58.1 4.6 %copy-start.5 = (s32[4,4,8]{2,1,0:T(4,128)}, s32[4,4,8]{2,1,0:T(4,128)S(1)}, u32[]{:S(2)}) copy-start(s32[4,4,8]{2,1,0:T(4,128)S(1)} %broadcast_add_fusion) | copy-start | bytes 1540
  93.4 20.3 %copy-start.1 = (bf16[256,4,768]{2,0,1:T(8,128)(2,1)}, bf16[256,4,768]{2,0,1:T(8,128)(2,1)S(1)}, u32[]{:S(2)}) copy-start(bf16[256,4,768]{2,0,1:T(8,128)(2,1)S(1)} %all-to-all-done.1) | copy-start | bytes 4718596
  93.4 56.6 %all-to-all-start = ((bf16[256,4,384]{2,0,1:T(8,128)(2,1)}), bf16[256,4,384]{2,0,1:T(8,128)(2,1)}, u32[]{:S(2)}, u32[]{:S(2)}) async-start(bf16[256,4,384]{2,0,1:T(8,128)(2,1)} %copy.40), calls=%async_computation | async-start | bytes 1572864 | tf_op jit(solution)/shard_map/all_to_all | solution.py:159
  97.6 97.7 %all-gather.3.cloned.1.call-start = ((), (), s32[]{:S(2)}) async-start(), calls=%async_computation.6 | async-start | bytes 1966080 | tf_op jit(solution)/shard_map/all_gather | solution.py:161
  104.5 7.2 %collective-permute-start.2 = (bf16[2,128,768]{2,1,0:T(8,128)(2,1)}, bf16[2,128,768]{2,1,0:T(8,128)(2,1)}, u32[]{:S(2)}, u32[]{:S(2)}) collective-permute-start(bf16[2,128,768]{2,1,0:T(8,128)(2,1)} %get-tuple-element.28), channel_id=1, source_target_pairs={{0,12},{4,0},{8,4},{12,8},{1,13},{5,1},{9,5},{13,9},{2,14},{6,2},{... | collective-permute-start | bytes 1179656 | tf_op jit(solution)/shard_map/ppermute | solution.py:189
  106.9 16.7 %collective-permute-start.1 = (bf16[2,128,768]{2,1,0:T(8,128)(2,1)}, bf16[2,128,768]{2,1,0:T(8,128)(2,1)}, u32[]{:S(2)}, u32[]{:S(2)}) collective-permute-start(bf16[2,128,768]{2,1,0:T(8,128)(2,1)} %get-tuple-element.29), channel_id=1, source_target_pairs={{0,8},{4,12},{8,0},{12,4},{1,9},{5,13},{9,1},{13,5},{2,10},{6,14},... | collective-permute-start | bytes 1179656 | tf_op jit(solution)/shard_map/ppermute | solution.py:189
  108.3 18.9 %collective-permute-start = (bf16[2,128,768]{2,1,0:T(8,128)(2,1)S(1)}, bf16[2,128,768]{2,1,0:T(8,128)(2,1)}, u32[]{:S(2)}, u32[]{:S(2)}) collective-permute-start(bf16[2,128,768]{2,1,0:T(8,128)(2,1)S(1)} %get-tuple-element.30), channel_id=1, source_target_pairs={{0,4},{4,8},{8,12},{12,0},{1,5},{5,9},{9,13},{13,1},{2,6},{6,10},{... | collective-permute-start | bytes 1179656 | tf_op jit(solution)/shard_map/ppermute | solution.py:189
  109.6 18.5 %collective-permute-start.5 = (bf16[2,128,768]{2,1,0:T(8,128)(2,1)}, bf16[2,128,768]{2,1,0:T(8,128)(2,1)}, u32[]{:S(2)}, u32[]{:S(2)}) collective-permute-start(bf16[2,128,768]{2,1,0:T(8,128)(2,1)} %get-tuple-element.25), channel_id=1, source_target_pairs={{0,12},{4,0},{8,4},{12,8},{1,13},{5,1},{9,5},{13,9},{2,14},{6,2},{... | collective-permute-start | bytes 1179656 | tf_op jit(solution)/shard_map/ppermute | solution.py:189
  111.1 32.7 %collective-permute-start.4 = (bf16[2,128,768]{2,1,0:T(8,128)(2,1)}, bf16[2,128,768]{2,1,0:T(8,128)(2,1)}, u32[]{:S(2)}, u32[]{:S(2)}) collective-permute-start(bf16[2,128,768]{2,1,0:T(8,128)(2,1)} %get-tuple-element.26), channel_id=1, source_target_pairs={{0,8},{4,12},{8,0},{12,4},{1,9},{5,13},{9,1},{13,5},{2,10},{6,14},... | collective-permute-start | bytes 1179656 | tf_op jit(solution)/shard_map/ppermute | solution.py:189
  111.8 38.2 %collective-permute-start.3 = (bf16[2,128,768]{2,1,0:T(8,128)(2,1)}, bf16[2,128,768]{2,1,0:T(8,128)(2,1)}, u32[]{:S(2)}, u32[]{:S(2)}) collective-permute-start(bf16[2,128,768]{2,1,0:T(8,128)(2,1)} %get-tuple-element.27), channel_id=1, source_target_pairs={{0,4},{4,8},{8,12},{12,0},{1,5},{5,9},{9,13},{13,1},{2,6},{6,10},{... | collective-permute-start | bytes 1179656 | tf_op jit(solution)/shard_map/ppermute | solution.py:189
  150.0 23.7 %all-to-all-start.3 = ((bf16[256,4,384]{0,2,1:T(8,128)(2,1)}), bf16[256,4,384]{0,2,1:T(8,128)(2,1)S(1)}, u32[]{:S(2)}, u32[]{:S(2)}) async-start(bf16[256,4,384]{0,2,1:T(8,128)(2,1)} %bitcast.23), calls=%async_computation.3 | async-start | bytes 1572864 | tf_op jit(solution)/shard_map/all_to_all | solution.py:159
  173.7 22.9 %all-to-all-start.4 = ((bf16[4,256,384]{2,1,0:T(8,128)(2,1)}), bf16[4,256,384]{2,1,0:T(8,128)(2,1)S(1)}, u32[]{:S(2)}, u32[]{:S(2)}) async-start(bf16[4,256,384]{2,1,0:T(8,128)(2,1)} %bitcast.78), calls=%async_computation.4 | async-start | bytes 1572864 | tf_op jit(solution)/shard_map/all_to_all | solution.py:221
  196.6 22.5 %all-to-all-start.5 = ((bf16[4,256,384]{2,1,0:T(8,128)(2,1)}), bf16[4,256,384]{2,1,0:T(8,128)(2,1)S(1)}, u32[]{:S(2)}, u32[]{:S(2)}) async-start(bf16[4,256,384]{2,1,0:T(8,128)(2,1)} %bitcast.77), calls=%async_computation.5 | async-start | bytes 1572864 | tf_op jit(solution)/shard_map/all_to_all | solution.py:221
  207.0 6.6 %copy-start.3 = (bf16[256,384]{1,0:T(8,128)(2,1)S(1)}, bf16[256,384]{1,0:T(8,128)(2,1)}, u32[]{:S(2)}) copy-start(bf16[256,384]{1,0:T(8,128)(2,1)} %shard_map.61) | copy-start | bytes 589828
Sparse Core Ops, SparseCore 0:
  76.2 20.9 all-gather.4
  123.8 27.0 all-gather.2

commit v10 on v9

--- a/solution.py
+++ b/solution.py
@@ -142,9 +142,25 @@
     )(queries, keys, values)
 
 
+def head_permutes(matrix):
+    count = lax.axis_size("head")
+    me = lax.axis_index("head")
+    rows, total = matrix.shape
+    chunks = matrix.reshape(rows, count, total // count)
+    by_shift = [lax.dynamic_index_in_dim(chunks, me, axis=1, keepdims=False)]
+    for shift in range(1, count):
+        piece = lax.dynamic_index_in_dim(chunks, (me + shift) % count, axis=1, keepdims=False)
+        by_shift.append(
+            lax.ppermute(piece, "head", [(i, (i + shift) % count) for i in range(count)])
+        )
+    stacked = jnp.stack(by_shift, axis=0)
+    order = (me - jnp.arange(count, dtype=jnp.int32)) % count
+    return jnp.take(stacked, order, axis=0).reshape(count * rows, total // count)
+
+
 def on_device(query_in, key_in, value_in, block_lists):
     key_rows = lax.all_to_all(key_in, "head", split_axis=1, concat_axis=0, tiled=True)
-    value_rows = lax.all_to_all(value_in, "head", split_axis=1, concat_axis=0, tiled=True)
+    value_rows = head_permutes(value_in)
     seq_rows, width = key_rows.shape
     head_count = lax.axis_size("head")
     heads = width // HD

time: 229 us -> 222 us (0.969)
  waiting for transfers between devices: 80.5 us -> 71.5 us
  local copies, waits for them, and re-layouts: 34 us -> 37.8 us
  starting transfers between devices: 34.2 us -> 30.7 us
    all_to_all x1 -> x0, waiting for transfers between devices: 35.6 us -> none  [on_device(): lax.all_to_all(value_in, 'head', split_axis=1, concat_axis=0, tiled=True)]
    all_to_all x1, waiting for transfers between devices: 13.5 us -> 26 us  [on_device(): lax.all_to_all(key_in, 'head', split_axis=1, concat_axis=0, tiled=True)]
    ppermute x0 -> x3, waiting for transfers between devices: none -> 9.81 us  [head_permutes(): lax.ppermute(piece, 'head', [(i, (i + shift) % count) for i in range(coun...]
    ppermute x0 -> x3, starting transfers between devices: none -> 6.96 us  [head_permutes(): lax.ppermute(piece, 'head', [(i, (i + shift) % count) for i in range(coun...]
    all_to_all x1 -> x0, starting transfers between devices: 6.45 us -> none  [on_device(): lax.all_to_all(value_in, 'head', split_axis=1, concat_axis=0, tiled=True)]
    all_to_all x2, waiting for transfers between devices: 5.04 us -> 9.22 us  [on_device(): lax.all_to_all(rows_part, 'head', split_axis=0, concat_axis=1, tiled=True)]
    gather x0 -> x2, local copies, waits for them, and re-layouts: none -> 3.42 us  [head_permutes(): jnp.take(stacked, order, axis=0).reshape(count * rows, total // count)]
    convert_element_type x2 -> x1, local copies, waits for them, and re-layouts: 7.94 us -> 4.85 us  [pool_tokens(): matrix.astype(jnp.float32)]
  transfers between devices with their start and end apart: 14 -> 16, of which waited for: 8 -> 9; matrix products, arithmetic and copies ran while one was open for 22% -> 25% of each run, Pallas kernels for 19% -> 20%
where the time goes in v10:
time: 222 us; the launch traced here: 221 us
  waiting for transfers between devices  71.5 us (32%)
  Pallas kernels  43.9 us (20%)
  local copies, waits for them, and re-layouts  37.8 us (17%)
  starting transfers between devices  30.7 us (14%)
  other arithmetic  22.6 us (10%)
  between operations  14.4 us (6%)
    pallas_call x2, Pallas kernels, sparse_attention(): pl.pallas_call(sparse_kernel, out_shape=jax.ShapeDtypeStruct((rows, heads...  30.7 us
    all_to_all x1, waiting for transfers between devices, on_device(): lax.all_to_all(key_in, 'head', split_axis=1, concat_axis=0, tiled=True)  26 us
    ppermute x6, waiting for transfers between devices, exchange(): lax.ppermute(parcel, 'seq', [(i, (i + shift) % seq_count) for i in range(...  25 us
    pallas_call x2, Pallas kernels, draft_attention(): pl.pallas_call(draft_kernel, out_shape=jax.ShapeDtypeStruct((rows, width)...  13.1 us
    ppermute x3, waiting for transfers between devices, head_permutes(): lax.ppermute(piece, 'head', [(i, (i + shift) % count) for i in range(coun...  9.81 us
    all_to_all x2, waiting for transfers between devices, on_device(): lax.all_to_all(rows_part, 'head', split_axis=0, concat_axis=1, tiled=True)  9.22 us
    all_to_all x2, starting transfers between devices, query_a2a(): lax.all_to_all(piece, 'head', split_axis=1, concat_axis=0, tiled=True)  9.22 us
    reduce_sum x2, other arithmetic, pool_tokens(): return (grouped.sum(axis=1) * POOL ** (-0.5)).astype(jnp.bfloat16)  7.33 us
  transfers between devices with their start and end apart: 16, of which 9 were waited for; matrix products, arithmetic and copies ran while one was open for 25% of the time, Pallas kernels for 20%

profile of v10, /device:TPU:0, one launch (start us, length us, event | category | flops | bytes accessed | tf_op | source)
XLA Modules:
  0.0 220.8 jit_solution(9000822973849814081)
XLA Ops:
  10.0 3.0 %collective-permute-start.3 = (bf16[256,768]{1,0:T(8,128)(2,1)}, bf16[256,768]{1,0:T(8,128)(2,1)}, u32[]{:S(2)}, u32[]{:S(2)}) collective-permute-start(bf16[256,768]{1,0:T(8,128)(2,1)} %bitcast.16), channel_id=1, source_target_pairs={{0,1},{1,2},{2,3},{3,0},{4,5},{5,6},{6,7},{7,4},{8,9},{9,10},{10,1... | collective-permute-start | bytes 1179656 | tf_op jit(solution)/shard_map/ppermute | solution.py:154
  13.9 2.6 %collective-permute-start.4 = (bf16[256,768]{1,0:T(8,128)(2,1)}, bf16[256,768]{1,0:T(8,128)(2,1)}, u32[]{:S(2)}, u32[]{:S(2)}) collective-permute-start(bf16[256,768]{1,0:T(8,128)(2,1)} %bitcast.18), channel_id=1, source_target_pairs={{0,2},{1,3},{2,0},{3,1},{4,6},{5,7},{6,4},{7,5},{8,10},{9,11},{10,... | collective-permute-start | bytes 1179656 | tf_op jit(solution)/shard_map/ppermute | solution.py:154
  20.1 3.7 %all-to-all-start.1 = ((bf16[256,4,768]{2,0,1:T(8,128)(2,1)}), bf16[256,4,768]{2,0,1:T(8,128)(2,1)S(1)}, u32[]{:S(2)}, u32[]{:S(2)}) async-start(bf16[256,4,768]{2,0,1:T(8,128)(2,1)} %bitcast.61), calls=%async_computation.1 | async-start | bytes 3145728 | tf_op jit(solution)/shard_map/all_to_all | solution.py:162
  26.6 3.3 %reshape.152 = bf16[256,4,768]{2,1,0:T(4,128)(2,1)S(1)} reshape(bf16[256,3072]{1,0:T(8,128)(2,1)} %param.6) | data formatting | bytes 3145728 | tf_op jit(solution)/shard_map/reshape | solution.py:169
  32.5 9.8 %collective-permute-done.4 = bf16[256,768]{1,0:T(8,128)(2,1)} collective-permute-done((bf16[256,768]{1,0:T(8,128)(2,1)}, bf16[256,768]{1,0:T(8,128)(2,1)}, u32[]{:S(2)}, u32[]{:S(2)}) %collective-permute-start.4) | collective-permute-done | bytes 393248 | tf_op jit(solution)/shard_map/ppermute | solution.py:154
  42.4 2.6 %pad_maximum_fusion = bf16[4,256,768]{2,1,0:T(8,128)(2,1)} fusion(bf16[1,256,768]{2,1,0:T(8,128)(2,1)} %bitcast.21, bf16[1,256,768]{2,1,0:T(8,128)(2,1)} %bitcast.19, bf16[1,256,768]{2,1,0:T(8,128)(2,1)} %bitcast.17, bf16[1,256,768]{2,1,0:T(8,128)(2,1)S(1)} %bitcast.77), kind=kLoop, calls=%fused_computation.6 | loop fusion | flops 2359296 | bytes 3145728 | tf_op jit(solution)/shard_map/stack | solution.py:156
  48.4 3.6 %convert_reduce_fusion = f32[256,768]{1,0:T(8,128)S(1)} fusion(bf16[256,4,768]{2,1,0:T(4,128)(2,1)} %gather.20, pred[256]{0:T(512)(128)(4,1)S(1)} %broadcast_in_dim.76), kind=kLoop, calls=%fused_computation.4 | loop fusion | flops 2162688 | bytes 2359552 | tf_op jit(solution)/shard_map/reduce_sum | solution.py:20
  54.2 3.2 %gather_fusion.3 = bf16[8,128,768]{2,1,0:T(8,128)(2,1)} fusion(bf16[8,128,768]{2,1,0:T(8,128)(2,1)} %broadcast_select_fusion.2, s32[1024]{0:T(1024)S(1)} %pad_clamp_fusion.1), kind=kCustom, calls=%fused_computation.1.clone | custom fusion | bytes 3145760 | tf_op jit(solution)/shard_map/jit(_take)/gather | solution.py:197
  57.4 26.0 %all-to-all-done.1 = bf16[256,4,768]{2,0,1:T(8,128)(2,1)S(1)} async-done(((bf16[256,4,768]{2,0,1:T(8,128)(2,1)}), bf16[256,4,768]{2,0,1:T(8,128)(2,1)S(1)}, u32[]{:S(2)}, u32[]{:S(2)}) %all-to-all-start.1) | async-done | bytes 1572896 | tf_op jit(solution)/shard_map/all_to_all | solution.py:162
  83.4 4.2 %all-to-all-start = ((bf16[256,4,384]{2,0,1:T(8,128)(2,1)}), bf16[256,4,384]{2,0,1:T(8,128)(2,1)}, u32[]{:S(2)}, u32[]{:S(2)}) async-start(bf16[256,4,384]{2,0,1:T(8,128)(2,1)} %copy.58), calls=%async_computation | async-start | bytes 1572864 | tf_op jit(solution)/shard_map/all_to_all | solution.py:175
  89.5 3.4 %broadcast_select_fusion = (bf16[8,128,768]{2,1,0:T(8,128)(2,1)S(1)}, bf16[8,128,768]{2,1,0:T(8,128)(2,1)}) fusion(bf16[8,128,768]{2,1,0:T(8,128)(2,1)} %gather_fusion.3, pred[8]{0:T(512)(128)(4,1)S(1)} %compare_and_fusion, bf16[8,128,768]{2,1,0:T(8,128)(2,1)} %gather_fusion.2), kind=kLoop, calls=%fused_computation.10 | loop fusion | flops 1572864 | bytes 6291464 | tf_op jit(solution)/shard_map/jit(_take)/select_n | solution.py:197
  104.5 4.9 %reshape.168 = f32[256,4,768]{2,1,0:T(4,128)} reshape(f32[4,256,768]{2,1,0:T(8,128)} %bitcast_convert_fusion) | data formatting | bytes 6291456 | tf_op jit(solution)/shard_map/convert_element_type | solution.py:19
  109.3 3.8 %reduce_sum.28 = f32[256,768]{1,0:T(8,128)S(1)} reduce(f32[256,4,768]{2,1,0:T(4,128)} %reshape.168, f32[]{:T(128)} %constant.170.clone.1), dimensions={1}, to_apply=%region_4.6 | reduce | flops 589824 | bytes 3932164 | tf_op jit(solution)/shard_map/reduce_sum | solution.py:20
  116.0 9.4 %collective-permute-done.1 = bf16[2,128,768]{2,1,0:T(8,128)(2,1)} collective-permute-done((bf16[2,128,768]{2,1,0:T(8,128)(2,1)}, bf16[2,128,768]{2,1,0:T(8,128)(2,1)}, u32[]{:S(2)}, u32[]{:S(2)}) %collective-permute-start.1) | collective-permute-done | bytes 393248 | tf_op jit(solution)/shard_map/ppermute | solution.py:205
  125.5 12.9 %collective-permute-done.2 = bf16[2,128,768]{2,1,0:T(8,128)(2,1)} collective-permute-done((bf16[2,128,768]{2,1,0:T(8,128)(2,1)}, bf16[2,128,768]{2,1,0:T(8,128)(2,1)}, u32[]{:S(2)}, u32[]{:S(2)}) %collective-permute-start.2) | collective-permute-done | bytes 393248 | tf_op jit(solution)/shard_map/ppermute | solution.py:205
  138.3 5.0 %all-to-all-start.2 = ((bf16[256,4,384]{0,2,1:T(8,128)(2,1)}), bf16[256,4,384]{0,2,1:T(8,128)(2,1)S(1)}, u32[]{:S(2)}, u32[]{:S(2)}) async-start(bf16[256,4,384]{0,2,1:T(8,128)(2,1)} %bitcast.31), calls=%async_computation.2 | async-start | bytes 1572864 | tf_op jit(solution)/shard_map/all_to_all | solution.py:175
  147.9 15.3 %shard_map.62 = bf16[1024,384]{1,0:T(8,128)(2,1)} custom-call(s32[96]{0:T(128)} %reshape.154.tbl_ref, bf16[1024,384]{1,0:T(8,128)(2,1)} %bitcast.1.q_ref, bf16[1024,768]{1,0:T(8,128)(2,1)} %bitcast.65, bf16[1024,768]{1,0:T(8,128)(2,1)} %bitcast_select_fusion.refs_1_, bf16[256,768]{1,0:T(8,128)(2,1)} %bitcast.9.refs_2_, bf16[256,768]{1,0:T(8,128)(2,1)} %bitcast.11.refs_3_, ...), custom_call_target="tpu_custom_call" | custom-call | flops 2415919104 | bytes 4325376 | tf_op jit(solution)/shard_map/pallas_call | solution.py:86
  164.7 3.7 %all-to-all-start.3 = ((bf16[4,256,384]{2,1,0:T(8,128)(2,1)}), bf16[4,256,384]{2,1,0:T(8,128)(2,1)S(1)}, u32[]{:S(2)}, u32[]{:S(2)}) async-start(bf16[4,256,384]{2,1,0:T(8,128)(2,1)} %bitcast.79), calls=%async_computation.3 | async-start | bytes 1572864 | tf_op jit(solution)/shard_map/all_to_all | solution.py:237
  169.6 15.4 %shard_map.59 = bf16[1024,384]{1,0:T(8,128)(2,1)} custom-call(s32[96]{0:T(128)} %reshape.154.tbl_ref, bf16[1024,384]{1,0:T(8,128)(2,1)} %bitcast.73, bf16[1024,768]{1,0:T(8,128)(2,1)} %bitcast.66, bf16[1024,768]{1,0:T(8,128)(2,1)} %bitcast_select_fusion.refs_1_, bf16[256,768]{1,0:T(8,128)(2,1)} %bitcast.9.refs_2_, bf16[256,768]{1,0:T(8,128)(2,1)} %bitcast.11.refs_3_, ...), custom_call_target="tpu_custom_call" | custom-call | flops 2415919104 | bytes 4325376 | tf_op jit(solution)/shard_map/pallas_call | solution.py:86
  185.0 4.2 %all-to-all-done.3 = bf16[4,256,384]{2,1,0:T(8,128)(2,1)S(1)} async-done(((bf16[4,256,384]{2,1,0:T(8,128)(2,1)}), bf16[4,256,384]{2,1,0:T(8,128)(2,1)S(1)}, u32[]{:S(2)}, u32[]{:S(2)}) %all-to-all-start.3) | async-done | bytes 786464 | tf_op jit(solution)/shard_map/all_to_all | solution.py:237
  189.1 3.5 %all-to-all-start.4 = ((bf16[4,256,384]{2,1,0:T(8,128)(2,1)}), bf16[4,256,384]{2,1,0:T(8,128)(2,1)S(1)}, u32[]{:S(2)}, u32[]{:S(2)}) async-start(bf16[4,256,384]{2,1,0:T(8,128)(2,1)} %bitcast.78), calls=%async_computation.4 | async-start | bytes 1572864 | tf_op jit(solution)/shard_map/all_to_all | solution.py:237
  192.6 6.5 %shard_map.60 = bf16[256,384]{1,0:T(8,128)(2,1)} custom-call(bf16[1024,384]{1,0:T(8,128)(2,1)} %bitcast.1.q_ref, bf16[1024,768]{1,0:T(8,128)(2,1)} %all-gather.3.cloned.1.call-done.k_ref, bf16[1024,768]{1,0:T(8,128)(2,1)} %all-gather.5.cloned.1.call-done.v_ref), custom_call_target="tpu_custom_call" | custom-call | flops 503316480 | bytes 2555904 | tf_op jit(solution)/shard_map/pallas_call | solution.py:131
  199.2 6.6 %shard_map.61 = bf16[256,384]{1,0:T(8,128)(2,1)} custom-call(bf16[1024,384]{1,0:T(8,128)(2,1)} %bitcast.74, bf16[1024,768]{1,0:T(8,128)(2,1)} %all-gather.3.cloned.1.call-done.k_ref, bf16[1024,768]{1,0:T(8,128)(2,1)} %all-gather.5.cloned.1.call-done.v_ref), custom_call_target="tpu_custom_call" | custom-call | flops 503316480 | bytes 2555904 | tf_op jit(solution)/shard_map/pallas_call | solution.py:131
  207.5 5.1 %all-to-all-done.4 = bf16[4,256,384]{2,1,0:T(8,128)(2,1)S(1)} async-done(((bf16[4,256,384]{2,1,0:T(8,128)(2,1)}), bf16[4,256,384]{2,1,0:T(8,128)(2,1)S(1)}, u32[]{:S(2)}, u32[]{:S(2)}) %all-to-all-start.4) | async-done | bytes 786464 | tf_op jit(solution)/shard_map/all_to_all | solution.py:237
  (97 shorter events, 44.8 us)
Async XLA Ops:
  9.1 9.8 %copy-start.1 = (bf16[256,3072]{1,0:T(8,128)(2,1)S(1)}, bf16[256,3072]{1,0:T(8,128)(2,1)}, u32[]{:S(2)}) copy-start(bf16[256,3072]{1,0:T(8,128)(2,1)} %param.7) | copy-start | bytes 4718596
  10.0 22.5 %collective-permute-start.3 = (bf16[256,768]{1,0:T(8,128)(2,1)}, bf16[256,768]{1,0:T(8,128)(2,1)}, u32[]{:S(2)}, u32[]{:S(2)}) collective-permute-start(bf16[256,768]{1,0:T(8,128)(2,1)} %bitcast.16), channel_id=1, source_target_pairs={{0,1},{1,2},{2,3},{3,0},{4,5},{5,6},{6,7},{7,4},{8,9},{9,10},{10,1... | collective-permute-start | bytes 1179656 | tf_op jit(solution)/shard_map/ppermute | solution.py:154
  13.9 28.4 %collective-permute-start.4 = (bf16[256,768]{1,0:T(8,128)(2,1)}, bf16[256,768]{1,0:T(8,128)(2,1)}, u32[]{:S(2)}, u32[]{:S(2)}) collective-permute-start(bf16[256,768]{1,0:T(8,128)(2,1)} %bitcast.18), channel_id=1, source_target_pairs={{0,2},{1,3},{2,0},{3,1},{4,6},{5,7},{6,4},{7,5},{8,10},{9,11},{10,... | collective-permute-start | bytes 1179656 | tf_op jit(solution)/shard_map/ppermute | solution.py:154
  17.5 24.9 %collective-permute-start.5 = (bf16[256,768]{1,0:T(8,128)(2,1)}, bf16[256,768]{1,0:T(8,128)(2,1)}, u32[]{:S(2)}, u32[]{:S(2)}) collective-permute-start(bf16[256,768]{1,0:T(8,128)(2,1)} %bitcast.20), channel_id=1, source_target_pairs={{0,3},{1,0},{2,1},{3,2},{4,7},{5,4},{6,5},{7,6},{8,11},{9,8},{10,9... | collective-permute-start | bytes 1179656 | tf_op jit(solution)/shard_map/ppermute | solution.py:154
  20.1 3.8 %copy-start.3 = (s32[32,12]{0,1:T(8,128)S(1)}, s32[32,12]{0,1:T(8,128)}, u32[]{:S(2)}) copy-start(s32[32,12]{0,1:T(8,128)} %param.9) | copy-start | bytes 4612
  20.1 63.4 %all-to-all-start.1 = ((bf16[256,4,768]{2,0,1:T(8,128)(2,1)}), bf16[256,4,768]{2,0,1:T(8,128)(2,1)S(1)}, u32[]{:S(2)}, u32[]{:S(2)}) async-start(bf16[256,4,768]{2,0,1:T(8,128)(2,1)} %bitcast.61), calls=%async_computation.1 | async-start | bytes 3145728 | tf_op jit(solution)/shard_map/all_to_all | solution.py:162
  23.8 161.2 %all-gather.5.cloned.1.call-start = ((), (), s32[]{:S(2)}) async-start(), calls=%async_computation.6 | async-start | bytes 1966080 | tf_op jit(solution)/shard_map/all_gather | solution.py:178
  24.9 7.5 %copy-start.7 = (pred[4]{0:T(512)(128)(4,1)}, pred[4]{0:T(512)(128)(4,1)S(1)}, u32[]{:S(2)}) copy-start(pred[4]{0:T(512)(128)(4,1)S(1)} %compare_and_fusion.1) | copy-start | bytes 16
  48.4 4.4 %copy-start.5 = (s32[8]{0:T(128)S(1)}, s32[8]{0:T(128)}, u32[]{:S(2)}) copy-start(s32[8]{0:T(128)} %reshape.157) | copy-start | bytes 100
  48.4 4.5 %copy-start.6 = (pred[8]{0:T(512)(128)(4,1)S(1)}, pred[8]{0:T(512)(128)(4,1)}, u32[]{:S(2)}) copy-start(pred[8]{0:T(512)(128)(4,1)} %broadcast_in_dim.68) | copy-start | bytes 28
  83.4 19.1 %copy-start = (bf16[256,4,768]{2,0,1:T(8,128)(2,1)}, bf16[256,4,768]{2,0,1:T(8,128)(2,1)S(1)}, u32[]{:S(2)}) copy-start(bf16[256,4,768]{2,0,1:T(8,128)(2,1)S(1)} %all-to-all-done.1) | copy-start | bytes 4718596
  83.4 54.9 %all-to-all-start = ((bf16[256,4,384]{2,0,1:T(8,128)(2,1)}), bf16[256,4,384]{2,0,1:T(8,128)(2,1)}, u32[]{:S(2)}, u32[]{:S(2)}) async-start(bf16[256,4,384]{2,0,1:T(8,128)(2,1)} %copy.58), calls=%async_computation | async-start | bytes 1572864 | tf_op jit(solution)/shard_map/all_to_all | solution.py:175
  87.7 97.3 %all-gather.3.cloned.1.call-start = ((), (), s32[]{:S(2)}) async-start(), calls=%async_computation.5 | async-start | bytes 1966080 | tf_op jit(solution)/shard_map/all_gather | solution.py:177
  93.9 8.7 %collective-permute-start.6 = (bf16[2,128,768]{2,1,0:T(8,128)(2,1)}, bf16[2,128,768]{2,1,0:T(8,128)(2,1)}, u32[]{:S(2)}, u32[]{:S(2)}) collective-permute-start(bf16[2,128,768]{2,1,0:T(8,128)(2,1)} %get-tuple-element.27), channel_id=1, source_target_pairs={{0,4},{4,8},{8,12},{12,0},{1,5},{5,9},{9,13},{13,1},{2,6},{6,10},{... | collective-permute-start | bytes 1179656 | tf_op jit(solution)/shard_map/ppermute | solution.py:205
  96.2 17.7 %collective-permute-start.7 = (bf16[2,128,768]{2,1,0:T(8,128)(2,1)}, bf16[2,128,768]{2,1,0:T(8,128)(2,1)}, u32[]{:S(2)}, u32[]{:S(2)}) collective-permute-start(bf16[2,128,768]{2,1,0:T(8,128)(2,1)} %get-tuple-element.26), channel_id=1, source_target_pairs={{0,8},{4,12},{8,0},{12,4},{1,9},{5,13},{9,1},{13,5},{2,10},{6,14},... | collective-permute-start | bytes 1179656 | tf_op jit(solution)/shard_map/ppermute | solution.py:205
  97.8 18.2 %collective-permute-start.8 = (bf16[2,128,768]{2,1,0:T(8,128)(2,1)S(1)}, bf16[2,128,768]{2,1,0:T(8,128)(2,1)}, u32[]{:S(2)}, u32[]{:S(2)}) collective-permute-start(bf16[2,128,768]{2,1,0:T(8,128)(2,1)S(1)} %get-tuple-element.25), channel_id=1, source_target_pairs={{0,12},{4,0},{8,4},{12,8},{1,13},{5,1},{9,5},{13,9},{2,14},{6,2},{... | collective-permute-start | bytes 1179656 | tf_op jit(solution)/shard_map/ppermute | solution.py:205
  101.5 24.0 %collective-permute-start.1 = (bf16[2,128,768]{2,1,0:T(8,128)(2,1)}, bf16[2,128,768]{2,1,0:T(8,128)(2,1)}, u32[]{:S(2)}, u32[]{:S(2)}) collective-permute-start(bf16[2,128,768]{2,1,0:T(8,128)(2,1)} %get-tuple-element.33), channel_id=1, source_target_pairs={{0,8},{4,12},{8,0},{12,4},{1,9},{5,13},{9,1},{13,5},{2,10},{6,14},... | collective-permute-start | bytes 1179656 | tf_op jit(solution)/shard_map/ppermute | solution.py:205
  102.0 36.3 %collective-permute-start.2 = (bf16[2,128,768]{2,1,0:T(8,128)(2,1)}, bf16[2,128,768]{2,1,0:T(8,128)(2,1)}, u32[]{:S(2)}, u32[]{:S(2)}) collective-permute-start(bf16[2,128,768]{2,1,0:T(8,128)(2,1)} %get-tuple-element.32), channel_id=1, source_target_pairs={{0,12},{4,0},{8,4},{12,8},{1,13},{5,1},{9,5},{13,9},{2,14},{6,2},{... | collective-permute-start | bytes 1179656 | tf_op jit(solution)/shard_map/ppermute | solution.py:205
  102.6 35.8 %collective-permute-start = (bf16[2,128,768]{2,1,0:T(8,128)(2,1)}, bf16[2,128,768]{2,1,0:T(8,128)(2,1)}, u32[]{:S(2)}, u32[]{:S(2)}) collective-permute-start(bf16[2,128,768]{2,1,0:T(8,128)(2,1)} %get-tuple-element.34), channel_id=1, source_target_pairs={{0,4},{4,8},{8,12},{12,0},{1,5},{5,9},{9,13},{13,1},{2,6},{6,10},{... | collective-permute-start | bytes 1179656 | tf_op jit(solution)/shard_map/ppermute | solution.py:205
  113.1 30.3 %copy-start.8 = (pred[4]{0:T(512)(128)(4,1)S(1)}, pred[4]{0:T(512)(128)(4,1)}, u32[]{:S(2)}) copy-start(pred[4]{0:T(512)(128)(4,1)} %copy-done.7) | copy-start | bytes 16
  138.3 26.4 %all-to-all-start.2 = ((bf16[256,4,384]{0,2,1:T(8,128)(2,1)}), bf16[256,4,384]{0,2,1:T(8,128)(2,1)S(1)}, u32[]{:S(2)}, u32[]{:S(2)}) async-start(bf16[256,4,384]{0,2,1:T(8,128)(2,1)} %bitcast.31), calls=%async_computation.2 | async-start | bytes 1572864 | tf_op jit(solution)/shard_map/all_to_all | solution.py:175
  164.7 24.4 %all-to-all-start.3 = ((bf16[4,256,384]{2,1,0:T(8,128)(2,1)}), bf16[4,256,384]{2,1,0:T(8,128)(2,1)S(1)}, u32[]{:S(2)}, u32[]{:S(2)}) async-start(bf16[4,256,384]{2,1,0:T(8,128)(2,1)} %bitcast.79), calls=%async_computation.3 | async-start | bytes 1572864 | tf_op jit(solution)/shard_map/all_to_all | solution.py:237
  189.1 23.4 %all-to-all-start.4 = ((bf16[4,256,384]{2,1,0:T(8,128)(2,1)}), bf16[4,256,384]{2,1,0:T(8,128)(2,1)S(1)}, u32[]{:S(2)}, u32[]{:S(2)}) async-start(bf16[4,256,384]{2,1,0:T(8,128)(2,1)} %bitcast.78), calls=%async_computation.4 | async-start | bytes 1572864 | tf_op jit(solution)/shard_map/all_to_all | solution.py:237
  199.2 6.6 %copy-start.2 = (bf16[256,384]{1,0:T(8,128)(2,1)S(1)}, bf16[256,384]{1,0:T(8,128)(2,1)}, u32[]{:S(2)}) copy-start(bf16[256,384]{1,0:T(8,128)(2,1)} %shard_map.60) | copy-start | bytes 589828
  (1 other events, 1.2 us)
Sparse Core Ops, SparseCore 0:
  52.9 44.3 all-gather.4
  114.1 26.5 all-gather.2

commit v11 on v10

--- a/solution.py
+++ b/solution.py
@@ -172,7 +172,7 @@
     ]
 
     def query_a2a(piece):
-        return lax.all_to_all(piece, "head", split_axis=1, concat_axis=0, tiled=True)
+        return head_permutes(piece)
 
     draft_keys = lax.all_gather(pool_tokens(key_rows), "seq", axis=0, tiled=True)
     draft_values = lax.all_gather(pool_tokens(value_rows), "seq", axis=0, tiled=True)
@@ -210,11 +210,7 @@
 
     remote_keys = exchange(key_rows)
     remote_values = exchange(value_rows)
-    query_parts = [query_a2a(query_slices[0])]
-    later, remote_keys, remote_values = lax.optimization_barrier(
-        (query_slices[1:], remote_keys, remote_values)
-    )
-    query_parts += [query_a2a(piece) for piece in later]
+    query_parts = [query_a2a(piece) for piece in query_slices]
 
     own_lists = lax.dynamic_slice_in_dim(block_lists, seq_index * per_dev, per_dev, 0)
     owners = own_lists // per_dev

time: 222 us -> 238 us (1.072)
  starting transfers between devices: 30.7 us -> 54.6 us
  waiting for transfers between devices: 71.5 us -> 52.5 us
  other arithmetic: 22.6 us -> 31.2 us
  local copies, waits for them, and re-layouts: 37.8 us -> 40.6 us
    ppermute x3 -> x9, starting transfers between devices: 6.96 us -> 40.4 us  [head_permutes(): lax.ppermute(piece, 'head', [(i, (i + shift) % count) for i in range(coun...]
    all_to_all x1, waiting for transfers between devices: 26 us -> 10.2 us  [on_device(): lax.all_to_all(key_in, 'head', split_axis=1, concat_axis=0, tiled=True)]
    all_to_all x2 -> x0, starting transfers between devices: 9.22 us -> none  [query_a2a(): lax.all_to_all(piece, 'head', split_axis=1, concat_axis=0, tiled=True)]
    ppermute x3 -> x9, waiting for transfers between devices: 9.81 us -> 4.38 us  [head_permutes(): lax.ppermute(piece, 'head', [(i, (i + shift) % count) for i in range(coun...]
    dynamic_slice x3 -> x9, local copies, waits for them, and re-layouts: 2.77 us -> 7.7 us  [head_permutes(): lax.dynamic_index_in_dim(chunks, (me + shift) % count, axis=1, keepdims=F...]
    gather x2 -> x4, local copies, waits for them, and re-layouts: 3.42 us -> 7.73 us  [head_permutes(): jnp.take(stacked, order, axis=0).reshape(count * rows, total // count)]
    another operation x1 -> x3, other arithmetic: 2.6 us -> 6.13 us  [head_permutes(): stacked = jnp.stack(by_shift, axis=0)]
    reshape x1 -> x0, local copies, waits for them, and re-layouts: 3.27 us -> none  [on_device(): grouped_q = query_in.reshape(query_in.shape[0], head_count, width)]
  transfers between devices with their start and end apart: 16 -> 20, of which waited for: 9 -> 10; matrix products, arithmetic and copies ran while one was open for 25% -> 28% of each run, Pallas kernels for 20% -> 19%
where the time goes in v11:
time: 238 us; the launch traced here: 237 us
  starting transfers between devices  54.6 us (23%)
  waiting for transfers between devices  52.5 us (22%)
  Pallas kernels  43.9 us (18%)
  local copies, waits for them, and re-layouts  40.6 us (17%)
  other arithmetic  31.2 us (13%)
  between operations  14.5 us (6%)
    ppermute x9, starting transfers between devices, head_permutes(): lax.ppermute(piece, 'head', [(i, (i + shift) % count) for i in range(coun...  40.4 us
    pallas_call x2, Pallas kernels, sparse_attention(): pl.pallas_call(sparse_kernel, out_shape=jax.ShapeDtypeStruct((rows, heads...  30.8 us
    ppermute x6, waiting for transfers between devices, exchange(): lax.ppermute(parcel, 'seq', [(i, (i + shift) % seq_count) for i in range(...  26 us
    pallas_call x2, Pallas kernels, draft_attention(): pl.pallas_call(draft_kernel, out_shape=jax.ShapeDtypeStruct((rows, width)...  13.1 us
    all_to_all x2, waiting for transfers between devices, on_device(): lax.all_to_all(rows_part, 'head', split_axis=0, concat_axis=1, tiled=True)  11.8 us
    all_to_all x1, waiting for transfers between devices, on_device(): lax.all_to_all(key_in, 'head', split_axis=1, concat_axis=0, tiled=True)  10.2 us
    reduce_sum x2, other arithmetic, pool_tokens(): return (grouped.sum(axis=1) * POOL ** (-0.5)).astype(jnp.bfloat16)  8.22 us
    gather x4, local copies, waits for them, and re-layouts, head_permutes(): jnp.take(stacked, order, axis=0).reshape(count * rows, total // count)  7.73 us
  transfers between devices with their start and end apart: 20, of which 10 were waited for; matrix products, arithmetic and copies ran while one was open for 28% of the time, Pallas kernels for 19%

profile of v11, /device:TPU:0, one launch (start us, length us, event | category | flops | bytes accessed | tf_op | source)
XLA Modules:
  0.0 237.3 jit_solution(5743072538742058424)
XLA Ops:
  10.0 3.0 %collective-permute-start.6 = (bf16[256,768]{1,0:T(8,128)(2,1)}, bf16[256,768]{1,0:T(8,128)(2,1)}, u32[]{:S(2)}, u32[]{:S(2)}) collective-permute-start(bf16[256,768]{1,0:T(8,128)(2,1)} %bitcast.22), channel_id=1, source_target_pairs={{0,1},{1,2},{2,3},{3,0},{4,5},{5,6},{6,7},{7,4},{8,9},{9,10},{10,1... | collective-permute-start | bytes 1179656 | tf_op jit(solution)/shard_map/ppermute | solution.py:154
  20.0 3.6 %all-to-all-start = ((bf16[256,4,768]{2,0,1:T(8,128)(2,1)}), bf16[256,4,768]{2,0,1:T(8,128)(2,1)S(1)}, u32[]{:S(2)}, u32[]{:S(2)}) async-start(bf16[256,4,768]{2,0,1:T(8,128)(2,1)} %bitcast.71), calls=%async_computation | async-start | bytes 3145728 | tf_op jit(solution)/shard_map/all_to_all | solution.py:162
  42.3 23.8 %collective-permute-start = (bf16[256,384]{1,0:T(8,128)(2,1)}, bf16[256,384]{1,0:T(8,128)(2,1)}, u32[]{:S(2)}, u32[]{:S(2)}) collective-permute-start(bf16[256,384]{1,0:T(8,128)(2,1)} %bitcast.2), channel_id=1, source_target_pairs={{0,1},{1,2},{2,3},{3,0},{4,5},{5,6},{6,7},{7,4},{8,9},{9,10},{10,1... | collective-permute-start | bytes 589832 | tf_op jit(solution)/shard_map/ppermute | solution.py:154
  66.1 3.9 %collective-permute-start.1 = (bf16[256,384]{1,0:T(8,128)(2,1)}, bf16[256,384]{1,0:T(8,128)(2,1)}, u32[]{:S(2)}, u32[]{:S(2)}) collective-permute-start(bf16[256,384]{1,0:T(8,128)(2,1)} %bitcast.4), channel_id=1, source_target_pairs={{0,2},{1,3},{2,0},{3,1},{4,6},{5,7},{6,4},{7,5},{8,10},{9,11},{10,... | collective-permute-start | bytes 589832 | tf_op jit(solution)/shard_map/ppermute | solution.py:154
  76.0 3.6 %convert_reduce_fusion = f32[256,768]{1,0:T(8,128)S(1)} fusion(bf16[256,4,768]{2,1,0:T(4,128)(2,1)} %gather.23, pred[256]{0:T(512)(128)(4,1)S(1)} %broadcast_in_dim.85), kind=kLoop, calls=%fused_computation.6 | loop fusion | flops 2162688 | bytes 2359552 | tf_op jit(solution)/shard_map/reduce_sum | solution.py:20
  86.9 3.3 %gather_fusion.5 = bf16[8,128,768]{2,1,0:T(8,128)(2,1)} fusion(bf16[8,128,768]{2,1,0:T(8,128)(2,1)} %broadcast_select_fusion.2, s32[1024]{0:T(1024)S(1)} %pad_clamp_fusion), kind=kCustom, calls=%fused_computation.3.clone | custom fusion | bytes 3145760 | tf_op jit(solution)/shard_map/jit(_take)/gather | solution.py:197
  90.2 10.2 %all-to-all-done = bf16[256,4,768]{2,0,1:T(8,128)(2,1)S(1)} async-done(((bf16[256,4,768]{2,0,1:T(8,128)(2,1)}), bf16[256,4,768]{2,0,1:T(8,128)(2,1)S(1)}, u32[]{:S(2)}, u32[]{:S(2)}) %all-to-all-start) | async-done | bytes 1572896 | tf_op jit(solution)/shard_map/all_to_all | solution.py:162
  104.1 4.8 %reshape.171 = f32[256,4,768]{2,1,0:T(4,128)} reshape(f32[4,256,768]{2,1,0:T(8,128)} %bitcast_convert_fusion) | data formatting | bytes 6291456 | tf_op jit(solution)/shard_map/convert_element_type | solution.py:19
  109.0 4.6 %reduce_sum.28 = f32[256,768]{1,0:T(8,128)} reduce(f32[256,4,768]{2,1,0:T(4,128)} %reshape.171, f32[]{:T(128)} %constant.216.clone.1), dimensions={1}, to_apply=%region_4.7 | reduce | flops 589824 | bytes 3932164 | tf_op jit(solution)/shard_map/reduce_sum | solution.py:20
  115.7 2.9 %broadcast_select_fusion = (bf16[8,128,768]{2,1,0:T(8,128)(2,1)}, bf16[8,128,768]{2,1,0:T(8,128)(2,1)S(1)}) fusion(bf16[8,128,768]{2,1,0:T(8,128)(2,1)S(1)} %copy-done.1, pred[8]{0:T(512)(128)(4,1)S(1)} %compare_and_fusion, bf16[8,128,768]{2,1,0:T(8,128)(2,1)} %gather_fusion.4), kind=kLoop, calls=%fused_computation.12 | loop fusion | flops 1572864 | bytes 6291464 | tf_op jit(solution)/shard_map/jit(_take)/select_n | solution.py:197
  122.6 3.0 %collective-permute-done.2 = bf16[256,384]{1,0:T(8,128)(2,1)S(1)} collective-permute-done((bf16[256,384]{1,0:T(8,128)(2,1)}, bf16[256,384]{1,0:T(8,128)(2,1)S(1)}, u32[]{:S(2)}, u32[]{:S(2)}) %collective-permute-start.2) | collective-permute-done | bytes 196640 | tf_op jit(solution)/shard_map/ppermute | solution.py:154
  128.5 2.7 %gather_fusion.2 = bf16[4,256,384]{2,1,0:T(8,128)(2,1)} fusion(bf16[4,256,384]{2,1,0:T(8,128)(2,1)} %pad_maximum_fusion.1, s32[1024]{0:T(1024)S(1)} %pad_clamp_fusion.2), kind=kCustom, calls=%fused_computation.clone | custom fusion | bytes 1572880 | tf_op jit(solution)/shard_map/jit(_take)/gather | solution.py:158
  137.7 6.6 %collective-permute-done.10 = bf16[2,128,768]{2,1,0:T(8,128)(2,1)S(1)} collective-permute-done((bf16[2,128,768]{2,1,0:T(8,128)(2,1)}, bf16[2,128,768]{2,1,0:T(8,128)(2,1)S(1)}, u32[]{:S(2)}, u32[]{:S(2)}) %collective-permute-start.10) | collective-permute-done | bytes 393248 | tf_op jit(solution)/shard_map/ppermute | solution.py:205
  144.3 6.6 %collective-permute-done.11 = bf16[2,128,768]{2,1,0:T(8,128)(2,1)S(1)} collective-permute-done((bf16[2,128,768]{2,1,0:T(8,128)(2,1)S(1)}, bf16[2,128,768]{2,1,0:T(8,128)(2,1)S(1)}, u32[]{:S(2)}, u32[]{:S(2)}) %collective-permute-start.11) | collective-permute-done | bytes 393248 | tf_op jit(solution)/shard_map/ppermute | solution.py:205
  151.9 8.8 %collective-permute-done.13 = bf16[2,128,768]{2,1,0:T(8,128)(2,1)S(1)} collective-permute-done((bf16[2,128,768]{2,1,0:T(8,128)(2,1)S(1)}, bf16[2,128,768]{2,1,0:T(8,128)(2,1)S(1)}, u32[]{:S(2)}, u32[]{:S(2)}) %collective-permute-start.13) | collective-permute-done | bytes 393248 | tf_op jit(solution)/shard_map/ppermute | solution.py:205
  160.8 3.0 %collective-permute-done.14 = bf16[2,128,768]{2,1,0:T(8,128)(2,1)S(1)} collective-permute-done((bf16[2,128,768]{2,1,0:T(8,128)(2,1)S(1)}, bf16[2,128,768]{2,1,0:T(8,128)(2,1)S(1)}, u32[]{:S(2)}, u32[]{:S(2)}) %collective-permute-start.14) | collective-permute-done | bytes 393248 | tf_op jit(solution)/shard_map/ppermute | solution.py:205
  164.5 15.4 %shard_map.62 = bf16[1024,384]{1,0:T(8,128)(2,1)} custom-call(s32[96]{0:T(128)} %reshape.157.tbl_ref, bf16[1024,384]{1,0:T(8,128)(2,1)} %bitcast.85, bf16[1024,768]{1,0:T(8,128)(2,1)} %bitcast.75, bf16[1024,768]{1,0:T(8,128)(2,1)} %bitcast_select_fusion.refs_1_, bf16[256,768]{1,0:T(8,128)(2,1)} %bitcast.34.refs_2_, bf16[256,768]{1,0:T(8,128)(2,1)} %bitcast.98, ...), custom_call_target="tpu_custom_call" | custom-call | flops 2415919104 | bytes 4325376 | tf_op jit(solution)/shard_map/pallas_call | solution.py:86
  179.9 3.5 %all-to-all-start.1 = ((bf16[4,256,384]{2,1,0:T(8,128)(2,1)}), bf16[4,256,384]{2,1,0:T(8,128)(2,1)S(1)}, u32[]{:S(2)}, u32[]{:S(2)}) async-start(bf16[4,256,384]{2,1,0:T(8,128)(2,1)} %bitcast.93), calls=%async_computation.1 | async-start | bytes 1572864 | tf_op jit(solution)/shard_map/all_to_all | solution.py:233
  183.4 15.4 %shard_map.59 = bf16[1024,384]{1,0:T(8,128)(2,1)} custom-call(s32[96]{0:T(128)} %reshape.157.tbl_ref, bf16[1024,384]{1,0:T(8,128)(2,1)} %bitcast.83, bf16[1024,768]{1,0:T(8,128)(2,1)} %bitcast.76, bf16[1024,768]{1,0:T(8,128)(2,1)} %bitcast_select_fusion.refs_1_, bf16[256,768]{1,0:T(8,128)(2,1)} %bitcast.34.refs_2_, bf16[256,768]{1,0:T(8,128)(2,1)} %bitcast.99, ...), custom_call_target="tpu_custom_call" | custom-call | flops 2415919104 | bytes 4325376 | tf_op jit(solution)/shard_map/pallas_call | solution.py:86
  198.8 6.0 %all-to-all-done.1 = bf16[4,256,384]{2,1,0:T(8,128)(2,1)S(1)} async-done(((bf16[4,256,384]{2,1,0:T(8,128)(2,1)}), bf16[4,256,384]{2,1,0:T(8,128)(2,1)S(1)}, u32[]{:S(2)}, u32[]{:S(2)}) %all-to-all-start.1) | async-done | bytes 786464 | tf_op jit(solution)/shard_map/all_to_all | solution.py:233
  204.8 3.5 %all-to-all-start.2 = ((bf16[4,256,384]{2,1,0:T(8,128)(2,1)}), bf16[4,256,384]{2,1,0:T(8,128)(2,1)S(1)}, u32[]{:S(2)}, u32[]{:S(2)}) async-start(bf16[4,256,384]{2,1,0:T(8,128)(2,1)} %bitcast.92), calls=%async_computation.2 | async-start | bytes 1572864 | tf_op jit(solution)/shard_map/all_to_all | solution.py:233
  208.3 6.5 %shard_map.60 = bf16[256,384]{1,0:T(8,128)(2,1)} custom-call(bf16[1024,384]{1,0:T(8,128)(2,1)} %bitcast.86, bf16[1024,768]{1,0:T(8,128)(2,1)} %all-gather.3.cloned.1.call-done.k_ref, bf16[1024,768]{1,0:T(8,128)(2,1)} %all-gather.5.cloned.1.call-done.v_ref), custom_call_target="tpu_custom_call" | custom-call | flops 503316480 | bytes 2555904 | tf_op jit(solution)/shard_map/pallas_call | solution.py:131
  214.9 6.6 %shard_map.61 = bf16[256,384]{1,0:T(8,128)(2,1)} custom-call(bf16[1024,384]{1,0:T(8,128)(2,1)} %bitcast.84, bf16[1024,768]{1,0:T(8,128)(2,1)} %all-gather.3.cloned.1.call-done.k_ref, bf16[1024,768]{1,0:T(8,128)(2,1)} %all-gather.5.cloned.1.call-done.v_ref), custom_call_target="tpu_custom_call" | custom-call | flops 503316480 | bytes 2555904 | tf_op jit(solution)/shard_map/pallas_call | solution.py:131
  223.1 5.8 %all-to-all-done.2 = bf16[4,256,384]{2,1,0:T(8,128)(2,1)S(1)} async-done(((bf16[4,256,384]{2,1,0:T(8,128)(2,1)}), bf16[4,256,384]{2,1,0:T(8,128)(2,1)S(1)}, u32[]{:S(2)}, u32[]{:S(2)}) %all-to-all-start.2) | async-done | bytes 786464 | tf_op jit(solution)/shard_map/all_to_all | solution.py:233
  (140 shorter events, 65.7 us)
Async XLA Ops:
  9.1 9.7 %copy-start.5 = (bf16[256,3072]{1,0:T(8,128)(2,1)S(1)}, bf16[256,3072]{1,0:T(8,128)(2,1)}, u32[]{:S(2)}) copy-start(bf16[256,3072]{1,0:T(8,128)(2,1)} %param.9) | copy-start | bytes 4718596
  10.0 29.4 %collective-permute-start.6 = (bf16[256,768]{1,0:T(8,128)(2,1)}, bf16[256,768]{1,0:T(8,128)(2,1)}, u32[]{:S(2)}, u32[]{:S(2)}) collective-permute-start(bf16[256,768]{1,0:T(8,128)(2,1)} %bitcast.22), channel_id=1, source_target_pairs={{0,1},{1,2},{2,3},{3,0},{4,5},{5,6},{6,7},{7,4},{8,9},{9,10},{10,1... | collective-permute-start | bytes 1179656 | tf_op jit(solution)/shard_map/ppermute | solution.py:154
  13.9 28.4 %collective-permute-start.7 = (bf16[256,768]{1,0:T(8,128)(2,1)}, bf16[256,768]{1,0:T(8,128)(2,1)}, u32[]{:S(2)}, u32[]{:S(2)}) collective-permute-start(bf16[256,768]{1,0:T(8,128)(2,1)} %bitcast.24), channel_id=1, source_target_pairs={{0,2},{1,3},{2,0},{3,1},{4,6},{5,7},{6,4},{7,5},{8,10},{9,11},{10,... | collective-permute-start | bytes 1179656 | tf_op jit(solution)/shard_map/ppermute | solution.py:154
  17.4 48.7 %collective-permute-start.8 = (bf16[256,768]{1,0:T(8,128)(2,1)}, bf16[256,768]{1,0:T(8,128)(2,1)}, u32[]{:S(2)}, u32[]{:S(2)}) collective-permute-start(bf16[256,768]{1,0:T(8,128)(2,1)} %bitcast.26), channel_id=1, source_target_pairs={{0,3},{1,0},{2,1},{3,2},{4,7},{5,4},{6,5},{7,6},{8,11},{9,8},{10,9... | collective-permute-start | bytes 1179656 | tf_op jit(solution)/shard_map/ppermute | solution.py:154
  20.0 80.3 %all-to-all-start = ((bf16[256,4,768]{2,0,1:T(8,128)(2,1)}), bf16[256,4,768]{2,0,1:T(8,128)(2,1)S(1)}, u32[]{:S(2)}, u32[]{:S(2)}) async-start(bf16[256,4,768]{2,0,1:T(8,128)(2,1)} %bitcast.71), calls=%async_computation | async-start | bytes 3145728 | tf_op jit(solution)/shard_map/all_to_all | solution.py:162
  23.6 175.2 %all-gather.5.cloned.1.call-start = ((), (), s32[]{:S(2)}) async-start(), calls=%async_computation.4 | async-start | bytes 1966080 | tf_op jit(solution)/shard_map/all_gather | solution.py:178
  26.4 92.1 %collective-permute-start.3 = (bf16[256,384]{1,0:T(8,128)(2,1)}, bf16[256,384]{1,0:T(8,128)(2,1)}, u32[]{:S(2)}, u32[]{:S(2)}) collective-permute-start(bf16[256,384]{1,0:T(8,128)(2,1)} %bitcast.95), channel_id=1, source_target_pairs={{0,1},{1,2},{2,3},{3,0},{4,5},{5,6},{6,7},{7,4},{8,9},{9,10},{10,1... | collective-permute-start | bytes 589832 | tf_op jit(solution)/shard_map/ppermute | solution.py:154
  29.2 90.5 %collective-permute-start.4 = (bf16[256,384]{1,0:T(8,128)(2,1)}, bf16[256,384]{1,0:T(8,128)(2,1)}, u32[]{:S(2)}, u32[]{:S(2)}) collective-permute-start(bf16[256,384]{1,0:T(8,128)(2,1)} %bitcast.13), channel_id=1, source_target_pairs={{0,2},{1,3},{2,0},{3,1},{4,6},{5,7},{6,4},{7,5},{8,10},{9,11},{10,... | collective-permute-start | bytes 589832 | tf_op jit(solution)/shard_map/ppermute | solution.py:154
  39.4 80.2 %collective-permute-start.5 = (bf16[256,384]{1,0:T(8,128)(2,1)}, bf16[256,384]{1,0:T(8,128)(2,1)}, u32[]{:S(2)}, u32[]{:S(2)}) collective-permute-start(bf16[256,384]{1,0:T(8,128)(2,1)} %bitcast.15), channel_id=1, source_target_pairs={{0,3},{1,0},{2,1},{3,2},{4,7},{5,4},{6,5},{7,6},{8,11},{9,8},{10,9... | collective-permute-start | bytes 589832 | tf_op jit(solution)/shard_map/ppermute | solution.py:154
  42.3 80.2 %collective-permute-start = (bf16[256,384]{1,0:T(8,128)(2,1)}, bf16[256,384]{1,0:T(8,128)(2,1)}, u32[]{:S(2)}, u32[]{:S(2)}) collective-permute-start(bf16[256,384]{1,0:T(8,128)(2,1)} %bitcast.2), channel_id=1, source_target_pairs={{0,1},{1,2},{2,3},{3,0},{4,5},{5,6},{6,7},{7,4},{8,9},{9,10},{10,1... | collective-permute-start | bytes 589832 | tf_op jit(solution)/shard_map/ppermute | solution.py:154
  66.1 56.4 %collective-permute-start.1 = (bf16[256,384]{1,0:T(8,128)(2,1)}, bf16[256,384]{1,0:T(8,128)(2,1)}, u32[]{:S(2)}, u32[]{:S(2)}) collective-permute-start(bf16[256,384]{1,0:T(8,128)(2,1)} %bitcast.4), channel_id=1, source_target_pairs={{0,2},{1,3},{2,0},{3,1},{4,6},{5,7},{6,4},{7,5},{8,10},{9,11},{10,... | collective-permute-start | bytes 589832 | tf_op jit(solution)/shard_map/ppermute | solution.py:154
  80.4 118.4 %all-gather.3.cloned.1.call-start = ((), (), s32[]{:S(2)}) async-start(), calls=%async_computation.3 | async-start | bytes 1966080 | tf_op jit(solution)/shard_map/all_gather | solution.py:177
  118.6 6.9 %collective-permute-start.2 = (bf16[256,384]{1,0:T(8,128)(2,1)}, bf16[256,384]{1,0:T(8,128)(2,1)S(1)}, u32[]{:S(2)}, u32[]{:S(2)}) collective-permute-start(bf16[256,384]{1,0:T(8,128)(2,1)} %bitcast.6), channel_id=1, source_target_pairs={{0,3},{1,0},{2,1},{3,2},{4,7},{5,4},{6,5},{7,6},{8,11},{9,8},{10,9... | collective-permute-start | bytes 589832 | tf_op jit(solution)/shard_map/ppermute | solution.py:154
  119.7 14.2 %collective-permute-start.9 = (bf16[2,128,768]{2,1,0:T(8,128)(2,1)}, bf16[2,128,768]{2,1,0:T(8,128)(2,1)}, u32[]{:S(2)}, u32[]{:S(2)}) collective-permute-start(bf16[2,128,768]{2,1,0:T(8,128)(2,1)} %get-tuple-element.17), channel_id=1, source_target_pairs={{0,4},{4,8},{8,12},{12,0},{1,5},{5,9},{9,13},{13,1},{2,6},{6,10},{... | collective-permute-start | bytes 1179656 | tf_op jit(solution)/shard_map/ppermute | solution.py:205
  131.2 13.2 %collective-permute-start.10 = (bf16[2,128,768]{2,1,0:T(8,128)(2,1)}, bf16[2,128,768]{2,1,0:T(8,128)(2,1)S(1)}, u32[]{:S(2)}, u32[]{:S(2)}) collective-permute-start(bf16[2,128,768]{2,1,0:T(8,128)(2,1)} %get-tuple-element.16), channel_id=1, source_target_pairs={{0,8},{4,12},{8,0},{12,4},{1,9},{5,13},{9,1},{13,5},{2,10},{6,14},... | collective-permute-start | bytes 1179656 | tf_op jit(solution)/shard_map/ppermute | solution.py:205
  132.7 18.3 %collective-permute-start.11 = (bf16[2,128,768]{2,1,0:T(8,128)(2,1)S(1)}, bf16[2,128,768]{2,1,0:T(8,128)(2,1)S(1)}, u32[]{:S(2)}, u32[]{:S(2)}) collective-permute-start(bf16[2,128,768]{2,1,0:T(8,128)(2,1)S(1)} %copy-done.7), channel_id=1, source_target_pairs={{0,12},{4,0},{8,4},{12,8},{1,13},{5,1},{9,5},{13,9},{2,14},{6,2},{... | collective-permute-start | bytes 1179656 | tf_op jit(solution)/shard_map/ppermute | solution.py:205
  132.8 19.1 %collective-permute-start.12 = (bf16[2,128,768]{2,1,0:T(8,128)(2,1)S(1)}, bf16[2,128,768]{2,1,0:T(8,128)(2,1)S(1)}, u32[]{:S(2)}, u32[]{:S(2)}) collective-permute-start(bf16[2,128,768]{2,1,0:T(8,128)(2,1)S(1)} %get-tuple-element.14), channel_id=1, source_target_pairs={{0,4},{4,8},{8,12},{12,0},{1,5},{5,9},{9,13},{13,1},{2,6},{6,10},{... | collective-permute-start | bytes 1179656 | tf_op jit(solution)/shard_map/ppermute | solution.py:205
  133.3 27.5 %collective-permute-start.13 = (bf16[2,128,768]{2,1,0:T(8,128)(2,1)S(1)}, bf16[2,128,768]{2,1,0:T(8,128)(2,1)S(1)}, u32[]{:S(2)}, u32[]{:S(2)}) collective-permute-start(bf16[2,128,768]{2,1,0:T(8,128)(2,1)S(1)} %get-tuple-element.13), channel_id=1, source_target_pairs={{0,8},{4,12},{8,0},{12,4},{1,9},{5,13},{9,1},{13,5},{2,10},{6,14},... | collective-permute-start | bytes 1179656 | tf_op jit(solution)/shard_map/ppermute | solution.py:205
  133.9 29.9 %collective-permute-start.14 = (bf16[2,128,768]{2,1,0:T(8,128)(2,1)S(1)}, bf16[2,128,768]{2,1,0:T(8,128)(2,1)S(1)}, u32[]{:S(2)}, u32[]{:S(2)}) collective-permute-start(bf16[2,128,768]{2,1,0:T(8,128)(2,1)S(1)} %get-tuple-element.12), channel_id=1, source_target_pairs={{0,12},{4,0},{8,4},{12,8},{1,13},{5,1},{9,5},{13,9},{2,14},{6,2},{... | collective-permute-start | bytes 1179656 | tf_op jit(solution)/shard_map/ppermute | solution.py:205
  144.3 19.4 %copy-start.15 = (bf16[2,128,768]{2,1,0:T(8,128)(2,1)}, bf16[2,128,768]{2,1,0:T(8,128)(2,1)S(1)}, u32[]{:S(2)}) copy-start(bf16[2,128,768]{2,1,0:T(8,128)(2,1)S(1)} %collective-permute-done.10) | copy-start | bytes 1179652
  151.0 12.8 %copy-start.16 = (bf16[2,128,768]{2,1,0:T(8,128)(2,1)}, bf16[2,128,768]{2,1,0:T(8,128)(2,1)S(1)}, u32[]{:S(2)}) copy-start(bf16[2,128,768]{2,1,0:T(8,128)(2,1)S(1)} %collective-permute-done.11) | copy-start | bytes 1179652
  151.9 11.8 %copy-start.17 = (bf16[2,128,768]{2,1,0:T(8,128)(2,1)}, bf16[2,128,768]{2,1,0:T(8,128)(2,1)S(1)}, u32[]{:S(2)}) copy-start(bf16[2,128,768]{2,1,0:T(8,128)(2,1)S(1)} %collective-permute-done.12) | copy-start | bytes 1179652
  179.9 24.9 %all-to-all-start.1 = ((bf16[4,256,384]{2,1,0:T(8,128)(2,1)}), bf16[4,256,384]{2,1,0:T(8,128)(2,1)S(1)}, u32[]{:S(2)}, u32[]{:S(2)}) async-start(bf16[4,256,384]{2,1,0:T(8,128)(2,1)} %bitcast.93), calls=%async_computation.1 | async-start | bytes 1572864 | tf_op jit(solution)/shard_map/all_to_all | solution.py:233
  204.8 24.1 %all-to-all-start.2 = ((bf16[4,256,384]{2,1,0:T(8,128)(2,1)}), bf16[4,256,384]{2,1,0:T(8,128)(2,1)S(1)}, u32[]{:S(2)}, u32[]{:S(2)}) async-start(bf16[4,256,384]{2,1,0:T(8,128)(2,1)} %bitcast.92), calls=%async_computation.2 | async-start | bytes 1572864 | tf_op jit(solution)/shard_map/all_to_all | solution.py:233
  (16 other events, 52.1 us)
Sparse Core Ops, SparseCore 0:
  80.6 17.8 all-gather.4
  115.8 22.5 all-gather.2

commit v12 on v11

--- a/solution.py
+++ b/solution.py
@@ -69,7 +69,7 @@
         one_block(i)
 
 
-def sparse_attention(tbl, queries, keys, values, far_keys, far_values, head_lo, heads):
+def sparse_attention(tbl, queries, keys, values, far_keys, far_values, head_lo, heads, q_lo):
     rows = queries.shape[0]
 
     def column(h, t):
@@ -90,7 +90,7 @@
         grid_spec=pltpu.PrefetchScalarGridSpec(
             num_scalar_prefetch=1,
             grid=(heads,),
-            in_specs=[pl.BlockSpec((rows, HD), lambda h, t: (0, h))]
+            in_specs=[pl.BlockSpec((rows, HD), lambda h, t: (0, h + q_lo))]
             + [pl.BlockSpec((x.shape[0], HD), column) for x in operands],
             out_specs=pl.BlockSpec((rows, HD), lambda h, t: (0, h)),
             scratch_shapes=[
@@ -166,13 +166,7 @@
     heads = width // HD
     first = max(1, heads // 2)
     spans = [(lo, n) for lo, n in ((0, first), (first, heads - first)) if n > 0]
-    grouped_q = query_in.reshape(query_in.shape[0], head_count, width)
-    query_slices = [
-        grouped_q[:, :, lo * HD:(lo + n) * HD].reshape(query_in.shape[0], -1) for lo, n in spans
-    ]
-
-    def query_a2a(piece):
-        return head_permutes(piece)
+    queries = lax.all_to_all(query_in, "head", split_axis=1, concat_axis=0, tiled=True)
 
     draft_keys = lax.all_gather(pool_tokens(key_rows), "seq", axis=0, tiled=True)
     draft_values = lax.all_gather(pool_tokens(value_rows), "seq", axis=0, tiled=True)
@@ -210,7 +204,6 @@
 
     remote_keys = exchange(key_rows)
     remote_values = exchange(value_rows)
-    query_parts = [query_a2a(piece) for piece in query_slices]
 
     own_lists = lax.dynamic_slice_in_dim(block_lists, seq_index * per_dev, per_dev, 0)
     owners = own_lists // per_dev
@@ -222,9 +215,10 @@
     table = jnp.clip(joint_pos, 0, per_dev + (seq_count - 1) * CAP - 1).reshape(-1).astype(jnp.int32)
 
     pieces = []
-    for index, ((head_lo, count), queries) in enumerate(zip(spans, query_parts)):
+    for index, (head_lo, count) in enumerate(spans):
         rows_part = sparse_attention(
-            table, queries, key_rows, value_rows, remote_keys, remote_values, head_lo, count,
+            table, queries, key_rows, value_rows, remote_keys, remote_values,
+            head_lo, count, head_lo,
         )
         if index == len(spans) - 1:
             rows_part, draft_keys, draft_values = lax.optimization_barrier(
@@ -233,13 +227,7 @@
         back = lax.all_to_all(rows_part, "head", split_axis=0, concat_axis=1, tiled=True)
         pieces.append(back.reshape(back.shape[0], -1, count * HD))
     sparse_out = jnp.concatenate(pieces, axis=2).reshape(pieces[0].shape[0], -1)
-    draft_out = jnp.concatenate(
-        [
-            draft_attention(queries, draft_keys, draft_values, head_lo)
-            for (head_lo, count), queries in zip(spans, query_parts)
-        ],
-        axis=1,
-    )
+    draft_out = draft_attention(queries, draft_keys, draft_values, 0)
     return (draft_out, sparse_out)
 
 

time: 238 us -> 228 us (0.958)
  waiting for transfers between devices: 52.5 us -> 90.1 us
  starting transfers between devices: 54.6 us -> 29 us
  local copies, waits for them, and re-layouts: 40.6 us -> 30.1 us
  other arithmetic: 31.2 us -> 20.9 us
    ppermute x9 -> x3, starting transfers between devices: 40.4 us -> 6.06 us  [head_permutes(): lax.ppermute(piece, 'head', [(i, (i + shift) % count) for i in range(coun...]
    ppermute x9 -> x3, waiting for transfers between devices: 4.38 us -> 26.1 us  [head_permutes(): lax.ppermute(piece, 'head', [(i, (i + shift) % count) for i in range(coun...]
    all_to_all x1, waiting for transfers between devices: 10.2 us -> 17.3 us  [on_device(): lax.all_to_all(key_in, 'head', split_axis=1, concat_axis=0, tiled=True)]
    dynamic_slice x9 -> x3, local copies, waits for them, and re-layouts: 7.7 us -> 2.77 us  [head_permutes(): lax.dynamic_index_in_dim(chunks, (me + shift) % count, axis=1, keepdims=F...]
    all_to_all x0 -> x1, starting transfers between devices: none -> 4.81 us  [on_device(): lax.all_to_all(query_in, 'head', split_axis=1, concat_axis=0, tiled=True)]
    all_to_all x0 -> x1, waiting for transfers between devices: none -> 4.41 us  [on_device(): lax.all_to_all(query_in, 'head', split_axis=1, concat_axis=0, tiled=True)]
    gather x4 -> x2, local copies, waits for them, and re-layouts: 7.73 us -> 3.39 us  [head_permutes(): jnp.take(stacked, order, axis=0).reshape(count * rows, total // count)]
    another operation x3 -> x1, other arithmetic: 6.13 us -> 2.57 us  [head_permutes(): stacked = jnp.stack(by_shift, axis=0)]
  transfers between devices with their start and end apart: 20 -> 15, of which waited for: 10 -> 11; matrix products, arithmetic and copies ran while one was open for 28% -> 20% of each run, Pallas kernels for 19% -> 19%
where the time goes in v12:
time: 228 us; the launch traced here: 227 us
  waiting for transfers between devices  90.1 us (40%)
  Pallas kernels  42.6 us (19%)
  local copies, waits for them, and re-layouts  30.1 us (13%)
  starting transfers between devices  29 us (13%)
  other arithmetic  20.9 us (9%)
  between operations  14.4 us (6%)
    pallas_call x2, Pallas kernels, sparse_attention(): pl.pallas_call(sparse_kernel, out_shape=jax.ShapeDtypeStruct((rows, heads...  30.7 us
    ppermute x6, waiting for transfers between devices, exchange(): lax.ppermute(parcel, 'seq', [(i, (i + shift) % seq_count) for i in range(...  27.8 us
    ppermute x3, waiting for transfers between devices, head_permutes(): lax.ppermute(piece, 'head', [(i, (i + shift) % count) for i in range(coun...  26.1 us
    all_to_all x1, waiting for transfers between devices, on_device(): lax.all_to_all(key_in, 'head', split_axis=1, concat_axis=0, tiled=True)  17.3 us
    all_to_all x2, waiting for transfers between devices, on_device(): lax.all_to_all(rows_part, 'head', split_axis=0, concat_axis=1, tiled=True)  14.5 us
    pallas_call x1, Pallas kernels, draft_attention(): pl.pallas_call(draft_kernel, out_shape=jax.ShapeDtypeStruct((rows, width)...  11.8 us
    all_to_all x2, starting transfers between devices, on_device(): lax.all_to_all(rows_part, 'head', split_axis=0, concat_axis=1, tiled=True)  8.59 us
    reduce_sum x2, other arithmetic, pool_tokens(): return (grouped.sum(axis=1) * POOL ** (-0.5)).astype(jnp.bfloat16)  7.34 us
  transfers between devices with their start and end apart: 15, of which 11 were waited for; matrix products, arithmetic and copies ran while one was open for 20% of the time, Pallas kernels for 19%

profile of v12, /device:TPU:0, one launch (start us, length us, event | category | flops | bytes accessed | tf_op | source)
XLA Modules:
  0.0 227.0 jit_solution(13066364578287586702)
XLA Ops:
  10.0 4.0 %collective-permute-start.1 = (bf16[256,768]{1,0:T(8,128)(2,1)}, bf16[256,768]{1,0:T(8,128)(2,1)}, u32[]{:S(2)}, u32[]{:S(2)}) collective-permute-start(bf16[256,768]{1,0:T(8,128)(2,1)} %bitcast.10), channel_id=1, source_target_pairs={{0,2},{1,3},{2,0},{3,1},{4,6},{5,7},{6,4},{7,5},{8,10},{9,11},{10,... | collective-permute-start | bytes 1179656 | tf_op jit(solution)/shard_map/ppermute | solution.py:154
  19.2 4.5 %all-to-all-start.1 = ((bf16[256,4,768]{2,0,1:T(8,128)(2,1)}), bf16[256,4,768]{2,0,1:T(8,128)(2,1)S(1)}, u32[]{:S(2)}, u32[]{:S(2)}) async-start(bf16[256,4,768]{2,0,1:T(8,128)(2,1)} %bitcast.60), calls=%async_computation.1 | async-start | bytes 3145728 | tf_op jit(solution)/shard_map/all_to_all | solution.py:162
  25.2 8.4 %collective-permute-done.1 = bf16[256,768]{1,0:T(8,128)(2,1)} collective-permute-done((bf16[256,768]{1,0:T(8,128)(2,1)}, bf16[256,768]{1,0:T(8,128)(2,1)}, u32[]{:S(2)}, u32[]{:S(2)}) %collective-permute-start.1) | collective-permute-done | bytes 393248 | tf_op jit(solution)/shard_map/ppermute | solution.py:154
  33.6 17.6 %collective-permute-done.2 = bf16[256,768]{1,0:T(8,128)(2,1)} collective-permute-done((bf16[256,768]{1,0:T(8,128)(2,1)}, bf16[256,768]{1,0:T(8,128)(2,1)}, u32[]{:S(2)}, u32[]{:S(2)}) %collective-permute-start.2) | collective-permute-done | bytes 393248 | tf_op jit(solution)/shard_map/ppermute | solution.py:154
  57.2 3.6 %convert_reduce_fusion = f32[256,768]{1,0:T(8,128)S(1)} fusion(bf16[256,4,768]{2,1,0:T(4,128)(2,1)} %gather.20, pred[256]{0:T(512)(128)(4,1)S(1)} %broadcast_in_dim.76), kind=kLoop, calls=%fused_computation.4 | loop fusion | flops 2162688 | bytes 2359552 | tf_op jit(solution)/shard_map/reduce_sum | solution.py:20
  62.4 2.7 %copy.58 = bf16[32,4,8,768]{3,2,0,1:T(8,128)(2,1)} copy(bf16[32,4,8,768]{3,2,1,0:T(8,128)(2,1)} %bitcast.74) | data formatting | bytes 3145728 | tf_op jit(solution)/shard_map/all_to_all | solution.py:169
  65.1 17.3 %all-to-all-done.1 = bf16[256,4,768]{2,0,1:T(8,128)(2,1)S(1)} async-done(((bf16[256,4,768]{2,0,1:T(8,128)(2,1)}), bf16[256,4,768]{2,0,1:T(8,128)(2,1)S(1)}, u32[]{:S(2)}, u32[]{:S(2)}) %all-to-all-start.1) | async-done | bytes 1572896 | tf_op jit(solution)/shard_map/all_to_all | solution.py:162
  82.4 4.8 %all-to-all-start = ((bf16[256,4,768]{2,0,1:T(8,128)(2,1)}), bf16[256,4,768]{2,0,1:T(8,128)(2,1)}, u32[]{:S(2)}, u32[]{:S(2)}) async-start(bf16[256,4,768]{2,0,1:T(8,128)(2,1)} %bitcast.67), calls=%async_computation | async-start | bytes 3145728 | tf_op jit(solution)/shard_map/all_to_all | solution.py:169
  88.6 3.2 %gather_fusion.3 = bf16[8,128,768]{2,1,0:T(8,128)(2,1)} fusion(bf16[8,128,768]{2,1,0:T(8,128)(2,1)} %broadcast_select_fusion.2, s32[1024]{0:T(1024)S(1)} %pad_clamp_fusion), kind=kCustom, calls=%fused_computation.1.clone | custom fusion | bytes 3145760 | tf_op jit(solution)/shard_map/jit(_take)/gather | solution.py:191
  93.6 3.4 %broadcast_select_fusion = (bf16[8,128,768]{2,1,0:T(8,128)(2,1)S(1)}, bf16[8,128,768]{2,1,0:T(8,128)(2,1)}) fusion(bf16[8,128,768]{2,1,0:T(8,128)(2,1)} %gather_fusion.3, pred[8]{0:T(512)(128)(4,1)S(1)} %compare_and_fusion, bf16[8,128,768]{2,1,0:T(8,128)(2,1)} %gather_fusion.2), kind=kLoop, calls=%fused_computation.11 | loop fusion | flops 1572864 | bytes 6291464 | tf_op jit(solution)/shard_map/jit(_take)/select_n | solution.py:191
  99.9 4.9 %reshape.155 = f32[256,4,768]{2,1,0:T(4,128)} reshape(f32[4,256,768]{2,1,0:T(8,128)} %bitcast_convert_fusion) | data formatting | bytes 6291456 | tf_op jit(solution)/shard_map/convert_element_type | solution.py:19
  104.8 3.8 %reduce_sum.28 = f32[256,768]{1,0:T(8,128)S(1)} reduce(f32[256,4,768]{2,1,0:T(4,128)} %reshape.155, f32[]{:T(128)} %constant.170.clone.1), dimensions={1}, to_apply=%region_4.6 | reduce | flops 589824 | bytes 3932164 | tf_op jit(solution)/shard_map/reduce_sum | solution.py:20
  120.0 4.4 %all-to-all-done = bf16[256,4,768]{2,0,1:T(8,128)(2,1)} async-done(((bf16[256,4,768]{2,0,1:T(8,128)(2,1)}), bf16[256,4,768]{2,0,1:T(8,128)(2,1)}, u32[]{:S(2)}, u32[]{:S(2)}) %all-to-all-start) | async-done | bytes 1572896 | tf_op jit(solution)/shard_map/all_to_all | solution.py:169
  124.4 2.6 %collective-permute-done.7 = bf16[2,128,768]{2,1,0:T(8,128)(2,1)} collective-permute-done((bf16[2,128,768]{2,1,0:T(8,128)(2,1)}, bf16[2,128,768]{2,1,0:T(8,128)(2,1)}, u32[]{:S(2)}, u32[]{:S(2)}) %collective-permute-start.7) | collective-permute-done | bytes 393248 | tf_op jit(solution)/shard_map/ppermute | solution.py:199
  127.1 12.8 %collective-permute-done.8 = bf16[2,128,768]{2,1,0:T(8,128)(2,1)} collective-permute-done((bf16[2,128,768]{2,1,0:T(8,128)(2,1)S(1)}, bf16[2,128,768]{2,1,0:T(8,128)(2,1)}, u32[]{:S(2)}, u32[]{:S(2)}) %collective-permute-start.8) | collective-permute-done | bytes 393248 | tf_op jit(solution)/shard_map/ppermute | solution.py:199
  141.4 7.4 %collective-permute-done.4 = bf16[2,128,768]{2,1,0:T(8,128)(2,1)S(1)} collective-permute-done((bf16[2,128,768]{2,1,0:T(8,128)(2,1)}, bf16[2,128,768]{2,1,0:T(8,128)(2,1)S(1)}, u32[]{:S(2)}, u32[]{:S(2)}) %collective-permute-start.4) | collective-permute-done | bytes 393248 | tf_op jit(solution)/shard_map/ppermute | solution.py:199
  148.7 3.5 %collective-permute-done.5 = bf16[2,128,768]{2,1,0:T(8,128)(2,1)S(1)} collective-permute-done((bf16[2,128,768]{2,1,0:T(8,128)(2,1)}, bf16[2,128,768]{2,1,0:T(8,128)(2,1)S(1)}, u32[]{:S(2)}, u32[]{:S(2)}) %collective-permute-start.5) | collective-permute-done | bytes 393248 | tf_op jit(solution)/shard_map/ppermute | solution.py:199
  153.0 15.4 %shard_map.61 = bf16[1024,384]{1,0:T(8,128)(2,1)} custom-call(s32[96]{0:T(128)} %reshape.142.tbl_ref, bf16[1024,768]{1,0:T(8,128)(2,1)} %bitcast.1.q_ref, bf16[1024,768]{1,0:T(8,128)(2,1)} %bitcast.65, bf16[1024,768]{1,0:T(8,128)(2,1)} %bitcast_select_fusion.refs_1_, bf16[256,768]{1,0:T(8,128)(2,1)} %bitcast.81, bf16[256,768]{1,0:T(8,128)(2,1)} %bitcast.83, ...), custom_call_target="tpu_custom_call" | custom-call | flops 2415919104 | bytes 4325376 | tf_op jit(solution)/shard_map/pallas_call | solution.py:86
  168.4 5.1 %all-to-all-start.2 = ((bf16[4,256,384]{2,1,0:T(8,128)(2,1)}), bf16[4,256,384]{2,1,0:T(8,128)(2,1)S(1)}, u32[]{:S(2)}, u32[]{:S(2)}) async-start(bf16[4,256,384]{2,1,0:T(8,128)(2,1)} %bitcast.78), calls=%async_computation.2 | async-start | bytes 1572864 | tf_op jit(solution)/shard_map/all_to_all | solution.py:227
  173.5 15.4 %shard_map.59 = bf16[1024,384]{1,0:T(8,128)(2,1)} custom-call(s32[96]{0:T(128)} %reshape.142.tbl_ref, bf16[1024,768]{1,0:T(8,128)(2,1)} %bitcast.1.q_ref, bf16[1024,768]{1,0:T(8,128)(2,1)} %bitcast.66, bf16[1024,768]{1,0:T(8,128)(2,1)} %bitcast_select_fusion.refs_1_, bf16[256,768]{1,0:T(8,128)(2,1)} %bitcast.82, bf16[256,768]{1,0:T(8,128)(2,1)} %bitcast.84, ...), custom_call_target="tpu_custom_call" | custom-call | flops 2415919104 | bytes 4325376 | tf_op jit(solution)/shard_map/pallas_call | solution.py:86
  188.9 5.9 %all-to-all-done.2 = bf16[4,256,384]{2,1,0:T(8,128)(2,1)S(1)} async-done(((bf16[4,256,384]{2,1,0:T(8,128)(2,1)}), bf16[4,256,384]{2,1,0:T(8,128)(2,1)S(1)}, u32[]{:S(2)}, u32[]{:S(2)}) %all-to-all-start.2) | async-done | bytes 786464 | tf_op jit(solution)/shard_map/all_to_all | solution.py:227
  194.8 3.5 %all-to-all-start.3 = ((bf16[4,256,384]{2,1,0:T(8,128)(2,1)}), bf16[4,256,384]{2,1,0:T(8,128)(2,1)S(1)}, u32[]{:S(2)}, u32[]{:S(2)}) async-start(bf16[4,256,384]{2,1,0:T(8,128)(2,1)} %bitcast.77), calls=%async_computation.3 | async-start | bytes 1572864 | tf_op jit(solution)/shard_map/all_to_all | solution.py:227
  198.3 11.8 %shard_map.60 = bf16[256,768]{1,0:T(8,128)(2,1)} custom-call(bf16[1024,768]{1,0:T(8,128)(2,1)} %bitcast.1.q_ref, bf16[1024,768]{1,0:T(8,128)(2,1)} %all-gather.3.cloned.1.call-done.k_ref, bf16[1024,768]{1,0:T(8,128)(2,1)} %all-gather.5.cloned.1.call-done.v_ref), custom_call_target="tpu_custom_call" | custom-call | flops 1006632960 | bytes 5111808 | tf_op jit(solution)/shard_map/pallas_call | solution.py:131
  210.1 8.6 %all-to-all-done.3 = bf16[4,256,384]{2,1,0:T(8,128)(2,1)S(1)} async-done(((bf16[4,256,384]{2,1,0:T(8,128)(2,1)}), bf16[4,256,384]{2,1,0:T(8,128)(2,1)S(1)}, u32[]{:S(2)}, u32[]{:S(2)}) %all-to-all-start.3) | async-done | bytes 786464 | tf_op jit(solution)/shard_map/all_to_all | solution.py:227
  (91 shorter events, 38.0 us)
Async XLA Ops:
  9.1 8.8 %copy-start.2 = (bf16[256,3072]{1,0:T(8,128)(2,1)S(1)}, bf16[256,3072]{1,0:T(8,128)(2,1)}, u32[]{:S(2)}) copy-start(bf16[256,3072]{1,0:T(8,128)(2,1)} %param.7) | copy-start | bytes 4718596
  10.0 23.6 %collective-permute-start.1 = (bf16[256,768]{1,0:T(8,128)(2,1)}, bf16[256,768]{1,0:T(8,128)(2,1)}, u32[]{:S(2)}, u32[]{:S(2)}) collective-permute-start(bf16[256,768]{1,0:T(8,128)(2,1)} %bitcast.10), channel_id=1, source_target_pairs={{0,2},{1,3},{2,0},{3,1},{4,6},{5,7},{6,4},{7,5},{8,10},{9,11},{10,... | collective-permute-start | bytes 1179656 | tf_op jit(solution)/shard_map/ppermute | solution.py:154
  14.9 36.3 %collective-permute-start.2 = (bf16[256,768]{1,0:T(8,128)(2,1)}, bf16[256,768]{1,0:T(8,128)(2,1)}, u32[]{:S(2)}, u32[]{:S(2)}) collective-permute-start(bf16[256,768]{1,0:T(8,128)(2,1)} %bitcast.12), channel_id=1, source_target_pairs={{0,3},{1,0},{2,1},{3,2},{4,7},{5,4},{6,5},{7,6},{8,11},{9,8},{10,9... | collective-permute-start | bytes 1179656 | tf_op jit(solution)/shard_map/ppermute | solution.py:154
  17.2 34.0 %collective-permute-start = (bf16[256,768]{1,0:T(8,128)(2,1)}, bf16[256,768]{1,0:T(8,128)(2,1)}, u32[]{:S(2)}, u32[]{:S(2)}) collective-permute-start(bf16[256,768]{1,0:T(8,128)(2,1)} %bitcast.8), channel_id=1, source_target_pairs={{0,1},{1,2},{2,3},{3,0},{4,5},{5,6},{6,7},{7,4},{8,9},{9,10},{10,1... | collective-permute-start | bytes 1179656 | tf_op jit(solution)/shard_map/ppermute | solution.py:154
  19.2 4.7 %copy-start.3 = (s32[32,12]{0,1:T(8,128)S(1)}, s32[32,12]{0,1:T(8,128)}, u32[]{:S(2)}) copy-start(s32[32,12]{0,1:T(8,128)} %param.9) | copy-start | bytes 4612
  19.2 63.2 %all-to-all-start.1 = ((bf16[256,4,768]{2,0,1:T(8,128)(2,1)}), bf16[256,4,768]{2,0,1:T(8,128)(2,1)S(1)}, u32[]{:S(2)}, u32[]{:S(2)}) async-start(bf16[256,4,768]{2,0,1:T(8,128)(2,1)} %bitcast.60), calls=%async_computation.1 | async-start | bytes 3145728 | tf_op jit(solution)/shard_map/all_to_all | solution.py:162
  23.7 165.1 %all-gather.5.cloned.1.call-start = ((), (), s32[]{:S(2)}) async-start(), calls=%async_computation.5 | async-start | bytes 1966080 | tf_op jit(solution)/shard_map/all_gather | solution.py:172
  25.0 36.9 %copy-start.8 = (pred[4]{0:T(512)(128)(4,1)}, pred[4]{0:T(512)(128)(4,1)S(1)}, u32[]{:S(2)}) copy-start(pred[4]{0:T(512)(128)(4,1)S(1)} %compare_and_fusion.1) | copy-start | bytes 16
  25.1 28.7 %copy-start.4 = (s32[4,4,8]{2,1,0:T(4,128)}, s32[4,4,8]{2,1,0:T(4,128)S(1)}, u32[]{:S(2)}) copy-start(s32[4,4,8]{2,1,0:T(4,128)S(1)} %broadcast_add_fusion) | copy-start | bytes 1540
  82.4 15.6 %copy-start = (bf16[256,4,768]{2,0,1:T(8,128)(2,1)}, bf16[256,4,768]{2,0,1:T(8,128)(2,1)S(1)}, u32[]{:S(2)}) copy-start(bf16[256,4,768]{2,0,1:T(8,128)(2,1)S(1)} %all-to-all-done.1) | copy-start | bytes 4718596
  82.4 42.1 %all-to-all-start = ((bf16[256,4,768]{2,0,1:T(8,128)(2,1)}), bf16[256,4,768]{2,0,1:T(8,128)(2,1)}, u32[]{:S(2)}, u32[]{:S(2)}) async-start(bf16[256,4,768]{2,0,1:T(8,128)(2,1)} %bitcast.67), calls=%async_computation | async-start | bytes 3145728 | tf_op jit(solution)/shard_map/all_to_all | solution.py:169
  87.2 101.7 %all-gather.3.cloned.1.call-start = ((), (), s32[]{:S(2)}) async-start(), calls=%async_computation.4 | async-start | bytes 1966080 | tf_op jit(solution)/shard_map/all_gather | solution.py:171
  98.0 18.4 %collective-permute-start.6 = (bf16[2,128,768]{2,1,0:T(8,128)(2,1)}, bf16[2,128,768]{2,1,0:T(8,128)(2,1)}, u32[]{:S(2)}, u32[]{:S(2)}) collective-permute-start(bf16[2,128,768]{2,1,0:T(8,128)(2,1)} %get-tuple-element.11), channel_id=1, source_target_pairs={{0,4},{4,8},{8,12},{12,0},{1,5},{5,9},{9,13},{13,1},{2,6},{6,10},{... | collective-permute-start | bytes 1179656 | tf_op jit(solution)/shard_map/ppermute | solution.py:199
  110.1 4.5 %copy-start.1 = (bf16[8,128,768]{2,1,0:T(8,128)(2,1)S(1)}, bf16[8,128,768]{2,1,0:T(8,128)(2,1)}, u32[]{:S(2)}) copy-start(bf16[8,128,768]{2,1,0:T(8,128)(2,1)} %get-tuple-element.20) | copy-start | bytes 4718596
  111.7 6.2 %copy-start.9 = (pred[4]{0:T(512)(128)(4,1)S(1)}, pred[4]{0:T(512)(128)(4,1)}, u32[]{:S(2)}) copy-start(pred[4]{0:T(512)(128)(4,1)} %copy-done.8) | copy-start | bytes 16
  111.8 15.3 %collective-permute-start.7 = (bf16[2,128,768]{2,1,0:T(8,128)(2,1)}, bf16[2,128,768]{2,1,0:T(8,128)(2,1)}, u32[]{:S(2)}, u32[]{:S(2)}) collective-permute-start(bf16[2,128,768]{2,1,0:T(8,128)(2,1)} %get-tuple-element.10), channel_id=1, source_target_pairs={{0,8},{4,12},{8,0},{12,4},{1,9},{5,13},{9,1},{13,5},{2,10},{6,14},... | collective-permute-start | bytes 1179656 | tf_op jit(solution)/shard_map/ppermute | solution.py:199
  113.3 26.6 %collective-permute-start.8 = (bf16[2,128,768]{2,1,0:T(8,128)(2,1)S(1)}, bf16[2,128,768]{2,1,0:T(8,128)(2,1)}, u32[]{:S(2)}, u32[]{:S(2)}) collective-permute-start(bf16[2,128,768]{2,1,0:T(8,128)(2,1)S(1)} %get-tuple-element.9), channel_id=1, source_target_pairs={{0,12},{4,0},{8,4},{12,8},{1,13},{5,1},{9,5},{13,9},{2,14},{6,2},{... | collective-permute-start | bytes 1179656 | tf_op jit(solution)/shard_map/ppermute | solution.py:199
  115.8 25.6 %collective-permute-start.3 = (bf16[2,128,768]{2,1,0:T(8,128)(2,1)}, bf16[2,128,768]{2,1,0:T(8,128)(2,1)S(1)}, u32[]{:S(2)}, u32[]{:S(2)}) collective-permute-start(bf16[2,128,768]{2,1,0:T(8,128)(2,1)} %get-tuple-element.14), channel_id=1, source_target_pairs={{0,4},{4,8},{8,12},{12,0},{1,5},{5,9},{9,13},{13,1},{2,6},{6,10},{... | collective-permute-start | bytes 1179656 | tf_op jit(solution)/shard_map/ppermute | solution.py:199
  115.8 32.9 %collective-permute-start.4 = (bf16[2,128,768]{2,1,0:T(8,128)(2,1)}, bf16[2,128,768]{2,1,0:T(8,128)(2,1)S(1)}, u32[]{:S(2)}, u32[]{:S(2)}) collective-permute-start(bf16[2,128,768]{2,1,0:T(8,128)(2,1)} %get-tuple-element.13), channel_id=1, source_target_pairs={{0,8},{4,12},{8,0},{12,4},{1,9},{5,13},{9,1},{13,5},{2,10},{6,14},... | collective-permute-start | bytes 1179656 | tf_op jit(solution)/shard_map/ppermute | solution.py:199
  116.4 35.8 %collective-permute-start.5 = (bf16[2,128,768]{2,1,0:T(8,128)(2,1)}, bf16[2,128,768]{2,1,0:T(8,128)(2,1)S(1)}, u32[]{:S(2)}, u32[]{:S(2)}) collective-permute-start(bf16[2,128,768]{2,1,0:T(8,128)(2,1)} %get-tuple-element.12), channel_id=1, source_target_pairs={{0,12},{4,0},{8,4},{12,8},{1,13},{5,1},{9,5},{13,9},{2,14},{6,2},{... | collective-permute-start | bytes 1179656 | tf_op jit(solution)/shard_map/ppermute | solution.py:199
  141.4 10.9 %copy-start.5 = (bf16[2,128,768]{2,1,0:T(8,128)(2,1)}, bf16[2,128,768]{2,1,0:T(8,128)(2,1)S(1)}, u32[]{:S(2)}) copy-start(bf16[2,128,768]{2,1,0:T(8,128)(2,1)S(1)} %collective-permute-done.3) | copy-start | bytes 1179652
  148.7 3.5 %copy-start.6 = (bf16[2,128,768]{2,1,0:T(8,128)(2,1)}, bf16[2,128,768]{2,1,0:T(8,128)(2,1)S(1)}, u32[]{:S(2)}) copy-start(bf16[2,128,768]{2,1,0:T(8,128)(2,1)S(1)} %collective-permute-done.4) | copy-start | bytes 1179652
  168.4 26.4 %all-to-all-start.2 = ((bf16[4,256,384]{2,1,0:T(8,128)(2,1)}), bf16[4,256,384]{2,1,0:T(8,128)(2,1)S(1)}, u32[]{:S(2)}, u32[]{:S(2)}) async-start(bf16[4,256,384]{2,1,0:T(8,128)(2,1)} %bitcast.78), calls=%async_computation.2 | async-start | bytes 1572864 | tf_op jit(solution)/shard_map/all_to_all | solution.py:227
  194.8 23.9 %all-to-all-start.3 = ((bf16[4,256,384]{2,1,0:T(8,128)(2,1)}), bf16[4,256,384]{2,1,0:T(8,128)(2,1)S(1)}, u32[]{:S(2)}, u32[]{:S(2)}) async-start(bf16[4,256,384]{2,1,0:T(8,128)(2,1)} %bitcast.77), calls=%async_computation.3 | async-start | bytes 1572864 | tf_op jit(solution)/shard_map/all_to_all | solution.py:227
  (1 other events, 0.7 us)
Sparse Core Ops, SparseCore 0:
  61.8 26.1 all-gather.4
  109.5 29.9 all-gather.2

commit v13 on v12

--- a/solution.py
+++ b/solution.py
@@ -15,9 +15,32 @@
 EXP2_SCALE = SCALE * 1.4426950408889634
 
 
+def pooling_matrix(tile):
+    token = lax.broadcasted_iota(jnp.int32, (tile, tile * POOL), 1)
+    draft = lax.broadcasted_iota(jnp.int32, (tile, tile * POOL), 0)
+    return jnp.where(token // POOL == draft, POOL ** (-0.5), 0.0).astype(jnp.bfloat16)
+
+
+def pool_kernel(x_ref, o_ref):
+    pooled = jnp.dot(pooling_matrix(o_ref.shape[0]), x_ref[...], preferred_element_type=jnp.float32)
+    o_ref[...] = pooled.astype(o_ref.dtype)
+
+
 def pool_tokens(matrix):
-    grouped = matrix.astype(jnp.float32).reshape(matrix.shape[0] // POOL, POOL, matrix.shape[1])
-    return (grouped.sum(axis=1) * POOL ** (-0.5)).astype(jnp.bfloat16)
+    token_rows, width = matrix.shape
+    rows = token_rows // POOL
+    tile = min(DRAFT_ROWS, rows)
+    return pl.pallas_call(
+        pool_kernel,
+        out_shape=jax.ShapeDtypeStruct((rows, width), jnp.bfloat16),
+        grid=(width // HD, rows // tile),
+        in_specs=[pl.BlockSpec((tile * POOL, HD), lambda h, r: (r, h))],
+        out_specs=pl.BlockSpec((tile, HD), lambda h, r: (r, h)),
+        cost_estimate=pl.CostEstimate(
+            flops=2 * rows * tile * POOL * width, transcendentals=0,
+            bytes_accessed=2 * width * (token_rows + rows),
+        ),
+    )(matrix)
 
 
 def sparse_kernel(tbl_ref, q_ref, *refs):
@@ -102,10 +125,7 @@
 
 
 def draft_kernel(q_ref, k_ref, v_ref, o_ref):
-    tile = o_ref.shape[0]
-    token = lax.broadcasted_iota(jnp.int32, (tile, tile * POOL), 1)
-    draft = lax.broadcasted_iota(jnp.int32, (tile, tile * POOL), 0)
-    pooling = jnp.where(token // POOL == draft, POOL ** (-0.5), 0.0).astype(jnp.bfloat16)
+    pooling = pooling_matrix(o_ref.shape[0])
     pooled = jnp.dot(pooling, q_ref[...], preferred_element_type=jnp.float32).astype(jnp.bfloat16)
     raw = lax.dot_general(
         pooled, k_ref[...], (((1,), (1,)), ((), ())), preferred_element_type=jnp.float32
@@ -162,7 +182,6 @@
     key_rows = lax.all_to_all(key_in, "head", split_axis=1, concat_axis=0, tiled=True)
     value_rows = head_permutes(value_in)
     seq_rows, width = key_rows.shape
-    head_count = lax.axis_size("head")
     heads = width // HD
     first = max(1, heads // 2)
     spans = [(lo, n) for lo, n in ((0, first), (first, heads - first)) if n > 0]

time: 228 us -> 242 us (1.061)
  Pallas kernels: 42.6 us -> 58.6 us
  other arithmetic: 20.9 us -> 7.05 us
  waiting for transfers between devices: 90.1 us -> 103 us
  local copies, waits for them, and re-layouts: 30.1 us -> 25 us
  starting transfers between devices: 29 us -> 32.8 us
    ppermute x3, waiting for transfers between devices: 26.1 us -> 50.5 us  [head_permutes(): lax.ppermute(piece, 'head', [(i, (i + shift) % count) for i in range(coun...]
    all_to_all x1, waiting for transfers between devices: 17.3 us -> 0.01 us  [on_device(): lax.all_to_all(key_in, 'head', split_axis=1, concat_axis=0, tiled=True)]
    pallas_call x0 -> x2, Pallas kernels: none -> 16 us  [pool_tokens(): pl.pallas_call(pool_kernel, out_shape=jax.ShapeDtypeStruct((rows, width),...]
    reduce_sum x2 -> x0, other arithmetic: 7.34 us -> none  [pool_tokens(): return (grouped.sum(axis=1) * POOL ** (-0.5)).astype(jnp.bfloat16)]
    all_to_all x1, waiting for transfers between devices: 4.41 us -> 9.4 us  [on_device(): lax.all_to_all(query_in, 'head', split_axis=1, concat_axis=0, tiled=True)]
    convert_element_type x1 -> x0, local copies, waits for them, and re-layouts: 4.88 us -> none  [pool_tokens(): matrix.astype(jnp.float32)]
    all_to_all x1, starting transfers between devices: 4.81 us -> 9.22 us  [on_device(): lax.all_to_all(query_in, 'head', split_axis=1, concat_axis=0, tiled=True)]
    convert_element_type x3 -> x0, other arithmetic: 3.52 us -> none  [the longest x1 1.91 us: pool_tokens(): matrix.astype(jnp.float32)]
  transfers between devices with their start and end apart: 15 -> 15, of which waited for: 11 -> 9; matrix products, arithmetic and copies ran while one was open for 20% -> 11% of each run, Pallas kernels for 19% -> 24%
where the time goes in v13:
time: 242 us; the launch traced here: 241 us
  waiting for transfers between devices  103 us (43%)
  Pallas kernels  58.6 us (24%)
  starting transfers between devices  32.8 us (14%)
  local copies, waits for them, and re-layouts  25 us (10%)
  between operations  14.2 us (6%)
  other arithmetic  7.05 us (3%)
    ppermute x3, waiting for transfers between devices, head_permutes(): lax.ppermute(piece, 'head', [(i, (i + shift) % count) for i in range(coun...  50.5 us
    pallas_call x2, Pallas kernels, sparse_attention(): pl.pallas_call(sparse_kernel, out_shape=jax.ShapeDtypeStruct((rows, heads...  30.7 us
    ppermute x6, waiting for transfers between devices, exchange(): lax.ppermute(parcel, 'seq', [(i, (i + shift) % seq_count) for i in range(...  28.7 us
    pallas_call x2, Pallas kernels, pool_tokens(): pl.pallas_call(pool_kernel, out_shape=jax.ShapeDtypeStruct((rows, width),...  16 us
    all_to_all x2, waiting for transfers between devices, on_device(): lax.all_to_all(rows_part, 'head', split_axis=0, concat_axis=1, tiled=True)  14.2 us
    pallas_call x1, Pallas kernels, draft_attention(): pl.pallas_call(draft_kernel, out_shape=jax.ShapeDtypeStruct((rows, width)...  11.8 us
    all_to_all x1, waiting for transfers between devices, on_device(): lax.all_to_all(query_in, 'head', split_axis=1, concat_axis=0, tiled=True)  9.4 us
    all_to_all x1, starting transfers between devices, on_device(): lax.all_to_all(query_in, 'head', split_axis=1, concat_axis=0, tiled=True)  9.22 us
  transfers between devices with their start and end apart: 15, of which 9 were waited for; matrix products, arithmetic and copies ran while one was open for 11% of the time, Pallas kernels for 24%

profile of v13, /device:TPU:0, one launch (start us, length us, event | category | flops | bytes accessed | tf_op | source)
XLA Modules:
  0.0 240.5 jit_solution(17759407252078865598)
XLA Ops:
  7.2 2.6 %copy.57 = bf16[32,4,8,768]{3,2,0,1:T(8,128)(2,1)} copy(bf16[32,4,8,768]{3,2,1,0:T(8,128)(2,1)} %bitcast.73) | data formatting | bytes 3145728 | tf_op jit(solution)/shard_map/all_to_all | solution.py:182
  9.8 6.3 %all-to-all-start.1 = ((bf16[256,4,768]{2,0,1:T(8,128)(2,1)}), bf16[256,4,768]{2,0,1:T(8,128)(2,1)S(1)}, u32[]{:S(2)}, u32[]{:S(2)}) async-start(bf16[256,4,768]{2,0,1:T(8,128)(2,1)} %bitcast.59), calls=%async_computation.1 | async-start | bytes 3145728 | tf_op jit(solution)/shard_map/all_to_all | solution.py:182
  18.9 2.0 copy.44
  20.9 2.9 %collective-permute-start.1 = (bf16[256,768]{1,0:T(8,128)(2,1)}, bf16[256,768]{1,0:T(8,128)(2,1)S(1)}, u32[]{:S(2)}, u32[]{:S(2)}) collective-permute-start(bf16[256,768]{1,0:T(8,128)(2,1)} %bitcast.10), channel_id=1, source_target_pairs={{0,2},{1,3},{2,0},{3,1},{4,6},{5,7},{6,4},{7,5},{8,10},{9,11},{10,... | collective-permute-start | bytes 1179656 | tf_op jit(solution)/shard_map/ppermute | solution.py:174
  29.0 50.5 %collective-permute-done.1 = bf16[256,768]{1,0:T(8,128)(2,1)S(1)} collective-permute-done((bf16[256,768]{1,0:T(8,128)(2,1)}, bf16[256,768]{1,0:T(8,128)(2,1)S(1)}, u32[]{:S(2)}, u32[]{:S(2)}) %collective-permute-start.1) | collective-permute-done | bytes 393248 | tf_op jit(solution)/shard_map/ppermute | solution.py:174
  80.8 2.1 gather_fusion.1
  84.3 8.0 %shard_map.61 = bf16[256,768]{1,0:T(8,128)(2,1)} custom-call(bf16[1024,768]{1,0:T(8,128)(2,1)} %bitcast_select_fusion.refs_1_.x_ref), custom_call_target="tpu_custom_call" | custom-call | flops 201326592 | bytes 1966080 | tf_op jit(solution)/shard_map/pallas_call | solution.py:33
  93.4 2.7 %copy.58 = bf16[32,4,8,768]{3,2,0,1:T(8,128)(2,1)} copy(bf16[32,4,8,768]{3,2,1,0:T(8,128)(2,1)} %bitcast.74) | data formatting | bytes 3145728 | tf_op jit(solution)/shard_map/all_to_all | solution.py:188
  96.2 9.2 %all-to-all-start = ((bf16[256,4,768]{2,0,1:T(8,128)(2,1)}), bf16[256,4,768]{2,0,1:T(8,128)(2,1)}, u32[]{:S(2)}, u32[]{:S(2)}) async-start(bf16[256,4,768]{2,0,1:T(8,128)(2,1)} %bitcast.67), calls=%async_computation | async-start | bytes 3145728 | tf_op jit(solution)/shard_map/all_to_all | solution.py:188
  107.3 2.1 gather_fusion.3
  111.3 8.1 %shard_map.60 = bf16[256,768]{1,0:T(8,128)(2,1)} custom-call(bf16[1024,768]{1,0:T(8,128)(2,1)} %bitcast.63), custom_call_target="tpu_custom_call" | custom-call | flops 201326592 | bytes 1966080 | tf_op jit(solution)/shard_map/pallas_call | solution.py:33
  127.2 4.6 %collective-permute-done.6 = bf16[2,128,768]{2,1,0:T(8,128)(2,1)} collective-permute-done((bf16[2,128,768]{2,1,0:T(8,128)(2,1)}, bf16[2,128,768]{2,1,0:T(8,128)(2,1)}, u32[]{:S(2)}, u32[]{:S(2)}) %collective-permute-start.6) | collective-permute-done | bytes 393248 | tf_op jit(solution)/shard_map/ppermute | solution.py:218
  132.6 9.4 %all-to-all-done = bf16[256,4,768]{2,0,1:T(8,128)(2,1)} async-done(((bf16[256,4,768]{2,0,1:T(8,128)(2,1)}), bf16[256,4,768]{2,0,1:T(8,128)(2,1)}, u32[]{:S(2)}, u32[]{:S(2)}) %all-to-all-start) | async-done | bytes 1572896 | tf_op jit(solution)/shard_map/all_to_all | solution.py:188
  142.0 9.4 %collective-permute-done.8 = bf16[2,128,768]{2,1,0:T(8,128)(2,1)} collective-permute-done((bf16[2,128,768]{2,1,0:T(8,128)(2,1)S(1)}, bf16[2,128,768]{2,1,0:T(8,128)(2,1)}, u32[]{:S(2)}, u32[]{:S(2)}) %collective-permute-start.8) | collective-permute-done | bytes 393248 | tf_op jit(solution)/shard_map/ppermute | solution.py:218
  151.4 5.2 %collective-permute-done.3 = bf16[2,128,768]{2,1,0:T(8,128)(2,1)S(1)} collective-permute-done((bf16[2,128,768]{2,1,0:T(8,128)(2,1)S(1)}, bf16[2,128,768]{2,1,0:T(8,128)(2,1)S(1)}, u32[]{:S(2)}, u32[]{:S(2)}) %collective-permute-start.3) | collective-permute-done | bytes 393248 | tf_op jit(solution)/shard_map/ppermute | solution.py:218
  156.5 4.3 %collective-permute-done.4 = bf16[2,128,768]{2,1,0:T(8,128)(2,1)S(1)} collective-permute-done((bf16[2,128,768]{2,1,0:T(8,128)(2,1)S(1)}, bf16[2,128,768]{2,1,0:T(8,128)(2,1)S(1)}, u32[]{:S(2)}, u32[]{:S(2)}) %collective-permute-start.4) | collective-permute-done | bytes 393248 | tf_op jit(solution)/shard_map/ppermute | solution.py:218
  160.8 5.3 %collective-permute-done.5 = bf16[2,128,768]{2,1,0:T(8,128)(2,1)S(1)} collective-permute-done((bf16[2,128,768]{2,1,0:T(8,128)(2,1)S(1)}, bf16[2,128,768]{2,1,0:T(8,128)(2,1)S(1)}, u32[]{:S(2)}, u32[]{:S(2)}) %collective-permute-start.5) | collective-permute-done | bytes 393248 | tf_op jit(solution)/shard_map/ppermute | solution.py:218
  166.9 15.4 %shard_map.63 = bf16[1024,384]{1,0:T(8,128)(2,1)} custom-call(s32[96]{0:T(128)} %reshape.130.tbl_ref, bf16[1024,768]{1,0:T(8,128)(2,1)} %bitcast.1.q_ref, bf16[1024,768]{1,0:T(8,128)(2,1)} %bitcast.64, bf16[1024,768]{1,0:T(8,128)(2,1)} %bitcast_select_fusion.refs_1_.x_ref, bf16[256,768]{1,0:T(8,128)(2,1)} %bitcast.85, bf16[256,768]{1,0:T(8,128)(2,1)} %bitcast.87, ...), custom_call_target="tpu_custom_call" | custom-call | flops 2415919104 | bytes 4325376 | tf_op jit(solution)/shard_map/pallas_call | solution.py:109
  182.2 5.1 %all-to-all-start.2 = ((bf16[4,256,384]{2,1,0:T(8,128)(2,1)}), bf16[4,256,384]{2,1,0:T(8,128)(2,1)S(1)}, u32[]{:S(2)}, u32[]{:S(2)}) async-start(bf16[4,256,384]{2,1,0:T(8,128)(2,1)} %bitcast.78), calls=%async_computation.2 | async-start | bytes 1572864 | tf_op jit(solution)/shard_map/all_to_all | solution.py:246
  187.3 15.4 %shard_map.59 = bf16[1024,384]{1,0:T(8,128)(2,1)} custom-call(s32[96]{0:T(128)} %reshape.130.tbl_ref, bf16[1024,768]{1,0:T(8,128)(2,1)} %bitcast.1.q_ref, bf16[1024,768]{1,0:T(8,128)(2,1)} %bitcast.65, bf16[1024,768]{1,0:T(8,128)(2,1)} %bitcast_select_fusion.refs_1_.x_ref, bf16[256,768]{1,0:T(8,128)(2,1)} %bitcast.86, bf16[256,768]{1,0:T(8,128)(2,1)} %bitcast.88, ...), custom_call_target="tpu_custom_call" | custom-call | flops 2415919104 | bytes 4325376 | tf_op jit(solution)/shard_map/pallas_call | solution.py:109
  202.7 5.7 %all-to-all-done.2 = bf16[4,256,384]{2,1,0:T(8,128)(2,1)S(1)} async-done(((bf16[4,256,384]{2,1,0:T(8,128)(2,1)}), bf16[4,256,384]{2,1,0:T(8,128)(2,1)S(1)}, u32[]{:S(2)}, u32[]{:S(2)}) %all-to-all-start.2) | async-done | bytes 786464 | tf_op jit(solution)/shard_map/all_to_all | solution.py:246
  208.4 3.5 %all-to-all-start.3 = ((bf16[4,256,384]{2,1,0:T(8,128)(2,1)}), bf16[4,256,384]{2,1,0:T(8,128)(2,1)S(1)}, u32[]{:S(2)}, u32[]{:S(2)}) async-start(bf16[4,256,384]{2,1,0:T(8,128)(2,1)} %bitcast.77), calls=%async_computation.3 | async-start | bytes 1572864 | tf_op jit(solution)/shard_map/all_to_all | solution.py:246
  211.9 11.8 %shard_map.62 = bf16[256,768]{1,0:T(8,128)(2,1)} custom-call(bf16[1024,768]{1,0:T(8,128)(2,1)} %bitcast.1.q_ref, bf16[1024,768]{1,0:T(8,128)(2,1)} %all-gather.3.cloned.1.call-done.k_ref, bf16[1024,768]{1,0:T(8,128)(2,1)} %all-gather.5.cloned.1.call-done.v_ref), custom_call_target="tpu_custom_call" | custom-call | flops 1006632960 | bytes 5111808 | tf_op jit(solution)/shard_map/pallas_call | solution.py:151
  223.8 8.4 %all-to-all-done.3 = bf16[4,256,384]{2,1,0:T(8,128)(2,1)S(1)} async-done(((bf16[4,256,384]{2,1,0:T(8,128)(2,1)}), bf16[4,256,384]{2,1,0:T(8,128)(2,1)S(1)}, u32[]{:S(2)}, u32[]{:S(2)}) %all-to-all-start.3) | async-done | bytes 786464 | tf_op jit(solution)/shard_map/all_to_all | solution.py:246
  (80 shorter events, 26.5 us)
Async XLA Ops:
  9.8 86.4 %all-to-all-start.1 = ((bf16[256,4,768]{2,0,1:T(8,128)(2,1)}), bf16[256,4,768]{2,0,1:T(8,128)(2,1)S(1)}, u32[]{:S(2)}, u32[]{:S(2)}) async-start(bf16[256,4,768]{2,0,1:T(8,128)(2,1)} %bitcast.59), calls=%async_computation.1 | async-start | bytes 3145728 | tf_op jit(solution)/shard_map/all_to_all | solution.py:182
  16.1 186.6 %all-gather.5.cloned.1.call-start = ((), (), s32[]{:S(2)}) async-start(), calls=%async_computation.5 | async-start | bytes 1966080 | tf_op jit(solution)/shard_map/all_gather | solution.py:191
  18.9 8.3 %copy-start.3 = (bf16[256,1,768]{0,2,1:T(8,128)(2,1)S(1)}, bf16[256,1,768]{0,2,1:T(8,128)(2,1)}, u32[]{:S(2)}) copy-start(bf16[256,1,768]{0,2,1:T(8,128)(2,1)} %get-tuple-element.18) | copy-start | bytes 1179652
  20.9 58.5 %collective-permute-start.1 = (bf16[256,768]{1,0:T(8,128)(2,1)}, bf16[256,768]{1,0:T(8,128)(2,1)S(1)}, u32[]{:S(2)}, u32[]{:S(2)}) collective-permute-start(bf16[256,768]{1,0:T(8,128)(2,1)} %bitcast.10), channel_id=1, source_target_pairs={{0,2},{1,3},{2,0},{3,1},{4,6},{5,7},{6,4},{7,5},{8,10},{9,11},{10,... | collective-permute-start | bytes 1179656 | tf_op jit(solution)/shard_map/ppermute | solution.py:174
  25.7 53.7 %collective-permute-start.2 = (bf16[256,768]{1,0:T(8,128)(2,1)}, bf16[256,768]{1,0:T(8,128)(2,1)S(1)}, u32[]{:S(2)}, u32[]{:S(2)}) collective-permute-start(bf16[256,768]{1,0:T(8,128)(2,1)} %bitcast.12), channel_id=1, source_target_pairs={{0,3},{1,0},{2,1},{3,2},{4,7},{5,4},{6,5},{7,6},{8,11},{9,8},{10,9... | collective-permute-start | bytes 1179656 | tf_op jit(solution)/shard_map/ppermute | solution.py:174
  28.1 51.3 %collective-permute-start = (bf16[256,768]{1,0:T(8,128)(2,1)}, bf16[256,768]{1,0:T(8,128)(2,1)S(1)}, u32[]{:S(2)}, u32[]{:S(2)}) collective-permute-start(bf16[256,768]{1,0:T(8,128)(2,1)} %bitcast.82), channel_id=1, source_target_pairs={{0,1},{1,2},{2,3},{3,0},{4,5},{5,6},{6,7},{7,4},{8,9},{9,10},{10,1... | collective-permute-start | bytes 1179656 | tf_op jit(solution)/shard_map/ppermute | solution.py:174
  84.3 8.0 %copy-start.4 = (s32[32,12]{0,1:T(8,128)S(1)}, s32[32,12]{0,1:T(8,128)}, u32[]{:S(2)}) copy-start(s32[32,12]{0,1:T(8,128)} %param.9) | copy-start | bytes 4612
  96.2 13.2 %copy-start = (bf16[256,4,768]{2,0,1:T(8,128)(2,1)}, bf16[256,4,768]{2,0,1:T(8,128)(2,1)S(1)}, u32[]{:S(2)}) copy-start(bf16[256,4,768]{2,0,1:T(8,128)(2,1)S(1)} %all-to-all-done.1) | copy-start | bytes 4718596
  96.2 45.8 %all-to-all-start = ((bf16[256,4,768]{2,0,1:T(8,128)(2,1)}), bf16[256,4,768]{2,0,1:T(8,128)(2,1)}, u32[]{:S(2)}, u32[]{:S(2)}) async-start(bf16[256,4,768]{2,0,1:T(8,128)(2,1)} %bitcast.67), calls=%async_computation | async-start | bytes 3145728 | tf_op jit(solution)/shard_map/all_to_all | solution.py:188
  105.4 97.3 %all-gather.3.cloned.1.call-start = ((), (), s32[]{:S(2)}) async-start(), calls=%async_computation.4 | async-start | bytes 1966080 | tf_op jit(solution)/shard_map/all_gather | solution.py:190
  111.3 8.1 %copy-start.1 = (bf16[8,128,768]{2,1,0:T(8,128)(2,1)S(1)}, bf16[8,128,768]{2,1,0:T(8,128)(2,1)}, u32[]{:S(2)}) copy-start(bf16[8,128,768]{2,1,0:T(8,128)(2,1)} %gather_fusion.2) | copy-start | bytes 4718596
  121.8 10.0 %collective-permute-start.6 = (bf16[2,128,768]{2,1,0:T(8,128)(2,1)}, bf16[2,128,768]{2,1,0:T(8,128)(2,1)}, u32[]{:S(2)}, u32[]{:S(2)}) collective-permute-start(bf16[2,128,768]{2,1,0:T(8,128)(2,1)} %get-tuple-element.11), channel_id=1, source_target_pairs={{0,4},{4,8},{8,12},{12,0},{1,5},{5,9},{9,13},{13,1},{2,6},{6,10},{... | collective-permute-start | bytes 1179656 | tf_op jit(solution)/shard_map/ppermute | solution.py:218
  121.9 4.6 %copy-start.2 = (bf16[8,128,768]{2,1,0:T(8,128)(2,1)S(1)}, bf16[8,128,768]{2,1,0:T(8,128)(2,1)}, u32[]{:S(2)}) copy-start(bf16[8,128,768]{2,1,0:T(8,128)(2,1)} %get-tuple-element.20) | copy-start | bytes 4718596
  123.4 18.6 %collective-permute-start.7 = (bf16[2,128,768]{2,1,0:T(8,128)(2,1)S(1)}, bf16[2,128,768]{2,1,0:T(8,128)(2,1)}, u32[]{:S(2)}, u32[]{:S(2)}) collective-permute-start(bf16[2,128,768]{2,1,0:T(8,128)(2,1)S(1)} %get-tuple-element.10), channel_id=1, source_target_pairs={{0,8},{4,12},{8,0},{12,4},{1,9},{5,13},{9,1},{13,5},{2,10},{6,14},... | collective-permute-start | bytes 1179656 | tf_op jit(solution)/shard_map/ppermute | solution.py:218
  125.0 26.4 %collective-permute-start.8 = (bf16[2,128,768]{2,1,0:T(8,128)(2,1)S(1)}, bf16[2,128,768]{2,1,0:T(8,128)(2,1)}, u32[]{:S(2)}, u32[]{:S(2)}) collective-permute-start(bf16[2,128,768]{2,1,0:T(8,128)(2,1)S(1)} %get-tuple-element.9), channel_id=1, source_target_pairs={{0,12},{4,0},{8,4},{12,8},{1,13},{5,1},{9,5},{13,9},{2,14},{6,2},{... | collective-permute-start | bytes 1179656 | tf_op jit(solution)/shard_map/ppermute | solution.py:218
  126.5 30.0 %collective-permute-start.3 = (bf16[2,128,768]{2,1,0:T(8,128)(2,1)S(1)}, bf16[2,128,768]{2,1,0:T(8,128)(2,1)S(1)}, u32[]{:S(2)}, u32[]{:S(2)}) collective-permute-start(bf16[2,128,768]{2,1,0:T(8,128)(2,1)S(1)} %get-tuple-element.14), channel_id=1, source_target_pairs={{0,4},{4,8},{8,12},{12,0},{1,5},{5,9},{9,13},{13,1},{2,6},{6,10},{... | collective-permute-start | bytes 1179656 | tf_op jit(solution)/shard_map/ppermute | solution.py:218
  126.6 34.2 %collective-permute-start.4 = (bf16[2,128,768]{2,1,0:T(8,128)(2,1)S(1)}, bf16[2,128,768]{2,1,0:T(8,128)(2,1)S(1)}, u32[]{:S(2)}, u32[]{:S(2)}) collective-permute-start(bf16[2,128,768]{2,1,0:T(8,128)(2,1)S(1)} %get-tuple-element.13), channel_id=1, source_target_pairs={{0,8},{4,12},{8,0},{12,4},{1,9},{5,13},{9,1},{13,5},{2,10},{6,14},... | collective-permute-start | bytes 1179656 | tf_op jit(solution)/shard_map/ppermute | solution.py:218
  131.8 34.3 %collective-permute-start.5 = (bf16[2,128,768]{2,1,0:T(8,128)(2,1)S(1)}, bf16[2,128,768]{2,1,0:T(8,128)(2,1)S(1)}, u32[]{:S(2)}, u32[]{:S(2)}) collective-permute-start(bf16[2,128,768]{2,1,0:T(8,128)(2,1)S(1)} %get-tuple-element.12), channel_id=1, source_target_pairs={{0,12},{4,0},{8,4},{12,8},{1,13},{5,1},{9,5},{13,9},{2,14},{6,2},{... | collective-permute-start | bytes 1179656 | tf_op jit(solution)/shard_map/ppermute | solution.py:218
  156.5 9.6 %copy-start.5 = (bf16[2,128,768]{2,1,0:T(8,128)(2,1)}, bf16[2,128,768]{2,1,0:T(8,128)(2,1)S(1)}, u32[]{:S(2)}) copy-start(bf16[2,128,768]{2,1,0:T(8,128)(2,1)S(1)} %collective-permute-done.3) | copy-start | bytes 1179652
  160.8 5.3 %copy-start.6 = (bf16[2,128,768]{2,1,0:T(8,128)(2,1)}, bf16[2,128,768]{2,1,0:T(8,128)(2,1)S(1)}, u32[]{:S(2)}) copy-start(bf16[2,128,768]{2,1,0:T(8,128)(2,1)S(1)} %collective-permute-done.4) | copy-start | bytes 1179652
  166.1 0.7 copy-start.7
  182.2 26.2 %all-to-all-start.2 = ((bf16[4,256,384]{2,1,0:T(8,128)(2,1)}), bf16[4,256,384]{2,1,0:T(8,128)(2,1)S(1)}, u32[]{:S(2)}, u32[]{:S(2)}) async-start(bf16[4,256,384]{2,1,0:T(8,128)(2,1)} %bitcast.78), calls=%async_computation.2 | async-start | bytes 1572864 | tf_op jit(solution)/shard_map/all_to_all | solution.py:246
  208.4 23.8 %all-to-all-start.3 = ((bf16[4,256,384]{2,1,0:T(8,128)(2,1)}), bf16[4,256,384]{2,1,0:T(8,128)(2,1)S(1)}, u32[]{:S(2)}, u32[]{:S(2)}) async-start(bf16[4,256,384]{2,1,0:T(8,128)(2,1)} %bitcast.77), calls=%async_computation.3 | async-start | bytes 1572864 | tf_op jit(solution)/shard_map/all_to_all | solution.py:246
Sparse Core Ops, SparseCore 0:
  92.4 25.2 all-gather.4
  119.9 29.2 all-gather.2

commit v14 on v11

--- a/solution.py
+++ b/solution.py
@@ -172,7 +172,7 @@
     ]
 
     def query_a2a(piece):
-        return head_permutes(piece)
+        return lax.all_to_all(piece, "head", split_axis=1, concat_axis=0, tiled=True)
 
     draft_keys = lax.all_gather(pool_tokens(key_rows), "seq", axis=0, tiled=True)
     draft_values = lax.all_gather(pool_tokens(value_rows), "seq", axis=0, tiled=True)
@@ -210,7 +210,10 @@
 
     remote_keys = exchange(key_rows)
     remote_values = exchange(value_rows)
-    query_parts = [query_a2a(piece) for piece in query_slices]
+    leading, remote_values = lax.optimization_barrier((query_slices[0], remote_values))
+    query_parts = [query_a2a(leading)]
+    later, remote_keys = lax.optimization_barrier((query_slices[1:], remote_keys))
+    query_parts += [query_a2a(piece) for piece in later]
 
     own_lists = lax.dynamic_slice_in_dim(block_lists, seq_index * per_dev, per_dev, 0)
     owners = own_lists // per_dev

time: 238 us -> 222 us (0.933)
  starting transfers between devices: 54.6 us -> 35.5 us
  waiting for transfers between devices: 52.5 us -> 65.9 us
  other arithmetic: 31.2 us -> 23.1 us
  local copies, waits for them, and re-layouts: 40.6 us -> 37.7 us
    ppermute x9 -> x3, starting transfers between devices: 40.4 us -> 6.06 us  [head_permutes(): lax.ppermute(piece, 'head', [(i, (i + shift) % count) for i in range(coun...]
    ppermute x9 -> x3, waiting for transfers between devices: 4.38 us -> 30.4 us  [head_permutes(): lax.ppermute(piece, 'head', [(i, (i + shift) % count) for i in range(coun...]
    all_to_all x0 -> x2, starting transfers between devices: none -> 9.93 us  [query_a2a(): lax.all_to_all(piece, 'head', split_axis=1, concat_axis=0, tiled=True)]
    ppermute x6, waiting for transfers between devices: 26 us -> 17.6 us  [exchange(): lax.ppermute(parcel, 'seq', [(i, (i + shift) % seq_count) for i in range(...]
    dynamic_slice x9 -> x3, local copies, waits for them, and re-layouts: 7.7 us -> 2.76 us  [head_permutes(): lax.dynamic_index_in_dim(chunks, (me + shift) % count, axis=1, keepdims=F...]
    another operation x3 -> x1, other arithmetic: 6.13 us -> 1.37 us  [head_permutes(): stacked = jnp.stack(by_shift, axis=0)]
    gather x4 -> x2, local copies, waits for them, and re-layouts: 7.73 us -> 3.55 us  [head_permutes(): jnp.take(stacked, order, axis=0).reshape(count * rows, total // count)]
    unnamed x44 -> x21, local copies, waits for them, and re-layouts: 5.3 us -> 1.83 us
  transfers between devices with their start and end apart: 20 -> 16, of which waited for: 10 -> 9; matrix products, arithmetic and copies ran while one was open for 28% -> 26% of each run, Pallas kernels for 19% -> 20%
where the time goes in v14:
time: 222 us; the launch traced here: 220 us
  waiting for transfers between devices  65.9 us (30%)
  Pallas kernels  43.9 us (20%)
  local copies, waits for them, and re-layouts  37.7 us (17%)
  starting transfers between devices  35.5 us (16%)
  other arithmetic  23.1 us (10%)
  between operations  14.4 us (6%)
    pallas_call x2, Pallas kernels, sparse_attention(): pl.pallas_call(sparse_kernel, out_shape=jax.ShapeDtypeStruct((rows, heads...  30.8 us
    ppermute x3, waiting for transfers between devices, head_permutes(): lax.ppermute(piece, 'head', [(i, (i + shift) % count) for i in range(coun...  30.4 us
    ppermute x6, waiting for transfers between devices, exchange(): lax.ppermute(parcel, 'seq', [(i, (i + shift) % seq_count) for i in range(...  17.6 us
    pallas_call x2, Pallas kernels, draft_attention(): pl.pallas_call(draft_kernel, out_shape=jax.ShapeDtypeStruct((rows, width)...  13.1 us
    all_to_all x2, starting transfers between devices, query_a2a(): lax.all_to_all(piece, 'head', split_axis=1, concat_axis=0, tiled=True)  9.93 us
    all_to_all x2, waiting for transfers between devices, on_device(): lax.all_to_all(rows_part, 'head', split_axis=0, concat_axis=1, tiled=True)  9.01 us
    all_to_all x1, waiting for transfers between devices, on_device(): lax.all_to_all(key_in, 'head', split_axis=1, concat_axis=0, tiled=True)  8.93 us
    all_to_all x2, starting transfers between devices, on_device(): lax.all_to_all(rows_part, 'head', split_axis=0, concat_axis=1, tiled=True)  8.64 us
  transfers between devices with their start and end apart: 16, of which 9 were waited for; matrix products, arithmetic and copies ran while one was open for 26% of the time, Pallas kernels for 20%

profile of v14, /device:TPU:0, one launch (start us, length us, event | category | flops | bytes accessed | tf_op | source)
XLA Modules:
  0.0 220.5 jit_solution(5225946306941589933)
XLA Ops:
  10.0 5.0 %collective-permute-start.2 = (bf16[256,768]{1,0:T(8,128)(2,1)}, bf16[256,768]{1,0:T(8,128)(2,1)S(1)}, u32[]{:S(2)}, u32[]{:S(2)}) collective-permute-start(bf16[256,768]{1,0:T(8,128)(2,1)} %bitcast.9), channel_id=1, source_target_pairs={{0,3},{1,0},{2,1},{3,2},{4,7},{5,4},{6,5},{7,6},{8,11},{9,8},{10,9... | collective-permute-start | bytes 1179656 | tf_op jit(solution)/shard_map/ppermute | solution.py:154
  19.1 4.8 %all-to-all-start.1 = ((bf16[256,4,768]{2,0,1:T(8,128)(2,1)}), bf16[256,4,768]{2,0,1:T(8,128)(2,1)S(1)}, u32[]{:S(2)}, u32[]{:S(2)}) async-start(bf16[256,4,768]{2,0,1:T(8,128)(2,1)} %bitcast.63), calls=%async_computation.1 | async-start | bytes 3145728 | tf_op jit(solution)/shard_map/all_to_all | solution.py:162
  29.2 5.0 %collective-permute-done = bf16[256,768]{1,0:T(8,128)(2,1)S(1)} collective-permute-done((bf16[256,768]{1,0:T(8,128)(2,1)}, bf16[256,768]{1,0:T(8,128)(2,1)S(1)}, u32[]{:S(2)}, u32[]{:S(2)}) %collective-permute-start) | collective-permute-done | bytes 393248 | tf_op jit(solution)/shard_map/ppermute | solution.py:154
  34.2 25.3 %collective-permute-done.1 = bf16[256,768]{1,0:T(8,128)(2,1)S(1)} collective-permute-done((bf16[256,768]{1,0:T(8,128)(2,1)}, bf16[256,768]{1,0:T(8,128)(2,1)S(1)}, u32[]{:S(2)}, u32[]{:S(2)}) %collective-permute-start.1) | collective-permute-done | bytes 393248 | tf_op jit(solution)/shard_map/ppermute | solution.py:154
  64.5 3.6 %convert_reduce_fusion = f32[256,768]{1,0:T(8,128)S(1)} fusion(bf16[256,4,768]{2,1,0:T(4,128)(2,1)} %gather.20, pred[256]{0:T(512)(128)(4,1)S(1)} %copy-done.5), kind=kLoop, calls=%fused_computation.4 | loop fusion | flops 2162688 | bytes 2359552 | tf_op jit(solution)/shard_map/reduce_sum | solution.py:20
  70.3 3.3 %gather_fusion.2 = bf16[8,128,768]{2,1,0:T(8,128)(2,1)} fusion(bf16[8,128,768]{2,1,0:T(8,128)(2,1)} %broadcast_select_fusion.2, s32[1024]{0:T(1024)} %pad_clamp_fusion), kind=kCustom, calls=%fused_computation.clone | custom fusion | bytes 3145760 | tf_op jit(solution)/shard_map/jit(_take)/gather | solution.py:197
  73.6 8.9 %all-to-all-done.1 = bf16[256,4,768]{2,0,1:T(8,128)(2,1)S(1)} async-done(((bf16[256,4,768]{2,0,1:T(8,128)(2,1)}), bf16[256,4,768]{2,0,1:T(8,128)(2,1)S(1)}, u32[]{:S(2)}, u32[]{:S(2)}) %all-to-all-start.1) | async-done | bytes 1572896 | tf_op jit(solution)/shard_map/all_to_all | solution.py:162
  84.6 3.5 %broadcast_select_fusion.1 = (bf16[8,128,768]{2,1,0:T(8,128)(2,1)S(1)}, bf16[8,128,768]{2,1,0:T(8,128)(2,1)}) fusion(bf16[8,128,768]{2,1,0:T(8,128)(2,1)} %gather_fusion.2, pred[8]{0:T(512)(128)(4,1)S(1)} %copy-done.4, bf16[8,128,768]{2,1,0:T(8,128)(2,1)} %gather_fusion.3), kind=kLoop, calls=%fused_computation.11 | loop fusion | flops 1572864 | bytes 6291464 | tf_op jit(solution)/shard_map/jit(_take)/select_n | solution.py:197
  94.7 2.6 %fusion.14 = (bf16[256,4,384]{0,2,1:T(8,128)(2,1)}, bf16[256,4,384]{0,2,1:T(8,128)(2,1)}) fusion(bf16[256,4,768]{0,2,1:T(8,128)(2,1)} %bitcast.69), kind=kLoop, calls=%fused_computation.75 | loop fusion | bytes 3145728 | tf_op jit(solution)/shard_map/slice | solution.py:171
  97.3 6.5 %collective-permute-done.3 = bf16[2,128,768]{2,1,0:T(8,128)(2,1)} collective-permute-done((bf16[2,128,768]{2,1,0:T(8,128)(2,1)}, bf16[2,128,768]{2,1,0:T(8,128)(2,1)}, u32[]{:S(2)}, u32[]{:S(2)}) %collective-permute-start.3) | collective-permute-done | bytes 393248 | tf_op jit(solution)/shard_map/ppermute | solution.py:205
  104.3 6.0 %collective-permute-done.5 = bf16[2,128,768]{2,1,0:T(8,128)(2,1)} collective-permute-done((bf16[2,128,768]{2,1,0:T(8,128)(2,1)S(1)}, bf16[2,128,768]{2,1,0:T(8,128)(2,1)}, u32[]{:S(2)}, u32[]{:S(2)}) %collective-permute-start.5) | collective-permute-done | bytes 393248 | tf_op jit(solution)/shard_map/ppermute | solution.py:205
  110.2 4.8 %all-to-all-start = ((bf16[256,4,384]{0,2,1:T(8,128)(2,1)}), bf16[256,4,384]{0,2,1:T(8,128)(2,1)}, u32[]{:S(2)}, u32[]{:S(2)}) async-start(bf16[256,4,384]{0,2,1:T(8,128)(2,1)} %get-tuple-element.28), calls=%async_computation | async-start | bytes 1572864 | tf_op jit(solution)/shard_map/all_to_all | solution.py:175
  122.3 4.9 %reshape.170 = f32[256,4,768]{2,1,0:T(4,128)} reshape(f32[4,256,768]{2,1,0:T(8,128)} %bitcast_convert_fusion) | data formatting | bytes 6291456 | tf_op jit(solution)/shard_map/convert_element_type | solution.py:19
  127.1 3.8 %reduce_sum.28 = f32[256,768]{1,0:T(8,128)S(1)} reduce(f32[256,4,768]{2,1,0:T(4,128)} %reshape.170, f32[]{:T(128)} %constant.170.clone.1), dimensions={1}, to_apply=%region_4.6 | reduce | flops 589824 | bytes 3932164 | tf_op jit(solution)/shard_map/reduce_sum | solution.py:20
  131.7 4.7 %collective-permute-done.8 = bf16[2,128,768]{2,1,0:T(8,128)(2,1)} collective-permute-done((bf16[2,128,768]{2,1,0:T(8,128)(2,1)S(1)}, bf16[2,128,768]{2,1,0:T(8,128)(2,1)}, u32[]{:S(2)}, u32[]{:S(2)}) %collective-permute-start.8) | collective-permute-done | bytes 393248 | tf_op jit(solution)/shard_map/ppermute | solution.py:205
  136.5 5.1 %all-to-all-start.2 = ((bf16[256,4,384]{0,2,1:T(8,128)(2,1)}), bf16[256,4,384]{0,2,1:T(8,128)(2,1)S(1)}, u32[]{:S(2)}, u32[]{:S(2)}) async-start(bf16[256,4,384]{0,2,1:T(8,128)(2,1)} %get-tuple-element.29), calls=%async_computation.2 | async-start | bytes 1572864 | tf_op jit(solution)/shard_map/all_to_all | solution.py:175
  147.7 15.4 %shard_map.62 = bf16[1024,384]{1,0:T(8,128)(2,1)} custom-call(s32[96]{0:T(128)} %reshape.162.tbl_ref, bf16[1024,384]{1,0:T(8,128)(2,1)} %bitcast.76, bf16[1024,768]{1,0:T(8,128)(2,1)} %bitcast.67, bf16[1024,768]{1,0:T(8,128)(2,1)} %bitcast_select_fusion.refs_1_, bf16[256,768]{1,0:T(8,128)(2,1)} %bitcast.29.refs_2_, bf16[256,768]{1,0:T(8,128)(2,1)} %bitcast.31.refs_3_, ...), custom_call_target="tpu_custom_call" | custom-call | flops 2415919104 | bytes 4325376 | tf_op jit(solution)/shard_map/pallas_call | solution.py:86
  163.1 5.1 %all-to-all-start.3 = ((bf16[4,256,384]{2,1,0:T(8,128)(2,1)}), bf16[4,256,384]{2,1,0:T(8,128)(2,1)S(1)}, u32[]{:S(2)}, u32[]{:S(2)}) async-start(bf16[4,256,384]{2,1,0:T(8,128)(2,1)} %bitcast.84), calls=%async_computation.3 | async-start | bytes 1572864 | tf_op jit(solution)/shard_map/all_to_all | solution.py:236
  169.4 15.4 %shard_map.59 = bf16[1024,384]{1,0:T(8,128)(2,1)} custom-call(s32[96]{0:T(128)} %reshape.162.tbl_ref, bf16[1024,384]{1,0:T(8,128)(2,1)} %bitcast.78, bf16[1024,768]{1,0:T(8,128)(2,1)} %bitcast.68, bf16[1024,768]{1,0:T(8,128)(2,1)} %bitcast_select_fusion.refs_1_, bf16[256,768]{1,0:T(8,128)(2,1)} %bitcast.29.refs_2_, bf16[256,768]{1,0:T(8,128)(2,1)} %bitcast.31.refs_3_, ...), custom_call_target="tpu_custom_call" | custom-call | flops 2415919104 | bytes 4325376 | tf_op jit(solution)/shard_map/pallas_call | solution.py:86
  184.8 4.1 %all-to-all-done.3 = bf16[4,256,384]{2,1,0:T(8,128)(2,1)S(1)} async-done(((bf16[4,256,384]{2,1,0:T(8,128)(2,1)}), bf16[4,256,384]{2,1,0:T(8,128)(2,1)S(1)}, u32[]{:S(2)}, u32[]{:S(2)}) %all-to-all-start.3) | async-done | bytes 786464 | tf_op jit(solution)/shard_map/all_to_all | solution.py:236
  188.9 3.5 %all-to-all-start.4 = ((bf16[4,256,384]{2,1,0:T(8,128)(2,1)}), bf16[4,256,384]{2,1,0:T(8,128)(2,1)S(1)}, u32[]{:S(2)}, u32[]{:S(2)}) async-start(bf16[4,256,384]{2,1,0:T(8,128)(2,1)} %bitcast.83), calls=%async_computation.4 | async-start | bytes 1572864 | tf_op jit(solution)/shard_map/all_to_all | solution.py:236
  192.4 6.5 %shard_map.60 = bf16[256,384]{1,0:T(8,128)(2,1)} custom-call(bf16[1024,384]{1,0:T(8,128)(2,1)} %bitcast.77, bf16[1024,768]{1,0:T(8,128)(2,1)} %all-gather.3.cloned.1.call-done.k_ref, bf16[1024,768]{1,0:T(8,128)(2,1)} %all-gather.5.cloned.1.call-done.v_ref), custom_call_target="tpu_custom_call" | custom-call | flops 503316480 | bytes 2555904 | tf_op jit(solution)/shard_map/pallas_call | solution.py:131
  199.0 6.6 %shard_map.61 = bf16[256,384]{1,0:T(8,128)(2,1)} custom-call(bf16[1024,384]{1,0:T(8,128)(2,1)} %bitcast.79, bf16[1024,768]{1,0:T(8,128)(2,1)} %all-gather.3.cloned.1.call-done.k_ref, bf16[1024,768]{1,0:T(8,128)(2,1)} %all-gather.5.cloned.1.call-done.v_ref), custom_call_target="tpu_custom_call" | custom-call | flops 503316480 | bytes 2555904 | tf_op jit(solution)/shard_map/pallas_call | solution.py:131
  207.2 4.9 %all-to-all-done.4 = bf16[4,256,384]{2,1,0:T(8,128)(2,1)S(1)} async-done(((bf16[4,256,384]{2,1,0:T(8,128)(2,1)}), bf16[4,256,384]{2,1,0:T(8,128)(2,1)S(1)}, u32[]{:S(2)}, u32[]{:S(2)}) %all-to-all-start.4) | async-done | bytes 786464 | tf_op jit(solution)/shard_map/all_to_all | solution.py:236
  (96 shorter events, 46.7 us)
Async XLA Ops:
  9.1 8.8 %copy-start.1 = (bf16[256,3072]{1,0:T(8,128)(2,1)S(1)}, bf16[256,3072]{1,0:T(8,128)(2,1)}, u32[]{:S(2)}) copy-start(bf16[256,3072]{1,0:T(8,128)(2,1)} %param.7) | copy-start | bytes 4718596
  10.0 19.2 %collective-permute-start.2 = (bf16[256,768]{1,0:T(8,128)(2,1)}, bf16[256,768]{1,0:T(8,128)(2,1)S(1)}, u32[]{:S(2)}, u32[]{:S(2)}) collective-permute-start(bf16[256,768]{1,0:T(8,128)(2,1)} %bitcast.9), channel_id=1, source_target_pairs={{0,3},{1,0},{2,1},{3,2},{4,7},{5,4},{6,5},{7,6},{8,11},{9,8},{10,9... | collective-permute-start | bytes 1179656 | tf_op jit(solution)/shard_map/ppermute | solution.py:154
  16.0 18.3 %collective-permute-start = (bf16[256,768]{1,0:T(8,128)(2,1)}, bf16[256,768]{1,0:T(8,128)(2,1)S(1)}, u32[]{:S(2)}, u32[]{:S(2)}) collective-permute-start(bf16[256,768]{1,0:T(8,128)(2,1)} %bitcast.5), channel_id=1, source_target_pairs={{0,1},{1,2},{2,3},{3,0},{4,5},{5,6},{6,7},{7,4},{8,9},{9,10},{10,1... | collective-permute-start | bytes 1179656 | tf_op jit(solution)/shard_map/ppermute | solution.py:154
  16.9 42.7 %collective-permute-start.1 = (bf16[256,768]{1,0:T(8,128)(2,1)}, bf16[256,768]{1,0:T(8,128)(2,1)S(1)}, u32[]{:S(2)}, u32[]{:S(2)}) collective-permute-start(bf16[256,768]{1,0:T(8,128)(2,1)} %bitcast.88), channel_id=1, source_target_pairs={{0,2},{1,3},{2,0},{3,1},{4,6},{5,7},{6,4},{7,5},{8,10},{9,11},{10,... | collective-permute-start | bytes 1179656 | tf_op jit(solution)/shard_map/ppermute | solution.py:154
  19.1 4.8 %copy-start.3 = (s32[32,12]{0,1:T(8,128)S(1)}, s32[32,12]{0,1:T(8,128)}, u32[]{:S(2)}) copy-start(s32[32,12]{0,1:T(8,128)} %param.9) | copy-start | bytes 4612
  19.1 63.4 %all-to-all-start.1 = ((bf16[256,4,768]{2,0,1:T(8,128)(2,1)}), bf16[256,4,768]{2,0,1:T(8,128)(2,1)S(1)}, u32[]{:S(2)}, u32[]{:S(2)}) async-start(bf16[256,4,768]{2,0,1:T(8,128)(2,1)} %bitcast.63), calls=%async_computation.1 | async-start | bytes 3145728 | tf_op jit(solution)/shard_map/all_to_all | solution.py:162
  23.9 160.9 %all-gather.5.cloned.1.call-start = ((), (), s32[]{:S(2)}) async-start(), calls=%async_computation.6 | async-start | bytes 1966080 | tf_op jit(solution)/shard_map/all_gather | solution.py:178
  23.9 1.9 copy-start.7
  64.5 4.4 %copy-start.6 = (pred[8]{0:T(512)(128)(4,1)S(1)}, pred[8]{0:T(512)(128)(4,1)}, u32[]{:S(2)}) copy-start(pred[8]{0:T(512)(128)(4,1)} %broadcast_in_dim.64) | copy-start | bytes 28
  82.5 37.8 %copy-start = (bf16[256,4,768]{2,0,1:T(8,128)(2,1)}, bf16[256,4,768]{2,0,1:T(8,128)(2,1)S(1)}, u32[]{:S(2)}) copy-start(bf16[256,4,768]{2,0,1:T(8,128)(2,1)S(1)} %all-to-all-done.1) | copy-start | bytes 4718596
  82.5 2.0 copy-start.4
  89.1 14.8 %collective-permute-start.3 = (bf16[2,128,768]{2,1,0:T(8,128)(2,1)}, bf16[2,128,768]{2,1,0:T(8,128)(2,1)}, u32[]{:S(2)}, u32[]{:S(2)}) collective-permute-start(bf16[2,128,768]{2,1,0:T(8,128)(2,1)} %get-tuple-element.27), channel_id=1, source_target_pairs={{0,4},{4,8},{8,12},{12,0},{1,5},{5,9},{9,13},{13,1},{2,6},{6,10},{... | collective-permute-start | bytes 1179656 | tf_op jit(solution)/shard_map/ppermute | solution.py:205
  89.1 15.2 %collective-permute-start.4 = (bf16[2,128,768]{2,1,0:T(8,128)(2,1)}, bf16[2,128,768]{2,1,0:T(8,128)(2,1)}, u32[]{:S(2)}, u32[]{:S(2)}) collective-permute-start(bf16[2,128,768]{2,1,0:T(8,128)(2,1)} %get-tuple-element.26), channel_id=1, source_target_pairs={{0,8},{4,12},{8,0},{12,4},{1,9},{5,13},{9,1},{13,5},{2,10},{6,14},... | collective-permute-start | bytes 1179656 | tf_op jit(solution)/shard_map/ppermute | solution.py:205
  90.7 19.5 %collective-permute-start.5 = (bf16[2,128,768]{2,1,0:T(8,128)(2,1)S(1)}, bf16[2,128,768]{2,1,0:T(8,128)(2,1)}, u32[]{:S(2)}, u32[]{:S(2)}) collective-permute-start(bf16[2,128,768]{2,1,0:T(8,128)(2,1)S(1)} %get-tuple-element.25), channel_id=1, source_target_pairs={{0,12},{4,0},{8,4},{12,8},{1,13},{5,1},{9,5},{13,9},{2,14},{6,2},{... | collective-permute-start | bytes 1179656 | tf_op jit(solution)/shard_map/ppermute | solution.py:205
  110.2 26.2 %all-to-all-start = ((bf16[256,4,384]{0,2,1:T(8,128)(2,1)}), bf16[256,4,384]{0,2,1:T(8,128)(2,1)}, u32[]{:S(2)}, u32[]{:S(2)}) async-start(bf16[256,4,384]{0,2,1:T(8,128)(2,1)} %get-tuple-element.28), calls=%async_computation | async-start | bytes 1572864 | tf_op jit(solution)/shard_map/all_to_all | solution.py:175
  115.1 69.8 %all-gather.3.cloned.1.call-start = ((), (), s32[]{:S(2)}) async-start(), calls=%async_computation.5 | async-start | bytes 1966080 | tf_op jit(solution)/shard_map/all_gather | solution.py:177
  117.4 14.3 %collective-permute-start.6 = (bf16[2,128,768]{2,1,0:T(8,128)(2,1)}, bf16[2,128,768]{2,1,0:T(8,128)(2,1)}, u32[]{:S(2)}, u32[]{:S(2)}) collective-permute-start(bf16[2,128,768]{2,1,0:T(8,128)(2,1)} %get-tuple-element.36), channel_id=1, source_target_pairs={{0,4},{4,8},{8,12},{12,0},{1,5},{5,9},{9,13},{13,1},{2,6},{6,10},{... | collective-permute-start | bytes 1179656 | tf_op jit(solution)/shard_map/ppermute | solution.py:205
  119.0 12.7 %collective-permute-start.7 = (bf16[2,128,768]{2,1,0:T(8,128)(2,1)}, bf16[2,128,768]{2,1,0:T(8,128)(2,1)}, u32[]{:S(2)}, u32[]{:S(2)}) collective-permute-start(bf16[2,128,768]{2,1,0:T(8,128)(2,1)} %get-tuple-element.35), channel_id=1, source_target_pairs={{0,8},{4,12},{8,0},{12,4},{1,9},{5,13},{9,1},{13,5},{2,10},{6,14},... | collective-permute-start | bytes 1179656 | tf_op jit(solution)/shard_map/ppermute | solution.py:205
  119.5 16.9 %collective-permute-start.8 = (bf16[2,128,768]{2,1,0:T(8,128)(2,1)S(1)}, bf16[2,128,768]{2,1,0:T(8,128)(2,1)}, u32[]{:S(2)}, u32[]{:S(2)}) collective-permute-start(bf16[2,128,768]{2,1,0:T(8,128)(2,1)S(1)} %get-tuple-element.34), channel_id=1, source_target_pairs={{0,12},{4,0},{8,4},{12,8},{1,13},{5,1},{9,5},{13,9},{2,14},{6,2},{... | collective-permute-start | bytes 1179656 | tf_op jit(solution)/shard_map/ppermute | solution.py:205
  130.9 10.7 %copy-start.8 = (pred[4]{0:T(512)(128)(4,1)S(1)}, pred[4]{0:T(512)(128)(4,1)}, u32[]{:S(2)}) copy-start(pred[4]{0:T(512)(128)(4,1)} %copy-done.7) | copy-start | bytes 16
  136.5 26.7 %all-to-all-start.2 = ((bf16[256,4,384]{0,2,1:T(8,128)(2,1)}), bf16[256,4,384]{0,2,1:T(8,128)(2,1)S(1)}, u32[]{:S(2)}, u32[]{:S(2)}) async-start(bf16[256,4,384]{0,2,1:T(8,128)(2,1)} %get-tuple-element.29), calls=%async_computation.2 | async-start | bytes 1572864 | tf_op jit(solution)/shard_map/all_to_all | solution.py:175
  163.1 25.8 %all-to-all-start.3 = ((bf16[4,256,384]{2,1,0:T(8,128)(2,1)}), bf16[4,256,384]{2,1,0:T(8,128)(2,1)S(1)}, u32[]{:S(2)}, u32[]{:S(2)}) async-start(bf16[4,256,384]{2,1,0:T(8,128)(2,1)} %bitcast.84), calls=%async_computation.3 | async-start | bytes 1572864 | tf_op jit(solution)/shard_map/all_to_all | solution.py:236
  188.9 23.3 %all-to-all-start.4 = ((bf16[4,256,384]{2,1,0:T(8,128)(2,1)}), bf16[4,256,384]{2,1,0:T(8,128)(2,1)S(1)}, u32[]{:S(2)}, u32[]{:S(2)}) async-start(bf16[4,256,384]{2,1,0:T(8,128)(2,1)} %bitcast.83), calls=%async_computation.4 | async-start | bytes 1572864 | tf_op jit(solution)/shard_map/all_to_all | solution.py:236
  199.0 6.6 %copy-start.2 = (bf16[256,384]{1,0:T(8,128)(2,1)S(1)}, bf16[256,384]{1,0:T(8,128)(2,1)}, u32[]{:S(2)}) copy-start(bf16[256,384]{1,0:T(8,128)(2,1)} %shard_map.60) | copy-start | bytes 589828
  (1 other events, 1.4 us)
Sparse Core Ops, SparseCore 0:
  69.0 31.2 all-gather.4
  131.8 20.1 all-gather.2

commit v15 on v12

--- a/solution.py
+++ b/solution.py
@@ -158,6 +158,32 @@
     return jnp.take(stacked, order, axis=0).reshape(count * rows, total // count)
 
 
+def parcel_kernel(tbl_ref, k_ref, v_ref, ko_ref, vo_ref):
+    ko_ref[...] = k_ref[...]
+    vo_ref[...] = v_ref[...]
+
+
+def build_parcels(send_table, keys, values):
+    slots = send_table.shape[0]
+    width = keys.shape[1]
+    pick = pl.BlockSpec((BLOCK, width), lambda s, t: (t[s], 0))
+    place = pl.BlockSpec((BLOCK, width), lambda s, t: (s, 0))
+    shape = jax.ShapeDtypeStruct((slots * BLOCK, width), keys.dtype)
+    return pl.pallas_call(
+        parcel_kernel,
+        out_shape=(shape, shape),
+        grid_spec=pltpu.PrefetchScalarGridSpec(
+            num_scalar_prefetch=1,
+            grid=(slots,),
+            in_specs=[pick, pick],
+            out_specs=(place, place),
+        ),
+        cost_estimate=pl.CostEstimate(
+            flops=0, transcendentals=0, bytes_accessed=8 * slots * BLOCK * width
+        ),
+    )(send_table, keys, values)
+
+
 def on_device(query_in, key_in, value_in, block_lists):
     key_rows = lax.all_to_all(key_in, "head", split_axis=1, concat_axis=0, tiled=True)
     value_rows = head_permutes(value_in)
@@ -186,24 +212,24 @@
     )
     send_idx = jnp.sum(
         jnp.where(slot_hit, jnp.arange(per_dev, dtype=jnp.int32)[None, None, :], 0), axis=2
-    ).reshape(-1)
-    def exchange(rows):
-        blocks = jnp.take(rows.reshape(per_dev, BLOCK, width), send_idx, axis=0)
-        outgoing = blocks.reshape(seq_count, CAP, BLOCK, width)
+    )
+    peers = (seq_index + jnp.arange(1, seq_count, dtype=jnp.int32)) % seq_count
+    send_table = jnp.clip(jnp.take(send_idx, peers, axis=0), 0, per_dev - 1).reshape(-1)
+    key_parcels, value_parcels = build_parcels(send_table, key_rows, value_rows)
+
+    def exchange(parcels):
         arrivals = []
         for shift in range(1, seq_count):
-            parcel = lax.dynamic_index_in_dim(
-                outgoing, (seq_index + shift) % seq_count, axis=0, keepdims=False
-            )
+            parcel = parcels[(shift - 1) * CAP * BLOCK:shift * CAP * BLOCK]
             arrivals.append(
                 lax.ppermute(
                     parcel, "seq", [(i, (i + shift) % seq_count) for i in range(seq_count)]
                 )
             )
-        return [a.reshape(CAP * BLOCK, width) for a in arrivals]
-
-    remote_keys = exchange(key_rows)
-    remote_values = exchange(value_rows)
+        return arrivals
+
+    remote_keys = exchange(key_parcels)
+    remote_values = exchange(value_parcels)
 
     own_lists = lax.dynamic_slice_in_dim(block_lists, seq_index * per_dev, per_dev, 0)
     owners = own_lists // per_dev

time: 228 us -> 240 us (1.053)
  waiting for transfers between devices: 90.1 us -> 96.7 us
  starting transfers between devices: 29 us -> 34.8 us
  Pallas kernels: 42.6 us -> 48.3 us
  other arithmetic: 20.9 us -> 15.4 us
    ppermute x3, waiting for transfers between devices: 26.1 us -> 48.6 us  [head_permutes(): lax.ppermute(piece, 'head', [(i, (i + shift) % count) for i in range(coun...]
    all_to_all x1, waiting for transfers between devices: 17.3 us -> 0.01 us  [on_device(): lax.all_to_all(key_in, 'head', split_axis=1, concat_axis=0, tiled=True)]
    pallas_call x0 -> x1, Pallas kernels: none -> 5.72 us  [build_parcels(): pl.pallas_call(parcel_kernel, out_shape=(shape, shape), grid_spec=pltpu.P...]
    all_to_all x1, starting transfers between devices: 4.81 us -> 10.1 us  [on_device(): lax.all_to_all(query_in, 'head', split_axis=1, concat_axis=0, tiled=True)]
    all_to_all x1, waiting for transfers between devices: 4.41 us -> 9.23 us  [on_device(): lax.all_to_all(query_in, 'head', split_axis=1, concat_axis=0, tiled=True)]
    gather x2 -> x1, local copies, waits for them, and re-layouts: 5.05 us -> 0.56 us  [on_device(): jnp.take(send_idx, peers, axis=0)]
    select_n x2 -> x1, other arithmetic: 3.4 us -> 0.01 us  [on_device(): jnp.take(send_idx, peers, axis=0)]
    all_to_all x2, waiting for transfers between devices: 14.5 us -> 11.7 us  [on_device(): lax.all_to_all(rows_part, 'head', split_axis=0, concat_axis=1, tiled=True)]
  transfers between devices with their start and end apart: 15 -> 15, of which waited for: 11 -> 9; matrix products, arithmetic and copies ran while one was open for 20% -> 16% of each run, Pallas kernels for 19% -> 20%
where the time goes in v15:
time: 240 us; the launch traced here: 239 us
  waiting for transfers between devices  96.7 us (40%)
  Pallas kernels  48.3 us (20%)
  starting transfers between devices  34.8 us (14%)
  local copies, waits for them, and re-layouts  30 us (12%)
  other arithmetic  15.4 us (6%)
  between operations  14.3 us (6%)
    ppermute x3, waiting for transfers between devices, head_permutes(): lax.ppermute(piece, 'head', [(i, (i + shift) % count) for i in range(coun...  48.6 us
    pallas_call x2, Pallas kernels, sparse_attention(): pl.pallas_call(sparse_kernel, out_shape=jax.ShapeDtypeStruct((rows, heads...  30.7 us
    ppermute x6, waiting for transfers between devices, exchange(): lax.ppermute(parcel, 'seq', [(i, (i + shift) % seq_count) for i in range(...  27.1 us
    pallas_call x1, Pallas kernels, draft_attention(): pl.pallas_call(draft_kernel, out_shape=jax.ShapeDtypeStruct((rows, width)...  11.8 us
    all_to_all x2, waiting for transfers between devices, on_device(): lax.all_to_all(rows_part, 'head', split_axis=0, concat_axis=1, tiled=True)  11.7 us
    all_to_all x1, starting transfers between devices, on_device(): lax.all_to_all(query_in, 'head', split_axis=1, concat_axis=0, tiled=True)  10.1 us
    all_to_all x1, waiting for transfers between devices, on_device(): lax.all_to_all(query_in, 'head', split_axis=1, concat_axis=0, tiled=True)  9.23 us
    all_to_all x2, starting transfers between devices, on_device(): lax.all_to_all(rows_part, 'head', split_axis=0, concat_axis=1, tiled=True)  8.59 us
  transfers between devices with their start and end apart: 15, of which 9 were waited for; matrix products, arithmetic and copies ran while one was open for 16% of the time, Pallas kernels for 20%

profile of v15, /device:TPU:0, one launch (start us, length us, event | category | flops | bytes accessed | tf_op | source)
XLA Modules:
  0.0 239.4 jit_solution(7277452244242912237)
XLA Ops:
  7.2 2.7 %copy.57 = bf16[32,4,8,768]{3,2,0,1:T(8,128)(2,1)} copy(bf16[32,4,8,768]{3,2,1,0:T(8,128)(2,1)} %bitcast.49) | data formatting | bytes 3145728 | tf_op jit(solution)/shard_map/all_to_all | solution.py:188
  9.9 6.3 %all-to-all-start.1 = ((bf16[256,4,768]{2,0,1:T(8,128)(2,1)}), bf16[256,4,768]{2,0,1:T(8,128)(2,1)S(1)}, u32[]{:S(2)}, u32[]{:S(2)}) async-start(bf16[256,4,768]{2,0,1:T(8,128)(2,1)} %bitcast.39), calls=%async_computation.1 | async-start | bytes 3145728 | tf_op jit(solution)/shard_map/all_to_all | solution.py:188
  24.9 2.4 collective-permute-start.1
  30.8 24.8 %collective-permute-done = bf16[256,768]{1,0:T(8,128)(2,1)S(1)} collective-permute-done((bf16[256,768]{1,0:T(8,128)(2,1)}, bf16[256,768]{1,0:T(8,128)(2,1)S(1)}, u32[]{:S(2)}, u32[]{:S(2)}) %collective-permute-start) | collective-permute-done | bytes 393248 | tf_op jit(solution)/shard_map/ppermute | solution.py:154
  55.6 23.9 %collective-permute-done.1 = bf16[256,768]{1,0:T(8,128)(2,1)S(1)} collective-permute-done((bf16[256,768]{1,0:T(8,128)(2,1)}, bf16[256,768]{1,0:T(8,128)(2,1)S(1)}, u32[]{:S(2)}, u32[]{:S(2)}) %collective-permute-start.1) | collective-permute-done | bytes 393248 | tf_op jit(solution)/shard_map/ppermute | solution.py:154
  80.8 2.1 gather_fusion.1
  84.2 3.6 %convert_reduce_fusion = f32[256,768]{1,0:T(8,128)S(1)} fusion(bf16[256,4,768]{2,1,0:T(4,128)(2,1)} %gather.19, pred[256]{0:T(512)(128)(4,1)S(1)} %copy-done.6), kind=kLoop, calls=%fused_computation.3 | loop fusion | flops 2162688 | bytes 2359552 | tf_op jit(solution)/shard_map/reduce_sum | solution.py:20
  89.9 2.7 %copy.58 = bf16[32,4,8,768]{3,2,0,1:T(8,128)(2,1)} copy(bf16[32,4,8,768]{3,2,1,0:T(8,128)(2,1)} %bitcast.50) | data formatting | bytes 3145728 | tf_op jit(solution)/shard_map/all_to_all | solution.py:195
  94.3 10.1 %all-to-all-start = ((bf16[256,4,768]{2,0,1:T(8,128)(2,1)}), bf16[256,4,768]{2,0,1:T(8,128)(2,1)}, u32[]{:S(2)}, u32[]{:S(2)}) async-start(bf16[256,4,768]{2,0,1:T(8,128)(2,1)} %bitcast.45), calls=%async_computation | async-start | bytes 3145728 | tf_op jit(solution)/shard_map/all_to_all | solution.py:195
  106.7 5.7 %shard_map.59 = (bf16[768,768]{1,0:T(8,128)(2,1)}, bf16[768,768]{1,0:T(8,128)(2,1)}) custom-call(s32[6]{0:T(128)} %min.27.tbl_ref, bf16[1024,768]{1,0:T(8,128)(2,1)} %bitcast.42, bf16[1024,768]{1,0:T(8,128)(2,1)} %bitcast_select_fusion.v_ref.refs_1_), custom_call_target="tpu_custom_call" | custom-call | bytes 4718592 | tf_op jit(solution)/shard_map/pallas_call | solution.py:172
  112.4 2.3 fusion.17
  116.6 3.1 %reshape.172 = f32[256,4,768]{2,1,0:T(4,128)S(1)} reshape(f32[4,256,768]{2,1,0:T(8,128)} %bitcast_convert_fusion) | data formatting | bytes 6291456 | tf_op jit(solution)/shard_map/convert_element_type | solution.py:19
  119.7 3.0 %reduce_sum.28 = f32[256,768]{1,0:T(8,128)} reduce(f32[256,4,768]{2,1,0:T(4,128)S(1)} %reshape.172, f32[]{:T(128)} %constant.153.clone.1), dimensions={1}, to_apply=%region_4.5 | reduce | flops 589824 | bytes 3932164 | tf_op jit(solution)/shard_map/reduce_sum | solution.py:20
  131.1 9.2 %all-to-all-done = bf16[256,4,768]{2,0,1:T(8,128)(2,1)} async-done(((bf16[256,4,768]{2,0,1:T(8,128)(2,1)}), bf16[256,4,768]{2,0,1:T(8,128)(2,1)}, u32[]{:S(2)}, u32[]{:S(2)}) %all-to-all-start) | async-done | bytes 1572896 | tf_op jit(solution)/shard_map/all_to_all | solution.py:195
  140.4 14.1 %collective-permute-done.3.refs_2_ = bf16[256,768]{1,0:T(8,128)(2,1)} collective-permute-done((bf16[256,768]{1,0:T(8,128)(2,1)S(1)}, bf16[256,768]{1,0:T(8,128)(2,1)}, u32[]{:S(2)}, u32[]{:S(2)}) %collective-permute-start.3) | collective-permute-done | bytes 393248 | tf_op jit(solution)/shard_map/ppermute | solution.py:225
  154.5 9.1 %collective-permute-done.7.refs_6_ = bf16[256,768]{1,0:T(8,128)(2,1)S(1)} collective-permute-done((bf16[256,768]{1,0:T(8,128)(2,1)S(1)}, bf16[256,768]{1,0:T(8,128)(2,1)S(1)}, u32[]{:S(2)}, u32[]{:S(2)}) %collective-permute-start.7) | collective-permute-done | bytes 393248 | tf_op jit(solution)/shard_map/ppermute | solution.py:225
  163.6 3.8 %collective-permute-done.6.refs_5_ = bf16[256,768]{1,0:T(8,128)(2,1)S(1)} collective-permute-done((bf16[256,768]{1,0:T(8,128)(2,1)S(1)}, bf16[256,768]{1,0:T(8,128)(2,1)S(1)}, u32[]{:S(2)}, u32[]{:S(2)}) %collective-permute-start.6) | collective-permute-done | bytes 393248 | tf_op jit(solution)/shard_map/ppermute | solution.py:225
  168.2 15.4 %shard_map.62 = bf16[1024,384]{1,0:T(8,128)(2,1)} custom-call(s32[96]{0:T(128)} %reshape.169.tbl_ref, bf16[1024,768]{1,0:T(8,128)(2,1)} %bitcast.1.q_ref, bf16[1024,768]{1,0:T(8,128)(2,1)} %bitcast.43, bf16[1024,768]{1,0:T(8,128)(2,1)} %bitcast_select_fusion.v_ref.refs_1_, bf16[256,768]{1,0:T(8,128)(2,1)} %collective-permute-done.3.refs_2_, ...), custom_call_target="tpu_custom_call" | custom-call | flops 2415919104 | bytes 4325376 | tf_op jit(solution)/shard_map/pallas_call | solution.py:86
  183.5 5.1 %all-to-all-start.2 = ((bf16[4,256,384]{2,1,0:T(8,128)(2,1)}), bf16[4,256,384]{2,1,0:T(8,128)(2,1)S(1)}, u32[]{:S(2)}, u32[]{:S(2)}) async-start(bf16[4,256,384]{2,1,0:T(8,128)(2,1)} %bitcast.54), calls=%async_computation.2 | async-start | bytes 1572864 | tf_op jit(solution)/shard_map/all_to_all | solution.py:253
  188.6 15.4 %shard_map.60 = bf16[1024,384]{1,0:T(8,128)(2,1)} custom-call(s32[96]{0:T(128)} %reshape.169.tbl_ref, bf16[1024,768]{1,0:T(8,128)(2,1)} %bitcast.1.q_ref, bf16[1024,768]{1,0:T(8,128)(2,1)} %bitcast.44, bf16[1024,768]{1,0:T(8,128)(2,1)} %bitcast_select_fusion.v_ref.refs_1_, bf16[256,768]{1,0:T(8,128)(2,1)} %collective-permute-done.3.refs_2_, ...), custom_call_target="tpu_custom_call" | custom-call | flops 2415919104 | bytes 4325376 | tf_op jit(solution)/shard_map/pallas_call | solution.py:86
  204.0 4.0 %all-to-all-done.2 = bf16[4,256,384]{2,1,0:T(8,128)(2,1)S(1)} async-done(((bf16[4,256,384]{2,1,0:T(8,128)(2,1)}), bf16[4,256,384]{2,1,0:T(8,128)(2,1)S(1)}, u32[]{:S(2)}, u32[]{:S(2)}) %all-to-all-start.2) | async-done | bytes 786464 | tf_op jit(solution)/shard_map/all_to_all | solution.py:253
  208.0 3.5 %all-to-all-start.3 = ((bf16[4,256,384]{2,1,0:T(8,128)(2,1)}), bf16[4,256,384]{2,1,0:T(8,128)(2,1)S(1)}, u32[]{:S(2)}, u32[]{:S(2)}) async-start(bf16[4,256,384]{2,1,0:T(8,128)(2,1)} %bitcast.53), calls=%async_computation.3 | async-start | bytes 1572864 | tf_op jit(solution)/shard_map/all_to_all | solution.py:253
  211.5 11.8 %shard_map.61 = bf16[256,768]{1,0:T(8,128)(2,1)} custom-call(bf16[1024,768]{1,0:T(8,128)(2,1)} %bitcast.1.q_ref, bf16[1024,768]{1,0:T(8,128)(2,1)} %all-gather.3.cloned.1.call-done.k_ref, bf16[1024,768]{1,0:T(8,128)(2,1)} %all-gather.5.cloned.1.call-done.v_ref), custom_call_target="tpu_custom_call" | custom-call | flops 1006632960 | bytes 5111808 | tf_op jit(solution)/shard_map/pallas_call | solution.py:131
  223.4 7.7 %all-to-all-done.3 = bf16[4,256,384]{2,1,0:T(8,128)(2,1)S(1)} async-done(((bf16[4,256,384]{2,1,0:T(8,128)(2,1)}), bf16[4,256,384]{2,1,0:T(8,128)(2,1)S(1)}, u32[]{:S(2)}, u32[]{:S(2)}) %all-to-all-start.3) | async-done | bytes 786464 | tf_op jit(solution)/shard_map/all_to_all | solution.py:253
  (88 shorter events, 33.5 us)
Async XLA Ops:
  9.9 83.3 %all-to-all-start.1 = ((bf16[256,4,768]{2,0,1:T(8,128)(2,1)}), bf16[256,4,768]{2,0,1:T(8,128)(2,1)S(1)}, u32[]{:S(2)}, u32[]{:S(2)}) async-start(bf16[256,4,768]{2,0,1:T(8,128)(2,1)} %bitcast.39), calls=%async_computation.1 | async-start | bytes 3145728 | tf_op jit(solution)/shard_map/all_to_all | solution.py:188
  16.2 187.8 %all-gather.5.cloned.1.call-start = ((), (), s32[]{:S(2)}) async-start(), calls=%async_computation.5 | async-start | bytes 1966080 | tf_op jit(solution)/shard_map/all_gather | solution.py:198
  18.9 8.3 %copy-start.2 = (bf16[256,1,768]{0,2,1:T(8,128)(2,1)S(1)}, bf16[256,1,768]{0,2,1:T(8,128)(2,1)}, u32[]{:S(2)}) copy-start(bf16[256,1,768]{0,2,1:T(8,128)(2,1)} %get-tuple-element.13) | copy-start | bytes 1179652
  19.0 11.5 %copy-start.5 = (s32[32,12]{0,1:T(8,128)S(1)}, s32[32,12]{0,1:T(8,128)}, u32[]{:S(2)}) copy-start(s32[32,12]{0,1:T(8,128)} %param.7) | copy-start | bytes 4612
  20.9 34.7 %collective-permute-start = (bf16[256,768]{1,0:T(8,128)(2,1)}, bf16[256,768]{1,0:T(8,128)(2,1)S(1)}, u32[]{:S(2)}, u32[]{:S(2)}) collective-permute-start(bf16[256,768]{1,0:T(8,128)(2,1)} %bitcast.8), channel_id=1, source_target_pairs={{0,1},{1,2},{2,3},{3,0},{4,5},{5,6},{6,7},{7,4},{8,9},{9,10},{10,1... | collective-permute-start | bytes 1179656 | tf_op jit(solution)/shard_map/ppermute | solution.py:154
  24.9 54.6 %collective-permute-start.1 = (bf16[256,768]{1,0:T(8,128)(2,1)}, bf16[256,768]{1,0:T(8,128)(2,1)S(1)}, u32[]{:S(2)}, u32[]{:S(2)}) collective-permute-start(bf16[256,768]{1,0:T(8,128)(2,1)} %bitcast.10), channel_id=1, source_target_pairs={{0,2},{1,3},{2,0},{3,1},{4,6},{5,7},{6,4},{7,5},{8,10},{9,11},{10,... | collective-permute-start | bytes 1179656 | tf_op jit(solution)/shard_map/ppermute | solution.py:154
  28.2 51.3 %collective-permute-start.2 = (bf16[256,768]{1,0:T(8,128)(2,1)}, bf16[256,768]{1,0:T(8,128)(2,1)S(1)}, u32[]{:S(2)}, u32[]{:S(2)}) collective-permute-start(bf16[256,768]{1,0:T(8,128)(2,1)} %bitcast.58), channel_id=1, source_target_pairs={{0,3},{1,0},{2,1},{3,2},{4,7},{5,4},{6,5},{7,6},{8,11},{9,8},{10,9... | collective-permute-start | bytes 1179656 | tf_op jit(solution)/shard_map/ppermute | solution.py:154
  82.9 1.4 copy-start.6
  93.2 1.2 copy-start
  94.3 46.0 %all-to-all-start = ((bf16[256,4,768]{2,0,1:T(8,128)(2,1)}), bf16[256,4,768]{2,0,1:T(8,128)(2,1)}, u32[]{:S(2)}, u32[]{:S(2)}) async-start(bf16[256,4,768]{2,0,1:T(8,128)(2,1)} %bitcast.45), calls=%async_computation | async-start | bytes 3145728 | tf_op jit(solution)/shard_map/all_to_all | solution.py:195
  104.4 99.5 %all-gather.3.cloned.1.call-start = ((), (), s32[]{:S(2)}) async-start(), calls=%async_computation.4 | async-start | bytes 1966080 | tf_op jit(solution)/shard_map/all_gather | solution.py:197
  112.4 2.3 copy-start.1
  114.7 15.6 %collective-permute-start.5 = (bf16[256,768]{1,0:T(8,128)(2,1)}, bf16[256,768]{1,0:T(8,128)(2,1)}, u32[]{:S(2)}, u32[]{:S(2)}) collective-permute-start(bf16[256,768]{1,0:T(8,128)(2,1)} %get-tuple-element.19), channel_id=1, source_target_pairs={{0,12},{4,0},{8,4},{12,8},{1,13},{5,1},{9,5},{13,9},{2,14},{6,2},{... | collective-permute-start | bytes 1179656 | tf_op jit(solution)/shard_map/ppermute | solution.py:225
  124.8 1.5 copy-start.4
  124.8 3.4 %copy-start.3 = (bf16[768,768]{1,0:T(8,128)(2,1)S(1)}, bf16[768,768]{1,0:T(8,128)(2,1)}, u32[]{:S(2)}) copy-start(bf16[768,768]{1,0:T(8,128)(2,1)} %get-tuple-element.8) | copy-start | bytes 3538948
  126.3 14.1 %collective-permute-start.4 = (bf16[256,768]{1,0:T(8,128)(2,1)S(1)}, bf16[256,768]{1,0:T(8,128)(2,1)}, u32[]{:S(2)}, u32[]{:S(2)}) collective-permute-start(bf16[256,768]{1,0:T(8,128)(2,1)S(1)} %copy-done.4), channel_id=1, source_target_pairs={{0,8},{4,12},{8,0},{12,4},{1,9},{5,13},{9,1},{13,5},{2,10},{6,14},... | collective-permute-start | bytes 1179656 | tf_op jit(solution)/shard_map/ppermute | solution.py:225
  127.9 26.6 %collective-permute-start.3 = (bf16[256,768]{1,0:T(8,128)(2,1)S(1)}, bf16[256,768]{1,0:T(8,128)(2,1)}, u32[]{:S(2)}, u32[]{:S(2)}) collective-permute-start(bf16[256,768]{1,0:T(8,128)(2,1)S(1)} %get-tuple-element.21), channel_id=1, source_target_pairs={{0,4},{4,8},{8,12},{12,0},{1,5},{5,9},{9,13},{13,1},{2,6},{6,10},{... | collective-permute-start | bytes 1179656 | tf_op jit(solution)/shard_map/ppermute | solution.py:225
  128.2 26.3 %collective-permute-start.8 = (bf16[256,768]{1,0:T(8,128)(2,1)S(1)}, bf16[256,768]{1,0:T(8,128)(2,1)S(1)}, u32[]{:S(2)}, u32[]{:S(2)}) collective-permute-start(bf16[256,768]{1,0:T(8,128)(2,1)S(1)} %get-tuple-element.16), channel_id=1, source_target_pairs={{0,12},{4,0},{8,4},{12,8},{1,13},{5,1},{9,5},{13,9},{2,14},{6,2},{... | collective-permute-start | bytes 1179656 | tf_op jit(solution)/shard_map/ppermute | solution.py:225
  129.8 33.8 %collective-permute-start.7 = (bf16[256,768]{1,0:T(8,128)(2,1)S(1)}, bf16[256,768]{1,0:T(8,128)(2,1)S(1)}, u32[]{:S(2)}, u32[]{:S(2)}) collective-permute-start(bf16[256,768]{1,0:T(8,128)(2,1)S(1)} %get-tuple-element.17), channel_id=1, source_target_pairs={{0,8},{4,12},{8,0},{12,4},{1,9},{5,13},{9,1},{13,5},{2,10},{6,14},... | collective-permute-start | bytes 1179656 | tf_op jit(solution)/shard_map/ppermute | solution.py:225
  130.3 37.1 %collective-permute-start.6 = (bf16[256,768]{1,0:T(8,128)(2,1)S(1)}, bf16[256,768]{1,0:T(8,128)(2,1)S(1)}, u32[]{:S(2)}, u32[]{:S(2)}) collective-permute-start(bf16[256,768]{1,0:T(8,128)(2,1)S(1)} %get-tuple-element.18), channel_id=1, source_target_pairs={{0,4},{4,8},{8,12},{12,0},{1,5},{5,9},{9,13},{13,1},{2,6},{6,10},{... | collective-permute-start | bytes 1179656 | tf_op jit(solution)/shard_map/ppermute | solution.py:225
  154.5 12.9 %copy-start.7 = (bf16[256,768]{1,0:T(8,128)(2,1)}, bf16[256,768]{1,0:T(8,128)(2,1)S(1)}, u32[]{:S(2)}) copy-start(bf16[256,768]{1,0:T(8,128)(2,1)S(1)} %collective-permute-done.8.refs_7_) | copy-start | bytes 1179652
  163.6 3.8 %copy-start.8 = (bf16[256,768]{1,0:T(8,128)(2,1)}, bf16[256,768]{1,0:T(8,128)(2,1)S(1)}, u32[]{:S(2)}) copy-start(bf16[256,768]{1,0:T(8,128)(2,1)S(1)} %collective-permute-done.7.refs_6_) | copy-start | bytes 1179652
  183.5 24.5 %all-to-all-start.2 = ((bf16[4,256,384]{2,1,0:T(8,128)(2,1)}), bf16[4,256,384]{2,1,0:T(8,128)(2,1)S(1)}, u32[]{:S(2)}, u32[]{:S(2)}) async-start(bf16[4,256,384]{2,1,0:T(8,128)(2,1)} %bitcast.54), calls=%async_computation.2 | async-start | bytes 1572864 | tf_op jit(solution)/shard_map/all_to_all | solution.py:253
  208.0 23.1 %all-to-all-start.3 = ((bf16[4,256,384]{2,1,0:T(8,128)(2,1)}), bf16[4,256,384]{2,1,0:T(8,128)(2,1)S(1)}, u32[]{:S(2)}, u32[]{:S(2)}) async-start(bf16[4,256,384]{2,1,0:T(8,128)(2,1)} %bitcast.53), calls=%async_computation.3 | async-start | bytes 1572864 | tf_op jit(solution)/shard_map/all_to_all | solution.py:253
  (1 other events, 0.8 us)
Sparse Core Ops, SparseCore 0:
  88.7 26.1 all-gather.4
  124.8 29.9 all-gather.2

commit v16 on v14

--- a/solution.py
+++ b/solution.py
@@ -11,7 +11,7 @@
 CAP = 2
 SCALE = HD ** (-0.5)
 DRAFT_ROWS = 128
-PAIR = 2
+PAIR = 4
 EXP2_SCALE = SCALE * 1.4426950408889634
 
 

time: 222 us -> 220 us (level)
  Pallas kernels: 43.9 us -> 41.3 us
    pallas_call x2, Pallas kernels: 30.8 us -> 28.2 us  [sparse_attention(): pl.pallas_call(sparse_kernel, out_shape=jax.ShapeDtypeStruct((rows, heads...]
  transfers between devices with their start and end apart: 16 -> 16, of which waited for: 9 -> 10; matrix products, arithmetic and copies ran while one was open for 26% -> 26% of each run, Pallas kernels for 20% -> 19%
where the time goes in v16:
time: 220 us; the launch traced here: 219 us
  waiting for transfers between devices  68.1 us (31%)
  Pallas kernels  41.3 us (19%)
  local copies, waits for them, and re-layouts  37.7 us (17%)
  starting transfers between devices  34.6 us (16%)
  other arithmetic  23.1 us (10%)
  between operations  14.4 us (7%)
    ppermute x3, waiting for transfers between devices, head_permutes(): lax.ppermute(piece, 'head', [(i, (i + shift) % count) for i in range(coun...  30.4 us
    pallas_call x2, Pallas kernels, sparse_attention(): pl.pallas_call(sparse_kernel, out_shape=jax.ShapeDtypeStruct((rows, heads...  28.2 us
    ppermute x6, waiting for transfers between devices, exchange(): lax.ppermute(parcel, 'seq', [(i, (i + shift) % seq_count) for i in range(...  17.6 us
    pallas_call x2, Pallas kernels, draft_attention(): pl.pallas_call(draft_kernel, out_shape=jax.ShapeDtypeStruct((rows, width)...  13.1 us
    all_to_all x2, waiting for transfers between devices, on_device(): lax.all_to_all(rows_part, 'head', split_axis=0, concat_axis=1, tiled=True)  10.3 us
    all_to_all x2, starting transfers between devices, query_a2a(): lax.all_to_all(piece, 'head', split_axis=1, concat_axis=0, tiled=True)  9.93 us
    all_to_all x1, waiting for transfers between devices, on_device(): lax.all_to_all(key_in, 'head', split_axis=1, concat_axis=0, tiled=True)  8.93 us
    all_to_all x2, starting transfers between devices, on_device(): lax.all_to_all(rows_part, 'head', split_axis=0, concat_axis=1, tiled=True)  7.75 us
  transfers between devices with their start and end apart: 16, of which 10 were waited for; matrix products, arithmetic and copies ran while one was open for 26% of the time, Pallas kernels for 19%

profile of v16, /device:TPU:0, one launch (start us, length us, event | category | flops | bytes accessed | tf_op | source)
XLA Modules:
  0.0 219.2 jit_solution(16897397898521996529)
XLA Ops:
  10.0 5.0 %collective-permute-start.2 = (bf16[256,768]{1,0:T(8,128)(2,1)}, bf16[256,768]{1,0:T(8,128)(2,1)S(1)}, u32[]{:S(2)}, u32[]{:S(2)}) collective-permute-start(bf16[256,768]{1,0:T(8,128)(2,1)} %bitcast.9), channel_id=1, source_target_pairs={{0,3},{1,0},{2,1},{3,2},{4,7},{5,4},{6,5},{7,6},{8,11},{9,8},{10,9... | collective-permute-start | bytes 1179656 | tf_op jit(solution)/shard_map/ppermute | solution.py:154
  19.1 4.8 %all-to-all-start.1 = ((bf16[256,4,768]{2,0,1:T(8,128)(2,1)}), bf16[256,4,768]{2,0,1:T(8,128)(2,1)S(1)}, u32[]{:S(2)}, u32[]{:S(2)}) async-start(bf16[256,4,768]{2,0,1:T(8,128)(2,1)} %bitcast.63), calls=%async_computation.1 | async-start | bytes 3145728 | tf_op jit(solution)/shard_map/all_to_all | solution.py:162
  29.2 5.0 %collective-permute-done = bf16[256,768]{1,0:T(8,128)(2,1)S(1)} collective-permute-done((bf16[256,768]{1,0:T(8,128)(2,1)}, bf16[256,768]{1,0:T(8,128)(2,1)S(1)}, u32[]{:S(2)}, u32[]{:S(2)}) %collective-permute-start) | collective-permute-done | bytes 393248 | tf_op jit(solution)/shard_map/ppermute | solution.py:154
  34.2 25.3 %collective-permute-done.1 = bf16[256,768]{1,0:T(8,128)(2,1)S(1)} collective-permute-done((bf16[256,768]{1,0:T(8,128)(2,1)}, bf16[256,768]{1,0:T(8,128)(2,1)S(1)}, u32[]{:S(2)}, u32[]{:S(2)}) %collective-permute-start.1) | collective-permute-done | bytes 393248 | tf_op jit(solution)/shard_map/ppermute | solution.py:154
  64.5 3.6 %convert_reduce_fusion = f32[256,768]{1,0:T(8,128)S(1)} fusion(bf16[256,4,768]{2,1,0:T(4,128)(2,1)} %gather.20, pred[256]{0:T(512)(128)(4,1)S(1)} %copy-done.5), kind=kLoop, calls=%fused_computation.4 | loop fusion | flops 2162688 | bytes 2359552 | tf_op jit(solution)/shard_map/reduce_sum | solution.py:20
  70.3 3.3 %gather_fusion.2 = bf16[8,128,768]{2,1,0:T(8,128)(2,1)} fusion(bf16[8,128,768]{2,1,0:T(8,128)(2,1)} %broadcast_select_fusion.2, s32[1024]{0:T(1024)} %pad_clamp_fusion), kind=kCustom, calls=%fused_computation.clone | custom fusion | bytes 3145760 | tf_op jit(solution)/shard_map/jit(_take)/gather | solution.py:197
  73.6 8.9 %all-to-all-done.1 = bf16[256,4,768]{2,0,1:T(8,128)(2,1)S(1)} async-done(((bf16[256,4,768]{2,0,1:T(8,128)(2,1)}), bf16[256,4,768]{2,0,1:T(8,128)(2,1)S(1)}, u32[]{:S(2)}, u32[]{:S(2)}) %all-to-all-start.1) | async-done | bytes 1572896 | tf_op jit(solution)/shard_map/all_to_all | solution.py:162
  84.6 3.5 %broadcast_select_fusion.1 = (bf16[8,128,768]{2,1,0:T(8,128)(2,1)S(1)}, bf16[8,128,768]{2,1,0:T(8,128)(2,1)}) fusion(bf16[8,128,768]{2,1,0:T(8,128)(2,1)} %gather_fusion.2, pred[8]{0:T(512)(128)(4,1)S(1)} %copy-done.4, bf16[8,128,768]{2,1,0:T(8,128)(2,1)} %gather_fusion.3), kind=kLoop, calls=%fused_computation.11 | loop fusion | flops 1572864 | bytes 6291464 | tf_op jit(solution)/shard_map/jit(_take)/select_n | solution.py:197
  94.7 2.6 %fusion.14 = (bf16[256,4,384]{0,2,1:T(8,128)(2,1)}, bf16[256,4,384]{0,2,1:T(8,128)(2,1)}) fusion(bf16[256,4,768]{0,2,1:T(8,128)(2,1)} %bitcast.69), kind=kLoop, calls=%fused_computation.75 | loop fusion | bytes 3145728 | tf_op jit(solution)/shard_map/slice | solution.py:171
  97.3 6.5 %collective-permute-done.3 = bf16[2,128,768]{2,1,0:T(8,128)(2,1)} collective-permute-done((bf16[2,128,768]{2,1,0:T(8,128)(2,1)}, bf16[2,128,768]{2,1,0:T(8,128)(2,1)}, u32[]{:S(2)}, u32[]{:S(2)}) %collective-permute-start.3) | collective-permute-done | bytes 393248 | tf_op jit(solution)/shard_map/ppermute | solution.py:205
  104.3 6.0 %collective-permute-done.5 = bf16[2,128,768]{2,1,0:T(8,128)(2,1)} collective-permute-done((bf16[2,128,768]{2,1,0:T(8,128)(2,1)S(1)}, bf16[2,128,768]{2,1,0:T(8,128)(2,1)}, u32[]{:S(2)}, u32[]{:S(2)}) %collective-permute-start.5) | collective-permute-done | bytes 393248 | tf_op jit(solution)/shard_map/ppermute | solution.py:205
  110.2 4.8 %all-to-all-start = ((bf16[256,4,384]{0,2,1:T(8,128)(2,1)}), bf16[256,4,384]{0,2,1:T(8,128)(2,1)}, u32[]{:S(2)}, u32[]{:S(2)}) async-start(bf16[256,4,384]{0,2,1:T(8,128)(2,1)} %get-tuple-element.28), calls=%async_computation | async-start | bytes 1572864 | tf_op jit(solution)/shard_map/all_to_all | solution.py:175
  122.3 4.9 %reshape.170 = f32[256,4,768]{2,1,0:T(4,128)} reshape(f32[4,256,768]{2,1,0:T(8,128)} %bitcast_convert_fusion) | data formatting | bytes 6291456 | tf_op jit(solution)/shard_map/convert_element_type | solution.py:19
  127.1 3.8 %reduce_sum.28 = f32[256,768]{1,0:T(8,128)S(1)} reduce(f32[256,4,768]{2,1,0:T(4,128)} %reshape.170, f32[]{:T(128)} %constant.170.clone.1), dimensions={1}, to_apply=%region_4.6 | reduce | flops 589824 | bytes 3932164 | tf_op jit(solution)/shard_map/reduce_sum | solution.py:20
  131.7 4.7 %collective-permute-done.8 = bf16[2,128,768]{2,1,0:T(8,128)(2,1)} collective-permute-done((bf16[2,128,768]{2,1,0:T(8,128)(2,1)S(1)}, bf16[2,128,768]{2,1,0:T(8,128)(2,1)}, u32[]{:S(2)}, u32[]{:S(2)}) %collective-permute-start.8) | collective-permute-done | bytes 393248 | tf_op jit(solution)/shard_map/ppermute | solution.py:205
  136.5 5.1 %all-to-all-start.2 = ((bf16[256,4,384]{0,2,1:T(8,128)(2,1)}), bf16[256,4,384]{0,2,1:T(8,128)(2,1)S(1)}, u32[]{:S(2)}, u32[]{:S(2)}) async-start(bf16[256,4,384]{0,2,1:T(8,128)(2,1)} %get-tuple-element.29), calls=%async_computation.2 | async-start | bytes 1572864 | tf_op jit(solution)/shard_map/all_to_all | solution.py:175
  147.7 14.1 %shard_map.62 = bf16[1024,384]{1,0:T(8,128)(2,1)} custom-call(s32[96]{0:T(128)} %reshape.162.tbl_ref, bf16[1024,384]{1,0:T(8,128)(2,1)} %bitcast.76, bf16[1024,768]{1,0:T(8,128)(2,1)} %bitcast.67, bf16[1024,768]{1,0:T(8,128)(2,1)} %bitcast_select_fusion.refs_1_, bf16[256,768]{1,0:T(8,128)(2,1)} %bitcast.29.refs_2_, bf16[256,768]{1,0:T(8,128)(2,1)} %bitcast.31.refs_3_, ...), custom_call_target="tpu_custom_call" | custom-call | flops 2415919104 | bytes 4325376 | tf_op jit(solution)/shard_map/pallas_call | solution.py:86
  162.8 4.3 %all-to-all-start.3 = ((bf16[4,256,384]{2,1,0:T(8,128)(2,1)}), bf16[4,256,384]{2,1,0:T(8,128)(2,1)S(1)}, u32[]{:S(2)}, u32[]{:S(2)}) async-start(bf16[4,256,384]{2,1,0:T(8,128)(2,1)} %bitcast.84), calls=%async_computation.3 | async-start | bytes 1572864 | tf_op jit(solution)/shard_map/all_to_all | solution.py:236
  168.2 14.1 %shard_map.59 = bf16[1024,384]{1,0:T(8,128)(2,1)} custom-call(s32[96]{0:T(128)} %reshape.162.tbl_ref, bf16[1024,384]{1,0:T(8,128)(2,1)} %bitcast.78, bf16[1024,768]{1,0:T(8,128)(2,1)} %bitcast.68, bf16[1024,768]{1,0:T(8,128)(2,1)} %bitcast_select_fusion.refs_1_, bf16[256,768]{1,0:T(8,128)(2,1)} %bitcast.29.refs_2_, bf16[256,768]{1,0:T(8,128)(2,1)} %bitcast.31.refs_3_, ...), custom_call_target="tpu_custom_call" | custom-call | flops 2415919104 | bytes 4325376 | tf_op jit(solution)/shard_map/pallas_call | solution.py:86
  182.3 5.3 %all-to-all-done.3 = bf16[4,256,384]{2,1,0:T(8,128)(2,1)S(1)} async-done(((bf16[4,256,384]{2,1,0:T(8,128)(2,1)}), bf16[4,256,384]{2,1,0:T(8,128)(2,1)S(1)}, u32[]{:S(2)}, u32[]{:S(2)}) %all-to-all-start.3) | async-done | bytes 786464 | tf_op jit(solution)/shard_map/all_to_all | solution.py:236
  187.7 3.5 %all-to-all-start.4 = ((bf16[4,256,384]{2,1,0:T(8,128)(2,1)}), bf16[4,256,384]{2,1,0:T(8,128)(2,1)S(1)}, u32[]{:S(2)}, u32[]{:S(2)}) async-start(bf16[4,256,384]{2,1,0:T(8,128)(2,1)} %bitcast.83), calls=%async_computation.4 | async-start | bytes 1572864 | tf_op jit(solution)/shard_map/all_to_all | solution.py:236
  191.2 6.5 %shard_map.60 = bf16[256,384]{1,0:T(8,128)(2,1)} custom-call(bf16[1024,384]{1,0:T(8,128)(2,1)} %bitcast.77, bf16[1024,768]{1,0:T(8,128)(2,1)} %all-gather.3.cloned.1.call-done.k_ref, bf16[1024,768]{1,0:T(8,128)(2,1)} %all-gather.5.cloned.1.call-done.v_ref), custom_call_target="tpu_custom_call" | custom-call | flops 503316480 | bytes 2555904 | tf_op jit(solution)/shard_map/pallas_call | solution.py:131
  197.7 6.6 %shard_map.61 = bf16[256,384]{1,0:T(8,128)(2,1)} custom-call(bf16[1024,384]{1,0:T(8,128)(2,1)} %bitcast.79, bf16[1024,768]{1,0:T(8,128)(2,1)} %all-gather.3.cloned.1.call-done.k_ref, bf16[1024,768]{1,0:T(8,128)(2,1)} %all-gather.5.cloned.1.call-done.v_ref), custom_call_target="tpu_custom_call" | custom-call | flops 503316480 | bytes 2555904 | tf_op jit(solution)/shard_map/pallas_call | solution.py:131
  206.0 4.9 %all-to-all-done.4 = bf16[4,256,384]{2,1,0:T(8,128)(2,1)S(1)} async-done(((bf16[4,256,384]{2,1,0:T(8,128)(2,1)}), bf16[4,256,384]{2,1,0:T(8,128)(2,1)S(1)}, u32[]{:S(2)}, u32[]{:S(2)}) %all-to-all-start.4) | async-done | bytes 786464 | tf_op jit(solution)/shard_map/all_to_all | solution.py:236
  (96 shorter events, 47.6 us)
Async XLA Ops:
  9.1 8.8 %copy-start.1 = (bf16[256,3072]{1,0:T(8,128)(2,1)S(1)}, bf16[256,3072]{1,0:T(8,128)(2,1)}, u32[]{:S(2)}) copy-start(bf16[256,3072]{1,0:T(8,128)(2,1)} %param.7) | copy-start | bytes 4718596
  10.0 19.2 %collective-permute-start.2 = (bf16[256,768]{1,0:T(8,128)(2,1)}, bf16[256,768]{1,0:T(8,128)(2,1)S(1)}, u32[]{:S(2)}, u32[]{:S(2)}) collective-permute-start(bf16[256,768]{1,0:T(8,128)(2,1)} %bitcast.9), channel_id=1, source_target_pairs={{0,3},{1,0},{2,1},{3,2},{4,7},{5,4},{6,5},{7,6},{8,11},{9,8},{10,9... | collective-permute-start | bytes 1179656 | tf_op jit(solution)/shard_map/ppermute | solution.py:154
  16.0 18.3 %collective-permute-start = (bf16[256,768]{1,0:T(8,128)(2,1)}, bf16[256,768]{1,0:T(8,128)(2,1)S(1)}, u32[]{:S(2)}, u32[]{:S(2)}) collective-permute-start(bf16[256,768]{1,0:T(8,128)(2,1)} %bitcast.5), channel_id=1, source_target_pairs={{0,1},{1,2},{2,3},{3,0},{4,5},{5,6},{6,7},{7,4},{8,9},{9,10},{10,1... | collective-permute-start | bytes 1179656 | tf_op jit(solution)/shard_map/ppermute | solution.py:154
  16.9 42.7 %collective-permute-start.1 = (bf16[256,768]{1,0:T(8,128)(2,1)}, bf16[256,768]{1,0:T(8,128)(2,1)S(1)}, u32[]{:S(2)}, u32[]{:S(2)}) collective-permute-start(bf16[256,768]{1,0:T(8,128)(2,1)} %bitcast.88), channel_id=1, source_target_pairs={{0,2},{1,3},{2,0},{3,1},{4,6},{5,7},{6,4},{7,5},{8,10},{9,11},{10,... | collective-permute-start | bytes 1179656 | tf_op jit(solution)/shard_map/ppermute | solution.py:154
  19.1 4.8 %copy-start.3 = (s32[32,12]{0,1:T(8,128)S(1)}, s32[32,12]{0,1:T(8,128)}, u32[]{:S(2)}) copy-start(s32[32,12]{0,1:T(8,128)} %param.9) | copy-start | bytes 4612
  19.1 63.4 %all-to-all-start.1 = ((bf16[256,4,768]{2,0,1:T(8,128)(2,1)}), bf16[256,4,768]{2,0,1:T(8,128)(2,1)S(1)}, u32[]{:S(2)}, u32[]{:S(2)}) async-start(bf16[256,4,768]{2,0,1:T(8,128)(2,1)} %bitcast.63), calls=%async_computation.1 | async-start | bytes 3145728 | tf_op jit(solution)/shard_map/all_to_all | solution.py:162
  23.9 158.4 %all-gather.5.cloned.1.call-start = ((), (), s32[]{:S(2)}) async-start(), calls=%async_computation.6 | async-start | bytes 1966080 | tf_op jit(solution)/shard_map/all_gather | solution.py:178
  23.9 1.9 copy-start.7
  64.5 4.4 %copy-start.6 = (pred[8]{0:T(512)(128)(4,1)S(1)}, pred[8]{0:T(512)(128)(4,1)}, u32[]{:S(2)}) copy-start(pred[8]{0:T(512)(128)(4,1)} %broadcast_in_dim.64) | copy-start | bytes 28
  82.5 37.8 %copy-start = (bf16[256,4,768]{2,0,1:T(8,128)(2,1)}, bf16[256,4,768]{2,0,1:T(8,128)(2,1)S(1)}, u32[]{:S(2)}) copy-start(bf16[256,4,768]{2,0,1:T(8,128)(2,1)S(1)} %all-to-all-done.1) | copy-start | bytes 4718596
  82.5 2.0 copy-start.4
  89.1 14.8 %collective-permute-start.3 = (bf16[2,128,768]{2,1,0:T(8,128)(2,1)}, bf16[2,128,768]{2,1,0:T(8,128)(2,1)}, u32[]{:S(2)}, u32[]{:S(2)}) collective-permute-start(bf16[2,128,768]{2,1,0:T(8,128)(2,1)} %get-tuple-element.27), channel_id=1, source_target_pairs={{0,4},{4,8},{8,12},{12,0},{1,5},{5,9},{9,13},{13,1},{2,6},{6,10},{... | collective-permute-start | bytes 1179656 | tf_op jit(solution)/shard_map/ppermute | solution.py:205
  89.1 15.2 %collective-permute-start.4 = (bf16[2,128,768]{2,1,0:T(8,128)(2,1)}, bf16[2,128,768]{2,1,0:T(8,128)(2,1)}, u32[]{:S(2)}, u32[]{:S(2)}) collective-permute-start(bf16[2,128,768]{2,1,0:T(8,128)(2,1)} %get-tuple-element.26), channel_id=1, source_target_pairs={{0,8},{4,12},{8,0},{12,4},{1,9},{5,13},{9,1},{13,5},{2,10},{6,14},... | collective-permute-start | bytes 1179656 | tf_op jit(solution)/shard_map/ppermute | solution.py:205
  90.7 19.5 %collective-permute-start.5 = (bf16[2,128,768]{2,1,0:T(8,128)(2,1)S(1)}, bf16[2,128,768]{2,1,0:T(8,128)(2,1)}, u32[]{:S(2)}, u32[]{:S(2)}) collective-permute-start(bf16[2,128,768]{2,1,0:T(8,128)(2,1)S(1)} %get-tuple-element.25), channel_id=1, source_target_pairs={{0,12},{4,0},{8,4},{12,8},{1,13},{5,1},{9,5},{13,9},{2,14},{6,2},{... | collective-permute-start | bytes 1179656 | tf_op jit(solution)/shard_map/ppermute | solution.py:205
  110.2 26.2 %all-to-all-start = ((bf16[256,4,384]{0,2,1:T(8,128)(2,1)}), bf16[256,4,384]{0,2,1:T(8,128)(2,1)}, u32[]{:S(2)}, u32[]{:S(2)}) async-start(bf16[256,4,384]{0,2,1:T(8,128)(2,1)} %get-tuple-element.28), calls=%async_computation | async-start | bytes 1572864 | tf_op jit(solution)/shard_map/all_to_all | solution.py:175
  115.1 67.3 %all-gather.3.cloned.1.call-start = ((), (), s32[]{:S(2)}) async-start(), calls=%async_computation.5 | async-start | bytes 1966080 | tf_op jit(solution)/shard_map/all_gather | solution.py:177
  117.4 14.3 %collective-permute-start.6 = (bf16[2,128,768]{2,1,0:T(8,128)(2,1)}, bf16[2,128,768]{2,1,0:T(8,128)(2,1)}, u32[]{:S(2)}, u32[]{:S(2)}) collective-permute-start(bf16[2,128,768]{2,1,0:T(8,128)(2,1)} %get-tuple-element.36), channel_id=1, source_target_pairs={{0,4},{4,8},{8,12},{12,0},{1,5},{5,9},{9,13},{13,1},{2,6},{6,10},{... | collective-permute-start | bytes 1179656 | tf_op jit(solution)/shard_map/ppermute | solution.py:205
  119.0 12.7 %collective-permute-start.7 = (bf16[2,128,768]{2,1,0:T(8,128)(2,1)}, bf16[2,128,768]{2,1,0:T(8,128)(2,1)}, u32[]{:S(2)}, u32[]{:S(2)}) collective-permute-start(bf16[2,128,768]{2,1,0:T(8,128)(2,1)} %get-tuple-element.35), channel_id=1, source_target_pairs={{0,8},{4,12},{8,0},{12,4},{1,9},{5,13},{9,1},{13,5},{2,10},{6,14},... | collective-permute-start | bytes 1179656 | tf_op jit(solution)/shard_map/ppermute | solution.py:205
  119.5 16.9 %collective-permute-start.8 = (bf16[2,128,768]{2,1,0:T(8,128)(2,1)S(1)}, bf16[2,128,768]{2,1,0:T(8,128)(2,1)}, u32[]{:S(2)}, u32[]{:S(2)}) collective-permute-start(bf16[2,128,768]{2,1,0:T(8,128)(2,1)S(1)} %get-tuple-element.34), channel_id=1, source_target_pairs={{0,12},{4,0},{8,4},{12,8},{1,13},{5,1},{9,5},{13,9},{2,14},{6,2},{... | collective-permute-start | bytes 1179656 | tf_op jit(solution)/shard_map/ppermute | solution.py:205
  130.9 10.7 %copy-start.8 = (pred[4]{0:T(512)(128)(4,1)S(1)}, pred[4]{0:T(512)(128)(4,1)}, u32[]{:S(2)}) copy-start(pred[4]{0:T(512)(128)(4,1)} %copy-done.7) | copy-start | bytes 16
  136.5 26.3 %all-to-all-start.2 = ((bf16[256,4,384]{0,2,1:T(8,128)(2,1)}), bf16[256,4,384]{0,2,1:T(8,128)(2,1)S(1)}, u32[]{:S(2)}, u32[]{:S(2)}) async-start(bf16[256,4,384]{0,2,1:T(8,128)(2,1)} %get-tuple-element.29), calls=%async_computation.2 | async-start | bytes 1572864 | tf_op jit(solution)/shard_map/all_to_all | solution.py:175
  162.8 24.9 %all-to-all-start.3 = ((bf16[4,256,384]{2,1,0:T(8,128)(2,1)}), bf16[4,256,384]{2,1,0:T(8,128)(2,1)S(1)}, u32[]{:S(2)}, u32[]{:S(2)}) async-start(bf16[4,256,384]{2,1,0:T(8,128)(2,1)} %bitcast.84), calls=%async_computation.3 | async-start | bytes 1572864 | tf_op jit(solution)/shard_map/all_to_all | solution.py:236
  187.7 23.3 %all-to-all-start.4 = ((bf16[4,256,384]{2,1,0:T(8,128)(2,1)}), bf16[4,256,384]{2,1,0:T(8,128)(2,1)S(1)}, u32[]{:S(2)}, u32[]{:S(2)}) async-start(bf16[4,256,384]{2,1,0:T(8,128)(2,1)} %bitcast.83), calls=%async_computation.4 | async-start | bytes 1572864 | tf_op jit(solution)/shard_map/all_to_all | solution.py:236
  197.7 6.6 %copy-start.2 = (bf16[256,384]{1,0:T(8,128)(2,1)S(1)}, bf16[256,384]{1,0:T(8,128)(2,1)}, u32[]{:S(2)}) copy-start(bf16[256,384]{1,0:T(8,128)(2,1)} %shard_map.60) | copy-start | bytes 589828
  (1 other events, 1.4 us)
Sparse Core Ops, SparseCore 0:
  69.0 31.2 all-gather.4
  131.8 20.1 all-gather.2

commit v17 on v12

--- a/solution.py
+++ b/solution.py
@@ -11,7 +11,7 @@
 CAP = 2
 SCALE = HD ** (-0.5)
 DRAFT_ROWS = 128
-PAIR = 2
+PAIR = 4
 EXP2_SCALE = SCALE * 1.4426950408889634
 
 
@@ -69,7 +69,7 @@
         one_block(i)
 
 
-def sparse_attention(tbl, queries, keys, values, far_keys, far_values, head_lo, heads, q_lo):
+def sparse_attention(tbl, queries, keys, values, far_keys, far_values, head_lo, heads):
     rows = queries.shape[0]
 
     def column(h, t):
@@ -90,7 +90,7 @@
         grid_spec=pltpu.PrefetchScalarGridSpec(
             num_scalar_prefetch=1,
             grid=(heads,),
-            in_specs=[pl.BlockSpec((rows, HD), lambda h, t: (0, h + q_lo))]
+            in_specs=[pl.BlockSpec((rows, HD), lambda h, t: (0, h))]
             + [pl.BlockSpec((x.shape[0], HD), column) for x in operands],
             out_specs=pl.BlockSpec((rows, HD), lambda h, t: (0, h)),
             scratch_shapes=[
@@ -159,17 +159,17 @@
 
 
 def on_device(query_in, key_in, value_in, block_lists):
-    key_rows = lax.all_to_all(key_in, "head", split_axis=1, concat_axis=0, tiled=True)
-    value_rows = head_permutes(value_in)
-    seq_rows, width = key_rows.shape
+    token_rows, total = query_in.shape
     head_count = lax.axis_size("head")
+    width = total // head_count
+    seq_rows = token_rows * head_count
     heads = width // HD
     first = max(1, heads // 2)
     spans = [(lo, n) for lo, n in ((0, first), (first, heads - first)) if n > 0]
-    queries = lax.all_to_all(query_in, "head", split_axis=1, concat_axis=0, tiled=True)
-
-    draft_keys = lax.all_gather(pool_tokens(key_rows), "seq", axis=0, tiled=True)
-    draft_values = lax.all_gather(pool_tokens(value_rows), "seq", axis=0, tiled=True)
+
+    def head_slice(matrix, lo, n):
+        grouped = matrix.reshape(token_rows, head_count, width)
+        return grouped[:, :, lo * HD:(lo + n) * HD].reshape(token_rows, -1)
 
     seq_count = lax.axis_size("seq")
     seq_index = lax.axis_index("seq")
@@ -187,9 +187,11 @@
     send_idx = jnp.sum(
         jnp.where(slot_hit, jnp.arange(per_dev, dtype=jnp.int32)[None, None, :], 0), axis=2
     ).reshape(-1)
+
     def exchange(rows):
-        blocks = jnp.take(rows.reshape(per_dev, BLOCK, width), send_idx, axis=0)
-        outgoing = blocks.reshape(seq_count, CAP, BLOCK, width)
+        span_width = rows.shape[1]
+        blocks = jnp.take(rows.reshape(per_dev, BLOCK, span_width), send_idx, axis=0)
+        outgoing = blocks.reshape(seq_count, CAP, BLOCK, span_width)
         arrivals = []
         for shift in range(1, seq_count):
             parcel = lax.dynamic_index_in_dim(
@@ -200,10 +202,7 @@
                     parcel, "seq", [(i, (i + shift) % seq_count) for i in range(seq_count)]
                 )
             )
-        return [a.reshape(CAP * BLOCK, width) for a in arrivals]
-
-    remote_keys = exchange(key_rows)
-    remote_values = exchange(value_rows)
+        return [a.reshape(CAP * BLOCK, span_width) for a in arrivals]
 
     own_lists = lax.dynamic_slice_in_dim(block_lists, seq_index * per_dev, per_dev, 0)
     owners = own_lists // per_dev
@@ -214,20 +213,42 @@
     joint_pos = jnp.where(distance == 0, within, per_dev + (distance - 1) * CAP + ranks_used)
     table = jnp.clip(joint_pos, 0, per_dev + (seq_count - 1) * CAP - 1).reshape(-1).astype(jnp.int32)
 
+    staged = []
+    for lo, n in spans:
+        key_rows = lax.all_to_all(
+            head_slice(key_in, lo, n), "head", split_axis=1, concat_axis=0, tiled=True
+        )
+        value_rows = head_permutes(head_slice(value_in, lo, n))
+        remote_keys = exchange(key_rows)
+        remote_values = exchange(value_rows)
+        query_piece, remote_keys, remote_values = lax.optimization_barrier(
+            (head_slice(query_in, lo, n), remote_keys, remote_values)
+        )
+        queries = lax.all_to_all(query_piece, "head", split_axis=1, concat_axis=0, tiled=True)
+        draft_keys = lax.all_gather(pool_tokens(key_rows), "seq", axis=0, tiled=True)
+        draft_values = lax.all_gather(pool_tokens(value_rows), "seq", axis=0, tiled=True)
+        staged.append(
+            (n, queries, key_rows, value_rows, remote_keys, remote_values, draft_keys, draft_values)
+        )
+
     pieces = []
-    for index, (head_lo, count) in enumerate(spans):
+    drafts = []
+    for index, item in enumerate(staged):
+        n, queries, key_rows, value_rows, remote_keys, remote_values, draft_keys, draft_values = item
         rows_part = sparse_attention(
-            table, queries, key_rows, value_rows, remote_keys, remote_values,
-            head_lo, count, head_lo,
-        )
-        if index == len(spans) - 1:
+            table, queries, key_rows, value_rows, remote_keys, remote_values, 0, n,
+        )
+        if index == len(staged) - 1:
             rows_part, draft_keys, draft_values = lax.optimization_barrier(
                 (rows_part, draft_keys, draft_values)
             )
         back = lax.all_to_all(rows_part, "head", split_axis=0, concat_axis=1, tiled=True)
-        pieces.append(back.reshape(back.shape[0], -1, count * HD))
+        pieces.append(back.reshape(back.shape[0], -1, n * HD))
+        drafts.append((queries, draft_keys, draft_values))
     sparse_out = jnp.concatenate(pieces, axis=2).reshape(pieces[0].shape[0], -1)
-    draft_out = draft_attention(queries, draft_keys, draft_values, 0)
+    draft_out = jnp.concatenate(
+        [draft_attention(q, k, v, 0) for q, k, v in drafts], axis=1
+    )
     return (draft_out, sparse_out)
 
 

time: 228 us -> 258 us (1.13)
  waiting for transfers between devices: 90.1 us -> 49.3 us
  blocking collectives: 0 us -> 36.4 us
  starting transfers between devices: 29 us -> 56.8 us
  local copies, waits for them, and re-layouts: 30.1 us -> 49.9 us
  between operations: 14.4 us -> 1.01 us
    all_gather x0 -> x4, blocking collectives: none -> 36.4 us  [the longest x2 18.2 us: on_device(): lax.all_gather(pool_tokens(value_rows), 'seq', axis=0, tiled=True)]
    all_to_all x2 -> x4, starting transfers between devices: 9.36 us -> 27.9 us  [the longest x2 18.1 us: on_device(): lax.all_to_all(query_piece, 'head', split_axis=1, concat_axis=0, tiled=True)]
    all_to_all x2, waiting for transfers between devices: 14.5 us -> 0.01 us  [on_device(): lax.all_to_all(rows_part, 'head', split_axis=0, concat_axis=1, tiled=True)]
    ppermute x3 -> x6, waiting for transfers between devices: 26.1 us -> 15.2 us  [head_permutes(): lax.ppermute(piece, 'head', [(i, (i + shift) % count) for i in range(coun...]
    all_to_all x2 -> x4, waiting for transfers between devices: 21.7 us -> 13.4 us  [the longest x2 13 us: on_device(): lax.all_to_all(head_slice(key_in, lo, n), 'head', split_axis=1, concat_ax...]
    ppermute x6 -> x12, waiting for transfers between devices: 27.8 us -> 20.8 us  [exchange(): lax.ppermute(parcel, 'seq', [(i, (i + shift) % seq_count) for i in range(...]
    reshape x0 -> x2, local copies, waits for them, and re-layouts: none -> 5.93 us  [head_slice(): grouped = matrix.reshape(token_rows, head_count, width)]
    ppermute x3 -> x6, starting transfers between devices: 6.06 us -> 10.8 us  [head_permutes(): lax.ppermute(piece, 'head', [(i, (i + shift) % count) for i in range(coun...]
  transfers between devices with their start and end apart: 15 -> 24, of which waited for: 11 -> 13; matrix products, arithmetic and copies ran while one was open for 20% -> 22% of each run, Pallas kernels for 19% -> 16%
where the time goes in v17:
time: 258 us; the launch traced here: 257 us
  starting transfers between devices  56.8 us (22%)
  local copies, waits for them, and re-layouts  49.9 us (19%)
  waiting for transfers between devices  49.3 us (19%)
  Pallas kernels  41.3 us (16%)
  blocking collectives  36.4 us (14%)
  other arithmetic  22.5 us (9%)
    pallas_call x2, Pallas kernels, sparse_attention(): pl.pallas_call(sparse_kernel, out_shape=jax.ShapeDtypeStruct((rows, heads...  28.2 us
    ppermute x12, waiting for transfers between devices, exchange(): lax.ppermute(parcel, 'seq', [(i, (i + shift) % seq_count) for i in range(...  20.8 us
    all_gather x2, blocking collectives, on_device(): lax.all_gather(pool_tokens(value_rows), 'seq', axis=0, tiled=True)  18.2 us
    all_gather x2, blocking collectives, on_device(): lax.all_gather(pool_tokens(key_rows), 'seq', axis=0, tiled=True)  18.2 us
    all_to_all x2, starting transfers between devices, on_device(): lax.all_to_all(query_piece, 'head', split_axis=1, concat_axis=0, tiled=True)  18.1 us
    ppermute x6, waiting for transfers between devices, head_permutes(): lax.ppermute(piece, 'head', [(i, (i + shift) % count) for i in range(coun...  15.2 us
    pallas_call x2, Pallas kernels, draft_attention(): pl.pallas_call(draft_kernel, out_shape=jax.ShapeDtypeStruct((rows, width)...  13.1 us
    all_to_all x2, waiting for transfers between devices, on_device(): lax.all_to_all(head_slice(key_in, lo, n), 'head', split_axis=1, concat_ax...  13 us
  transfers between devices with their start and end apart: 24, of which 13 were waited for; matrix products, arithmetic and copies ran while one was open for 22% of the time, Pallas kernels for 16%

profile of v17, /device:TPU:0, one launch (start us, length us, event | category | flops | bytes accessed | tf_op | source)
XLA Modules:
  0.0 257.2 jit_solution(6462989728522908949)
XLA Ops:
  0.6 3.3 %reshape.153 = bf16[256,4,768]{2,1,0:T(4,128)(2,1)S(1)} reshape(bf16[256,3072]{1,0:T(8,128)(2,1)} %param.9) | data formatting | bytes 3145728 | tf_op jit(solution)/shard_map/reshape | solution.py:171
  5.4 6.3 %all-to-all-start.2 = ((bf16[256,4,384]{2,0,1:T(8,128)(2,1)}), bf16[256,4,384]{2,0,1:T(8,128)(2,1)S(1)}, u32[]{:S(2)}, u32[]{:S(2)}) async-start(bf16[256,4,384]{2,0,1:T(8,128)(2,1)} %copy.61), calls=%async_computation.2 | async-start | bytes 1572864 | tf_op jit(solution)/shard_map/all_to_all | solution.py:218
  29.8 13.0 %all-to-all-done.2 = bf16[256,4,384]{2,0,1:T(8,128)(2,1)S(1)} async-done(((bf16[256,4,384]{2,0,1:T(8,128)(2,1)}), bf16[256,4,384]{2,0,1:T(8,128)(2,1)S(1)}, u32[]{:S(2)}, u32[]{:S(2)}) %all-to-all-start.2) | async-done | bytes 786464 | tf_op jit(solution)/shard_map/all_to_all | solution.py:218
  42.8 3.5 %all-to-all-start = ((bf16[256,4,384]{2,0,1:T(8,128)(2,1)}), bf16[256,4,384]{2,0,1:T(8,128)(2,1)S(1)}, u32[]{:S(2)}, u32[]{:S(2)}) async-start(bf16[256,4,384]{2,0,1:T(8,128)(2,1)} %copy.60), calls=%async_computation | async-start | bytes 1572864 | tf_op jit(solution)/shard_map/all_to_all | solution.py:218
  48.2 3.8 %collective-permute-start.5 = (bf16[256,384]{1,0:T(8,128)(2,1)}, bf16[256,384]{1,0:T(8,128)(2,1)S(1)}, u32[]{:S(2)}, u32[]{:S(2)}) collective-permute-start(bf16[256,384]{1,0:T(8,128)(2,1)} %bitcast.18), channel_id=1, source_target_pairs={{0,3},{1,0},{2,1},{3,2},{4,7},{5,4},{6,5},{7,6},{8,11},{9,8},{10,9... | collective-permute-start | bytes 589832 | tf_op jit(solution)/shard_map/ppermute | solution.py:154
  52.5 8.0 %collective-permute-done.13 = bf16[256,384]{1,0:T(8,128)(2,1)} collective-permute-done((bf16[256,384]{1,0:T(8,128)(2,1)}, bf16[256,384]{1,0:T(8,128)(2,1)}, u32[]{:S(2)}, u32[]{:S(2)}) %collective-permute-start.13) | collective-permute-done | bytes 196640 | tf_op jit(solution)/shard_map/ppermute | solution.py:154
  63.9 7.1 %collective-permute-done.4 = bf16[256,384]{1,0:T(8,128)(2,1)} collective-permute-done((bf16[256,384]{1,0:T(8,128)(2,1)}, bf16[256,384]{1,0:T(8,128)(2,1)}, u32[]{:S(2)}, u32[]{:S(2)}) %collective-permute-start.4) | collective-permute-done | bytes 196640 | tf_op jit(solution)/shard_map/ppermute | solution.py:154
  81.5 3.4 %broadcast_select_fusion.4 = (bf16[8,128,384]{2,1,0:T(8,128)(2,1)}, bf16[8,128,384]{2,1,0:T(8,128)(2,1)}, bf16[8,128,384]{2,1,0:T(8,128)(2,1)}, bf16[8,128,384]{2,1,0:T(8,128)(2,1)S(1)}) fusion(bf16[8,128,384]{2,1,0:T(8,128)(2,1)} %gather_fusion.3, pred[8]{0:T(512)(128)(4,1)S(1)} %copy-done.13, bf16[8,128,384]{2,1,0:T(8,128)(2,1)} %gather_fusion.4, ...), kind=kLoop, calls=%fused_computation.16 | loop fusion | flops 1572864 | bytes 6291464 | tf_op jit(solution)/shard_map/jit(_take)/select_n | solution.py:193
  96.7 3.2 %collective-permute-done.8 = bf16[2,128,384]{2,1,0:T(8,128)(2,1)S(1)} collective-permute-done((bf16[2,128,384]{2,1,0:T(8,128)(2,1)S(1)}, bf16[2,128,384]{2,1,0:T(8,128)(2,1)S(1)}, u32[]{:S(2)}, u32[]{:S(2)}) %collective-permute-start.8) | collective-permute-done | bytes 196640 | tf_op jit(solution)/shard_map/ppermute | solution.py:201
  99.9 3.2 %collective-permute-done = bf16[2,128,384]{2,1,0:T(8,128)(2,1)S(1)} collective-permute-done((bf16[2,128,384]{2,1,0:T(8,128)(2,1)S(1)}, bf16[2,128,384]{2,1,0:T(8,128)(2,1)S(1)}, u32[]{:S(2)}, u32[]{:S(2)}) %collective-permute-start) | collective-permute-done | bytes 196640 | tf_op jit(solution)/shard_map/ppermute | solution.py:201
  105.8 13.3 %all-to-all-start.1 = ((bf16[256,4,384]{0,2,1:T(8,128)(2,1)}), bf16[256,4,384]{0,2,1:T(8,128)(2,1)S(1)}, u32[]{:S(2)}, u32[]{:S(2)}) async-start(bf16[256,4,384]{0,2,1:T(8,128)(2,1)} %get-tuple-element.42), calls=%async_computation.1 | async-start | bytes 1572864 | tf_op jit(solution)/shard_map/all_to_all | solution.py:227
  132.8 2.8 %collective-permute-done.9 = bf16[2,128,384]{2,1,0:T(8,128)(2,1)} collective-permute-done((bf16[2,128,384]{2,1,0:T(8,128)(2,1)}, bf16[2,128,384]{2,1,0:T(8,128)(2,1)}, u32[]{:S(2)}, u32[]{:S(2)}) %collective-permute-start.9) | collective-permute-done | bytes 196640 | tf_op jit(solution)/shard_map/ppermute | solution.py:201
  140.4 4.8 %all-to-all-start.3 = ((bf16[256,4,384]{0,2,1:T(8,128)(2,1)}), bf16[256,4,384]{0,2,1:T(8,128)(2,1)}, u32[]{:S(2)}, u32[]{:S(2)}) async-start(bf16[256,4,384]{0,2,1:T(8,128)(2,1)} %get-tuple-element.43), calls=%async_computation.3 | async-start | bytes 1572864 | tf_op jit(solution)/shard_map/all_to_all | solution.py:227
  148.0 3.1 %reduce_sum.49 = f32[256,384]{1,0:T(8,128)} reduce(f32[256,4,384]{2,1,0:T(4,128)} %reshape.183, f32[]{:T(128)} %constant.202.clone.1), dimensions={1}, to_apply=%region_7.10 | reduce | flops 294912 | bytes 1966084 | tf_op jit(solution)/shard_map/reduce_sum | solution.py:20
  153.0 9.3 %all_gather.15.v_ref = bf16[1024,384]{1,0:T(8,128)(2,1)} all-gather(bf16[256,384]{1,0:T(8,128)(2,1)S(1)} %multiply_convert_fusion), channel_id=1, replica_groups=mesh['groups'=2,'seq'=4,'head'=4] {'seq'}, dimensions={0}, use_global_device_ids=true | all-gather | bytes 983040 | tf_op jit(solution)/shard_map/all_gather | solution.py:229
  163.5 14.1 %shard_map.62 = bf16[1024,384]{1,0:T(8,128)(2,1)} custom-call(s32[96]{0:T(128)} %reshape.176.tbl_ref, bf16[1024,384]{1,0:T(8,128)(2,1)} %bitcast.105, bf16[1024,384]{1,0:T(8,128)(2,1)} %bitcast.96, bf16[1024,384]{1,0:T(8,128)(2,1)} %bitcast.100, bf16[256,384]{1,0:T(8,128)(2,1)} %bitcast.127, bf16[256,384]{1,0:T(8,128)(2,1)} %bitcast.128, ...), custom_call_target="tpu_custom_call" | custom-call | flops 2415919104 | bytes 4325376 | tf_op jit(solution)/shard_map/pallas_call | solution.py:86
  177.6 4.8 %all-to-all-start.4 = ((bf16[4,256,384]{2,1,0:T(8,128)(2,1)}), bf16[4,256,384]{2,1,0:T(8,128)(2,1)S(1)}, u32[]{:S(2)}, u32[]{:S(2)}) async-start(bf16[4,256,384]{2,1,0:T(8,128)(2,1)} %bitcast.117), calls=%async_computation.4 | async-start | bytes 1572864 | tf_op jit(solution)/shard_map/all_to_all | solution.py:245
  187.2 9.0 %all_gather.14.k_ref = bf16[1024,384]{1,0:T(8,128)(2,1)} all-gather(bf16[256,384]{1,0:T(8,128)(2,1)S(1)} %multiply_convert_fusion.1), channel_id=1, replica_groups=mesh['groups'=2,'seq'=4,'head'=4] {'seq'}, dimensions={0}, use_global_device_ids=true | all-gather | bytes 983040 | tf_op jit(solution)/shard_map/all_gather | solution.py:228
  198.4 14.1 %shard_map.60 = bf16[1024,384]{1,0:T(8,128)(2,1)} custom-call(s32[96]{0:T(128)} %reshape.176.tbl_ref, bf16[1024,384]{1,0:T(8,128)(2,1)} %bitcast.107, bf16[1024,384]{1,0:T(8,128)(2,1)} %bitcast.94, bf16[1024,384]{1,0:T(8,128)(2,1)} %bitcast.98, bf16[256,384]{1,0:T(8,128)(2,1)} %bitcast.36.refs_2_, bf16[256,384]{1,0:T(8,128)(2,1)} %bitcast.38.refs_3_, ...), custom_call_target="tpu_custom_call" | custom-call | flops 2415919104 | bytes 4325376 | tf_op jit(solution)/shard_map/pallas_call | solution.py:86
  212.5 5.2 %all-to-all-start.5 = ((bf16[4,256,384]{2,1,0:T(8,128)(2,1)}), bf16[4,256,384]{2,1,0:T(8,128)(2,1)}, u32[]{:S(2)}, u32[]{:S(2)}) async-start(bf16[4,256,384]{2,1,0:T(8,128)(2,1)} %bitcast.116), calls=%async_computation.5 | async-start | bytes 1572864 | tf_op jit(solution)/shard_map/all_to_all | solution.py:245
  217.8 8.9 %all_gather.13.v_ref = bf16[1024,384]{1,0:T(8,128)(2,1)} all-gather(bf16[256,384]{1,0:T(8,128)(2,1)S(1)} %copy-done.9), channel_id=1, replica_groups=mesh['groups'=2,'seq'=4,'head'=4] {'seq'}, dimensions={0}, use_global_device_ids=true | all-gather | bytes 983040 | tf_op jit(solution)/shard_map/all_gather | solution.py:229
  230.6 9.2 %all_gather.12.k_ref = bf16[1024,384]{1,0:T(8,128)(2,1)} all-gather(bf16[256,384]{1,0:T(8,128)(2,1)S(1)} %multiply_convert_fusion.3), channel_id=1, replica_groups=mesh['groups'=2,'seq'=4,'head'=4] {'seq'}, dimensions={0}, use_global_device_ids=true | all-gather | bytes 983040 | tf_op jit(solution)/shard_map/all_gather | solution.py:228
  239.8 6.5 %shard_map.59 = bf16[256,384]{1,0:T(8,128)(2,1)} custom-call(bf16[1024,384]{1,0:T(8,128)(2,1)} %bitcast.106, bf16[1024,384]{1,0:T(8,128)(2,1)} %all_gather.12.k_ref, bf16[1024,384]{1,0:T(8,128)(2,1)} %all_gather.13.v_ref), custom_call_target="tpu_custom_call" | custom-call | flops 503316480 | bytes 2555904 | tf_op jit(solution)/shard_map/pallas_call | solution.py:131
  246.3 6.5 %shard_map.61 = bf16[256,384]{1,0:T(8,128)(2,1)} custom-call(bf16[1024,384]{1,0:T(8,128)(2,1)} %bitcast.108, bf16[1024,384]{1,0:T(8,128)(2,1)} %all_gather.14.k_ref, bf16[1024,384]{1,0:T(8,128)(2,1)} %all_gather.15.v_ref), custom_call_target="tpu_custom_call" | custom-call | flops 503316480 | bytes 2555904 | tf_op jit(solution)/shard_map/pallas_call | solution.py:131
  (150 shorter events, 89.6 us)
Async XLA Ops:
  5.4 37.4 %all-to-all-start.2 = ((bf16[256,4,384]{2,0,1:T(8,128)(2,1)}), bf16[256,4,384]{2,0,1:T(8,128)(2,1)S(1)}, u32[]{:S(2)}, u32[]{:S(2)}) async-start(bf16[256,4,384]{2,0,1:T(8,128)(2,1)} %copy.61), calls=%async_computation.2 | async-start | bytes 1572864 | tf_op jit(solution)/shard_map/all_to_all | solution.py:218
  17.1 31.0 %collective-permute-start.12 = (bf16[256,384]{1,0:T(8,128)(2,1)}, bf16[256,384]{1,0:T(8,128)(2,1)S(1)}, u32[]{:S(2)}, u32[]{:S(2)}) collective-permute-start(bf16[256,384]{1,0:T(8,128)(2,1)} %bitcast.42), channel_id=1, source_target_pairs={{0,1},{1,2},{2,3},{3,0},{4,5},{5,6},{6,7},{7,4},{8,9},{9,10},{10,1... | collective-permute-start | bytes 589832 | tf_op jit(solution)/shard_map/ppermute | solution.py:154
  20.0 40.6 %collective-permute-start.13 = (bf16[256,384]{1,0:T(8,128)(2,1)}, bf16[256,384]{1,0:T(8,128)(2,1)}, u32[]{:S(2)}, u32[]{:S(2)}) collective-permute-start(bf16[256,384]{1,0:T(8,128)(2,1)} %bitcast.44), channel_id=1, source_target_pairs={{0,2},{1,3},{2,0},{3,1},{4,6},{5,7},{6,4},{7,5},{8,10},{9,11},{10,... | collective-permute-start | bytes 589832 | tf_op jit(solution)/shard_map/ppermute | solution.py:154
  23.1 37.4 %collective-permute-start.14 = (bf16[256,384]{1,0:T(8,128)(2,1)}, bf16[256,384]{1,0:T(8,128)(2,1)S(1)}, u32[]{:S(2)}, u32[]{:S(2)}) collective-permute-start(bf16[256,384]{1,0:T(8,128)(2,1)} %bitcast.46), channel_id=1, source_target_pairs={{0,3},{1,0},{2,1},{3,2},{4,7},{5,4},{6,5},{7,6},{8,11},{9,8},{10,9... | collective-permute-start | bytes 589832 | tf_op jit(solution)/shard_map/ppermute | solution.py:154
  25.4 38.5 %collective-permute-start.3 = (bf16[256,384]{1,0:T(8,128)(2,1)}, bf16[256,384]{1,0:T(8,128)(2,1)S(1)}, u32[]{:S(2)}, u32[]{:S(2)}) collective-permute-start(bf16[256,384]{1,0:T(8,128)(2,1)} %bitcast.14), channel_id=1, source_target_pairs={{0,1},{1,2},{2,3},{3,0},{4,5},{5,6},{6,7},{7,4},{8,9},{9,10},{10,1... | collective-permute-start | bytes 589832 | tf_op jit(solution)/shard_map/ppermute | solution.py:154
  26.8 44.2 %collective-permute-start.4 = (bf16[256,384]{1,0:T(8,128)(2,1)}, bf16[256,384]{1,0:T(8,128)(2,1)}, u32[]{:S(2)}, u32[]{:S(2)}) collective-permute-start(bf16[256,384]{1,0:T(8,128)(2,1)} %bitcast.16), channel_id=1, source_target_pairs={{0,2},{1,3},{2,0},{3,1},{4,6},{5,7},{6,4},{7,5},{8,10},{9,11},{10,... | collective-permute-start | bytes 589832 | tf_op jit(solution)/shard_map/ppermute | solution.py:154
  42.8 37.1 %all-to-all-start = ((bf16[256,4,384]{2,0,1:T(8,128)(2,1)}), bf16[256,4,384]{2,0,1:T(8,128)(2,1)S(1)}, u32[]{:S(2)}, u32[]{:S(2)}) async-start(bf16[256,4,384]{2,0,1:T(8,128)(2,1)} %copy.60), calls=%async_computation | async-start | bytes 1572864 | tf_op jit(solution)/shard_map/all_to_all | solution.py:218
  48.2 22.9 %collective-permute-start.5 = (bf16[256,384]{1,0:T(8,128)(2,1)}, bf16[256,384]{1,0:T(8,128)(2,1)S(1)}, u32[]{:S(2)}, u32[]{:S(2)}) collective-permute-start(bf16[256,384]{1,0:T(8,128)(2,1)} %bitcast.18), channel_id=1, source_target_pairs={{0,3},{1,0},{2,1},{3,2},{4,7},{5,4},{6,5},{7,6},{8,11},{9,8},{10,9... | collective-permute-start | bytes 589832 | tf_op jit(solution)/shard_map/ppermute | solution.py:154
  85.7 5.7 %collective-permute-start.2 = (bf16[2,128,384]{2,1,0:T(8,128)(2,1)}, bf16[2,128,384]{2,1,0:T(8,128)(2,1)}, u32[]{:S(2)}, u32[]{:S(2)}) collective-permute-start(bf16[2,128,384]{2,1,0:T(8,128)(2,1)} %get-tuple-element.51), channel_id=1, source_target_pairs={{0,12},{4,0},{8,4},{12,8},{1,13},{5,1},{9,5},{13,9},{2,14},{6,2},{... | collective-permute-start | bytes 589832 | tf_op jit(solution)/shard_map/ppermute | solution.py:201
  88.4 6.2 %collective-permute-start.6 = (bf16[2,128,384]{2,1,0:T(8,128)(2,1)S(1)}, bf16[2,128,384]{2,1,0:T(8,128)(2,1)S(1)}, u32[]{:S(2)}, u32[]{:S(2)}) collective-permute-start(bf16[2,128,384]{2,1,0:T(8,128)(2,1)S(1)} %get-tuple-element.46), channel_id=1, source_target_pairs={{0,4},{4,8},{8,12},{12,0},{1,5},{5,9},{9,13},{13,1},{2,6},{6,10},{... | collective-permute-start | bytes 589832 | tf_op jit(solution)/shard_map/ppermute | solution.py:201
  88.9 7.8 %collective-permute-start.7 = (bf16[2,128,384]{2,1,0:T(8,128)(2,1)S(1)}, bf16[2,128,384]{2,1,0:T(8,128)(2,1)S(1)}, u32[]{:S(2)}, u32[]{:S(2)}) collective-permute-start(bf16[2,128,384]{2,1,0:T(8,128)(2,1)S(1)} %get-tuple-element.45), channel_id=1, source_target_pairs={{0,8},{4,12},{8,0},{12,4},{1,9},{5,13},{9,1},{13,5},{2,10},{6,14},... | collective-permute-start | bytes 589832 | tf_op jit(solution)/shard_map/ppermute | solution.py:201
  90.4 9.5 %collective-permute-start.8 = (bf16[2,128,384]{2,1,0:T(8,128)(2,1)S(1)}, bf16[2,128,384]{2,1,0:T(8,128)(2,1)S(1)}, u32[]{:S(2)}, u32[]{:S(2)}) collective-permute-start(bf16[2,128,384]{2,1,0:T(8,128)(2,1)S(1)} %get-tuple-element.44), channel_id=1, source_target_pairs={{0,12},{4,0},{8,4},{12,8},{1,13},{5,1},{9,5},{13,9},{2,14},{6,2},{... | collective-permute-start | bytes 589832 | tf_op jit(solution)/shard_map/ppermute | solution.py:201
  91.4 11.7 %collective-permute-start = (bf16[2,128,384]{2,1,0:T(8,128)(2,1)S(1)}, bf16[2,128,384]{2,1,0:T(8,128)(2,1)S(1)}, u32[]{:S(2)}, u32[]{:S(2)}) collective-permute-start(bf16[2,128,384]{2,1,0:T(8,128)(2,1)S(1)} %get-tuple-element.53), channel_id=1, source_target_pairs={{0,4},{4,8},{8,12},{12,0},{1,5},{5,9},{9,13},{13,1},{2,6},{6,10},{... | collective-permute-start | bytes 589832 | tf_op jit(solution)/shard_map/ppermute | solution.py:201
  91.4 13.7 %collective-permute-start.1 = (bf16[2,128,384]{2,1,0:T(8,128)(2,1)S(1)}, bf16[2,128,384]{2,1,0:T(8,128)(2,1)S(1)}, u32[]{:S(2)}, u32[]{:S(2)}) collective-permute-start(bf16[2,128,384]{2,1,0:T(8,128)(2,1)S(1)} %get-tuple-element.52), channel_id=1, source_target_pairs={{0,8},{4,12},{8,0},{12,4},{1,9},{5,13},{9,1},{13,5},{2,10},{6,14},... | collective-permute-start | bytes 589832 | tf_op jit(solution)/shard_map/ppermute | solution.py:201
  105.8 34.7 %all-to-all-start.1 = ((bf16[256,4,384]{0,2,1:T(8,128)(2,1)}), bf16[256,4,384]{0,2,1:T(8,128)(2,1)S(1)}, u32[]{:S(2)}, u32[]{:S(2)}) async-start(bf16[256,4,384]{0,2,1:T(8,128)(2,1)} %get-tuple-element.42), calls=%async_computation.1 | async-start | bytes 1572864 | tf_op jit(solution)/shard_map/all_to_all | solution.py:227
  120.9 6.2 %collective-permute-start.15 = (bf16[2,128,384]{2,1,0:T(8,128)(2,1)}, bf16[2,128,384]{2,1,0:T(8,128)(2,1)}, u32[]{:S(2)}, u32[]{:S(2)}) collective-permute-start(bf16[2,128,384]{2,1,0:T(8,128)(2,1)} %get-tuple-element.56), channel_id=1, source_target_pairs={{0,4},{4,8},{8,12},{12,0},{1,5},{5,9},{9,13},{13,1},{2,6},{6,10},{... | collective-permute-start | bytes 589832 | tf_op jit(solution)/shard_map/ppermute | solution.py:201
  121.9 8.4 %collective-permute-start.16 = (bf16[2,128,384]{2,1,0:T(8,128)(2,1)S(1)}, bf16[2,128,384]{2,1,0:T(8,128)(2,1)}, u32[]{:S(2)}, u32[]{:S(2)}) collective-permute-start(bf16[2,128,384]{2,1,0:T(8,128)(2,1)S(1)} %get-tuple-element.55), channel_id=1, source_target_pairs={{0,8},{4,12},{8,0},{12,4},{1,9},{5,13},{9,1},{13,5},{2,10},{6,14},... | collective-permute-start | bytes 589832 | tf_op jit(solution)/shard_map/ppermute | solution.py:201
  123.2 9.5 %collective-permute-start.17 = (bf16[2,128,384]{2,1,0:T(8,128)(2,1)S(1)}, bf16[2,128,384]{2,1,0:T(8,128)(2,1)}, u32[]{:S(2)}, u32[]{:S(2)}) collective-permute-start(bf16[2,128,384]{2,1,0:T(8,128)(2,1)S(1)} %get-tuple-element.54), channel_id=1, source_target_pairs={{0,12},{4,0},{8,4},{12,8},{1,13},{5,1},{9,5},{13,9},{2,14},{6,2},{... | collective-permute-start | bytes 589832 | tf_op jit(solution)/shard_map/ppermute | solution.py:201
  126.0 9.5 %collective-permute-start.9 = (bf16[2,128,384]{2,1,0:T(8,128)(2,1)}, bf16[2,128,384]{2,1,0:T(8,128)(2,1)}, u32[]{:S(2)}, u32[]{:S(2)}) collective-permute-start(bf16[2,128,384]{2,1,0:T(8,128)(2,1)} %get-tuple-element.63), channel_id=1, source_target_pairs={{0,4},{4,8},{8,12},{12,0},{1,5},{5,9},{9,13},{13,1},{2,6},{6,10},{... | collective-permute-start | bytes 589832 | tf_op jit(solution)/shard_map/ppermute | solution.py:201
  126.0 12.2 %collective-permute-start.10 = (bf16[2,128,384]{2,1,0:T(8,128)(2,1)}, bf16[2,128,384]{2,1,0:T(8,128)(2,1)}, u32[]{:S(2)}, u32[]{:S(2)}) collective-permute-start(bf16[2,128,384]{2,1,0:T(8,128)(2,1)} %get-tuple-element.62), channel_id=1, source_target_pairs={{0,8},{4,12},{8,0},{12,4},{1,9},{5,13},{9,1},{13,5},{2,10},{6,14},... | collective-permute-start | bytes 589832 | tf_op jit(solution)/shard_map/ppermute | solution.py:201
  127.1 13.0 %collective-permute-start.11 = (bf16[2,128,384]{2,1,0:T(8,128)(2,1)}, bf16[2,128,384]{2,1,0:T(8,128)(2,1)}, u32[]{:S(2)}, u32[]{:S(2)}) collective-permute-start(bf16[2,128,384]{2,1,0:T(8,128)(2,1)} %get-tuple-element.61), channel_id=1, source_target_pairs={{0,12},{4,0},{8,4},{12,8},{1,13},{5,1},{9,5},{13,9},{2,14},{6,2},{... | collective-permute-start | bytes 589832 | tf_op jit(solution)/shard_map/ppermute | solution.py:201
  140.4 37.2 %all-to-all-start.3 = ((bf16[256,4,384]{0,2,1:T(8,128)(2,1)}), bf16[256,4,384]{0,2,1:T(8,128)(2,1)}, u32[]{:S(2)}, u32[]{:S(2)}) async-start(bf16[256,4,384]{0,2,1:T(8,128)(2,1)} %get-tuple-element.43), calls=%async_computation.3 | async-start | bytes 1572864 | tf_op jit(solution)/shard_map/all_to_all | solution.py:227
  177.6 34.9 %all-to-all-start.4 = ((bf16[4,256,384]{2,1,0:T(8,128)(2,1)}), bf16[4,256,384]{2,1,0:T(8,128)(2,1)S(1)}, u32[]{:S(2)}, u32[]{:S(2)}) async-start(bf16[4,256,384]{2,1,0:T(8,128)(2,1)} %bitcast.117), calls=%async_computation.4 | async-start | bytes 1572864 | tf_op jit(solution)/shard_map/all_to_all | solution.py:245
  212.5 42.0 %all-to-all-start.5 = ((bf16[4,256,384]{2,1,0:T(8,128)(2,1)}), bf16[4,256,384]{2,1,0:T(8,128)(2,1)}, u32[]{:S(2)}, u32[]{:S(2)}) async-start(bf16[4,256,384]{2,1,0:T(8,128)(2,1)} %bitcast.116), calls=%async_computation.5 | async-start | bytes 1572864 | tf_op jit(solution)/shard_map/all_to_all | solution.py:245
  (20 other events, 395.3 us)

commit v18 on v16

--- a/solution.py
+++ b/solution.py
@@ -208,13 +208,6 @@
             )
         return [a.reshape(CAP * BLOCK, width) for a in arrivals]
 
-    remote_keys = exchange(key_rows)
-    remote_values = exchange(value_rows)
-    leading, remote_values = lax.optimization_barrier((query_slices[0], remote_values))
-    query_parts = [query_a2a(leading)]
-    later, remote_keys = lax.optimization_barrier((query_slices[1:], remote_keys))
-    query_parts += [query_a2a(piece) for piece in later]
-
     own_lists = lax.dynamic_slice_in_dim(block_lists, seq_index * per_dev, per_dev, 0)
     owners = own_lists // per_dev
     within = own_lists % per_dev
@@ -223,6 +216,15 @@
     distance = (seq_index - owners) % seq_count
     joint_pos = jnp.where(distance == 0, within, per_dev + (distance - 1) * CAP + ranks_used)
     table = jnp.clip(joint_pos, 0, per_dev + (seq_count - 1) * CAP - 1).reshape(-1).astype(jnp.int32)
+
+    remote_keys = exchange(key_rows)
+    remote_values = exchange(value_rows)
+    leading, remote_values, value_rows, table = lax.optimization_barrier(
+        (query_slices[0], remote_values, value_rows, table)
+    )
+    query_parts = [query_a2a(leading)]
+    later, remote_keys = lax.optimization_barrier((query_slices[1:], remote_keys))
+    query_parts += [query_a2a(piece) for piece in later]
 
     pieces = []
     for index, ((head_lo, count), queries) in enumerate(zip(spans, query_parts)):

time: 220 us -> 220 us (level)
  waiting for transfers between devices: 68.1 us -> 73.3 us
  local copies, waits for them, and re-layouts: 37.7 us -> 33.4 us
    ppermute x6, waiting for transfers between devices: 17.6 us -> 23.5 us  [exchange(): lax.ppermute(parcel, 'seq', [(i, (i + shift) % seq_count) for i in range(...]
    all_to_all x2, waiting for transfers between devices: 0.9 us -> 5.91 us  [query_a2a(): lax.all_to_all(piece, 'head', split_axis=1, concat_axis=0, tiled=True)]
    ppermute x3, waiting for transfers between devices: 30.4 us -> 26.2 us  [head_permutes(): lax.ppermute(piece, 'head', [(i, (i + shift) % count) for i in range(coun...]
  transfers between devices with their start and end apart: 16 -> 16, of which waited for: 10 -> 12; matrix products, arithmetic and copies ran while one was open for 26% -> 24% of each run, Pallas kernels for 19% -> 19%
where the time goes in v18:
time: 220 us; the launch traced here: 219 us
  waiting for transfers between devices  73.3 us (33%)
  Pallas kernels  41.3 us (19%)
  local copies, waits for them, and re-layouts  33.4 us (15%)
  starting transfers between devices  32.6 us (15%)
  other arithmetic  23.7 us (11%)
  between operations  14.4 us (7%)
    pallas_call x2, Pallas kernels, sparse_attention(): pl.pallas_call(sparse_kernel, out_shape=jax.ShapeDtypeStruct((rows, heads...  28.2 us
    ppermute x3, waiting for transfers between devices, head_permutes(): lax.ppermute(piece, 'head', [(i, (i + shift) % count) for i in range(coun...  26.2 us
    ppermute x6, waiting for transfers between devices, exchange(): lax.ppermute(parcel, 'seq', [(i, (i + shift) % seq_count) for i in range(...  23.5 us
    pallas_call x2, Pallas kernels, draft_attention(): pl.pallas_call(draft_kernel, out_shape=jax.ShapeDtypeStruct((rows, width)...  13.1 us
    all_to_all x2, waiting for transfers between devices, on_device(): lax.all_to_all(rows_part, 'head', split_axis=0, concat_axis=1, tiled=True)  9.8 us
    all_to_all x2, starting transfers between devices, query_a2a(): lax.all_to_all(piece, 'head', split_axis=1, concat_axis=0, tiled=True)  8.86 us
    all_to_all x1, waiting for transfers between devices, on_device(): lax.all_to_all(key_in, 'head', split_axis=1, concat_axis=0, tiled=True)  7.81 us
    all_to_all x2, starting transfers between devices, on_device(): lax.all_to_all(rows_part, 'head', split_axis=0, concat_axis=1, tiled=True)  6.99 us
  transfers between devices with their start and end apart: 16, of which 12 were waited for; matrix products, arithmetic and copies ran while one was open for 24% of the time, Pallas kernels for 19%

profile of v18, /device:TPU:0, one launch (start us, length us, event | category | flops | bytes accessed | tf_op | source)
XLA Modules:
  0.0 218.6 jit_solution(7094500042887655078)
XLA Ops:
  10.7 5.0 %collective-permute-start.2 = (bf16[256,768]{1,0:T(8,128)(2,1)}, bf16[256,768]{1,0:T(8,128)(2,1)}, u32[]{:S(2)}, u32[]{:S(2)}) collective-permute-start(bf16[256,768]{1,0:T(8,128)(2,1)} %bitcast.9), channel_id=1, source_target_pairs={{0,3},{1,0},{2,1},{3,2},{4,7},{5,4},{6,5},{7,6},{8,11},{9,8},{10,9... | collective-permute-start | bytes 1179656 | tf_op jit(solution)/shard_map/ppermute | solution.py:154
  19.9 4.8 %all-to-all-start.1 = ((bf16[256,4,768]{2,0,1:T(8,128)(2,1)}), bf16[256,4,768]{2,0,1:T(8,128)(2,1)S(1)}, u32[]{:S(2)}, u32[]{:S(2)}) async-start(bf16[256,4,768]{2,0,1:T(8,128)(2,1)} %bitcast.63), calls=%async_computation.1 | async-start | bytes 3145728 | tf_op jit(solution)/shard_map/all_to_all | solution.py:162
  35.1 25.3 %collective-permute-done.1 = bf16[256,768]{1,0:T(8,128)(2,1)} collective-permute-done((bf16[256,768]{1,0:T(8,128)(2,1)}, bf16[256,768]{1,0:T(8,128)(2,1)}, u32[]{:S(2)}, u32[]{:S(2)}) %collective-permute-start.1) | collective-permute-done | bytes 393248 | tf_op jit(solution)/shard_map/ppermute | solution.py:154
  60.4 2.6 %pad_maximum_fusion = bf16[4,256,768]{2,1,0:T(8,128)(2,1)} fusion(bf16[1,256,768]{2,1,0:T(8,128)(2,1)} %bitcast.10, bf16[1,256,768]{2,1,0:T(8,128)(2,1)} %bitcast.8, bf16[1,256,768]{2,1,0:T(8,128)(2,1)} %bitcast.6, bf16[1,256,768]{2,1,0:T(8,128)(2,1)S(1)} %bitcast.82), kind=kLoop, calls=%fused_computation.6 | loop fusion | flops 2359296 | bytes 3145728 | tf_op jit(solution)/shard_map/stack | solution.py:156
  66.4 3.6 %convert_reduce_fusion = f32[256,768]{1,0:T(8,128)S(1)} fusion(bf16[256,4,768]{2,1,0:T(4,128)(2,1)} %gather.20, pred[256]{0:T(512)(128)(4,1)S(1)} %copy-done.7), kind=kLoop, calls=%fused_computation.4 | loop fusion | flops 2162688 | bytes 2359552 | tf_op jit(solution)/shard_map/reduce_sum | solution.py:20
  72.2 3.2 %gather_fusion.2 = bf16[8,128,768]{2,1,0:T(8,128)(2,1)} fusion(bf16[8,128,768]{2,1,0:T(8,128)(2,1)} %broadcast_select_fusion.2, s32[1024]{0:T(1024)S(1)} %pad_clamp_fusion), kind=kCustom, calls=%fused_computation.clone | custom fusion | bytes 3145760 | tf_op jit(solution)/shard_map/jit(_take)/gather | solution.py:197
  75.5 7.8 %all-to-all-done.1 = bf16[256,4,768]{2,0,1:T(8,128)(2,1)S(1)} async-done(((bf16[256,4,768]{2,0,1:T(8,128)(2,1)}), bf16[256,4,768]{2,0,1:T(8,128)(2,1)S(1)}, u32[]{:S(2)}, u32[]{:S(2)}) %all-to-all-start.1) | async-done | bytes 1572896 | tf_op jit(solution)/shard_map/all_to_all | solution.py:162
  85.1 3.5 %broadcast_select_fusion.1 = (bf16[8,128,768]{2,1,0:T(8,128)(2,1)S(1)}, bf16[8,128,768]{2,1,0:T(8,128)(2,1)}) fusion(bf16[8,128,768]{2,1,0:T(8,128)(2,1)} %gather_fusion.2, pred[8]{0:T(512)(128)(4,1)S(1)} %copy-done.6, bf16[8,128,768]{2,1,0:T(8,128)(2,1)} %gather_fusion.3), kind=kLoop, calls=%fused_computation.11 | loop fusion | flops 1572864 | bytes 6291464 | tf_op jit(solution)/shard_map/jit(_take)/select_n | solution.py:197
  94.8 11.0 %collective-permute-done.3 = bf16[2,128,768]{2,1,0:T(8,128)(2,1)} collective-permute-done((bf16[2,128,768]{2,1,0:T(8,128)(2,1)}, bf16[2,128,768]{2,1,0:T(8,128)(2,1)}, u32[]{:S(2)}, u32[]{:S(2)}) %collective-permute-start.3) | collective-permute-done | bytes 393248 | tf_op jit(solution)/shard_map/ppermute | solution.py:205
  106.2 6.0 %collective-permute-done.5 = bf16[2,128,768]{2,1,0:T(8,128)(2,1)} collective-permute-done((bf16[2,128,768]{2,1,0:T(8,128)(2,1)S(1)}, bf16[2,128,768]{2,1,0:T(8,128)(2,1)}, u32[]{:S(2)}, u32[]{:S(2)}) %collective-permute-start.5) | collective-permute-done | bytes 393248 | tf_op jit(solution)/shard_map/ppermute | solution.py:205
  112.2 4.8 %all-to-all-start = ((bf16[256,4,384]{0,2,1:T(8,128)(2,1)}), bf16[256,4,384]{0,2,1:T(8,128)(2,1)}, u32[]{:S(2)}, u32[]{:S(2)}) async-start(bf16[256,4,384]{0,2,1:T(8,128)(2,1)} %get-tuple-element.36), calls=%async_computation | async-start | bytes 1572864 | tf_op jit(solution)/shard_map/all_to_all | solution.py:175
  122.9 3.1 %reshape.170 = f32[256,4,768]{2,1,0:T(4,128)S(1)} reshape(f32[4,256,768]{2,1,0:T(8,128)} %bitcast_convert_fusion) | data formatting | bytes 6291456 | tf_op jit(solution)/shard_map/convert_element_type | solution.py:19
  126.0 3.0 %reduce_sum.28 = f32[256,768]{1,0:T(8,128)} reduce(f32[256,4,768]{2,1,0:T(4,128)S(1)} %reshape.170, f32[]{:T(128)} %constant.170.clone.1), dimensions={1}, to_apply=%region_4.6 | reduce | flops 589824 | bytes 3932164 | tf_op jit(solution)/shard_map/reduce_sum | solution.py:20
  131.9 5.1 %collective-permute-done.8 = bf16[2,128,768]{2,1,0:T(8,128)(2,1)} collective-permute-done((bf16[2,128,768]{2,1,0:T(8,128)(2,1)S(1)}, bf16[2,128,768]{2,1,0:T(8,128)(2,1)}, u32[]{:S(2)}, u32[]{:S(2)}) %collective-permute-start.8) | collective-permute-done | bytes 393248 | tf_op jit(solution)/shard_map/ppermute | solution.py:205
  138.1 4.0 %all-to-all-start.2 = ((bf16[256,4,384]{0,2,1:T(8,128)(2,1)}), bf16[256,4,384]{0,2,1:T(8,128)(2,1)S(1)}, u32[]{:S(2)}, u32[]{:S(2)}) async-start(bf16[256,4,384]{0,2,1:T(8,128)(2,1)} %bitcast.35), calls=%async_computation.2 | async-start | bytes 1572864 | tf_op jit(solution)/shard_map/all_to_all | solution.py:175
  144.4 14.1 %shard_map.62 = bf16[1024,384]{1,0:T(8,128)(2,1)} custom-call(s32[96]{0:T(128)} %reshape.162.tbl_ref, bf16[1024,384]{1,0:T(8,128)(2,1)} %bitcast.76, bf16[1024,768]{1,0:T(8,128)(2,1)} %bitcast.67, bf16[1024,768]{1,0:T(8,128)(2,1)} %bitcast_select_fusion.refs_1_, bf16[256,768]{1,0:T(8,128)(2,1)} %bitcast.30.refs_2_, bf16[256,768]{1,0:T(8,128)(2,1)} %bitcast.32.refs_3_, ...), custom_call_target="tpu_custom_call" | custom-call | flops 2415919104 | bytes 4325376 | tf_op jit(solution)/shard_map/pallas_call | solution.py:86
  158.5 4.8 %all-to-all-done.2 = bf16[256,4,384]{0,2,1:T(8,128)(2,1)S(1)} async-done(((bf16[256,4,384]{0,2,1:T(8,128)(2,1)}), bf16[256,4,384]{0,2,1:T(8,128)(2,1)S(1)}, u32[]{:S(2)}, u32[]{:S(2)}) %all-to-all-start.2) | async-done | bytes 786464 | tf_op jit(solution)/shard_map/all_to_all | solution.py:175
  163.4 3.5 %all-to-all-start.3 = ((bf16[4,256,384]{2,1,0:T(8,128)(2,1)}), bf16[4,256,384]{2,1,0:T(8,128)(2,1)S(1)}, u32[]{:S(2)}, u32[]{:S(2)}) async-start(bf16[4,256,384]{2,1,0:T(8,128)(2,1)} %bitcast.84), calls=%async_computation.3 | async-start | bytes 1572864 | tf_op jit(solution)/shard_map/all_to_all | solution.py:238
  168.0 14.1 %shard_map.59 = bf16[1024,384]{1,0:T(8,128)(2,1)} custom-call(s32[96]{0:T(128)} %reshape.162.tbl_ref, bf16[1024,384]{1,0:T(8,128)(2,1)} %bitcast.78, bf16[1024,768]{1,0:T(8,128)(2,1)} %bitcast.68, bf16[1024,768]{1,0:T(8,128)(2,1)} %bitcast_select_fusion.refs_1_, bf16[256,768]{1,0:T(8,128)(2,1)} %bitcast.30.refs_2_, bf16[256,768]{1,0:T(8,128)(2,1)} %bitcast.32.refs_3_, ...), custom_call_target="tpu_custom_call" | custom-call | flops 2415919104 | bytes 4325376 | tf_op jit(solution)/shard_map/pallas_call | solution.py:86
  182.2 5.0 %all-to-all-done.3 = bf16[4,256,384]{2,1,0:T(8,128)(2,1)S(1)} async-done(((bf16[4,256,384]{2,1,0:T(8,128)(2,1)}), bf16[4,256,384]{2,1,0:T(8,128)(2,1)S(1)}, u32[]{:S(2)}, u32[]{:S(2)}) %all-to-all-start.3) | async-done | bytes 786464 | tf_op jit(solution)/shard_map/all_to_all | solution.py:238
  187.2 3.5 %all-to-all-start.4 = ((bf16[4,256,384]{2,1,0:T(8,128)(2,1)}), bf16[4,256,384]{2,1,0:T(8,128)(2,1)S(1)}, u32[]{:S(2)}, u32[]{:S(2)}) async-start(bf16[4,256,384]{2,1,0:T(8,128)(2,1)} %bitcast.83), calls=%async_computation.4 | async-start | bytes 1572864 | tf_op jit(solution)/shard_map/all_to_all | solution.py:238
  190.7 6.5 %shard_map.60 = bf16[256,384]{1,0:T(8,128)(2,1)} custom-call(bf16[1024,384]{1,0:T(8,128)(2,1)} %bitcast.77, bf16[1024,768]{1,0:T(8,128)(2,1)} %all-gather.3.cloned.1.call-done.k_ref, bf16[1024,768]{1,0:T(8,128)(2,1)} %all-gather.5.cloned.1.call-done.v_ref), custom_call_target="tpu_custom_call" | custom-call | flops 503316480 | bytes 2555904 | tf_op jit(solution)/shard_map/pallas_call | solution.py:131
  197.2 6.6 %shard_map.61 = bf16[256,384]{1,0:T(8,128)(2,1)} custom-call(bf16[1024,384]{1,0:T(8,128)(2,1)} %bitcast.79, bf16[1024,768]{1,0:T(8,128)(2,1)} %all-gather.3.cloned.1.call-done.k_ref, bf16[1024,768]{1,0:T(8,128)(2,1)} %all-gather.5.cloned.1.call-done.v_ref), custom_call_target="tpu_custom_call" | custom-call | flops 503316480 | bytes 2555904 | tf_op jit(solution)/shard_map/pallas_call | solution.py:131
  205.5 4.8 %all-to-all-done.4 = bf16[4,256,384]{2,1,0:T(8,128)(2,1)S(1)} async-done(((bf16[4,256,384]{2,1,0:T(8,128)(2,1)}), bf16[4,256,384]{2,1,0:T(8,128)(2,1)S(1)}, u32[]{:S(2)}, u32[]{:S(2)}) %all-to-all-start.4) | async-done | bytes 786464 | tf_op jit(solution)/shard_map/all_to_all | solution.py:238
  (100 shorter events, 48.4 us)
Async XLA Ops:
  9.8 8.9 %copy-start.2 = (bf16[256,3072]{1,0:T(8,128)(2,1)S(1)}, bf16[256,3072]{1,0:T(8,128)(2,1)}, u32[]{:S(2)}) copy-start(bf16[256,3072]{1,0:T(8,128)(2,1)} %param.7) | copy-start | bytes 4718596
  10.7 23.5 %collective-permute-start.2 = (bf16[256,768]{1,0:T(8,128)(2,1)}, bf16[256,768]{1,0:T(8,128)(2,1)}, u32[]{:S(2)}, u32[]{:S(2)}) collective-permute-start(bf16[256,768]{1,0:T(8,128)(2,1)} %bitcast.9), channel_id=1, source_target_pairs={{0,3},{1,0},{2,1},{3,2},{4,7},{5,4},{6,5},{7,6},{8,11},{9,8},{10,9... | collective-permute-start | bytes 1179656 | tf_op jit(solution)/shard_map/ppermute | solution.py:154
  16.7 18.4 %collective-permute-start = (bf16[256,768]{1,0:T(8,128)(2,1)}, bf16[256,768]{1,0:T(8,128)(2,1)}, u32[]{:S(2)}, u32[]{:S(2)}) collective-permute-start(bf16[256,768]{1,0:T(8,128)(2,1)} %bitcast.5), channel_id=1, source_target_pairs={{0,1},{1,2},{2,3},{3,0},{4,5},{5,6},{6,7},{7,4},{8,9},{9,10},{10,1... | collective-permute-start | bytes 1179656 | tf_op jit(solution)/shard_map/ppermute | solution.py:154
  17.6 42.8 %collective-permute-start.1 = (bf16[256,768]{1,0:T(8,128)(2,1)}, bf16[256,768]{1,0:T(8,128)(2,1)}, u32[]{:S(2)}, u32[]{:S(2)}) collective-permute-start(bf16[256,768]{1,0:T(8,128)(2,1)} %bitcast.7), channel_id=1, source_target_pairs={{0,2},{1,3},{2,0},{3,1},{4,6},{5,7},{6,4},{7,5},{8,10},{9,11},{10,... | collective-permute-start | bytes 1179656 | tf_op jit(solution)/shard_map/ppermute | solution.py:154
  19.9 4.8 %copy-start.5 = (s32[32,12]{0,1:T(8,128)S(1)}, s32[32,12]{0,1:T(8,128)}, u32[]{:S(2)}) copy-start(s32[32,12]{0,1:T(8,128)} %param.9) | copy-start | bytes 4612
  19.9 6.2 %copy-start.3 = (bf16[256,1,768]{0,2,1:T(8,128)(2,1)S(1)}, bf16[256,1,768]{0,2,1:T(8,128)(2,1)}, u32[]{:S(2)}) copy-start(bf16[256,1,768]{0,2,1:T(8,128)(2,1)} %get-tuple-element.32) | copy-start | bytes 1179652
  19.9 63.4 %all-to-all-start.1 = ((bf16[256,4,768]{2,0,1:T(8,128)(2,1)}), bf16[256,4,768]{2,0,1:T(8,128)(2,1)S(1)}, u32[]{:S(2)}, u32[]{:S(2)}) async-start(bf16[256,4,768]{2,0,1:T(8,128)(2,1)} %bitcast.63), calls=%async_computation.1 | async-start | bytes 3145728 | tf_op jit(solution)/shard_map/all_to_all | solution.py:162
  24.7 157.5 %all-gather.5.cloned.1.call-start = ((), (), s32[]{:S(2)}) async-start(), calls=%async_computation.6 | async-start | bytes 1966080 | tf_op jit(solution)/shard_map/all_gather | solution.py:178
  26.1 4.5 %copy-start.9 = (pred[4]{0:T(512)(128)(4,1)}, pred[4]{0:T(512)(128)(4,1)S(1)}, u32[]{:S(2)}) copy-start(pred[4]{0:T(512)(128)(4,1)S(1)} %compare_and_fusion.1) | copy-start | bytes 16
  66.4 4.5 %copy-start.8 = (pred[8]{0:T(512)(128)(4,1)S(1)}, pred[8]{0:T(512)(128)(4,1)}, u32[]{:S(2)}) copy-start(pred[8]{0:T(512)(128)(4,1)} %broadcast_in_dim.64) | copy-start | bytes 28
  83.3 37.7 %copy-start = (bf16[256,4,768]{2,0,1:T(8,128)(2,1)}, bf16[256,4,768]{2,0,1:T(8,128)(2,1)S(1)}, u32[]{:S(2)}) copy-start(bf16[256,4,768]{2,0,1:T(8,128)(2,1)S(1)} %all-to-all-done.1) | copy-start | bytes 4718596
  89.6 16.2 %collective-permute-start.3 = (bf16[2,128,768]{2,1,0:T(8,128)(2,1)}, bf16[2,128,768]{2,1,0:T(8,128)(2,1)}, u32[]{:S(2)}, u32[]{:S(2)}) collective-permute-start(bf16[2,128,768]{2,1,0:T(8,128)(2,1)} %get-tuple-element.31), channel_id=1, source_target_pairs={{0,4},{4,8},{8,12},{12,0},{1,5},{5,9},{9,13},{13,1},{2,6},{6,10},{... | collective-permute-start | bytes 1179656 | tf_op jit(solution)/shard_map/ppermute | solution.py:205
  89.6 16.6 %collective-permute-start.4 = (bf16[2,128,768]{2,1,0:T(8,128)(2,1)}, bf16[2,128,768]{2,1,0:T(8,128)(2,1)}, u32[]{:S(2)}, u32[]{:S(2)}) collective-permute-start(bf16[2,128,768]{2,1,0:T(8,128)(2,1)} %get-tuple-element.30), channel_id=1, source_target_pairs={{0,8},{4,12},{8,0},{12,4},{1,9},{5,13},{9,1},{13,5},{2,10},{6,14},... | collective-permute-start | bytes 1179656 | tf_op jit(solution)/shard_map/ppermute | solution.py:205
  91.1 21.0 %collective-permute-start.5 = (bf16[2,128,768]{2,1,0:T(8,128)(2,1)S(1)}, bf16[2,128,768]{2,1,0:T(8,128)(2,1)}, u32[]{:S(2)}, u32[]{:S(2)}) collective-permute-start(bf16[2,128,768]{2,1,0:T(8,128)(2,1)S(1)} %get-tuple-element.29), channel_id=1, source_target_pairs={{0,12},{4,0},{8,4},{12,8},{1,13},{5,1},{9,5},{13,9},{2,14},{6,2},{... | collective-permute-start | bytes 1179656 | tf_op jit(solution)/shard_map/ppermute | solution.py:205
  94.8 22.2 %copy-start.1 = (bf16[8,128,768]{2,1,0:T(8,128)(2,1)S(1)}, bf16[8,128,768]{2,1,0:T(8,128)(2,1)}, u32[]{:S(2)}) copy-start(bf16[8,128,768]{2,1,0:T(8,128)(2,1)} %get-tuple-element.42) | copy-start | bytes 4718596
  112.2 25.9 %all-to-all-start = ((bf16[256,4,384]{0,2,1:T(8,128)(2,1)}), bf16[256,4,384]{0,2,1:T(8,128)(2,1)}, u32[]{:S(2)}, u32[]{:S(2)}) async-start(bf16[256,4,384]{0,2,1:T(8,128)(2,1)} %get-tuple-element.36), calls=%async_computation | async-start | bytes 1572864 | tf_op jit(solution)/shard_map/all_to_all | solution.py:175
  117.0 65.1 %all-gather.3.cloned.1.call-start = ((), (), s32[]{:S(2)}) async-start(), calls=%async_computation.5 | async-start | bytes 1966080 | tf_op jit(solution)/shard_map/all_gather | solution.py:177
  118.0 12.9 %collective-permute-start.6 = (bf16[2,128,768]{2,1,0:T(8,128)(2,1)}, bf16[2,128,768]{2,1,0:T(8,128)(2,1)}, u32[]{:S(2)}, u32[]{:S(2)}) collective-permute-start(bf16[2,128,768]{2,1,0:T(8,128)(2,1)} %get-tuple-element.40), channel_id=1, source_target_pairs={{0,4},{4,8},{8,12},{12,0},{1,5},{5,9},{9,13},{13,1},{2,6},{6,10},{... | collective-permute-start | bytes 1179656 | tf_op jit(solution)/shard_map/ppermute | solution.py:205
  119.6 12.4 %collective-permute-start.7 = (bf16[2,128,768]{2,1,0:T(8,128)(2,1)}, bf16[2,128,768]{2,1,0:T(8,128)(2,1)}, u32[]{:S(2)}, u32[]{:S(2)}) collective-permute-start(bf16[2,128,768]{2,1,0:T(8,128)(2,1)} %get-tuple-element.39), channel_id=1, source_target_pairs={{0,8},{4,12},{8,0},{12,4},{1,9},{5,13},{9,1},{13,5},{2,10},{6,14},... | collective-permute-start | bytes 1179656 | tf_op jit(solution)/shard_map/ppermute | solution.py:205
  120.1 16.9 %collective-permute-start.8 = (bf16[2,128,768]{2,1,0:T(8,128)(2,1)S(1)}, bf16[2,128,768]{2,1,0:T(8,128)(2,1)}, u32[]{:S(2)}, u32[]{:S(2)}) collective-permute-start(bf16[2,128,768]{2,1,0:T(8,128)(2,1)S(1)} %get-tuple-element.38), channel_id=1, source_target_pairs={{0,12},{4,0},{8,4},{12,8},{1,13},{5,1},{9,5},{13,9},{2,14},{6,2},{... | collective-permute-start | bytes 1179656 | tf_op jit(solution)/shard_map/ppermute | solution.py:205
  138.1 25.2 %all-to-all-start.2 = ((bf16[256,4,384]{0,2,1:T(8,128)(2,1)}), bf16[256,4,384]{0,2,1:T(8,128)(2,1)S(1)}, u32[]{:S(2)}, u32[]{:S(2)}) async-start(bf16[256,4,384]{0,2,1:T(8,128)(2,1)} %bitcast.35), calls=%async_computation.2 | async-start | bytes 1572864 | tf_op jit(solution)/shard_map/all_to_all | solution.py:175
  163.4 23.8 %all-to-all-start.3 = ((bf16[4,256,384]{2,1,0:T(8,128)(2,1)}), bf16[4,256,384]{2,1,0:T(8,128)(2,1)S(1)}, u32[]{:S(2)}, u32[]{:S(2)}) async-start(bf16[4,256,384]{2,1,0:T(8,128)(2,1)} %bitcast.84), calls=%async_computation.3 | async-start | bytes 1572864 | tf_op jit(solution)/shard_map/all_to_all | solution.py:238
  187.2 23.1 %all-to-all-start.4 = ((bf16[4,256,384]{2,1,0:T(8,128)(2,1)}), bf16[4,256,384]{2,1,0:T(8,128)(2,1)S(1)}, u32[]{:S(2)}, u32[]{:S(2)}) async-start(bf16[4,256,384]{2,1,0:T(8,128)(2,1)} %bitcast.83), calls=%async_computation.4 | async-start | bytes 1572864 | tf_op jit(solution)/shard_map/all_to_all | solution.py:238
  197.2 6.6 %copy-start.4 = (bf16[256,384]{1,0:T(8,128)(2,1)S(1)}, bf16[256,384]{1,0:T(8,128)(2,1)}, u32[]{:S(2)}) copy-start(bf16[256,384]{1,0:T(8,128)(2,1)} %shard_map.60) | copy-start | bytes 589828
  (3 other events, 7.2 us)
Sparse Core Ops, SparseCore 0:
  71.0 32.6 all-gather.4
  131.0 20.1 all-gather.2

commit v19 on v18

--- a/solution.py
+++ b/solution.py
@@ -174,8 +174,6 @@
     def query_a2a(piece):
         return lax.all_to_all(piece, "head", split_axis=1, concat_axis=0, tiled=True)
 
-    draft_keys = lax.all_gather(pool_tokens(key_rows), "seq", axis=0, tiled=True)
-    draft_values = lax.all_gather(pool_tokens(value_rows), "seq", axis=0, tiled=True)
 
     seq_count = lax.axis_size("seq")
     seq_index = lax.axis_index("seq")
@@ -219,9 +217,16 @@
 
     remote_keys = exchange(key_rows)
     remote_values = exchange(value_rows)
-    leading, remote_values, value_rows, table = lax.optimization_barrier(
-        (query_slices[0], remote_values, value_rows, table)
-    )
+    leading, remote_values, value_rows, table, pooled_keys, pooled_values = (
+        lax.optimization_barrier(
+            (
+                query_slices[0], remote_values, value_rows, table,
+                pool_tokens(key_rows), pool_tokens(value_rows),
+            )
+        )
+    )
+    draft_keys = lax.all_gather(pooled_keys, "seq", axis=0, tiled=True)
+    draft_values = lax.all_gather(pooled_values, "seq", axis=0, tiled=True)
     query_parts = [query_a2a(leading)]
     later, remote_keys = lax.optimization_barrier((query_slices[1:], remote_keys))
     query_parts += [query_a2a(piece) for piece in later]

time: 220 us -> 224 us (1.018)
  waiting for transfers between devices: 73.3 us -> 79.1 us
  local copies, waits for them, and re-layouts: 33.4 us -> 30.3 us
    ppermute x6, waiting for transfers between devices: 23.5 us -> 29.9 us  [exchange(): lax.ppermute(parcel, 'seq', [(i, (i + shift) % seq_count) for i in range(...]
  transfers between devices with their start and end apart: 16 -> 16, of which waited for: 12 -> 10; matrix products, arithmetic and copies ran while one was open for 24% -> 19% of each run, Pallas kernels for 19% -> 19%
where the time goes in v19:
time: 224 us; the launch traced here: 223 us
  waiting for transfers between devices  79.1 us (35%)
  Pallas kernels  41.4 us (18%)
  starting transfers between devices  33.7 us (15%)
  local copies, waits for them, and re-layouts  30.3 us (14%)
  other arithmetic  23.6 us (11%)
  between operations  14.4 us (6%)
    ppermute x6, waiting for transfers between devices, exchange(): lax.ppermute(parcel, 'seq', [(i, (i + shift) % seq_count) for i in range(...  29.9 us
    pallas_call x2, Pallas kernels, sparse_attention(): pl.pallas_call(sparse_kernel, out_shape=jax.ShapeDtypeStruct((rows, heads...  28.3 us
    ppermute x3, waiting for transfers between devices, head_permutes(): lax.ppermute(piece, 'head', [(i, (i + shift) % count) for i in range(coun...  26.5 us
    pallas_call x2, Pallas kernels, draft_attention(): pl.pallas_call(draft_kernel, out_shape=jax.ShapeDtypeStruct((rows, width)...  13.1 us
    all_to_all x2, starting transfers between devices, query_a2a(): lax.all_to_all(piece, 'head', split_axis=1, concat_axis=0, tiled=True)  10.8 us
    all_to_all x2, waiting for transfers between devices, on_device(): lax.all_to_all(rows_part, 'head', split_axis=0, concat_axis=1, tiled=True)  10.7 us
    reduce_sum x2, other arithmetic, pool_tokens(): return (grouped.sum(axis=1) * POOL ** (-0.5)).astype(jnp.bfloat16)  7.5 us
    all_to_all x2, starting transfers between devices, on_device(): lax.all_to_all(rows_part, 'head', split_axis=0, concat_axis=1, tiled=True)  6.99 us
  transfers between devices with their start and end apart: 16, of which 10 were waited for; matrix products, arithmetic and copies ran while one was open for 19% of the time, Pallas kernels for 19%

profile of v19, /device:TPU:0, one launch (start us, length us, event | category | flops | bytes accessed | tf_op | source)
XLA Modules:
  0.0 222.5 jit_solution(1652063765410308925)
XLA Ops:
  10.0 5.0 %collective-permute-start.2 = (bf16[256,768]{1,0:T(8,128)(2,1)}, bf16[256,768]{1,0:T(8,128)(2,1)}, u32[]{:S(2)}, u32[]{:S(2)}) collective-permute-start(bf16[256,768]{1,0:T(8,128)(2,1)} %bitcast.9), channel_id=1, source_target_pairs={{0,3},{1,0},{2,1},{3,2},{4,7},{5,4},{6,5},{7,6},{8,11},{9,8},{10,9... | collective-permute-start | bytes 1179656 | tf_op jit(solution)/shard_map/ppermute | solution.py:154
  19.2 4.8 %all-to-all-start = ((bf16[256,4,768]{2,0,1:T(8,128)(2,1)}), bf16[256,4,768]{2,0,1:T(8,128)(2,1)S(1)}, u32[]{:S(2)}, u32[]{:S(2)}) async-start(bf16[256,4,768]{2,0,1:T(8,128)(2,1)} %bitcast.63), calls=%async_computation | async-start | bytes 3145728 | tf_op jit(solution)/shard_map/all_to_all | solution.py:162
  34.4 25.3 %collective-permute-done.1 = bf16[256,768]{1,0:T(8,128)(2,1)} collective-permute-done((bf16[256,768]{1,0:T(8,128)(2,1)}, bf16[256,768]{1,0:T(8,128)(2,1)}, u32[]{:S(2)}, u32[]{:S(2)}) %collective-permute-start.1) | collective-permute-done | bytes 393248 | tf_op jit(solution)/shard_map/ppermute | solution.py:154
  67.0 3.2 %gather_fusion.2 = bf16[8,128,768]{2,1,0:T(8,128)(2,1)} fusion(bf16[8,128,768]{2,1,0:T(8,128)(2,1)} %broadcast_select_fusion.2, s32[1024]{0:T(1024)S(1)} %pad_clamp_fusion), kind=kCustom, calls=%fused_computation.clone | custom fusion | bytes 3145760 | tf_op jit(solution)/shard_map/jit(_take)/gather | solution.py:195
  70.2 4.5 %convert_reduce_fusion = f32[256,768]{1,0:T(8,128)} fusion(bf16[256,4,768]{2,1,0:T(4,128)(2,1)} %gather.20, pred[256]{0:T(512)(128)(4,1)S(1)} %broadcast_in_dim.76), kind=kLoop, calls=%fused_computation.4 | loop fusion | flops 2162688 | bytes 2359552 | tf_op jit(solution)/shard_map/reduce_sum | solution.py:20
  76.2 6.3 %all-to-all-done = bf16[256,4,768]{2,0,1:T(8,128)(2,1)S(1)} async-done(((bf16[256,4,768]{2,0,1:T(8,128)(2,1)}), bf16[256,4,768]{2,0,1:T(8,128)(2,1)S(1)}, u32[]{:S(2)}, u32[]{:S(2)}) %all-to-all-start) | async-done | bytes 1572896 | tf_op jit(solution)/shard_map/all_to_all | solution.py:162
  85.1 2.9 %broadcast_select_fusion.1 = (bf16[8,128,768]{2,1,0:T(8,128)(2,1)S(1)}, bf16[8,128,768]{2,1,0:T(8,128)(2,1)}) fusion(bf16[8,128,768]{2,1,0:T(8,128)(2,1)S(1)} %copy-done.1, pred[8]{0:T(512)(128)(4,1)S(1)} %copy-done.6, bf16[8,128,768]{2,1,0:T(8,128)(2,1)} %gather_fusion.3), kind=kLoop, calls=%fused_computation.11 | loop fusion | flops 1572864 | bytes 6291464 | tf_op jit(solution)/shard_map/jit(_take)/select_n | solution.py:195
  93.9 3.1 %reshape.170 = f32[256,4,768]{2,1,0:T(4,128)S(1)} reshape(f32[4,256,768]{2,1,0:T(8,128)} %bitcast_convert_fusion) | data formatting | bytes 6291456 | tf_op jit(solution)/shard_map/convert_element_type | solution.py:19
  97.0 3.0 %reduce_sum.28 = f32[256,768]{1,0:T(8,128)} reduce(f32[256,4,768]{2,1,0:T(4,128)S(1)} %reshape.170, f32[]{:T(128)} %constant.170.clone.1), dimensions={1}, to_apply=%region_4.6 | reduce | flops 589824 | bytes 3932164 | tf_op jit(solution)/shard_map/reduce_sum | solution.py:20
  102.3 5.7 %collective-permute-done.5 = bf16[2,128,768]{2,1,0:T(8,128)(2,1)} collective-permute-done((bf16[2,128,768]{2,1,0:T(8,128)(2,1)S(1)}, bf16[2,128,768]{2,1,0:T(8,128)(2,1)}, u32[]{:S(2)}, u32[]{:S(2)}) %collective-permute-start.5) | collective-permute-done | bytes 393248 | tf_op jit(solution)/shard_map/ppermute | solution.py:203
  108.1 5.7 %all-to-all-start.1 = ((bf16[256,4,384]{0,2,1:T(8,128)(2,1)}), bf16[256,4,384]{0,2,1:T(8,128)(2,1)S(1)}, u32[]{:S(2)}, u32[]{:S(2)}) async-start(bf16[256,4,384]{0,2,1:T(8,128)(2,1)} %bitcast.23), calls=%async_computation.1 | async-start | bytes 1572864 | tf_op jit(solution)/shard_map/all_to_all | solution.py:175
  116.0 11.5 %collective-permute-done.6 = bf16[2,128,768]{2,1,0:T(8,128)(2,1)S(1)} collective-permute-done((bf16[2,128,768]{2,1,0:T(8,128)(2,1)S(1)}, bf16[2,128,768]{2,1,0:T(8,128)(2,1)S(1)}, u32[]{:S(2)}, u32[]{:S(2)}) %collective-permute-start.6) | collective-permute-done | bytes 393248 | tf_op jit(solution)/shard_map/ppermute | solution.py:203
  127.5 5.2 %collective-permute-done.7 = bf16[2,128,768]{2,1,0:T(8,128)(2,1)S(1)} collective-permute-done((bf16[2,128,768]{2,1,0:T(8,128)(2,1)S(1)}, bf16[2,128,768]{2,1,0:T(8,128)(2,1)S(1)}, u32[]{:S(2)}, u32[]{:S(2)}) %collective-permute-start.7) | collective-permute-done | bytes 393248 | tf_op jit(solution)/shard_map/ppermute | solution.py:203
  132.7 7.5 %collective-permute-done.8 = bf16[2,128,768]{2,1,0:T(8,128)(2,1)S(1)} collective-permute-done((bf16[2,128,768]{2,1,0:T(8,128)(2,1)S(1)}, bf16[2,128,768]{2,1,0:T(8,128)(2,1)S(1)}, u32[]{:S(2)}, u32[]{:S(2)}) %collective-permute-start.8) | collective-permute-done | bytes 393248 | tf_op jit(solution)/shard_map/ppermute | solution.py:203
  140.2 5.1 %all-to-all-start.2 = ((bf16[256,4,384]{0,2,1:T(8,128)(2,1)}), bf16[256,4,384]{0,2,1:T(8,128)(2,1)S(1)}, u32[]{:S(2)}, u32[]{:S(2)}) async-start(bf16[256,4,384]{0,2,1:T(8,128)(2,1)} %bitcast.35), calls=%async_computation.2 | async-start | bytes 1572864 | tf_op jit(solution)/shard_map/all_to_all | solution.py:175
  146.5 14.2 %shard_map.62 = bf16[1024,384]{1,0:T(8,128)(2,1)} custom-call(s32[96]{0:T(128)} %reshape.162.tbl_ref, bf16[1024,384]{1,0:T(8,128)(2,1)} %bitcast.77, bf16[1024,768]{1,0:T(8,128)(2,1)} %bitcast.67, bf16[1024,768]{1,0:T(8,128)(2,1)} %bitcast_select_fusion.refs_1_, bf16[256,768]{1,0:T(8,128)(2,1)} %bitcast.88, bf16[256,768]{1,0:T(8,128)(2,1)} %bitcast.90, ...), custom_call_target="tpu_custom_call" | custom-call | flops 2415919104 | bytes 4325376 | tf_op jit(solution)/shard_map/pallas_call | solution.py:86
  160.7 5.7 %all-to-all-done.2 = bf16[256,4,384]{0,2,1:T(8,128)(2,1)S(1)} async-done(((bf16[256,4,384]{0,2,1:T(8,128)(2,1)}), bf16[256,4,384]{0,2,1:T(8,128)(2,1)S(1)}, u32[]{:S(2)}, u32[]{:S(2)}) %all-to-all-start.2) | async-done | bytes 786464 | tf_op jit(solution)/shard_map/all_to_all | solution.py:175
  166.4 3.5 %all-to-all-start.3 = ((bf16[4,256,384]{2,1,0:T(8,128)(2,1)}), bf16[4,256,384]{2,1,0:T(8,128)(2,1)S(1)}, u32[]{:S(2)}, u32[]{:S(2)}) async-start(bf16[4,256,384]{2,1,0:T(8,128)(2,1)} %bitcast.85), calls=%async_computation.3 | async-start | bytes 1572864 | tf_op jit(solution)/shard_map/all_to_all | solution.py:243
  171.1 14.1 %shard_map.59 = bf16[1024,384]{1,0:T(8,128)(2,1)} custom-call(s32[96]{0:T(128)} %reshape.162.tbl_ref, bf16[1024,384]{1,0:T(8,128)(2,1)} %bitcast.79, bf16[1024,768]{1,0:T(8,128)(2,1)} %bitcast.68, bf16[1024,768]{1,0:T(8,128)(2,1)} %bitcast_select_fusion.refs_1_, bf16[256,768]{1,0:T(8,128)(2,1)} %bitcast.89, bf16[256,768]{1,0:T(8,128)(2,1)} %bitcast.91, ...), custom_call_target="tpu_custom_call" | custom-call | flops 2415919104 | bytes 4325376 | tf_op jit(solution)/shard_map/pallas_call | solution.py:86
  185.2 5.5 %all-to-all-done.3 = bf16[4,256,384]{2,1,0:T(8,128)(2,1)S(1)} async-done(((bf16[4,256,384]{2,1,0:T(8,128)(2,1)}), bf16[4,256,384]{2,1,0:T(8,128)(2,1)S(1)}, u32[]{:S(2)}, u32[]{:S(2)}) %all-to-all-start.3) | async-done | bytes 786464 | tf_op jit(solution)/shard_map/all_to_all | solution.py:243
  190.7 3.5 %all-to-all-start.4 = ((bf16[4,256,384]{2,1,0:T(8,128)(2,1)}), bf16[4,256,384]{2,1,0:T(8,128)(2,1)S(1)}, u32[]{:S(2)}, u32[]{:S(2)}) async-start(bf16[4,256,384]{2,1,0:T(8,128)(2,1)} %bitcast.84), calls=%async_computation.4 | async-start | bytes 1572864 | tf_op jit(solution)/shard_map/all_to_all | solution.py:243
  194.2 6.5 %shard_map.60 = bf16[256,384]{1,0:T(8,128)(2,1)} custom-call(bf16[1024,384]{1,0:T(8,128)(2,1)} %bitcast.78, bf16[1024,768]{1,0:T(8,128)(2,1)} %all-gather.3.cloned.1.call-done.k_ref, bf16[1024,768]{1,0:T(8,128)(2,1)} %all-gather.5.cloned.1.call-done.v_ref), custom_call_target="tpu_custom_call" | custom-call | flops 503316480 | bytes 2555904 | tf_op jit(solution)/shard_map/pallas_call | solution.py:131
  200.8 6.6 %shard_map.61 = bf16[256,384]{1,0:T(8,128)(2,1)} custom-call(bf16[1024,384]{1,0:T(8,128)(2,1)} %bitcast.80, bf16[1024,768]{1,0:T(8,128)(2,1)} %all-gather.3.cloned.1.call-done.k_ref, bf16[1024,768]{1,0:T(8,128)(2,1)} %all-gather.5.cloned.1.call-done.v_ref), custom_call_target="tpu_custom_call" | custom-call | flops 503316480 | bytes 2555904 | tf_op jit(solution)/shard_map/pallas_call | solution.py:131
  209.0 5.2 %all-to-all-done.4 = bf16[4,256,384]{2,1,0:T(8,128)(2,1)S(1)} async-done(((bf16[4,256,384]{2,1,0:T(8,128)(2,1)}), bf16[4,256,384]{2,1,0:T(8,128)(2,1)S(1)}, u32[]{:S(2)}, u32[]{:S(2)}) %all-to-all-start.4) | async-done | bytes 786464 | tf_op jit(solution)/shard_map/all_to_all | solution.py:243
  (101 shorter events, 44.5 us)
Async XLA Ops:
  9.1 8.8 %copy-start.3 = (bf16[256,3072]{1,0:T(8,128)(2,1)S(1)}, bf16[256,3072]{1,0:T(8,128)(2,1)}, u32[]{:S(2)}) copy-start(bf16[256,3072]{1,0:T(8,128)(2,1)} %param.7) | copy-start | bytes 4718596
  10.0 23.2 %collective-permute-start.2 = (bf16[256,768]{1,0:T(8,128)(2,1)}, bf16[256,768]{1,0:T(8,128)(2,1)}, u32[]{:S(2)}, u32[]{:S(2)}) collective-permute-start(bf16[256,768]{1,0:T(8,128)(2,1)} %bitcast.9), channel_id=1, source_target_pairs={{0,3},{1,0},{2,1},{3,2},{4,7},{5,4},{6,5},{7,6},{8,11},{9,8},{10,9... | collective-permute-start | bytes 1179656 | tf_op jit(solution)/shard_map/ppermute | solution.py:154
  16.0 18.4 %collective-permute-start = (bf16[256,768]{1,0:T(8,128)(2,1)}, bf16[256,768]{1,0:T(8,128)(2,1)}, u32[]{:S(2)}, u32[]{:S(2)}) collective-permute-start(bf16[256,768]{1,0:T(8,128)(2,1)} %bitcast.5), channel_id=1, source_target_pairs={{0,1},{1,2},{2,3},{3,0},{4,5},{5,6},{6,7},{7,4},{8,9},{9,10},{10,1... | collective-permute-start | bytes 1179656 | tf_op jit(solution)/shard_map/ppermute | solution.py:154
  16.9 42.8 %collective-permute-start.1 = (bf16[256,768]{1,0:T(8,128)(2,1)}, bf16[256,768]{1,0:T(8,128)(2,1)}, u32[]{:S(2)}, u32[]{:S(2)}) collective-permute-start(bf16[256,768]{1,0:T(8,128)(2,1)} %bitcast.7), channel_id=1, source_target_pairs={{0,2},{1,3},{2,0},{3,1},{4,6},{5,7},{6,4},{7,5},{8,10},{9,11},{10,... | collective-permute-start | bytes 1179656 | tf_op jit(solution)/shard_map/ppermute | solution.py:154
  19.2 4.8 %copy-start.5 = (s32[32,12]{0,1:T(8,128)S(1)}, s32[32,12]{0,1:T(8,128)}, u32[]{:S(2)}) copy-start(s32[32,12]{0,1:T(8,128)} %param.9) | copy-start | bytes 4612
  19.2 63.4 %all-to-all-start = ((bf16[256,4,768]{2,0,1:T(8,128)(2,1)}), bf16[256,4,768]{2,0,1:T(8,128)(2,1)S(1)}, u32[]{:S(2)}, u32[]{:S(2)}) async-start(bf16[256,4,768]{2,0,1:T(8,128)(2,1)} %bitcast.63), calls=%async_computation | async-start | bytes 3145728 | tf_op jit(solution)/shard_map/all_to_all | solution.py:162
  24.0 161.2 %all-gather.3.cloned.1.call-start = ((), (), s32[]{:S(2)}) async-start(), calls=%async_computation.5 | async-start | bytes 1966080 | tf_op jit(solution)/shard_map/all_gather | solution.py:228
  82.5 9.4 %copy-start = (bf16[256,4,768]{2,0,1:T(8,128)(2,1)}, bf16[256,4,768]{2,0,1:T(8,128)(2,1)S(1)}, u32[]{:S(2)}) copy-start(bf16[256,4,768]{2,0,1:T(8,128)(2,1)S(1)} %all-to-all-done) | copy-start | bytes 4718596
  89.0 13.3 %collective-permute-start.3 = (bf16[2,128,768]{2,1,0:T(8,128)(2,1)}, bf16[2,128,768]{2,1,0:T(8,128)(2,1)}, u32[]{:S(2)}, u32[]{:S(2)}) collective-permute-start(bf16[2,128,768]{2,1,0:T(8,128)(2,1)} %get-tuple-element.35), channel_id=1, source_target_pairs={{0,4},{4,8},{8,12},{12,0},{1,5},{5,9},{9,13},{13,1},{2,6},{6,10},{... | collective-permute-start | bytes 1179656 | tf_op jit(solution)/shard_map/ppermute | solution.py:203
  89.0 13.3 %collective-permute-start.4 = (bf16[2,128,768]{2,1,0:T(8,128)(2,1)}, bf16[2,128,768]{2,1,0:T(8,128)(2,1)}, u32[]{:S(2)}, u32[]{:S(2)}) collective-permute-start(bf16[2,128,768]{2,1,0:T(8,128)(2,1)} %get-tuple-element.34), channel_id=1, source_target_pairs={{0,8},{4,12},{8,0},{12,4},{1,9},{5,13},{9,1},{13,5},{2,10},{6,14},... | collective-permute-start | bytes 1179656 | tf_op jit(solution)/shard_map/ppermute | solution.py:203
  90.5 17.5 %collective-permute-start.5 = (bf16[2,128,768]{2,1,0:T(8,128)(2,1)S(1)}, bf16[2,128,768]{2,1,0:T(8,128)(2,1)}, u32[]{:S(2)}, u32[]{:S(2)}) collective-permute-start(bf16[2,128,768]{2,1,0:T(8,128)(2,1)S(1)} %get-tuple-element.33), channel_id=1, source_target_pairs={{0,12},{4,0},{8,4},{12,8},{1,13},{5,1},{9,5},{13,9},{2,14},{6,2},{... | collective-permute-start | bytes 1179656 | tf_op jit(solution)/shard_map/ppermute | solution.py:203
  102.3 11.4 %copy-start.2 = (bf16[8,128,768]{2,1,0:T(8,128)(2,1)S(1)}, bf16[8,128,768]{2,1,0:T(8,128)(2,1)}, u32[]{:S(2)}) copy-start(bf16[8,128,768]{2,1,0:T(8,128)(2,1)} %get-tuple-element.46) | copy-start | bytes 4718596
  108.1 32.1 %all-to-all-start.1 = ((bf16[256,4,384]{0,2,1:T(8,128)(2,1)}), bf16[256,4,384]{0,2,1:T(8,128)(2,1)S(1)}, u32[]{:S(2)}, u32[]{:S(2)}) async-start(bf16[256,4,384]{0,2,1:T(8,128)(2,1)} %bitcast.23), calls=%async_computation.1 | async-start | bytes 1572864 | tf_op jit(solution)/shard_map/all_to_all | solution.py:175
  113.8 71.4 %all-gather.5.cloned.1.call-start = ((), (), s32[]{:S(2)}) async-start(), calls=%async_computation.6 | async-start | bytes 1966080 | tf_op jit(solution)/shard_map/all_gather | solution.py:229
  113.8 13.6 %collective-permute-start.6 = (bf16[2,128,768]{2,1,0:T(8,128)(2,1)S(1)}, bf16[2,128,768]{2,1,0:T(8,128)(2,1)S(1)}, u32[]{:S(2)}, u32[]{:S(2)}) collective-permute-start(bf16[2,128,768]{2,1,0:T(8,128)(2,1)S(1)} %get-tuple-element.44), channel_id=1, source_target_pairs={{0,4},{4,8},{8,12},{12,0},{1,5},{5,9},{9,13},{13,1},{2,6},{6,10},{... | collective-permute-start | bytes 1179656 | tf_op jit(solution)/shard_map/ppermute | solution.py:203
  114.5 18.2 %collective-permute-start.7 = (bf16[2,128,768]{2,1,0:T(8,128)(2,1)S(1)}, bf16[2,128,768]{2,1,0:T(8,128)(2,1)S(1)}, u32[]{:S(2)}, u32[]{:S(2)}) collective-permute-start(bf16[2,128,768]{2,1,0:T(8,128)(2,1)S(1)} %get-tuple-element.43), channel_id=1, source_target_pairs={{0,8},{4,12},{8,0},{12,4},{1,9},{5,13},{9,1},{13,5},{2,10},{6,14},... | collective-permute-start | bytes 1179656 | tf_op jit(solution)/shard_map/ppermute | solution.py:203
  116.0 24.2 %collective-permute-start.8 = (bf16[2,128,768]{2,1,0:T(8,128)(2,1)S(1)}, bf16[2,128,768]{2,1,0:T(8,128)(2,1)S(1)}, u32[]{:S(2)}, u32[]{:S(2)}) collective-permute-start(bf16[2,128,768]{2,1,0:T(8,128)(2,1)S(1)} %get-tuple-element.42), channel_id=1, source_target_pairs={{0,12},{4,0},{8,4},{12,8},{1,13},{5,1},{9,5},{13,9},{2,14},{6,2},{... | collective-permute-start | bytes 1179656 | tf_op jit(solution)/shard_map/ppermute | solution.py:203
  127.5 19.0 %copy-start.9 = (bf16[2,128,768]{2,1,0:T(8,128)(2,1)}, bf16[2,128,768]{2,1,0:T(8,128)(2,1)S(1)}, u32[]{:S(2)}) copy-start(bf16[2,128,768]{2,1,0:T(8,128)(2,1)S(1)} %collective-permute-done.6) | copy-start | bytes 1179652
  132.7 13.8 %copy-start.10 = (bf16[2,128,768]{2,1,0:T(8,128)(2,1)}, bf16[2,128,768]{2,1,0:T(8,128)(2,1)S(1)}, u32[]{:S(2)}) copy-start(bf16[2,128,768]{2,1,0:T(8,128)(2,1)S(1)} %collective-permute-done.7) | copy-start | bytes 1179652
  140.2 6.3 %copy-start.11 = (bf16[2,128,768]{2,1,0:T(8,128)(2,1)}, bf16[2,128,768]{2,1,0:T(8,128)(2,1)S(1)}, u32[]{:S(2)}) copy-start(bf16[2,128,768]{2,1,0:T(8,128)(2,1)S(1)} %collective-permute-done.8) | copy-start | bytes 1179652
  140.2 26.1 %all-to-all-start.2 = ((bf16[256,4,384]{0,2,1:T(8,128)(2,1)}), bf16[256,4,384]{0,2,1:T(8,128)(2,1)S(1)}, u32[]{:S(2)}, u32[]{:S(2)}) async-start(bf16[256,4,384]{0,2,1:T(8,128)(2,1)} %bitcast.35), calls=%async_computation.2 | async-start | bytes 1572864 | tf_op jit(solution)/shard_map/all_to_all | solution.py:175
  166.4 24.3 %all-to-all-start.3 = ((bf16[4,256,384]{2,1,0:T(8,128)(2,1)}), bf16[4,256,384]{2,1,0:T(8,128)(2,1)S(1)}, u32[]{:S(2)}, u32[]{:S(2)}) async-start(bf16[4,256,384]{2,1,0:T(8,128)(2,1)} %bitcast.85), calls=%async_computation.3 | async-start | bytes 1572864 | tf_op jit(solution)/shard_map/all_to_all | solution.py:243
  190.7 23.5 %all-to-all-start.4 = ((bf16[4,256,384]{2,1,0:T(8,128)(2,1)}), bf16[4,256,384]{2,1,0:T(8,128)(2,1)S(1)}, u32[]{:S(2)}, u32[]{:S(2)}) async-start(bf16[4,256,384]{2,1,0:T(8,128)(2,1)} %bitcast.84), calls=%async_computation.4 | async-start | bytes 1572864 | tf_op jit(solution)/shard_map/all_to_all | solution.py:243
  200.7 6.6 %copy-start.4 = (bf16[256,384]{1,0:T(8,128)(2,1)S(1)}, bf16[256,384]{1,0:T(8,128)(2,1)}, u32[]{:S(2)}) copy-start(bf16[256,384]{1,0:T(8,128)(2,1)} %shard_map.60) | copy-start | bytes 589828
  (4 other events, 8.2 us)
Sparse Core Ops, SparseCore 0:
  108.2 30.7 all-gather.2
  141.2 20.7 all-gather.4

commit v20 on v18

--- a/solution.py
+++ b/solution.py
@@ -1,3 +1,5 @@
+import functools
+
 import jax
 import jax.numpy as jnp
 from jax import lax
@@ -101,12 +103,16 @@
     )(tbl, queries, *operands)
 
 
-def draft_kernel(q_ref, k_ref, v_ref, o_ref):
-    tile = o_ref.shape[0]
+def pooling_matrix(tile):
     token = lax.broadcasted_iota(jnp.int32, (tile, tile * POOL), 1)
     draft = lax.broadcasted_iota(jnp.int32, (tile, tile * POOL), 0)
-    pooling = jnp.where(token // POOL == draft, POOL ** (-0.5), 0.0).astype(jnp.bfloat16)
-    pooled = jnp.dot(pooling, q_ref[...], preferred_element_type=jnp.float32).astype(jnp.bfloat16)
+    return jnp.where(token // POOL == draft, POOL ** (-0.5), 0.0).astype(jnp.bfloat16)
+
+
+def draft_kernel(split, qa_ref, qb_ref, k_ref, v_ref, o_ref):
+    pooling = pooling_matrix(o_ref.shape[0])
+    chosen = jnp.where(pl.program_id(0) < split, qa_ref[...], qb_ref[...])
+    pooled = jnp.dot(pooling, chosen, preferred_element_type=jnp.float32).astype(jnp.bfloat16)
     raw = lax.dot_general(
         pooled, k_ref[...], (((1,), (1,)), ((), ())), preferred_element_type=jnp.float32
     )
@@ -117,29 +123,35 @@
     o_ref[...] = (weighted / totals).astype(o_ref.dtype)
 
 
-def draft_attention(queries, keys, values, head_lo):
-    token_rows, width = queries.shape
+def draft_attention(leading, trailing, keys, values):
+    token_rows = leading.shape[0]
+    split = leading.shape[1] // HD
+    later = trailing.shape[1] // HD
     rows = token_rows // POOL
+    width = keys.shape[1]
     heads = width // HD
     key_rows = keys.shape[0]
     tile = min(DRAFT_ROWS, rows)
     cost = pl.CostEstimate(
         flops=4 * rows * key_rows * HD * heads + 2 * rows * tile * POOL * HD * heads,
         transcendentals=rows * key_rows * heads,
-        bytes_accessed=2 * HD * heads * (token_rows + rows + 2 * key_rows),
+        bytes_accessed=2 * HD * heads * (2 * token_rows + rows + 2 * key_rows),
     )
     return pl.pallas_call(
-        draft_kernel,
+        functools.partial(draft_kernel, split),
         out_shape=jax.ShapeDtypeStruct((rows, width), jnp.bfloat16),
         cost_estimate=cost,
         grid=(heads, rows // tile),
         in_specs=[
-            pl.BlockSpec((tile * POOL, HD), lambda h, r: (r, h)),
-            pl.BlockSpec((key_rows, HD), lambda h, r: (0, h + head_lo)),
-            pl.BlockSpec((key_rows, HD), lambda h, r: (0, h + head_lo)),
+            pl.BlockSpec((tile * POOL, HD), lambda h, r: (r, jnp.minimum(h, split - 1))),
+            pl.BlockSpec(
+                (tile * POOL, HD), lambda h, r: (r, jnp.clip(h - split, 0, later - 1))
+            ),
+            pl.BlockSpec((key_rows, HD), lambda h, r: (0, h)),
+            pl.BlockSpec((key_rows, HD), lambda h, r: (0, h)),
         ],
         out_specs=pl.BlockSpec((tile, HD), lambda h, r: (r, h)),
-    )(queries, keys, values)
+    )(leading, trailing, keys, values)
 
 
 def head_permutes(matrix):
@@ -238,13 +250,7 @@
         back = lax.all_to_all(rows_part, "head", split_axis=0, concat_axis=1, tiled=True)
         pieces.append(back.reshape(back.shape[0], -1, count * HD))
     sparse_out = jnp.concatenate(pieces, axis=2).reshape(pieces[0].shape[0], -1)
-    draft_out = jnp.concatenate(
-        [
-            draft_attention(queries, draft_keys, draft_values, head_lo)
-            for (head_lo, count), queries in zip(spans, query_parts)
-        ],
-        axis=1,
-    )
+    draft_out = draft_attention(query_parts[0], query_parts[-1], draft_keys, draft_values)
     return (draft_out, sparse_out)
 
 

time: 220 us -> 219 us (level)
  waiting for transfers between devices: 73.3 us -> 76 us
    all_to_all x2, waiting for transfers between devices: 9.8 us -> 12.2 us  [on_device(): lax.all_to_all(rows_part, 'head', split_axis=0, concat_axis=1, tiled=True)]
    pallas_call x2 -> x1, Pallas kernels: 13.1 us -> 12.4 us  [draft_attention(): pl.pallas_call(functools.partial(draft_kernel, split), out_shape=jax.Shap...]
  transfers between devices with their start and end apart: 16 -> 16, of which waited for: 12 -> 12; matrix products, arithmetic and copies ran while one was open for 24% -> 23% of each run, Pallas kernels for 19% -> 19%
where the time goes in v20:
time: 219 us; the launch traced here: 218 us
  waiting for transfers between devices  76 us (35%)
  Pallas kernels  40.6 us (19%)
  local copies, waits for them, and re-layouts  32.7 us (15%)
  starting transfers between devices  32.6 us (15%)
  other arithmetic  21.5 us (10%)
  between operations  14.4 us (7%)
    pallas_call x2, Pallas kernels, sparse_attention(): pl.pallas_call(sparse_kernel, out_shape=jax.ShapeDtypeStruct((rows, heads...  28.3 us
    ppermute x3, waiting for transfers between devices, head_permutes(): lax.ppermute(piece, 'head', [(i, (i + shift) % count) for i in range(coun...  26.6 us
    ppermute x6, waiting for transfers between devices, exchange(): lax.ppermute(parcel, 'seq', [(i, (i + shift) % seq_count) for i in range(...  23.4 us
    pallas_call x1, Pallas kernels, draft_attention(): pl.pallas_call(functools.partial(draft_kernel, split), out_shape=jax.Shap...  12.4 us
    all_to_all x2, waiting for transfers between devices, on_device(): lax.all_to_all(rows_part, 'head', split_axis=0, concat_axis=1, tiled=True)  12.2 us
    all_to_all x2, starting transfers between devices, query_a2a(): lax.all_to_all(piece, 'head', split_axis=1, concat_axis=0, tiled=True)  8.87 us
    all_to_all x1, waiting for transfers between devices, on_device(): lax.all_to_all(key_in, 'head', split_axis=1, concat_axis=0, tiled=True)  7.87 us
    all_to_all x2, starting transfers between devices, on_device(): lax.all_to_all(rows_part, 'head', split_axis=0, concat_axis=1, tiled=True)  6.99 us
  transfers between devices with their start and end apart: 16, of which 12 were waited for; matrix products, arithmetic and copies ran while one was open for 23% of the time, Pallas kernels for 19%

profile of v20, /device:TPU:0, one launch (start us, length us, event | category | flops | bytes accessed | tf_op | source)
XLA Modules:
  0.0 217.8 jit_solution(14675921100063200147)
XLA Ops:
  10.0 5.0 %collective-permute-start.2 = (bf16[256,768]{1,0:T(8,128)(2,1)}, bf16[256,768]{1,0:T(8,128)(2,1)}, u32[]{:S(2)}, u32[]{:S(2)}) collective-permute-start(bf16[256,768]{1,0:T(8,128)(2,1)} %bitcast.9), channel_id=1, source_target_pairs={{0,3},{1,0},{2,1},{3,2},{4,7},{5,4},{6,5},{7,6},{8,11},{9,8},{10,9... | collective-permute-start | bytes 1179656 | tf_op jit(solution)/shard_map/ppermute | solution.py:166
  19.2 4.8 %all-to-all-start.1 = ((bf16[256,4,768]{2,0,1:T(8,128)(2,1)}), bf16[256,4,768]{2,0,1:T(8,128)(2,1)S(1)}, u32[]{:S(2)}, u32[]{:S(2)}) async-start(bf16[256,4,768]{2,0,1:T(8,128)(2,1)} %bitcast.63), calls=%async_computation.1 | async-start | bytes 3145728 | tf_op jit(solution)/shard_map/all_to_all | solution.py:174
  26.0 2.6 %copy.45 = bf16[256,3072]{0,1:T(8,128)(2,1)} copy(bf16[256,3072]{1,0:T(8,128)(2,1)} %param.6) | data formatting | bytes 3145728 | tf_op jit(solution)/shard_map/reshape | solution.py:181
  30.5 2.6 %fusion.14 = (bf16[256,4,384]{0,2,1:T(8,128)(2,1)}, bf16[256,4,384]{0,2,1:T(8,128)(2,1)}) fusion(bf16[256,4,768]{0,2,1:T(8,128)(2,1)} %bitcast.69), kind=kLoop, calls=%fused_computation.74 | loop fusion | bytes 3145728 | tf_op jit(solution)/shard_map/slice | solution.py:183
  34.4 25.3 %collective-permute-done.1 = bf16[256,768]{1,0:T(8,128)(2,1)} collective-permute-done((bf16[256,768]{1,0:T(8,128)(2,1)}, bf16[256,768]{1,0:T(8,128)(2,1)}, u32[]{:S(2)}, u32[]{:S(2)}) %collective-permute-start.1) | collective-permute-done | bytes 393248 | tf_op jit(solution)/shard_map/ppermute | solution.py:166
  65.6 3.6 %convert_reduce_fusion = f32[256,768]{1,0:T(8,128)S(1)} fusion(bf16[256,4,768]{2,1,0:T(4,128)(2,1)} %gather.20, pred[256]{0:T(512)(128)(4,1)S(1)} %broadcast_in_dim.76), kind=kLoop, calls=%fused_computation.4 | loop fusion | flops 2162688 | bytes 2359552 | tf_op jit(solution)/shard_map/reduce_sum | solution.py:22
  71.5 3.2 %gather_fusion.2 = bf16[8,128,768]{2,1,0:T(8,128)(2,1)} fusion(bf16[8,128,768]{2,1,0:T(8,128)(2,1)} %broadcast_select_fusion.2, s32[1024]{0:T(1024)S(1)} %pad_clamp_fusion), kind=kCustom, calls=%fused_computation.clone | custom fusion | bytes 3145760 | tf_op jit(solution)/shard_map/jit(_take)/gather | solution.py:209
  74.7 7.9 %all-to-all-done.1 = bf16[256,4,768]{2,0,1:T(8,128)(2,1)S(1)} async-done(((bf16[256,4,768]{2,0,1:T(8,128)(2,1)}), bf16[256,4,768]{2,0,1:T(8,128)(2,1)S(1)}, u32[]{:S(2)}, u32[]{:S(2)}) %all-to-all-start.1) | async-done | bytes 1572896 | tf_op jit(solution)/shard_map/all_to_all | solution.py:174
  84.4 3.6 %broadcast_select_fusion = (bf16[8,128,768]{2,1,0:T(8,128)(2,1)}, bf16[8,128,768]{2,1,0:T(8,128)(2,1)S(1)}) fusion(bf16[8,128,768]{2,1,0:T(8,128)(2,1)} %gather_fusion.3, pred[8]{0:T(512)(128)(4,1)S(1)} %compare_and_fusion, bf16[8,128,768]{2,1,0:T(8,128)(2,1)} %gather_fusion.2), kind=kLoop, calls=%fused_computation.10 | loop fusion | flops 1572864 | bytes 6291464 | tf_op jit(solution)/shard_map/jit(_take)/select_n | solution.py:209
  94.1 11.0 %collective-permute-done.3 = bf16[2,128,768]{2,1,0:T(8,128)(2,1)} collective-permute-done((bf16[2,128,768]{2,1,0:T(8,128)(2,1)}, bf16[2,128,768]{2,1,0:T(8,128)(2,1)}, u32[]{:S(2)}, u32[]{:S(2)}) %collective-permute-start.3) | collective-permute-done | bytes 393248 | tf_op jit(solution)/shard_map/ppermute | solution.py:217
  105.5 6.0 %collective-permute-done.5 = bf16[2,128,768]{2,1,0:T(8,128)(2,1)} collective-permute-done((bf16[2,128,768]{2,1,0:T(8,128)(2,1)S(1)}, bf16[2,128,768]{2,1,0:T(8,128)(2,1)}, u32[]{:S(2)}, u32[]{:S(2)}) %collective-permute-start.5) | collective-permute-done | bytes 393248 | tf_op jit(solution)/shard_map/ppermute | solution.py:217
  111.4 4.8 %all-to-all-start = ((bf16[256,4,384]{0,2,1:T(8,128)(2,1)}), bf16[256,4,384]{0,2,1:T(8,128)(2,1)}, u32[]{:S(2)}, u32[]{:S(2)}) async-start(bf16[256,4,384]{0,2,1:T(8,128)(2,1)} %get-tuple-element.33), calls=%async_computation | async-start | bytes 1572864 | tf_op jit(solution)/shard_map/all_to_all | solution.py:187
  122.1 3.1 %reshape.170 = f32[256,4,768]{2,1,0:T(4,128)S(1)} reshape(f32[4,256,768]{2,1,0:T(8,128)} %bitcast_convert_fusion) | data formatting | bytes 6291456 | tf_op jit(solution)/shard_map/convert_element_type | solution.py:21
  125.2 3.0 %reduce_sum.28 = f32[256,768]{1,0:T(8,128)} reduce(f32[256,4,768]{2,1,0:T(4,128)S(1)} %reshape.170, f32[]{:T(128)} %constant.170.clone.1), dimensions={1}, to_apply=%region_4.6 | reduce | flops 589824 | bytes 3932164 | tf_op jit(solution)/shard_map/reduce_sum | solution.py:22
  131.2 5.1 %collective-permute-done.8 = bf16[2,128,768]{2,1,0:T(8,128)(2,1)} collective-permute-done((bf16[2,128,768]{2,1,0:T(8,128)(2,1)S(1)}, bf16[2,128,768]{2,1,0:T(8,128)(2,1)}, u32[]{:S(2)}, u32[]{:S(2)}) %collective-permute-start.8) | collective-permute-done | bytes 393248 | tf_op jit(solution)/shard_map/ppermute | solution.py:217
  137.3 4.0 %all-to-all-start.2 = ((bf16[256,4,384]{0,2,1:T(8,128)(2,1)}), bf16[256,4,384]{0,2,1:T(8,128)(2,1)S(1)}, u32[]{:S(2)}, u32[]{:S(2)}) async-start(bf16[256,4,384]{0,2,1:T(8,128)(2,1)} %bitcast.35), calls=%async_computation.2 | async-start | bytes 1572864 | tf_op jit(solution)/shard_map/all_to_all | solution.py:187
  143.7 14.1 %shard_map.61 = bf16[1024,384]{1,0:T(8,128)(2,1)} custom-call(s32[96]{0:T(128)} %reshape.162.tbl_ref, bf16[1024,384]{1,0:T(8,128)(2,1)} %bitcast.73, bf16[1024,768]{1,0:T(8,128)(2,1)} %bitcast.67, bf16[1024,768]{1,0:T(8,128)(2,1)} %bitcast_select_fusion.refs_1_, bf16[256,768]{1,0:T(8,128)(2,1)} %bitcast.30.refs_2_, bf16[256,768]{1,0:T(8,128)(2,1)} %bitcast.32.refs_3_, ...), custom_call_target="tpu_custom_call" | custom-call | flops 2415919104 | bytes 4325376 | tf_op jit(solution)/shard_map/pallas_call | solution.py:88
  157.8 4.8 %all-to-all-done.2 = bf16[256,4,384]{0,2,1:T(8,128)(2,1)S(1)} async-done(((bf16[256,4,384]{0,2,1:T(8,128)(2,1)}), bf16[256,4,384]{0,2,1:T(8,128)(2,1)S(1)}, u32[]{:S(2)}, u32[]{:S(2)}) %all-to-all-start.2) | async-done | bytes 786464 | tf_op jit(solution)/shard_map/all_to_all | solution.py:187
  162.6 3.5 %all-to-all-start.3 = ((bf16[4,256,384]{2,1,0:T(8,128)(2,1)}), bf16[4,256,384]{2,1,0:T(8,128)(2,1)S(1)}, u32[]{:S(2)}, u32[]{:S(2)}) async-start(bf16[4,256,384]{2,1,0:T(8,128)(2,1)} %bitcast.84), calls=%async_computation.3 | async-start | bytes 1572864 | tf_op jit(solution)/shard_map/all_to_all | solution.py:250
  167.3 14.1 %shard_map.59 = bf16[1024,384]{1,0:T(8,128)(2,1)} custom-call(s32[96]{0:T(128)} %reshape.162.tbl_ref, bf16[1024,384]{1,0:T(8,128)(2,1)} %bitcast.75, bf16[1024,768]{1,0:T(8,128)(2,1)} %bitcast.68, bf16[1024,768]{1,0:T(8,128)(2,1)} %bitcast_select_fusion.refs_1_, bf16[256,768]{1,0:T(8,128)(2,1)} %bitcast.30.refs_2_, bf16[256,768]{1,0:T(8,128)(2,1)} %bitcast.32.refs_3_, ...), custom_call_target="tpu_custom_call" | custom-call | flops 2415919104 | bytes 4325376 | tf_op jit(solution)/shard_map/pallas_call | solution.py:88
  181.4 5.0 %all-to-all-done.3 = bf16[4,256,384]{2,1,0:T(8,128)(2,1)S(1)} async-done(((bf16[4,256,384]{2,1,0:T(8,128)(2,1)}), bf16[4,256,384]{2,1,0:T(8,128)(2,1)S(1)}, u32[]{:S(2)}, u32[]{:S(2)}) %all-to-all-start.3) | async-done | bytes 786464 | tf_op jit(solution)/shard_map/all_to_all | solution.py:250
  186.4 3.5 %all-to-all-start.4 = ((bf16[4,256,384]{2,1,0:T(8,128)(2,1)}), bf16[4,256,384]{2,1,0:T(8,128)(2,1)S(1)}, u32[]{:S(2)}, u32[]{:S(2)}) async-start(bf16[4,256,384]{2,1,0:T(8,128)(2,1)} %bitcast.83), calls=%async_computation.4 | async-start | bytes 1572864 | tf_op jit(solution)/shard_map/all_to_all | solution.py:250
  189.9 12.4 %shard_map.60 = bf16[256,768]{1,0:T(8,128)(2,1)} custom-call(bf16[1024,384]{1,0:T(8,128)(2,1)} %bitcast.74, bf16[1024,384]{1,0:T(8,128)(2,1)} %bitcast.76, bf16[1024,768]{1,0:T(8,128)(2,1)} %all-gather.3.cloned.1.call-done.k_ref, bf16[1024,768]{1,0:T(8,128)(2,1)} %all-gather.5.cloned.1.call-done.v_ref), custom_call_target="tpu_custom_call" | custom-call | flops 1006632960 | bytes 6684672 | tf_op jit(solution)/shard_map/pallas_call | solution.py:140
  202.3 7.2 %all-to-all-done.4 = bf16[4,256,384]{2,1,0:T(8,128)(2,1)S(1)} async-done(((bf16[4,256,384]{2,1,0:T(8,128)(2,1)}), bf16[4,256,384]{2,1,0:T(8,128)(2,1)S(1)}, u32[]{:S(2)}, u32[]{:S(2)}) %all-to-all-start.4) | async-done | bytes 786464 | tf_op jit(solution)/shard_map/all_to_all | solution.py:250
  (84 shorter events, 43.3 us)
Async XLA Ops:
  9.1 8.9 %copy-start.2 = (bf16[256,3072]{1,0:T(8,128)(2,1)S(1)}, bf16[256,3072]{1,0:T(8,128)(2,1)}, u32[]{:S(2)}) copy-start(bf16[256,3072]{1,0:T(8,128)(2,1)} %param.7) | copy-start | bytes 4718596
  10.0 23.1 %collective-permute-start.2 = (bf16[256,768]{1,0:T(8,128)(2,1)}, bf16[256,768]{1,0:T(8,128)(2,1)}, u32[]{:S(2)}, u32[]{:S(2)}) collective-permute-start(bf16[256,768]{1,0:T(8,128)(2,1)} %bitcast.9), channel_id=1, source_target_pairs={{0,3},{1,0},{2,1},{3,2},{4,7},{5,4},{6,5},{7,6},{8,11},{9,8},{10,9... | collective-permute-start | bytes 1179656 | tf_op jit(solution)/shard_map/ppermute | solution.py:166
  16.0 18.4 %collective-permute-start = (bf16[256,768]{1,0:T(8,128)(2,1)}, bf16[256,768]{1,0:T(8,128)(2,1)}, u32[]{:S(2)}, u32[]{:S(2)}) collective-permute-start(bf16[256,768]{1,0:T(8,128)(2,1)} %bitcast.5), channel_id=1, source_target_pairs={{0,1},{1,2},{2,3},{3,0},{4,5},{5,6},{6,7},{7,4},{8,9},{9,10},{10,1... | collective-permute-start | bytes 1179656 | tf_op jit(solution)/shard_map/ppermute | solution.py:166
  16.9 42.8 %collective-permute-start.1 = (bf16[256,768]{1,0:T(8,128)(2,1)}, bf16[256,768]{1,0:T(8,128)(2,1)}, u32[]{:S(2)}, u32[]{:S(2)}) collective-permute-start(bf16[256,768]{1,0:T(8,128)(2,1)} %bitcast.7), channel_id=1, source_target_pairs={{0,2},{1,3},{2,0},{3,1},{4,6},{5,7},{6,4},{7,5},{8,10},{9,11},{10,... | collective-permute-start | bytes 1179656 | tf_op jit(solution)/shard_map/ppermute | solution.py:166
  19.2 4.8 %copy-start.3 = (s32[32,12]{0,1:T(8,128)S(1)}, s32[32,12]{0,1:T(8,128)}, u32[]{:S(2)}) copy-start(s32[32,12]{0,1:T(8,128)} %param.9) | copy-start | bytes 4612
  19.2 63.3 %all-to-all-start.1 = ((bf16[256,4,768]{2,0,1:T(8,128)(2,1)}), bf16[256,4,768]{2,0,1:T(8,128)(2,1)S(1)}, u32[]{:S(2)}, u32[]{:S(2)}) async-start(bf16[256,4,768]{2,0,1:T(8,128)(2,1)} %bitcast.63), calls=%async_computation.1 | async-start | bytes 3145728 | tf_op jit(solution)/shard_map/all_to_all | solution.py:174
  24.0 157.4 %all-gather.5.cloned.1.call-start = ((), (), s32[]{:S(2)}) async-start(), calls=%async_computation.6 | async-start | bytes 1966080 | tf_op jit(solution)/shard_map/all_gather | solution.py:190
  82.5 37.6 %copy-start = (bf16[256,4,768]{2,0,1:T(8,128)(2,1)}, bf16[256,4,768]{2,0,1:T(8,128)(2,1)S(1)}, u32[]{:S(2)}) copy-start(bf16[256,4,768]{2,0,1:T(8,128)(2,1)S(1)} %all-to-all-done.1) | copy-start | bytes 4718596
  88.9 16.1 %collective-permute-start.3 = (bf16[2,128,768]{2,1,0:T(8,128)(2,1)}, bf16[2,128,768]{2,1,0:T(8,128)(2,1)}, u32[]{:S(2)}, u32[]{:S(2)}) collective-permute-start(bf16[2,128,768]{2,1,0:T(8,128)(2,1)} %get-tuple-element.36), channel_id=1, source_target_pairs={{0,4},{4,8},{8,12},{12,0},{1,5},{5,9},{9,13},{13,1},{2,6},{6,10},{... | collective-permute-start | bytes 1179656 | tf_op jit(solution)/shard_map/ppermute | solution.py:217
  88.9 16.5 %collective-permute-start.4 = (bf16[2,128,768]{2,1,0:T(8,128)(2,1)}, bf16[2,128,768]{2,1,0:T(8,128)(2,1)}, u32[]{:S(2)}, u32[]{:S(2)}) collective-permute-start(bf16[2,128,768]{2,1,0:T(8,128)(2,1)} %get-tuple-element.35), channel_id=1, source_target_pairs={{0,8},{4,12},{8,0},{12,4},{1,9},{5,13},{9,1},{13,5},{2,10},{6,14},... | collective-permute-start | bytes 1179656 | tf_op jit(solution)/shard_map/ppermute | solution.py:217
  90.5 20.9 %collective-permute-start.5 = (bf16[2,128,768]{2,1,0:T(8,128)(2,1)S(1)}, bf16[2,128,768]{2,1,0:T(8,128)(2,1)}, u32[]{:S(2)}, u32[]{:S(2)}) collective-permute-start(bf16[2,128,768]{2,1,0:T(8,128)(2,1)S(1)} %get-tuple-element.34), channel_id=1, source_target_pairs={{0,12},{4,0},{8,4},{12,8},{1,13},{5,1},{9,5},{13,9},{2,14},{6,2},{... | collective-permute-start | bytes 1179656 | tf_op jit(solution)/shard_map/ppermute | solution.py:217
  94.1 22.2 %copy-start.1 = (bf16[8,128,768]{2,1,0:T(8,128)(2,1)S(1)}, bf16[8,128,768]{2,1,0:T(8,128)(2,1)}, u32[]{:S(2)}) copy-start(bf16[8,128,768]{2,1,0:T(8,128)(2,1)} %get-tuple-element.41) | copy-start | bytes 4718596
  111.4 25.9 %all-to-all-start = ((bf16[256,4,384]{0,2,1:T(8,128)(2,1)}), bf16[256,4,384]{0,2,1:T(8,128)(2,1)}, u32[]{:S(2)}, u32[]{:S(2)}) async-start(bf16[256,4,384]{0,2,1:T(8,128)(2,1)} %get-tuple-element.33), calls=%async_computation | async-start | bytes 1572864 | tf_op jit(solution)/shard_map/all_to_all | solution.py:187
  116.3 65.1 %all-gather.3.cloned.1.call-start = ((), (), s32[]{:S(2)}) async-start(), calls=%async_computation.5 | async-start | bytes 1966080 | tf_op jit(solution)/shard_map/all_gather | solution.py:189
  117.2 12.9 %collective-permute-start.6 = (bf16[2,128,768]{2,1,0:T(8,128)(2,1)}, bf16[2,128,768]{2,1,0:T(8,128)(2,1)}, u32[]{:S(2)}, u32[]{:S(2)}) collective-permute-start(bf16[2,128,768]{2,1,0:T(8,128)(2,1)} %get-tuple-element.31), channel_id=1, source_target_pairs={{0,4},{4,8},{8,12},{12,0},{1,5},{5,9},{9,13},{13,1},{2,6},{6,10},{... | collective-permute-start | bytes 1179656 | tf_op jit(solution)/shard_map/ppermute | solution.py:217
  118.8 12.4 %collective-permute-start.7 = (bf16[2,128,768]{2,1,0:T(8,128)(2,1)}, bf16[2,128,768]{2,1,0:T(8,128)(2,1)}, u32[]{:S(2)}, u32[]{:S(2)}) collective-permute-start(bf16[2,128,768]{2,1,0:T(8,128)(2,1)} %get-tuple-element.30), channel_id=1, source_target_pairs={{0,8},{4,12},{8,0},{12,4},{1,9},{5,13},{9,1},{13,5},{2,10},{6,14},... | collective-permute-start | bytes 1179656 | tf_op jit(solution)/shard_map/ppermute | solution.py:217
  119.4 16.9 %collective-permute-start.8 = (bf16[2,128,768]{2,1,0:T(8,128)(2,1)S(1)}, bf16[2,128,768]{2,1,0:T(8,128)(2,1)}, u32[]{:S(2)}, u32[]{:S(2)}) collective-permute-start(bf16[2,128,768]{2,1,0:T(8,128)(2,1)S(1)} %get-tuple-element.29), channel_id=1, source_target_pairs={{0,12},{4,0},{8,4},{12,8},{1,13},{5,1},{9,5},{13,9},{2,14},{6,2},{... | collective-permute-start | bytes 1179656 | tf_op jit(solution)/shard_map/ppermute | solution.py:217
  137.3 25.2 %all-to-all-start.2 = ((bf16[256,4,384]{0,2,1:T(8,128)(2,1)}), bf16[256,4,384]{0,2,1:T(8,128)(2,1)S(1)}, u32[]{:S(2)}, u32[]{:S(2)}) async-start(bf16[256,4,384]{0,2,1:T(8,128)(2,1)} %bitcast.35), calls=%async_computation.2 | async-start | bytes 1572864 | tf_op jit(solution)/shard_map/all_to_all | solution.py:187
  162.6 23.8 %all-to-all-start.3 = ((bf16[4,256,384]{2,1,0:T(8,128)(2,1)}), bf16[4,256,384]{2,1,0:T(8,128)(2,1)S(1)}, u32[]{:S(2)}, u32[]{:S(2)}) async-start(bf16[4,256,384]{2,1,0:T(8,128)(2,1)} %bitcast.84), calls=%async_computation.3 | async-start | bytes 1572864 | tf_op jit(solution)/shard_map/all_to_all | solution.py:250
  186.4 23.1 %all-to-all-start.4 = ((bf16[4,256,384]{2,1,0:T(8,128)(2,1)}), bf16[4,256,384]{2,1,0:T(8,128)(2,1)S(1)}, u32[]{:S(2)}, u32[]{:S(2)}) async-start(bf16[4,256,384]{2,1,0:T(8,128)(2,1)} %bitcast.83), calls=%async_computation.4 | async-start | bytes 1572864 | tf_op jit(solution)/shard_map/all_to_all | solution.py:250
Sparse Core Ops, SparseCore 0:
  70.2 32.6 all-gather.4
  130.3 20.1 all-gather.2

commit v21 on v20

--- a/solution.py
+++ b/solution.py
@@ -13,7 +13,7 @@
 CAP = 2
 SCALE = HD ** (-0.5)
 DRAFT_ROWS = 128
-PAIR = 4
+PAIR = 8
 EXP2_SCALE = SCALE * 1.4426950408889634
 
 

time: 219 us -> 219 us (level)
  transfers between devices with their start and end apart: 16 -> 16, of which waited for: 12 -> 12; matrix products, arithmetic and copies ran while one was open for 23% -> 23% of each run, Pallas kernels for 19% -> 18%
where the time goes in v21:
time: 219 us; the launch traced here: 218 us
  waiting for transfers between devices  77.6 us (35%)
  Pallas kernels  39.1 us (18%)
  local copies, waits for them, and re-layouts  32.7 us (15%)
  starting transfers between devices  32.6 us (15%)
  other arithmetic  21.5 us (10%)
  between operations  14.4 us (7%)
    pallas_call x2, Pallas kernels, sparse_attention(): pl.pallas_call(sparse_kernel, out_shape=jax.ShapeDtypeStruct((rows, heads...  26.7 us
    ppermute x3, waiting for transfers between devices, head_permutes(): lax.ppermute(piece, 'head', [(i, (i + shift) % count) for i in range(coun...  26.6 us
    ppermute x6, waiting for transfers between devices, exchange(): lax.ppermute(parcel, 'seq', [(i, (i + shift) % seq_count) for i in range(...  23.4 us
    all_to_all x2, waiting for transfers between devices, on_device(): lax.all_to_all(rows_part, 'head', split_axis=0, concat_axis=1, tiled=True)  13 us
    pallas_call x1, Pallas kernels, draft_attention(): pl.pallas_call(functools.partial(draft_kernel, split), out_shape=jax.Shap...  12.4 us
    all_to_all x2, starting transfers between devices, query_a2a(): lax.all_to_all(piece, 'head', split_axis=1, concat_axis=0, tiled=True)  8.87 us
    all_to_all x1, waiting for transfers between devices, on_device(): lax.all_to_all(key_in, 'head', split_axis=1, concat_axis=0, tiled=True)  7.87 us
    all_to_all x2, starting transfers between devices, on_device(): lax.all_to_all(rows_part, 'head', split_axis=0, concat_axis=1, tiled=True)  6.99 us
  transfers between devices with their start and end apart: 16, of which 12 were waited for; matrix products, arithmetic and copies ran while one was open for 23% of the time, Pallas kernels for 18%

profile of v21, /device:TPU:0, one launch (start us, length us, event | category | flops | bytes accessed | tf_op | source)
XLA Modules:
  0.0 217.8 jit_solution(8736354085051457559)
XLA Ops:
  10.0 5.0 %collective-permute-start.2 = (bf16[256,768]{1,0:T(8,128)(2,1)}, bf16[256,768]{1,0:T(8,128)(2,1)}, u32[]{:S(2)}, u32[]{:S(2)}) collective-permute-start(bf16[256,768]{1,0:T(8,128)(2,1)} %bitcast.9), channel_id=1, source_target_pairs={{0,3},{1,0},{2,1},{3,2},{4,7},{5,4},{6,5},{7,6},{8,11},{9,8},{10,9... | collective-permute-start | bytes 1179656 | tf_op jit(solution)/shard_map/ppermute | solution.py:166
  19.2 4.8 %all-to-all-start.1 = ((bf16[256,4,768]{2,0,1:T(8,128)(2,1)}), bf16[256,4,768]{2,0,1:T(8,128)(2,1)S(1)}, u32[]{:S(2)}, u32[]{:S(2)}) async-start(bf16[256,4,768]{2,0,1:T(8,128)(2,1)} %bitcast.63), calls=%async_computation.1 | async-start | bytes 3145728 | tf_op jit(solution)/shard_map/all_to_all | solution.py:174
  26.0 2.6 %copy.45 = bf16[256,3072]{0,1:T(8,128)(2,1)} copy(bf16[256,3072]{1,0:T(8,128)(2,1)} %param.6) | data formatting | bytes 3145728 | tf_op jit(solution)/shard_map/reshape | solution.py:181
  30.5 2.6 %fusion.14 = (bf16[256,4,384]{0,2,1:T(8,128)(2,1)}, bf16[256,4,384]{0,2,1:T(8,128)(2,1)}) fusion(bf16[256,4,768]{0,2,1:T(8,128)(2,1)} %bitcast.69), kind=kLoop, calls=%fused_computation.74 | loop fusion | bytes 3145728 | tf_op jit(solution)/shard_map/slice | solution.py:183
  34.4 25.3 %collective-permute-done.1 = bf16[256,768]{1,0:T(8,128)(2,1)} collective-permute-done((bf16[256,768]{1,0:T(8,128)(2,1)}, bf16[256,768]{1,0:T(8,128)(2,1)}, u32[]{:S(2)}, u32[]{:S(2)}) %collective-permute-start.1) | collective-permute-done | bytes 393248 | tf_op jit(solution)/shard_map/ppermute | solution.py:166
  65.6 3.6 %convert_reduce_fusion = f32[256,768]{1,0:T(8,128)S(1)} fusion(bf16[256,4,768]{2,1,0:T(4,128)(2,1)} %gather.20, pred[256]{0:T(512)(128)(4,1)S(1)} %broadcast_in_dim.76), kind=kLoop, calls=%fused_computation.4 | loop fusion | flops 2162688 | bytes 2359552 | tf_op jit(solution)/shard_map/reduce_sum | solution.py:22
  71.5 3.2 %gather_fusion.2 = bf16[8,128,768]{2,1,0:T(8,128)(2,1)} fusion(bf16[8,128,768]{2,1,0:T(8,128)(2,1)} %broadcast_select_fusion.2, s32[1024]{0:T(1024)S(1)} %pad_clamp_fusion), kind=kCustom, calls=%fused_computation.clone | custom fusion | bytes 3145760 | tf_op jit(solution)/shard_map/jit(_take)/gather | solution.py:209
  74.7 7.9 %all-to-all-done.1 = bf16[256,4,768]{2,0,1:T(8,128)(2,1)S(1)} async-done(((bf16[256,4,768]{2,0,1:T(8,128)(2,1)}), bf16[256,4,768]{2,0,1:T(8,128)(2,1)S(1)}, u32[]{:S(2)}, u32[]{:S(2)}) %all-to-all-start.1) | async-done | bytes 1572896 | tf_op jit(solution)/shard_map/all_to_all | solution.py:174
  84.4 3.6 %broadcast_select_fusion = (bf16[8,128,768]{2,1,0:T(8,128)(2,1)}, bf16[8,128,768]{2,1,0:T(8,128)(2,1)S(1)}) fusion(bf16[8,128,768]{2,1,0:T(8,128)(2,1)} %gather_fusion.3, pred[8]{0:T(512)(128)(4,1)S(1)} %compare_and_fusion, bf16[8,128,768]{2,1,0:T(8,128)(2,1)} %gather_fusion.2), kind=kLoop, calls=%fused_computation.10 | loop fusion | flops 1572864 | bytes 6291464 | tf_op jit(solution)/shard_map/jit(_take)/select_n | solution.py:209
  94.1 11.0 %collective-permute-done.3 = bf16[2,128,768]{2,1,0:T(8,128)(2,1)} collective-permute-done((bf16[2,128,768]{2,1,0:T(8,128)(2,1)}, bf16[2,128,768]{2,1,0:T(8,128)(2,1)}, u32[]{:S(2)}, u32[]{:S(2)}) %collective-permute-start.3) | collective-permute-done | bytes 393248 | tf_op jit(solution)/shard_map/ppermute | solution.py:217
  105.5 6.0 %collective-permute-done.5 = bf16[2,128,768]{2,1,0:T(8,128)(2,1)} collective-permute-done((bf16[2,128,768]{2,1,0:T(8,128)(2,1)S(1)}, bf16[2,128,768]{2,1,0:T(8,128)(2,1)}, u32[]{:S(2)}, u32[]{:S(2)}) %collective-permute-start.5) | collective-permute-done | bytes 393248 | tf_op jit(solution)/shard_map/ppermute | solution.py:217
  111.4 4.8 %all-to-all-start = ((bf16[256,4,384]{0,2,1:T(8,128)(2,1)}), bf16[256,4,384]{0,2,1:T(8,128)(2,1)}, u32[]{:S(2)}, u32[]{:S(2)}) async-start(bf16[256,4,384]{0,2,1:T(8,128)(2,1)} %get-tuple-element.33), calls=%async_computation | async-start | bytes 1572864 | tf_op jit(solution)/shard_map/all_to_all | solution.py:187
  122.1 3.1 %reshape.170 = f32[256,4,768]{2,1,0:T(4,128)S(1)} reshape(f32[4,256,768]{2,1,0:T(8,128)} %bitcast_convert_fusion) | data formatting | bytes 6291456 | tf_op jit(solution)/shard_map/convert_element_type | solution.py:21
  125.2 3.0 %reduce_sum.28 = f32[256,768]{1,0:T(8,128)} reduce(f32[256,4,768]{2,1,0:T(4,128)S(1)} %reshape.170, f32[]{:T(128)} %constant.170.clone.1), dimensions={1}, to_apply=%region_4.6 | reduce | flops 589824 | bytes 3932164 | tf_op jit(solution)/shard_map/reduce_sum | solution.py:22
  131.2 5.1 %collective-permute-done.8 = bf16[2,128,768]{2,1,0:T(8,128)(2,1)} collective-permute-done((bf16[2,128,768]{2,1,0:T(8,128)(2,1)S(1)}, bf16[2,128,768]{2,1,0:T(8,128)(2,1)}, u32[]{:S(2)}, u32[]{:S(2)}) %collective-permute-start.8) | collective-permute-done | bytes 393248 | tf_op jit(solution)/shard_map/ppermute | solution.py:217
  137.3 4.0 %all-to-all-start.2 = ((bf16[256,4,384]{0,2,1:T(8,128)(2,1)}), bf16[256,4,384]{0,2,1:T(8,128)(2,1)S(1)}, u32[]{:S(2)}, u32[]{:S(2)}) async-start(bf16[256,4,384]{0,2,1:T(8,128)(2,1)} %bitcast.35), calls=%async_computation.2 | async-start | bytes 1572864 | tf_op jit(solution)/shard_map/all_to_all | solution.py:187
  143.7 13.3 %shard_map.61 = bf16[1024,384]{1,0:T(8,128)(2,1)} custom-call(s32[96]{0:T(128)} %reshape.162.tbl_ref, bf16[1024,384]{1,0:T(8,128)(2,1)} %bitcast.73, bf16[1024,768]{1,0:T(8,128)(2,1)} %bitcast.67, bf16[1024,768]{1,0:T(8,128)(2,1)} %bitcast_select_fusion.refs_1_, bf16[256,768]{1,0:T(8,128)(2,1)} %bitcast.30.refs_2_, bf16[256,768]{1,0:T(8,128)(2,1)} %bitcast.32.refs_3_, ...), custom_call_target="tpu_custom_call" | custom-call | flops 2415919104 | bytes 4325376 | tf_op jit(solution)/shard_map/pallas_call | solution.py:88
  157.0 5.6 %all-to-all-done.2 = bf16[256,4,384]{0,2,1:T(8,128)(2,1)S(1)} async-done(((bf16[256,4,384]{0,2,1:T(8,128)(2,1)}), bf16[256,4,384]{0,2,1:T(8,128)(2,1)S(1)}, u32[]{:S(2)}, u32[]{:S(2)}) %all-to-all-start.2) | async-done | bytes 786464 | tf_op jit(solution)/shard_map/all_to_all | solution.py:187
  162.6 3.5 %all-to-all-start.3 = ((bf16[4,256,384]{2,1,0:T(8,128)(2,1)}), bf16[4,256,384]{2,1,0:T(8,128)(2,1)S(1)}, u32[]{:S(2)}, u32[]{:S(2)}) async-start(bf16[4,256,384]{2,1,0:T(8,128)(2,1)} %bitcast.84), calls=%async_computation.3 | async-start | bytes 1572864 | tf_op jit(solution)/shard_map/all_to_all | solution.py:250
  167.3 13.3 %shard_map.59 = bf16[1024,384]{1,0:T(8,128)(2,1)} custom-call(s32[96]{0:T(128)} %reshape.162.tbl_ref, bf16[1024,384]{1,0:T(8,128)(2,1)} %bitcast.75, bf16[1024,768]{1,0:T(8,128)(2,1)} %bitcast.68, bf16[1024,768]{1,0:T(8,128)(2,1)} %bitcast_select_fusion.refs_1_, bf16[256,768]{1,0:T(8,128)(2,1)} %bitcast.30.refs_2_, bf16[256,768]{1,0:T(8,128)(2,1)} %bitcast.32.refs_3_, ...), custom_call_target="tpu_custom_call" | custom-call | flops 2415919104 | bytes 4325376 | tf_op jit(solution)/shard_map/pallas_call | solution.py:88
  180.6 5.8 %all-to-all-done.3 = bf16[4,256,384]{2,1,0:T(8,128)(2,1)S(1)} async-done(((bf16[4,256,384]{2,1,0:T(8,128)(2,1)}), bf16[4,256,384]{2,1,0:T(8,128)(2,1)S(1)}, u32[]{:S(2)}, u32[]{:S(2)}) %all-to-all-start.3) | async-done | bytes 786464 | tf_op jit(solution)/shard_map/all_to_all | solution.py:250
  186.4 3.5 %all-to-all-start.4 = ((bf16[4,256,384]{2,1,0:T(8,128)(2,1)}), bf16[4,256,384]{2,1,0:T(8,128)(2,1)S(1)}, u32[]{:S(2)}, u32[]{:S(2)}) async-start(bf16[4,256,384]{2,1,0:T(8,128)(2,1)} %bitcast.83), calls=%async_computation.4 | async-start | bytes 1572864 | tf_op jit(solution)/shard_map/all_to_all | solution.py:250
  189.9 12.4 %shard_map.60 = bf16[256,768]{1,0:T(8,128)(2,1)} custom-call(bf16[1024,384]{1,0:T(8,128)(2,1)} %bitcast.74, bf16[1024,384]{1,0:T(8,128)(2,1)} %bitcast.76, bf16[1024,768]{1,0:T(8,128)(2,1)} %all-gather.3.cloned.1.call-done.k_ref, bf16[1024,768]{1,0:T(8,128)(2,1)} %all-gather.5.cloned.1.call-done.v_ref), custom_call_target="tpu_custom_call" | custom-call | flops 1006632960 | bytes 6684672 | tf_op jit(solution)/shard_map/pallas_call | solution.py:140
  202.3 7.2 %all-to-all-done.4 = bf16[4,256,384]{2,1,0:T(8,128)(2,1)S(1)} async-done(((bf16[4,256,384]{2,1,0:T(8,128)(2,1)}), bf16[4,256,384]{2,1,0:T(8,128)(2,1)S(1)}, u32[]{:S(2)}, u32[]{:S(2)}) %all-to-all-start.4) | async-done | bytes 786464 | tf_op jit(solution)/shard_map/all_to_all | solution.py:250
  (84 shorter events, 43.3 us)
Async XLA Ops:
  9.1 8.9 %copy-start.2 = (bf16[256,3072]{1,0:T(8,128)(2,1)S(1)}, bf16[256,3072]{1,0:T(8,128)(2,1)}, u32[]{:S(2)}) copy-start(bf16[256,3072]{1,0:T(8,128)(2,1)} %param.7) | copy-start | bytes 4718596
  10.0 23.1 %collective-permute-start.2 = (bf16[256,768]{1,0:T(8,128)(2,1)}, bf16[256,768]{1,0:T(8,128)(2,1)}, u32[]{:S(2)}, u32[]{:S(2)}) collective-permute-start(bf16[256,768]{1,0:T(8,128)(2,1)} %bitcast.9), channel_id=1, source_target_pairs={{0,3},{1,0},{2,1},{3,2},{4,7},{5,4},{6,5},{7,6},{8,11},{9,8},{10,9... | collective-permute-start | bytes 1179656 | tf_op jit(solution)/shard_map/ppermute | solution.py:166
  16.0 18.4 %collective-permute-start = (bf16[256,768]{1,0:T(8,128)(2,1)}, bf16[256,768]{1,0:T(8,128)(2,1)}, u32[]{:S(2)}, u32[]{:S(2)}) collective-permute-start(bf16[256,768]{1,0:T(8,128)(2,1)} %bitcast.5), channel_id=1, source_target_pairs={{0,1},{1,2},{2,3},{3,0},{4,5},{5,6},{6,7},{7,4},{8,9},{9,10},{10,1... | collective-permute-start | bytes 1179656 | tf_op jit(solution)/shard_map/ppermute | solution.py:166
  16.9 42.8 %collective-permute-start.1 = (bf16[256,768]{1,0:T(8,128)(2,1)}, bf16[256,768]{1,0:T(8,128)(2,1)}, u32[]{:S(2)}, u32[]{:S(2)}) collective-permute-start(bf16[256,768]{1,0:T(8,128)(2,1)} %bitcast.7), channel_id=1, source_target_pairs={{0,2},{1,3},{2,0},{3,1},{4,6},{5,7},{6,4},{7,5},{8,10},{9,11},{10,... | collective-permute-start | bytes 1179656 | tf_op jit(solution)/shard_map/ppermute | solution.py:166
  19.2 4.8 %copy-start.3 = (s32[32,12]{0,1:T(8,128)S(1)}, s32[32,12]{0,1:T(8,128)}, u32[]{:S(2)}) copy-start(s32[32,12]{0,1:T(8,128)} %param.9) | copy-start | bytes 4612
  19.2 63.3 %all-to-all-start.1 = ((bf16[256,4,768]{2,0,1:T(8,128)(2,1)}), bf16[256,4,768]{2,0,1:T(8,128)(2,1)S(1)}, u32[]{:S(2)}, u32[]{:S(2)}) async-start(bf16[256,4,768]{2,0,1:T(8,128)(2,1)} %bitcast.63), calls=%async_computation.1 | async-start | bytes 3145728 | tf_op jit(solution)/shard_map/all_to_all | solution.py:174
  24.0 156.6 %all-gather.5.cloned.1.call-start = ((), (), s32[]{:S(2)}) async-start(), calls=%async_computation.6 | async-start | bytes 1966080 | tf_op jit(solution)/shard_map/all_gather | solution.py:190
  82.5 37.6 %copy-start = (bf16[256,4,768]{2,0,1:T(8,128)(2,1)}, bf16[256,4,768]{2,0,1:T(8,128)(2,1)S(1)}, u32[]{:S(2)}) copy-start(bf16[256,4,768]{2,0,1:T(8,128)(2,1)S(1)} %all-to-all-done.1) | copy-start | bytes 4718596
  88.9 16.1 %collective-permute-start.3 = (bf16[2,128,768]{2,1,0:T(8,128)(2,1)}, bf16[2,128,768]{2,1,0:T(8,128)(2,1)}, u32[]{:S(2)}, u32[]{:S(2)}) collective-permute-start(bf16[2,128,768]{2,1,0:T(8,128)(2,1)} %get-tuple-element.36), channel_id=1, source_target_pairs={{0,4},{4,8},{8,12},{12,0},{1,5},{5,9},{9,13},{13,1},{2,6},{6,10},{... | collective-permute-start | bytes 1179656 | tf_op jit(solution)/shard_map/ppermute | solution.py:217
  88.9 16.5 %collective-permute-start.4 = (bf16[2,128,768]{2,1,0:T(8,128)(2,1)}, bf16[2,128,768]{2,1,0:T(8,128)(2,1)}, u32[]{:S(2)}, u32[]{:S(2)}) collective-permute-start(bf16[2,128,768]{2,1,0:T(8,128)(2,1)} %get-tuple-element.35), channel_id=1, source_target_pairs={{0,8},{4,12},{8,0},{12,4},{1,9},{5,13},{9,1},{13,5},{2,10},{6,14},... | collective-permute-start | bytes 1179656 | tf_op jit(solution)/shard_map/ppermute | solution.py:217
  90.5 20.9 %collective-permute-start.5 = (bf16[2,128,768]{2,1,0:T(8,128)(2,1)S(1)}, bf16[2,128,768]{2,1,0:T(8,128)(2,1)}, u32[]{:S(2)}, u32[]{:S(2)}) collective-permute-start(bf16[2,128,768]{2,1,0:T(8,128)(2,1)S(1)} %get-tuple-element.34), channel_id=1, source_target_pairs={{0,12},{4,0},{8,4},{12,8},{1,13},{5,1},{9,5},{13,9},{2,14},{6,2},{... | collective-permute-start | bytes 1179656 | tf_op jit(solution)/shard_map/ppermute | solution.py:217
  94.1 22.2 %copy-start.1 = (bf16[8,128,768]{2,1,0:T(8,128)(2,1)S(1)}, bf16[8,128,768]{2,1,0:T(8,128)(2,1)}, u32[]{:S(2)}) copy-start(bf16[8,128,768]{2,1,0:T(8,128)(2,1)} %get-tuple-element.41) | copy-start | bytes 4718596
  111.4 25.9 %all-to-all-start = ((bf16[256,4,384]{0,2,1:T(8,128)(2,1)}), bf16[256,4,384]{0,2,1:T(8,128)(2,1)}, u32[]{:S(2)}, u32[]{:S(2)}) async-start(bf16[256,4,384]{0,2,1:T(8,128)(2,1)} %get-tuple-element.33), calls=%async_computation | async-start | bytes 1572864 | tf_op jit(solution)/shard_map/all_to_all | solution.py:187
  116.3 64.3 %all-gather.3.cloned.1.call-start = ((), (), s32[]{:S(2)}) async-start(), calls=%async_computation.5 | async-start | bytes 1966080 | tf_op jit(solution)/shard_map/all_gather | solution.py:189
  117.2 12.9 %collective-permute-start.6 = (bf16[2,128,768]{2,1,0:T(8,128)(2,1)}, bf16[2,128,768]{2,1,0:T(8,128)(2,1)}, u32[]{:S(2)}, u32[]{:S(2)}) collective-permute-start(bf16[2,128,768]{2,1,0:T(8,128)(2,1)} %get-tuple-element.31), channel_id=1, source_target_pairs={{0,4},{4,8},{8,12},{12,0},{1,5},{5,9},{9,13},{13,1},{2,6},{6,10},{... | collective-permute-start | bytes 1179656 | tf_op jit(solution)/shard_map/ppermute | solution.py:217
  118.8 12.4 %collective-permute-start.7 = (bf16[2,128,768]{2,1,0:T(8,128)(2,1)}, bf16[2,128,768]{2,1,0:T(8,128)(2,1)}, u32[]{:S(2)}, u32[]{:S(2)}) collective-permute-start(bf16[2,128,768]{2,1,0:T(8,128)(2,1)} %get-tuple-element.30), channel_id=1, source_target_pairs={{0,8},{4,12},{8,0},{12,4},{1,9},{5,13},{9,1},{13,5},{2,10},{6,14},... | collective-permute-start | bytes 1179656 | tf_op jit(solution)/shard_map/ppermute | solution.py:217
  119.4 16.9 %collective-permute-start.8 = (bf16[2,128,768]{2,1,0:T(8,128)(2,1)S(1)}, bf16[2,128,768]{2,1,0:T(8,128)(2,1)}, u32[]{:S(2)}, u32[]{:S(2)}) collective-permute-start(bf16[2,128,768]{2,1,0:T(8,128)(2,1)S(1)} %get-tuple-element.29), channel_id=1, source_target_pairs={{0,12},{4,0},{8,4},{12,8},{1,13},{5,1},{9,5},{13,9},{2,14},{6,2},{... | collective-permute-start | bytes 1179656 | tf_op jit(solution)/shard_map/ppermute | solution.py:217
  137.3 25.2 %all-to-all-start.2 = ((bf16[256,4,384]{0,2,1:T(8,128)(2,1)}), bf16[256,4,384]{0,2,1:T(8,128)(2,1)S(1)}, u32[]{:S(2)}, u32[]{:S(2)}) async-start(bf16[256,4,384]{0,2,1:T(8,128)(2,1)} %bitcast.35), calls=%async_computation.2 | async-start | bytes 1572864 | tf_op jit(solution)/shard_map/all_to_all | solution.py:187
  162.6 23.8 %all-to-all-start.3 = ((bf16[4,256,384]{2,1,0:T(8,128)(2,1)}), bf16[4,256,384]{2,1,0:T(8,128)(2,1)S(1)}, u32[]{:S(2)}, u32[]{:S(2)}) async-start(bf16[4,256,384]{2,1,0:T(8,128)(2,1)} %bitcast.84), calls=%async_computation.3 | async-start | bytes 1572864 | tf_op jit(solution)/shard_map/all_to_all | solution.py:250
  186.4 23.1 %all-to-all-start.4 = ((bf16[4,256,384]{2,1,0:T(8,128)(2,1)}), bf16[4,256,384]{2,1,0:T(8,128)(2,1)S(1)}, u32[]{:S(2)}, u32[]{:S(2)}) async-start(bf16[4,256,384]{2,1,0:T(8,128)(2,1)} %bitcast.83), calls=%async_computation.4 | async-start | bytes 1572864 | tf_op jit(solution)/shard_map/all_to_all | solution.py:250
Sparse Core Ops, SparseCore 0:
  70.2 32.6 all-gather.4
  130.3 20.1 all-gather.2

commit v22 on v20

--- a/solution.py
+++ b/solution.py
@@ -171,8 +171,8 @@
 
 
 def on_device(query_in, key_in, value_in, block_lists):
-    key_rows = lax.all_to_all(key_in, "head", split_axis=1, concat_axis=0, tiled=True)
-    value_rows = head_permutes(value_in)
+    key_rows = head_permutes(key_in)
+    value_rows = lax.all_to_all(value_in, "head", split_axis=1, concat_axis=0, tiled=True)
     seq_rows, width = key_rows.shape
     head_count = lax.axis_size("head")
     heads = width // HD
@@ -231,11 +231,11 @@
 
     remote_keys = exchange(key_rows)
     remote_values = exchange(value_rows)
-    leading, remote_values, value_rows, table = lax.optimization_barrier(
-        (query_slices[0], remote_values, value_rows, table)
+    leading, remote_keys, key_rows, table = lax.optimization_barrier(
+        (query_slices[0], remote_keys, key_rows, table)
     )
     query_parts = [query_a2a(leading)]
-    later, remote_keys = lax.optimization_barrier((query_slices[1:], remote_keys))
+    later, remote_values = lax.optimization_barrier((query_slices[1:], remote_values))
     query_parts += [query_a2a(piece) for piece in later]
 
     pieces = []

time: 219 us -> 218 us (level)
  starting transfers between devices: 32.6 us -> 30 us
    all_to_all x1, waiting for transfers between devices: 7.87 us -> 26.1 us  [on_device(): lax.all_to_all(value_in, 'head', split_axis=1, concat_axis=0, tiled=True)]
    ppermute x3, waiting for transfers between devices: 26.6 us -> 9.01 us  [head_permutes(): lax.ppermute(piece, 'head', [(i, (i + shift) % count) for i in range(coun...]
    ppermute x6, waiting for transfers between devices: 23.4 us -> 27.6 us  [exchange(): lax.ppermute(parcel, 'seq', [(i, (i + shift) % seq_count) for i in range(...]
    ppermute x6, starting transfers between devices: 5.91 us -> 2.59 us  [exchange(): lax.ppermute(parcel, 'seq', [(i, (i + shift) % seq_count) for i in range(...]
    all_to_all x2, waiting for transfers between devices: 5.83 us -> 2.98 us  [query_a2a(): lax.all_to_all(piece, 'head', split_axis=1, concat_axis=0, tiled=True)]
  transfers between devices with their start and end apart: 16 -> 16, of which waited for: 12 -> 9; matrix products, arithmetic and copies ran while one was open for 23% -> 23% of each run, Pallas kernels for 19% -> 19%
where the time goes in v22:
time: 218 us; the launch traced here: 217 us
  waiting for transfers between devices  77.2 us (35%)
  Pallas kernels  40.6 us (19%)
  local copies, waits for them, and re-layouts  33.4 us (15%)
  starting transfers between devices  30 us (14%)
  other arithmetic  21.7 us (10%)
  between operations  14.4 us (7%)
    pallas_call x2, Pallas kernels, sparse_attention(): pl.pallas_call(sparse_kernel, out_shape=jax.ShapeDtypeStruct((rows, heads...  28.2 us
    ppermute x6, waiting for transfers between devices, exchange(): lax.ppermute(parcel, 'seq', [(i, (i + shift) % seq_count) for i in range(...  27.6 us
    all_to_all x1, waiting for transfers between devices, on_device(): lax.all_to_all(value_in, 'head', split_axis=1, concat_axis=0, tiled=True)  26.1 us
    pallas_call x1, Pallas kernels, draft_attention(): pl.pallas_call(functools.partial(draft_kernel, split), out_shape=jax.Shap...  12.4 us
    all_to_all x2, waiting for transfers between devices, on_device(): lax.all_to_all(rows_part, 'head', split_axis=0, concat_axis=1, tiled=True)  11.4 us
    all_to_all x2, starting transfers between devices, query_a2a(): lax.all_to_all(piece, 'head', split_axis=1, concat_axis=0, tiled=True)  9.68 us
    ppermute x3, waiting for transfers between devices, head_permutes(): lax.ppermute(piece, 'head', [(i, (i + shift) % count) for i in range(coun...  9.01 us
    all_to_all x2, starting transfers between devices, on_device(): lax.all_to_all(rows_part, 'head', split_axis=0, concat_axis=1, tiled=True)  6.99 us
  transfers between devices with their start and end apart: 16, of which 9 were waited for; matrix products, arithmetic and copies ran while one was open for 23% of the time, Pallas kernels for 19%

profile of v22, /device:TPU:0, one launch (start us, length us, event | category | flops | bytes accessed | tf_op | source)
XLA Modules:
  0.0 217.2 jit_solution(4024419182079273019)
XLA Ops:
  10.7 3.0 %collective-permute-start = (bf16[256,768]{1,0:T(8,128)(2,1)}, bf16[256,768]{1,0:T(8,128)(2,1)}, u32[]{:S(2)}, u32[]{:S(2)}) collective-permute-start(bf16[256,768]{1,0:T(8,128)(2,1)} %bitcast.5), channel_id=1, source_target_pairs={{0,1},{1,2},{2,3},{3,0},{4,5},{5,6},{6,7},{7,4},{8,9},{9,10},{10,1... | collective-permute-start | bytes 1179656 | tf_op jit(solution)/shard_map/ppermute | solution.py:166
  14.7 2.6 %collective-permute-start.1 = (bf16[256,768]{1,0:T(8,128)(2,1)}, bf16[256,768]{1,0:T(8,128)(2,1)}, u32[]{:S(2)}, u32[]{:S(2)}) collective-permute-start(bf16[256,768]{1,0:T(8,128)(2,1)} %bitcast.7), channel_id=1, source_target_pairs={{0,2},{1,3},{2,0},{3,1},{4,6},{5,7},{6,4},{7,5},{8,10},{9,11},{10,... | collective-permute-start | bytes 1179656 | tf_op jit(solution)/shard_map/ppermute | solution.py:166
  20.8 3.7 %all-to-all-start.1 = ((bf16[256,4,768]{2,0,1:T(8,128)(2,1)}), bf16[256,4,768]{2,0,1:T(8,128)(2,1)S(1)}, u32[]{:S(2)}, u32[]{:S(2)}) async-start(bf16[256,4,768]{2,0,1:T(8,128)(2,1)} %bitcast.63), calls=%async_computation.1 | async-start | bytes 3145728 | tf_op jit(solution)/shard_map/all_to_all | solution.py:175
  34.1 9.0 %collective-permute-done.1 = bf16[256,768]{1,0:T(8,128)(2,1)} collective-permute-done((bf16[256,768]{1,0:T(8,128)(2,1)}, bf16[256,768]{1,0:T(8,128)(2,1)}, u32[]{:S(2)}, u32[]{:S(2)}) %collective-permute-start.1) | collective-permute-done | bytes 393248 | tf_op jit(solution)/shard_map/ppermute | solution.py:166
  43.1 2.6 %pad_maximum_fusion = bf16[4,256,768]{2,1,0:T(8,128)(2,1)} fusion(bf16[1,256,768]{2,1,0:T(8,128)(2,1)} %bitcast.10, bf16[1,256,768]{2,1,0:T(8,128)(2,1)} %bitcast.8, bf16[1,256,768]{2,1,0:T(8,128)(2,1)} %bitcast.6, bf16[1,256,768]{2,1,0:T(8,128)(2,1)S(1)} %bitcast.82), kind=kLoop, calls=%fused_computation.6 | loop fusion | flops 2359296 | bytes 3145728 | tf_op jit(solution)/shard_map/stack | solution.py:168
  49.1 3.6 %convert_reduce_fusion = f32[256,768]{1,0:T(8,128)S(1)} fusion(bf16[256,4,768]{2,1,0:T(4,128)(2,1)} %gather.20, pred[256]{0:T(512)(128)(4,1)S(1)} %copy-done.4), kind=kLoop, calls=%fused_computation.4 | loop fusion | flops 2162688 | bytes 2359552 | tf_op jit(solution)/shard_map/reduce_sum | solution.py:22
  54.8 3.2 %gather_fusion.2 = bf16[8,128,768]{2,1,0:T(8,128)(2,1)} fusion(bf16[8,128,768]{2,1,0:T(8,128)(2,1)} %broadcast_select_fusion.2, s32[1024]{0:T(1024)S(1)} %pad_clamp_fusion), kind=kCustom, calls=%fused_computation.clone | custom fusion | bytes 3145760 | tf_op jit(solution)/shard_map/jit(_take)/gather | solution.py:209
  58.0 26.1 %all-to-all-done.1 = bf16[256,4,768]{2,0,1:T(8,128)(2,1)S(1)} async-done(((bf16[256,4,768]{2,0,1:T(8,128)(2,1)}), bf16[256,4,768]{2,0,1:T(8,128)(2,1)S(1)}, u32[]{:S(2)}, u32[]{:S(2)}) %all-to-all-start.1) | async-done | bytes 1572896 | tf_op jit(solution)/shard_map/all_to_all | solution.py:175
  86.0 3.4 %broadcast_select_fusion = (bf16[8,128,768]{2,1,0:T(8,128)(2,1)}, bf16[8,128,768]{2,1,0:T(8,128)(2,1)S(1)}) fusion(bf16[8,128,768]{2,1,0:T(8,128)(2,1)} %gather_fusion.3, pred[8]{0:T(512)(128)(4,1)S(1)} %copy-done.5, bf16[8,128,768]{2,1,0:T(8,128)(2,1)} %gather_fusion.2), kind=kLoop, calls=%fused_computation.10 | loop fusion | flops 1572864 | bytes 6291464 | tf_op jit(solution)/shard_map/jit(_take)/select_n | solution.py:209
  94.4 8.5 %collective-permute-done.5 = bf16[2,128,768]{2,1,0:T(8,128)(2,1)} collective-permute-done((bf16[2,128,768]{2,1,0:T(8,128)(2,1)}, bf16[2,128,768]{2,1,0:T(8,128)(2,1)}, u32[]{:S(2)}, u32[]{:S(2)}) %collective-permute-start.5) | collective-permute-done | bytes 393248 | tf_op jit(solution)/shard_map/ppermute | solution.py:217
  102.9 10.5 %collective-permute-done.4 = bf16[2,128,768]{2,1,0:T(8,128)(2,1)} collective-permute-done((bf16[2,128,768]{2,1,0:T(8,128)(2,1)}, bf16[2,128,768]{2,1,0:T(8,128)(2,1)}, u32[]{:S(2)}, u32[]{:S(2)}) %collective-permute-start.4) | collective-permute-done | bytes 393248 | tf_op jit(solution)/shard_map/ppermute | solution.py:217
  113.5 4.6 %all-to-all-start = ((bf16[256,4,384]{0,2,1:T(8,128)(2,1)}), bf16[256,4,384]{0,2,1:T(8,128)(2,1)}, u32[]{:S(2)}, u32[]{:S(2)}) async-start(bf16[256,4,384]{0,2,1:T(8,128)(2,1)} %get-tuple-element.33), calls=%async_computation | async-start | bytes 1572864 | tf_op jit(solution)/shard_map/all_to_all | solution.py:187
  121.8 3.1 %reshape.170 = f32[256,4,768]{2,1,0:T(4,128)S(1)} reshape(f32[4,256,768]{2,1,0:T(8,128)} %bitcast_convert_fusion) | data formatting | bytes 6291456 | tf_op jit(solution)/shard_map/convert_element_type | solution.py:21
  124.9 3.0 %reduce_sum.29 = f32[256,768]{1,0:T(8,128)} reduce(f32[256,4,768]{2,1,0:T(4,128)S(1)} %reshape.170, f32[]{:T(128)} %constant.170.clone.1), dimensions={1}, to_apply=%region_5.7 | reduce | flops 589824 | bytes 3932164 | tf_op jit(solution)/shard_map/reduce_sum | solution.py:22
  129.8 7.5 %collective-permute-done.7 = bf16[2,128,768]{2,1,0:T(8,128)(2,1)} collective-permute-done((bf16[2,128,768]{2,1,0:T(8,128)(2,1)}, bf16[2,128,768]{2,1,0:T(8,128)(2,1)}, u32[]{:S(2)}, u32[]{:S(2)}) %collective-permute-start.7) | collective-permute-done | bytes 393248 | tf_op jit(solution)/shard_map/ppermute | solution.py:217
  138.3 5.1 %all-to-all-start.2 = ((bf16[256,4,384]{0,2,1:T(8,128)(2,1)}), bf16[256,4,384]{0,2,1:T(8,128)(2,1)S(1)}, u32[]{:S(2)}, u32[]{:S(2)}) async-start(bf16[256,4,384]{0,2,1:T(8,128)(2,1)} %bitcast.35), calls=%async_computation.2 | async-start | bytes 1572864 | tf_op jit(solution)/shard_map/all_to_all | solution.py:187
  145.7 14.1 %shard_map.61 = bf16[1024,384]{1,0:T(8,128)(2,1)} custom-call(s32[96]{0:T(128)} %reshape.162.tbl_ref, bf16[1024,384]{1,0:T(8,128)(2,1)} %bitcast.73, bf16[1024,768]{1,0:T(8,128)(2,1)} %bitcast_select_fusion.refs_0_, bf16[1024,768]{1,0:T(8,128)(2,1)} %bitcast.67, bf16[256,768]{1,0:T(8,128)(2,1)} %bitcast.15.refs_2_, bf16[256,768]{1,0:T(8,128)(2,1)} %bitcast.17.refs_3_, ...), custom_call_target="tpu_custom_call" | custom-call | flops 2415919104 | bytes 4325376 | tf_op jit(solution)/shard_map/pallas_call | solution.py:88
  159.8 3.0 %all-to-all-done.2 = bf16[256,4,384]{0,2,1:T(8,128)(2,1)S(1)} async-done(((bf16[256,4,384]{0,2,1:T(8,128)(2,1)}), bf16[256,4,384]{0,2,1:T(8,128)(2,1)S(1)}, u32[]{:S(2)}, u32[]{:S(2)}) %all-to-all-start.2) | async-done | bytes 786464 | tf_op jit(solution)/shard_map/all_to_all | solution.py:187
  162.8 3.5 %all-to-all-start.3 = ((bf16[4,256,384]{2,1,0:T(8,128)(2,1)}), bf16[4,256,384]{2,1,0:T(8,128)(2,1)S(1)}, u32[]{:S(2)}, u32[]{:S(2)}) async-start(bf16[4,256,384]{2,1,0:T(8,128)(2,1)} %bitcast.84), calls=%async_computation.3 | async-start | bytes 1572864 | tf_op jit(solution)/shard_map/all_to_all | solution.py:250
  167.4 14.1 %shard_map.59 = bf16[1024,384]{1,0:T(8,128)(2,1)} custom-call(s32[96]{0:T(128)} %reshape.162.tbl_ref, bf16[1024,384]{1,0:T(8,128)(2,1)} %bitcast.75, bf16[1024,768]{1,0:T(8,128)(2,1)} %bitcast_select_fusion.refs_0_, bf16[1024,768]{1,0:T(8,128)(2,1)} %bitcast.68, bf16[256,768]{1,0:T(8,128)(2,1)} %bitcast.15.refs_2_, bf16[256,768]{1,0:T(8,128)(2,1)} %bitcast.17.refs_3_, ...), custom_call_target="tpu_custom_call" | custom-call | flops 2415919104 | bytes 4325376 | tf_op jit(solution)/shard_map/pallas_call | solution.py:88
  181.6 4.3 %all-to-all-done.3 = bf16[4,256,384]{2,1,0:T(8,128)(2,1)S(1)} async-done(((bf16[4,256,384]{2,1,0:T(8,128)(2,1)}), bf16[4,256,384]{2,1,0:T(8,128)(2,1)S(1)}, u32[]{:S(2)}, u32[]{:S(2)}) %all-to-all-start.3) | async-done | bytes 786464 | tf_op jit(solution)/shard_map/all_to_all | solution.py:250
  185.8 3.5 %all-to-all-start.4 = ((bf16[4,256,384]{2,1,0:T(8,128)(2,1)}), bf16[4,256,384]{2,1,0:T(8,128)(2,1)S(1)}, u32[]{:S(2)}, u32[]{:S(2)}) async-start(bf16[4,256,384]{2,1,0:T(8,128)(2,1)} %bitcast.83), calls=%async_computation.4 | async-start | bytes 1572864 | tf_op jit(solution)/shard_map/all_to_all | solution.py:250
  189.3 12.4 %shard_map.60 = bf16[256,768]{1,0:T(8,128)(2,1)} custom-call(bf16[1024,384]{1,0:T(8,128)(2,1)} %bitcast.74, bf16[1024,384]{1,0:T(8,128)(2,1)} %bitcast.76, bf16[1024,768]{1,0:T(8,128)(2,1)} %all-gather.3.cloned.1.call-done.k_ref, bf16[1024,768]{1,0:T(8,128)(2,1)} %all-gather.5.cloned.1.call-done.v_ref), custom_call_target="tpu_custom_call" | custom-call | flops 1006632960 | bytes 6684672 | tf_op jit(solution)/shard_map/pallas_call | solution.py:140
  201.7 7.2 %all-to-all-done.4 = bf16[4,256,384]{2,1,0:T(8,128)(2,1)S(1)} async-done(((bf16[4,256,384]{2,1,0:T(8,128)(2,1)}), bf16[4,256,384]{2,1,0:T(8,128)(2,1)S(1)}, u32[]{:S(2)}, u32[]{:S(2)}) %all-to-all-start.4) | async-done | bytes 786464 | tf_op jit(solution)/shard_map/all_to_all | solution.py:250
  (94 shorter events, 41.3 us)
Async XLA Ops:
  9.8 9.7 %copy-start.2 = (bf16[256,3072]{1,0:T(8,128)(2,1)S(1)}, bf16[256,3072]{1,0:T(8,128)(2,1)}, u32[]{:S(2)}) copy-start(bf16[256,3072]{1,0:T(8,128)(2,1)} %param.8) | copy-start | bytes 4718596
  10.7 23.3 %collective-permute-start = (bf16[256,768]{1,0:T(8,128)(2,1)}, bf16[256,768]{1,0:T(8,128)(2,1)}, u32[]{:S(2)}, u32[]{:S(2)}) collective-permute-start(bf16[256,768]{1,0:T(8,128)(2,1)} %bitcast.5), channel_id=1, source_target_pairs={{0,1},{1,2},{2,3},{3,0},{4,5},{5,6},{6,7},{7,4},{8,9},{9,10},{10,1... | collective-permute-start | bytes 1179656 | tf_op jit(solution)/shard_map/ppermute | solution.py:166
  14.7 28.4 %collective-permute-start.1 = (bf16[256,768]{1,0:T(8,128)(2,1)}, bf16[256,768]{1,0:T(8,128)(2,1)}, u32[]{:S(2)}, u32[]{:S(2)}) collective-permute-start(bf16[256,768]{1,0:T(8,128)(2,1)} %bitcast.7), channel_id=1, source_target_pairs={{0,2},{1,3},{2,0},{3,1},{4,6},{5,7},{6,4},{7,5},{8,10},{9,11},{10,... | collective-permute-start | bytes 1179656 | tf_op jit(solution)/shard_map/ppermute | solution.py:166
  18.2 24.9 %collective-permute-start.2 = (bf16[256,768]{1,0:T(8,128)(2,1)}, bf16[256,768]{1,0:T(8,128)(2,1)}, u32[]{:S(2)}, u32[]{:S(2)}) collective-permute-start(bf16[256,768]{1,0:T(8,128)(2,1)} %bitcast.9), channel_id=1, source_target_pairs={{0,3},{1,0},{2,1},{3,2},{4,7},{5,4},{6,5},{7,6},{8,11},{9,8},{10,9... | collective-permute-start | bytes 1179656 | tf_op jit(solution)/shard_map/ppermute | solution.py:166
  20.8 3.8 %copy-start.3 = (s32[32,12]{0,1:T(8,128)S(1)}, s32[32,12]{0,1:T(8,128)}, u32[]{:S(2)}) copy-start(s32[32,12]{0,1:T(8,128)} %param.9) | copy-start | bytes 4612
  20.8 63.4 %all-to-all-start.1 = ((bf16[256,4,768]{2,0,1:T(8,128)(2,1)}), bf16[256,4,768]{2,0,1:T(8,128)(2,1)S(1)}, u32[]{:S(2)}, u32[]{:S(2)}) async-start(bf16[256,4,768]{2,0,1:T(8,128)(2,1)} %bitcast.63), calls=%async_computation.1 | async-start | bytes 3145728 | tf_op jit(solution)/shard_map/all_to_all | solution.py:175
  24.5 157.0 %all-gather.3.cloned.1.call-start = ((), (), s32[]{:S(2)}) async-start(), calls=%async_computation.5 | async-start | bytes 1966080 | tf_op jit(solution)/shard_map/all_gather | solution.py:189
  47.7 1.4 copy-start.4
  49.1 4.4 %copy-start.6 = (pred[8]{0:T(512)(128)(4,1)S(1)}, pred[8]{0:T(512)(128)(4,1)}, u32[]{:S(2)}) copy-start(pred[8]{0:T(512)(128)(4,1)} %broadcast_in_dim.64) | copy-start | bytes 28
  84.2 35.7 %copy-start = (bf16[256,4,768]{2,0,1:T(8,128)(2,1)}, bf16[256,4,768]{2,0,1:T(8,128)(2,1)S(1)}, u32[]{:S(2)}) copy-start(bf16[256,4,768]{2,0,1:T(8,128)(2,1)S(1)} %all-to-all-done.1) | copy-start | bytes 4718596
  84.2 1.8 copy-start.5
  89.3 2.9 %copy-start.8 = (pred[4]{0:T(512)(128)(4,1)S(1)}, pred[4]{0:T(512)(128)(4,1)}, u32[]{:S(2)}) copy-start(pred[4]{0:T(512)(128)(4,1)} %copy-done.7) | copy-start | bytes 16
  90.4 12.6 %collective-permute-start.5 = (bf16[2,128,768]{2,1,0:T(8,128)(2,1)}, bf16[2,128,768]{2,1,0:T(8,128)(2,1)}, u32[]{:S(2)}, u32[]{:S(2)}) collective-permute-start(bf16[2,128,768]{2,1,0:T(8,128)(2,1)} %get-tuple-element.34), channel_id=1, source_target_pairs={{0,12},{4,0},{8,4},{12,8},{1,13},{5,1},{9,5},{13,9},{2,14},{6,2},{... | collective-permute-start | bytes 1179656 | tf_op jit(solution)/shard_map/ppermute | solution.py:217
  91.7 21.8 %collective-permute-start.4 = (bf16[2,128,768]{2,1,0:T(8,128)(2,1)}, bf16[2,128,768]{2,1,0:T(8,128)(2,1)}, u32[]{:S(2)}, u32[]{:S(2)}) collective-permute-start(bf16[2,128,768]{2,1,0:T(8,128)(2,1)} %get-tuple-element.35), channel_id=1, source_target_pairs={{0,8},{4,12},{8,0},{12,4},{1,9},{5,13},{9,1},{13,5},{2,10},{6,14},... | collective-permute-start | bytes 1179656 | tf_op jit(solution)/shard_map/ppermute | solution.py:217
  92.1 21.4 %collective-permute-start.3 = (bf16[2,128,768]{2,1,0:T(8,128)(2,1)S(1)}, bf16[2,128,768]{2,1,0:T(8,128)(2,1)}, u32[]{:S(2)}, u32[]{:S(2)}) collective-permute-start(bf16[2,128,768]{2,1,0:T(8,128)(2,1)S(1)} %get-tuple-element.36), channel_id=1, source_target_pairs={{0,4},{4,8},{8,12},{12,0},{1,5},{5,9},{9,13},{13,1},{2,6},{6,10},{... | collective-permute-start | bytes 1179656 | tf_op jit(solution)/shard_map/ppermute | solution.py:217
  94.4 23.7 %copy-start.1 = (bf16[8,128,768]{2,1,0:T(8,128)(2,1)S(1)}, bf16[8,128,768]{2,1,0:T(8,128)(2,1)}, u32[]{:S(2)}) copy-start(bf16[8,128,768]{2,1,0:T(8,128)(2,1)} %get-tuple-element.41) | copy-start | bytes 4718596
  113.5 24.9 %all-to-all-start = ((bf16[256,4,384]{0,2,1:T(8,128)(2,1)}), bf16[256,4,384]{0,2,1:T(8,128)(2,1)}, u32[]{:S(2)}, u32[]{:S(2)}) async-start(bf16[256,4,384]{0,2,1:T(8,128)(2,1)} %get-tuple-element.33), calls=%async_computation | async-start | bytes 1572864 | tf_op jit(solution)/shard_map/all_to_all | solution.py:187
  118.1 63.5 %all-gather.5.cloned.1.call-start = ((), (), s32[]{:S(2)}) async-start(), calls=%async_computation.6 | async-start | bytes 1966080 | tf_op jit(solution)/shard_map/all_gather | solution.py:190
  119.1 10.7 %collective-permute-start.8 = (bf16[2,128,768]{2,1,0:T(8,128)(2,1)}, bf16[2,128,768]{2,1,0:T(8,128)(2,1)}, u32[]{:S(2)}, u32[]{:S(2)}) collective-permute-start(bf16[2,128,768]{2,1,0:T(8,128)(2,1)} %get-tuple-element.29), channel_id=1, source_target_pairs={{0,12},{4,0},{8,4},{12,8},{1,13},{5,1},{9,5},{13,9},{2,14},{6,2},{... | collective-permute-start | bytes 1179656 | tf_op jit(solution)/shard_map/ppermute | solution.py:217
  119.1 18.3 %collective-permute-start.7 = (bf16[2,128,768]{2,1,0:T(8,128)(2,1)}, bf16[2,128,768]{2,1,0:T(8,128)(2,1)}, u32[]{:S(2)}, u32[]{:S(2)}) collective-permute-start(bf16[2,128,768]{2,1,0:T(8,128)(2,1)} %get-tuple-element.30), channel_id=1, source_target_pairs={{0,8},{4,12},{8,0},{12,4},{1,9},{5,13},{9,1},{13,5},{2,10},{6,14},... | collective-permute-start | bytes 1179656 | tf_op jit(solution)/shard_map/ppermute | solution.py:217
  119.6 18.7 %collective-permute-start.6 = (bf16[2,128,768]{2,1,0:T(8,128)(2,1)S(1)}, bf16[2,128,768]{2,1,0:T(8,128)(2,1)}, u32[]{:S(2)}, u32[]{:S(2)}) collective-permute-start(bf16[2,128,768]{2,1,0:T(8,128)(2,1)S(1)} %get-tuple-element.31), channel_id=1, source_target_pairs={{0,4},{4,8},{8,12},{12,0},{1,5},{5,9},{9,13},{13,1},{2,6},{6,10},{... | collective-permute-start | bytes 1179656 | tf_op jit(solution)/shard_map/ppermute | solution.py:217
  138.3 24.5 %all-to-all-start.2 = ((bf16[256,4,384]{0,2,1:T(8,128)(2,1)}), bf16[256,4,384]{0,2,1:T(8,128)(2,1)S(1)}, u32[]{:S(2)}, u32[]{:S(2)}) async-start(bf16[256,4,384]{0,2,1:T(8,128)(2,1)} %bitcast.35), calls=%async_computation.2 | async-start | bytes 1572864 | tf_op jit(solution)/shard_map/all_to_all | solution.py:187
  162.8 23.1 %all-to-all-start.3 = ((bf16[4,256,384]{2,1,0:T(8,128)(2,1)}), bf16[4,256,384]{2,1,0:T(8,128)(2,1)S(1)}, u32[]{:S(2)}, u32[]{:S(2)}) async-start(bf16[4,256,384]{2,1,0:T(8,128)(2,1)} %bitcast.84), calls=%async_computation.3 | async-start | bytes 1572864 | tf_op jit(solution)/shard_map/all_to_all | solution.py:250
  185.8 23.1 %all-to-all-start.4 = ((bf16[4,256,384]{2,1,0:T(8,128)(2,1)}), bf16[4,256,384]{2,1,0:T(8,128)(2,1)S(1)}, u32[]{:S(2)}, u32[]{:S(2)}) async-start(bf16[4,256,384]{2,1,0:T(8,128)(2,1)} %bitcast.83), calls=%async_computation.4 | async-start | bytes 1572864 | tf_op jit(solution)/shard_map/all_to_all | solution.py:250
  (1 other events, 0.9 us)
Sparse Core Ops, SparseCore 0:
  53.6 47.3 all-gather.2
  129.9 21.1 all-gather.4

commit v23 on v22

--- a/solution.py
+++ b/solution.py
@@ -14,6 +14,7 @@
 SCALE = HD ** (-0.5)
 DRAFT_ROWS = 128
 PAIR = 4
+SPLITS = 3
 EXP2_SCALE = SCALE * 1.4426950408889634
 
 
@@ -109,9 +110,14 @@
     return jnp.where(token // POOL == draft, POOL ** (-0.5), 0.0).astype(jnp.bfloat16)
 
 
-def draft_kernel(split, qa_ref, qb_ref, k_ref, v_ref, o_ref):
+def draft_kernel(bounds, *refs):
+    q_refs = refs[:len(bounds)]
+    k_ref, v_ref, o_ref = refs[len(bounds):]
+    head = pl.program_id(0)
+    chosen = q_refs[-1][...]
+    for bound, q_ref in zip(bounds[-2::-1], q_refs[-2::-1]):
+        chosen = jnp.where(head < bound, q_ref[...], chosen)
     pooling = pooling_matrix(o_ref.shape[0])
-    chosen = jnp.where(pl.program_id(0) < split, qa_ref[...], qb_ref[...])
     pooled = jnp.dot(pooling, chosen, preferred_element_type=jnp.float32).astype(jnp.bfloat16)
     raw = lax.dot_general(
         pooled, k_ref[...], (((1,), (1,)), ((), ())), preferred_element_type=jnp.float32
@@ -123,35 +129,42 @@
     o_ref[...] = (weighted / totals).astype(o_ref.dtype)
 
 
-def draft_attention(leading, trailing, keys, values):
-    token_rows = leading.shape[0]
-    split = leading.shape[1] // HD
-    later = trailing.shape[1] // HD
+def draft_attention(parts, keys, values):
+    token_rows = parts[0].shape[0]
     rows = token_rows // POOL
     width = keys.shape[1]
     heads = width // HD
     key_rows = keys.shape[0]
     tile = min(DRAFT_ROWS, rows)
+    bounds = []
+    q_specs = []
+    lo = 0
+    for part in parts:
+        n = part.shape[1] // HD
+        q_specs.append(
+            pl.BlockSpec(
+                (tile * POOL, HD),
+                functools.partial(lambda base, size, h, r: (r, jnp.clip(h - base, 0, size - 1)), lo, n),
+            )
+        )
+        lo += n
+        bounds.append(lo)
     cost = pl.CostEstimate(
         flops=4 * rows * key_rows * HD * heads + 2 * rows * tile * POOL * HD * heads,
         transcendentals=rows * key_rows * heads,
         bytes_accessed=2 * HD * heads * (2 * token_rows + rows + 2 * key_rows),
     )
     return pl.pallas_call(
-        functools.partial(draft_kernel, split),
+        functools.partial(draft_kernel, tuple(bounds)),
         out_shape=jax.ShapeDtypeStruct((rows, width), jnp.bfloat16),
         cost_estimate=cost,
         grid=(heads, rows // tile),
-        in_specs=[
-            pl.BlockSpec((tile * POOL, HD), lambda h, r: (r, jnp.minimum(h, split - 1))),
-            pl.BlockSpec(
-                (tile * POOL, HD), lambda h, r: (r, jnp.clip(h - split, 0, later - 1))
-            ),
+        in_specs=q_specs + [
             pl.BlockSpec((key_rows, HD), lambda h, r: (0, h)),
             pl.BlockSpec((key_rows, HD), lambda h, r: (0, h)),
         ],
         out_specs=pl.BlockSpec((tile, HD), lambda h, r: (r, h)),
-    )(leading, trailing, keys, values)
+    )(*parts, keys, values)
 
 
 def head_permutes(matrix):
@@ -176,8 +189,9 @@
     seq_rows, width = key_rows.shape
     head_count = lax.axis_size("head")
     heads = width // HD
-    first = max(1, heads // 2)
-    spans = [(lo, n) for lo, n in ((0, first), (first, heads - first)) if n > 0]
+    piece_count = min(SPLITS, heads)
+    edges = [heads * k // piece_count for k in range(piece_count + 1)]
+    spans = [(edges[k], edges[k + 1] - edges[k]) for k in range(piece_count)]
     grouped_q = query_in.reshape(query_in.shape[0], head_count, width)
     query_slices = [
         grouped_q[:, :, lo * HD:(lo + n) * HD].reshape(query_in.shape[0], -1) for lo, n in spans
@@ -250,7 +264,7 @@
         back = lax.all_to_all(rows_part, "head", split_axis=0, concat_axis=1, tiled=True)
         pieces.append(back.reshape(back.shape[0], -1, count * HD))
     sparse_out = jnp.concatenate(pieces, axis=2).reshape(pieces[0].shape[0], -1)
-    draft_out = draft_attention(query_parts[0], query_parts[-1], draft_keys, draft_values)
+    draft_out = draft_attention(query_parts, draft_keys, draft_values)
     return (draft_out, sparse_out)
 
 

time: 218 us -> 237 us (1.087)
  starting transfers between devices: 30 us -> 38 us
  waiting for transfers between devices: 77.2 us -> 82.4 us
  Pallas kernels: 40.6 us -> 43.8 us
    ppermute x6, waiting for transfers between devices: 27.6 us -> 37.2 us  [exchange(): lax.ppermute(parcel, 'seq', [(i, (i + shift) % seq_count) for i in range(...]
    all_to_all x2 -> x3, waiting for transfers between devices: 11.4 us -> 5.83 us  [on_device(): lax.all_to_all(rows_part, 'head', split_axis=0, concat_axis=1, tiled=True)]
    all_to_all x2 -> x3, starting transfers between devices: 6.99 us -> 11.3 us  [on_device(): lax.all_to_all(rows_part, 'head', split_axis=0, concat_axis=1, tiled=True)]
    all_to_all x2 -> x3, starting transfers between devices: 9.68 us -> 13.2 us  [query_a2a(): lax.all_to_all(piece, 'head', split_axis=1, concat_axis=0, tiled=True)]
    pallas_call x2 -> x3, Pallas kernels: 28.2 us -> 31 us  [sparse_attention(): pl.pallas_call(sparse_kernel, out_shape=jax.ShapeDtypeStruct((rows, heads...]
  transfers between devices with their start and end apart: 16 -> 18, of which waited for: 9 -> 12; matrix products, arithmetic and copies ran while one was open for 23% -> 22% of each run, Pallas kernels for 19% -> 19%
where the time goes in v23:
time: 237 us; the launch traced here: 236 us
  waiting for transfers between devices  82.4 us (35%)
  Pallas kernels  43.8 us (18%)
  starting transfers between devices  38 us (16%)
  local copies, waits for them, and re-layouts  34.2 us (14%)
  other arithmetic  22.9 us (10%)
  between operations  14.4 us (6%)
    ppermute x6, waiting for transfers between devices, exchange(): lax.ppermute(parcel, 'seq', [(i, (i + shift) % seq_count) for i in range(...  37.2 us
    pallas_call x3, Pallas kernels, sparse_attention(): pl.pallas_call(sparse_kernel, out_shape=jax.ShapeDtypeStruct((rows, heads...  31 us
    all_to_all x1, waiting for transfers between devices, on_device(): lax.all_to_all(value_in, 'head', split_axis=1, concat_axis=0, tiled=True)  26.1 us
    all_to_all x3, starting transfers between devices, query_a2a(): lax.all_to_all(piece, 'head', split_axis=1, concat_axis=0, tiled=True)  13.2 us
    pallas_call x1, Pallas kernels, draft_attention(): pl.pallas_call(functools.partial(draft_kernel, tuple(bounds)), out_shape=...  12.8 us
    all_to_all x3, starting transfers between devices, on_device(): lax.all_to_all(rows_part, 'head', split_axis=0, concat_axis=1, tiled=True)  11.3 us
    ppermute x3, waiting for transfers between devices, head_permutes(): lax.ppermute(piece, 'head', [(i, (i + shift) % count) for i in range(coun...  8.01 us
    ppermute x3, starting transfers between devices, head_permutes(): lax.ppermute(piece, 'head', [(i, (i + shift) % count) for i in range(coun...  6.96 us
  transfers between devices with their start and end apart: 18, of which 12 were waited for; matrix products, arithmetic and copies ran while one was open for 22% of the time, Pallas kernels for 19%

profile of v23, /device:TPU:0, one launch (start us, length us, event | category | flops | bytes accessed | tf_op | source)
XLA Modules:
  0.0 235.6 jit_solution(1624821690138624835)
XLA Ops:
  10.7 3.0 %collective-permute-start = (bf16[256,768]{1,0:T(8,128)(2,1)}, bf16[256,768]{1,0:T(8,128)(2,1)}, u32[]{:S(2)}, u32[]{:S(2)}) collective-permute-start(bf16[256,768]{1,0:T(8,128)(2,1)} %bitcast.5), channel_id=1, source_target_pairs={{0,1},{1,2},{2,3},{3,0},{4,5},{5,6},{6,7},{7,4},{8,9},{9,10},{10,1... | collective-permute-start | bytes 1179656 | tf_op jit(solution)/shard_map/ppermute | solution.py:179
  20.8 3.7 %all-to-all-start.1 = ((bf16[256,4,768]{2,0,1:T(8,128)(2,1)}), bf16[256,4,768]{2,0,1:T(8,128)(2,1)S(1)}, u32[]{:S(2)}, u32[]{:S(2)}) async-start(bf16[256,4,768]{2,0,1:T(8,128)(2,1)} %bitcast.69), calls=%async_computation.1 | async-start | bytes 3145728 | tf_op jit(solution)/shard_map/all_to_all | solution.py:188
  35.1 8.0 %collective-permute-done.1 = bf16[256,768]{1,0:T(8,128)(2,1)} collective-permute-done((bf16[256,768]{1,0:T(8,128)(2,1)}, bf16[256,768]{1,0:T(8,128)(2,1)}, u32[]{:S(2)}, u32[]{:S(2)}) %collective-permute-start.1) | collective-permute-done | bytes 393248 | tf_op jit(solution)/shard_map/ppermute | solution.py:179
  49.0 3.6 %convert_reduce_fusion = f32[256,768]{1,0:T(8,128)S(1)} fusion(bf16[256,4,768]{2,1,0:T(4,128)(2,1)} %gather.20, pred[256]{0:T(512)(128)(4,1)S(1)} %copy-done.10), kind=kLoop, calls=%fused_computation.4 | loop fusion | flops 2162688 | bytes 2359552 | tf_op jit(solution)/shard_map/reduce_sum | solution.py:23
  54.8 3.2 %gather_fusion.2 = bf16[8,128,768]{2,1,0:T(8,128)(2,1)} fusion(bf16[8,128,768]{2,1,0:T(8,128)(2,1)} %broadcast_select_fusion.2, s32[1024]{0:T(1024)S(1)} %pad_clamp_fusion), kind=kCustom, calls=%fused_computation.clone | custom fusion | bytes 3145760 | tf_op jit(solution)/shard_map/jit(_take)/gather | solution.py:223
  58.0 26.1 %all-to-all-done.1 = bf16[256,4,768]{2,0,1:T(8,128)(2,1)S(1)} async-done(((bf16[256,4,768]{2,0,1:T(8,128)(2,1)}), bf16[256,4,768]{2,0,1:T(8,128)(2,1)S(1)}, u32[]{:S(2)}, u32[]{:S(2)}) %all-to-all-start.1) | async-done | bytes 1572896 | tf_op jit(solution)/shard_map/all_to_all | solution.py:188
  85.9 3.4 %broadcast_select_fusion = (bf16[8,128,768]{2,1,0:T(8,128)(2,1)}, bf16[8,128,768]{2,1,0:T(8,128)(2,1)S(1)}) fusion(bf16[8,128,768]{2,1,0:T(8,128)(2,1)} %gather_fusion.3, pred[8]{0:T(512)(128)(4,1)S(1)} %copy-done.9, bf16[8,128,768]{2,1,0:T(8,128)(2,1)} %gather_fusion.2), kind=kLoop, calls=%fused_computation.10 | loop fusion | flops 1572864 | bytes 6291464 | tf_op jit(solution)/shard_map/jit(_take)/select_n | solution.py:223
  94.4 8.5 %collective-permute-done.5 = bf16[2,128,768]{2,1,0:T(8,128)(2,1)S(1)} collective-permute-done((bf16[2,128,768]{2,1,0:T(8,128)(2,1)}, bf16[2,128,768]{2,1,0:T(8,128)(2,1)S(1)}, u32[]{:S(2)}, u32[]{:S(2)}) %collective-permute-start.5) | collective-permute-done | bytes 393248 | tf_op jit(solution)/shard_map/ppermute | solution.py:231
  102.9 10.5 %collective-permute-done.4 = bf16[2,128,768]{2,1,0:T(8,128)(2,1)} collective-permute-done((bf16[2,128,768]{2,1,0:T(8,128)(2,1)}, bf16[2,128,768]{2,1,0:T(8,128)(2,1)}, u32[]{:S(2)}, u32[]{:S(2)}) %collective-permute-start.4) | collective-permute-done | bytes 393248 | tf_op jit(solution)/shard_map/ppermute | solution.py:231
  113.4 4.6 %all-to-all-start = ((bf16[256,4,256]{0,2,1:T(8,128)(2,1)}), bf16[256,4,256]{0,2,1:T(8,128)(2,1)S(1)}, u32[]{:S(2)}, u32[]{:S(2)}) async-start(bf16[256,4,256]{0,2,1:T(8,128)(2,1)} %get-tuple-element.36), calls=%async_computation | async-start | bytes 1048576 | tf_op jit(solution)/shard_map/all_to_all | solution.py:201
  120.2 8.6 %collective-permute-done.8 = bf16[2,128,768]{2,1,0:T(8,128)(2,1)S(1)} collective-permute-done((bf16[2,128,768]{2,1,0:T(8,128)(2,1)S(1)}, bf16[2,128,768]{2,1,0:T(8,128)(2,1)S(1)}, u32[]{:S(2)}, u32[]{:S(2)}) %collective-permute-start.8) | collective-permute-done | bytes 393248 | tf_op jit(solution)/shard_map/ppermute | solution.py:231
  128.8 8.5 %collective-permute-done.7 = bf16[2,128,768]{2,1,0:T(8,128)(2,1)S(1)} collective-permute-done((bf16[2,128,768]{2,1,0:T(8,128)(2,1)S(1)}, bf16[2,128,768]{2,1,0:T(8,128)(2,1)S(1)}, u32[]{:S(2)}, u32[]{:S(2)}) %collective-permute-start.7) | collective-permute-done | bytes 393248 | tf_op jit(solution)/shard_map/ppermute | solution.py:231
  138.4 5.1 %all-to-all-start.2 = ((bf16[256,4,256]{0,2,1:T(8,128)(2,1)}), bf16[256,4,256]{0,2,1:T(8,128)(2,1)}, u32[]{:S(2)}, u32[]{:S(2)}) async-start(bf16[256,4,256]{0,2,1:T(8,128)(2,1)} %get-tuple-element.35), calls=%async_computation.2 | async-start | bytes 1048576 | tf_op jit(solution)/shard_map/all_to_all | solution.py:201
  145.4 3.1 %reshape.182 = f32[256,4,768]{2,1,0:T(4,128)S(1)} reshape(f32[4,256,768]{2,1,0:T(8,128)} %bitcast_convert_fusion) | data formatting | bytes 6291456 | tf_op jit(solution)/shard_map/convert_element_type | solution.py:22
  148.5 3.0 %reduce_sum.29 = f32[256,768]{1,0:T(8,128)} reduce(f32[256,4,768]{2,1,0:T(4,128)S(1)} %reshape.182, f32[]{:T(128)} %constant.170.clone.1), dimensions={1}, to_apply=%region_5.7 | reduce | flops 589824 | bytes 3932164 | tf_op jit(solution)/shard_map/reduce_sum | solution.py:23
  153.4 4.0 %all-to-all-done.2 = bf16[256,4,256]{0,2,1:T(8,128)(2,1)} async-done(((bf16[256,4,256]{0,2,1:T(8,128)(2,1)}), bf16[256,4,256]{0,2,1:T(8,128)(2,1)}, u32[]{:S(2)}, u32[]{:S(2)}) %all-to-all-start.2) | async-done | bytes 524320 | tf_op jit(solution)/shard_map/all_to_all | solution.py:201
  157.4 3.5 %all-to-all-start.3 = ((bf16[256,4,256]{0,2,1:T(8,128)(2,1)}), bf16[256,4,256]{0,2,1:T(8,128)(2,1)S(1)}, u32[]{:S(2)}, u32[]{:S(2)}) async-start(bf16[256,4,256]{0,2,1:T(8,128)(2,1)} %get-tuple-element.34), calls=%async_computation.3 | async-start | bytes 1048576 | tf_op jit(solution)/shard_map/all_to_all | solution.py:201
  163.7 10.4 %shard_map.62 = bf16[1024,256]{1,0:T(8,128)(2,1)} custom-call(s32[96]{0:T(128)} %reshape.173.tbl_ref, bf16[1024,256]{1,0:T(8,128)(2,1)} %bitcast.80, bf16[1024,768]{1,0:T(8,128)(2,1)} %bitcast_select_fusion.refs_0_, bf16[1024,768]{1,0:T(8,128)(2,1)} %bitcast.72, bf16[256,768]{1,0:T(8,128)(2,1)} %bitcast.15.refs_2_, bf16[256,768]{1,0:T(8,128)(2,1)} %bitcast.17.refs_3_, ...), custom_call_target="tpu_custom_call" | custom-call | flops 1610612736 | bytes 2883584 | tf_op jit(solution)/shard_map/pallas_call | solution.py:89
  174.8 4.3 %all-to-all-start.5 = ((bf16[4,256,256]{2,1,0:T(8,128)(2,1)}), bf16[4,256,256]{2,1,0:T(8,128)(2,1)S(1)}, u32[]{:S(2)}, u32[]{:S(2)}) async-start(bf16[4,256,256]{2,1,0:T(8,128)(2,1)} %bitcast.105), calls=%async_computation.5 | async-start | bytes 1048576 | tf_op jit(solution)/shard_map/all_to_all | solution.py:264
  180.2 10.3 %shard_map.61 = bf16[1024,256]{1,0:T(8,128)(2,1)} custom-call(s32[96]{0:T(128)} %reshape.173.tbl_ref, bf16[1024,256]{1,0:T(8,128)(2,1)} %bitcast.82, bf16[1024,768]{1,0:T(8,128)(2,1)} %bitcast_select_fusion.refs_0_, bf16[1024,768]{1,0:T(8,128)(2,1)} %bitcast.73, bf16[256,768]{1,0:T(8,128)(2,1)} %bitcast.15.refs_2_, bf16[256,768]{1,0:T(8,128)(2,1)} %bitcast.17.refs_3_, ...), custom_call_target="tpu_custom_call" | custom-call | flops 1610612736 | bytes 2883584 | tf_op jit(solution)/shard_map/pallas_call | solution.py:89
  192.6 3.5 %all-to-all-start.4 = ((bf16[4,256,256]{2,1,0:T(8,128)(2,1)}), bf16[4,256,256]{2,1,0:T(8,128)(2,1)S(1)}, u32[]{:S(2)}, u32[]{:S(2)}) async-start(bf16[4,256,256]{2,1,0:T(8,128)(2,1)} %bitcast.104), calls=%async_computation.4 | async-start | bytes 1048576 | tf_op jit(solution)/shard_map/all_to_all | solution.py:264
  197.1 10.2 %shard_map.59 = bf16[1024,256]{1,0:T(8,128)(2,1)} custom-call(s32[96]{0:T(128)} %reshape.173.tbl_ref, bf16[1024,256]{1,0:T(8,128)(2,1)} %bitcast.84, bf16[1024,768]{1,0:T(8,128)(2,1)} %bitcast_select_fusion.refs_0_, bf16[1024,768]{1,0:T(8,128)(2,1)} %bitcast.74, bf16[256,768]{1,0:T(8,128)(2,1)} %bitcast.15.refs_2_, bf16[256,768]{1,0:T(8,128)(2,1)} %bitcast.17.refs_3_, ...), custom_call_target="tpu_custom_call" | custom-call | flops 1610612736 | bytes 2883584 | tf_op jit(solution)/shard_map/pallas_call | solution.py:89
  209.9 3.5 %all-to-all-start.6 = ((bf16[4,256,256]{2,1,0:T(8,128)(2,1)}), bf16[4,256,256]{2,1,0:T(8,128)(2,1)S(1)}, u32[]{:S(2)}, u32[]{:S(2)}) async-start(bf16[4,256,256]{2,1,0:T(8,128)(2,1)} %bitcast.103), calls=%async_computation.6 | async-start | bytes 1048576 | tf_op jit(solution)/shard_map/all_to_all | solution.py:264
  213.4 12.8 %shard_map.60 = bf16[256,768]{1,0:T(8,128)(2,1)} custom-call(bf16[1024,256]{1,0:T(8,128)(2,1)} %bitcast.83, bf16[1024,256]{1,0:T(8,128)(2,1)} %bitcast.81, bf16[1024,256]{1,0:T(8,128)(2,1)} %bitcast.85, bf16[1024,768]{1,0:T(8,128)(2,1)} %all-gather.3.cloned.1.call-done.refs_3_, bf16[1024,768]{1,0:T(8,128)(2,1)} %all-gather.5.cloned.1.call-done.refs_4_), custom_call_target="tpu_custom_call" | custom-call | flops 1006632960 | bytes 6684672 | tf_op jit(solution)/shard_map/pallas_call | solution.py:157
  (110 shorter events, 55.8 us)
Async XLA Ops:
  9.8 9.7 %copy-start.7 = (bf16[256,3072]{1,0:T(8,128)(2,1)S(1)}, bf16[256,3072]{1,0:T(8,128)(2,1)}, u32[]{:S(2)}) copy-start(bf16[256,3072]{1,0:T(8,128)(2,1)} %param.8) | copy-start | bytes 4718596
  10.7 24.3 %collective-permute-start = (bf16[256,768]{1,0:T(8,128)(2,1)}, bf16[256,768]{1,0:T(8,128)(2,1)}, u32[]{:S(2)}, u32[]{:S(2)}) collective-permute-start(bf16[256,768]{1,0:T(8,128)(2,1)} %bitcast.5), channel_id=1, source_target_pairs={{0,1},{1,2},{2,3},{3,0},{4,5},{5,6},{6,7},{7,4},{8,9},{9,10},{10,1... | collective-permute-start | bytes 1179656 | tf_op jit(solution)/shard_map/ppermute | solution.py:179
  14.7 28.4 %collective-permute-start.1 = (bf16[256,768]{1,0:T(8,128)(2,1)}, bf16[256,768]{1,0:T(8,128)(2,1)}, u32[]{:S(2)}, u32[]{:S(2)}) collective-permute-start(bf16[256,768]{1,0:T(8,128)(2,1)} %bitcast.7), channel_id=1, source_target_pairs={{0,2},{1,3},{2,0},{3,1},{4,6},{5,7},{6,4},{7,5},{8,10},{9,11},{10,... | collective-permute-start | bytes 1179656 | tf_op jit(solution)/shard_map/ppermute | solution.py:179
  18.2 24.9 %collective-permute-start.2 = (bf16[256,768]{1,0:T(8,128)(2,1)}, bf16[256,768]{1,0:T(8,128)(2,1)}, u32[]{:S(2)}, u32[]{:S(2)}) collective-permute-start(bf16[256,768]{1,0:T(8,128)(2,1)} %bitcast.9), channel_id=1, source_target_pairs={{0,3},{1,0},{2,1},{3,2},{4,7},{5,4},{6,5},{7,6},{8,11},{9,8},{10,9... | collective-permute-start | bytes 1179656 | tf_op jit(solution)/shard_map/ppermute | solution.py:179
  20.8 63.3 %all-to-all-start.1 = ((bf16[256,4,768]{2,0,1:T(8,128)(2,1)}), bf16[256,4,768]{2,0,1:T(8,128)(2,1)S(1)}, u32[]{:S(2)}, u32[]{:S(2)}) async-start(bf16[256,4,768]{2,0,1:T(8,128)(2,1)} %bitcast.69), calls=%async_computation.1 | async-start | bytes 3145728 | tf_op jit(solution)/shard_map/all_to_all | solution.py:188
  24.5 182.8 %all-gather.3.cloned.1.call-start = ((), (), s32[]{:S(2)}) async-start(), calls=%async_computation.7 | async-start | bytes 1966080 | tf_op jit(solution)/shard_map/all_gather | solution.py:203
  84.2 59.3 %copy-start = (bf16[256,4,768]{2,0,1:T(8,128)(2,1)}, bf16[256,4,768]{2,0,1:T(8,128)(2,1)S(1)}, u32[]{:S(2)}) copy-start(bf16[256,4,768]{2,0,1:T(8,128)(2,1)S(1)} %all-to-all-done.1) | copy-start | bytes 4718596
  90.4 12.5 %collective-permute-start.5 = (bf16[2,128,768]{2,1,0:T(8,128)(2,1)}, bf16[2,128,768]{2,1,0:T(8,128)(2,1)S(1)}, u32[]{:S(2)}, u32[]{:S(2)}) collective-permute-start(bf16[2,128,768]{2,1,0:T(8,128)(2,1)} %get-tuple-element.37), channel_id=1, source_target_pairs={{0,12},{4,0},{8,4},{12,8},{1,13},{5,1},{9,5},{13,9},{2,14},{6,2},{... | collective-permute-start | bytes 1179656 | tf_op jit(solution)/shard_map/ppermute | solution.py:231
  91.7 21.7 %collective-permute-start.4 = (bf16[2,128,768]{2,1,0:T(8,128)(2,1)}, bf16[2,128,768]{2,1,0:T(8,128)(2,1)}, u32[]{:S(2)}, u32[]{:S(2)}) collective-permute-start(bf16[2,128,768]{2,1,0:T(8,128)(2,1)} %get-tuple-element.38), channel_id=1, source_target_pairs={{0,8},{4,12},{8,0},{12,4},{1,9},{5,13},{9,1},{13,5},{2,10},{6,14},... | collective-permute-start | bytes 1179656 | tf_op jit(solution)/shard_map/ppermute | solution.py:231
  92.1 21.3 %collective-permute-start.3 = (bf16[2,128,768]{2,1,0:T(8,128)(2,1)}, bf16[2,128,768]{2,1,0:T(8,128)(2,1)}, u32[]{:S(2)}, u32[]{:S(2)}) collective-permute-start(bf16[2,128,768]{2,1,0:T(8,128)(2,1)} %get-tuple-element.39), channel_id=1, source_target_pairs={{0,4},{4,8},{8,12},{12,0},{1,5},{5,9},{9,13},{13,1},{2,6},{6,10},{... | collective-permute-start | bytes 1179656 | tf_op jit(solution)/shard_map/ppermute | solution.py:231
  102.9 16.4 %copy-start.1 = (bf16[2,128,768]{2,1,0:T(8,128)(2,1)}, bf16[2,128,768]{2,1,0:T(8,128)(2,1)S(1)}, u32[]{:S(2)}) copy-start(bf16[2,128,768]{2,1,0:T(8,128)(2,1)S(1)} %collective-permute-done.5) | copy-start | bytes 1179652
  113.4 24.9 %all-to-all-start = ((bf16[256,4,256]{0,2,1:T(8,128)(2,1)}), bf16[256,4,256]{0,2,1:T(8,128)(2,1)S(1)}, u32[]{:S(2)}, u32[]{:S(2)}) async-start(bf16[256,4,256]{0,2,1:T(8,128)(2,1)} %get-tuple-element.36), calls=%async_computation | async-start | bytes 1048576 | tf_op jit(solution)/shard_map/all_to_all | solution.py:201
  119.4 9.5 %collective-permute-start.8 = (bf16[2,128,768]{2,1,0:T(8,128)(2,1)S(1)}, bf16[2,128,768]{2,1,0:T(8,128)(2,1)S(1)}, u32[]{:S(2)}, u32[]{:S(2)}) collective-permute-start(bf16[2,128,768]{2,1,0:T(8,128)(2,1)S(1)} %get-tuple-element.31), channel_id=1, source_target_pairs={{0,12},{4,0},{8,4},{12,8},{1,13},{5,1},{9,5},{13,9},{2,14},{6,2},{... | collective-permute-start | bytes 1179656 | tf_op jit(solution)/shard_map/ppermute | solution.py:231
  119.4 17.9 %collective-permute-start.7 = (bf16[2,128,768]{2,1,0:T(8,128)(2,1)S(1)}, bf16[2,128,768]{2,1,0:T(8,128)(2,1)S(1)}, u32[]{:S(2)}, u32[]{:S(2)}) collective-permute-start(bf16[2,128,768]{2,1,0:T(8,128)(2,1)S(1)} %get-tuple-element.32), channel_id=1, source_target_pairs={{0,8},{4,12},{8,0},{12,4},{1,9},{5,13},{9,1},{13,5},{2,10},{6,14},... | collective-permute-start | bytes 1179656 | tf_op jit(solution)/shard_map/ppermute | solution.py:231
  120.1 18.3 %collective-permute-start.6 = (bf16[2,128,768]{2,1,0:T(8,128)(2,1)S(1)}, bf16[2,128,768]{2,1,0:T(8,128)(2,1)S(1)}, u32[]{:S(2)}, u32[]{:S(2)}) collective-permute-start(bf16[2,128,768]{2,1,0:T(8,128)(2,1)S(1)} %get-tuple-element.33), channel_id=1, source_target_pairs={{0,4},{4,8},{8,12},{12,0},{1,5},{5,9},{9,13},{13,1},{2,6},{6,10},{... | collective-permute-start | bytes 1179656 | tf_op jit(solution)/shard_map/ppermute | solution.py:231
  128.8 16.6 %copy-start.2 = (bf16[2,128,768]{2,1,0:T(8,128)(2,1)}, bf16[2,128,768]{2,1,0:T(8,128)(2,1)S(1)}, u32[]{:S(2)}) copy-start(bf16[2,128,768]{2,1,0:T(8,128)(2,1)S(1)} %collective-permute-done.8) | copy-start | bytes 1179652
  137.3 6.1 %copy-start.3 = (bf16[2,128,768]{2,1,0:T(8,128)(2,1)}, bf16[2,128,768]{2,1,0:T(8,128)(2,1)S(1)}, u32[]{:S(2)}) copy-start(bf16[2,128,768]{2,1,0:T(8,128)(2,1)S(1)} %collective-permute-done.7) | copy-start | bytes 1179652
  138.4 19.0 %all-to-all-start.2 = ((bf16[256,4,256]{0,2,1:T(8,128)(2,1)}), bf16[256,4,256]{0,2,1:T(8,128)(2,1)}, u32[]{:S(2)}, u32[]{:S(2)}) async-start(bf16[256,4,256]{0,2,1:T(8,128)(2,1)} %get-tuple-element.35), calls=%async_computation.2 | async-start | bytes 1048576 | tf_op jit(solution)/shard_map/all_to_all | solution.py:201
  157.4 17.4 %all-to-all-start.3 = ((bf16[256,4,256]{0,2,1:T(8,128)(2,1)}), bf16[256,4,256]{0,2,1:T(8,128)(2,1)S(1)}, u32[]{:S(2)}, u32[]{:S(2)}) async-start(bf16[256,4,256]{0,2,1:T(8,128)(2,1)} %get-tuple-element.34), calls=%async_computation.3 | async-start | bytes 1048576 | tf_op jit(solution)/shard_map/all_to_all | solution.py:201
  160.9 46.4 %all-gather.5.cloned.1.call-start = ((), (), s32[]{:S(2)}) async-start(), calls=%async_computation.8 | async-start | bytes 1966080 | tf_op jit(solution)/shard_map/all_gather | solution.py:204
  163.7 15.5 %copy-start.6 = (bf16[256,4,256]{0,2,1:T(8,128)(2,1)S(1)}, bf16[256,4,256]{0,2,1:T(8,128)(2,1)}, u32[]{:S(2)}) copy-start(bf16[256,4,256]{0,2,1:T(8,128)(2,1)} %copy-done.5) | copy-start | bytes 1572868
  174.8 17.7 %all-to-all-start.5 = ((bf16[4,256,256]{2,1,0:T(8,128)(2,1)}), bf16[4,256,256]{2,1,0:T(8,128)(2,1)S(1)}, u32[]{:S(2)}, u32[]{:S(2)}) async-start(bf16[4,256,256]{2,1,0:T(8,128)(2,1)} %bitcast.105), calls=%async_computation.5 | async-start | bytes 1048576 | tf_op jit(solution)/shard_map/all_to_all | solution.py:264
  192.6 17.4 %all-to-all-start.4 = ((bf16[4,256,256]{2,1,0:T(8,128)(2,1)}), bf16[4,256,256]{2,1,0:T(8,128)(2,1)S(1)}, u32[]{:S(2)}, u32[]{:S(2)}) async-start(bf16[4,256,256]{2,1,0:T(8,128)(2,1)} %bitcast.104), calls=%async_computation.4 | async-start | bytes 1048576 | tf_op jit(solution)/shard_map/all_to_all | solution.py:264
  209.9 17.4 %all-to-all-start.6 = ((bf16[4,256,256]{2,1,0:T(8,128)(2,1)}), bf16[4,256,256]{2,1,0:T(8,128)(2,1)S(1)}, u32[]{:S(2)}, u32[]{:S(2)}) async-start(bf16[4,256,256]{2,1,0:T(8,128)(2,1)} %bitcast.103), calls=%async_computation.6 | async-start | bytes 1048576 | tf_op jit(solution)/shard_map/all_to_all | solution.py:264
  (8 other events, 25.3 us)
Sparse Core Ops, SparseCore 0:
  53.6 47.3 all-gather.2
  163.3 20.1 all-gather.4

commit v24 on v22

--- a/solution.py
+++ b/solution.py
@@ -13,7 +13,7 @@
 CAP = 2
 SCALE = HD ** (-0.5)
 DRAFT_ROWS = 128
-PAIR = 4
+PAIR = 8
 EXP2_SCALE = SCALE * 1.4426950408889634
 
 

time: 218 us -> 218 us (level)
  transfers between devices with their start and end apart: 16 -> 16, of which waited for: 9 -> 9; matrix products, arithmetic and copies ran while one was open for 23% -> 23% of each run, Pallas kernels for 19% -> 18%
where the time goes in v24:
time: 218 us; the launch traced here: 217 us
  waiting for transfers between devices  78.8 us (36%)
  Pallas kernels  39 us (18%)
  local copies, waits for them, and re-layouts  33.4 us (15%)
  starting transfers between devices  30 us (14%)
  other arithmetic  21.7 us (10%)
  between operations  14.4 us (7%)
    ppermute x6, waiting for transfers between devices, exchange(): lax.ppermute(parcel, 'seq', [(i, (i + shift) % seq_count) for i in range(...  27.6 us
    pallas_call x2, Pallas kernels, sparse_attention(): pl.pallas_call(sparse_kernel, out_shape=jax.ShapeDtypeStruct((rows, heads...  26.6 us
    all_to_all x1, waiting for transfers between devices, on_device(): lax.all_to_all(value_in, 'head', split_axis=1, concat_axis=0, tiled=True)  26.1 us
    pallas_call x1, Pallas kernels, draft_attention(): pl.pallas_call(functools.partial(draft_kernel, split), out_shape=jax.Shap...  12.4 us
    all_to_all x2, waiting for transfers between devices, on_device(): lax.all_to_all(rows_part, 'head', split_axis=0, concat_axis=1, tiled=True)  12.2 us
    all_to_all x2, starting transfers between devices, query_a2a(): lax.all_to_all(piece, 'head', split_axis=1, concat_axis=0, tiled=True)  9.68 us
    ppermute x3, waiting for transfers between devices, head_permutes(): lax.ppermute(piece, 'head', [(i, (i + shift) % count) for i in range(coun...  9.01 us
    all_to_all x2, starting transfers between devices, on_device(): lax.all_to_all(rows_part, 'head', split_axis=0, concat_axis=1, tiled=True)  6.99 us
  transfers between devices with their start and end apart: 16, of which 9 were waited for; matrix products, arithmetic and copies ran while one was open for 23% of the time, Pallas kernels for 18%

profile of v24, /device:TPU:0, one launch (start us, length us, event | category | flops | bytes accessed | tf_op | source)
XLA Modules:
  0.0 217.2 jit_solution(14315059816140306768)
XLA Ops:
  10.7 3.0 %collective-permute-start = (bf16[256,768]{1,0:T(8,128)(2,1)}, bf16[256,768]{1,0:T(8,128)(2,1)}, u32[]{:S(2)}, u32[]{:S(2)}) collective-permute-start(bf16[256,768]{1,0:T(8,128)(2,1)} %bitcast.5), channel_id=1, source_target_pairs={{0,1},{1,2},{2,3},{3,0},{4,5},{5,6},{6,7},{7,4},{8,9},{9,10},{10,1... | collective-permute-start | bytes 1179656 | tf_op jit(solution)/shard_map/ppermute | solution.py:166
  14.7 2.6 %collective-permute-start.1 = (bf16[256,768]{1,0:T(8,128)(2,1)}, bf16[256,768]{1,0:T(8,128)(2,1)}, u32[]{:S(2)}, u32[]{:S(2)}) collective-permute-start(bf16[256,768]{1,0:T(8,128)(2,1)} %bitcast.7), channel_id=1, source_target_pairs={{0,2},{1,3},{2,0},{3,1},{4,6},{5,7},{6,4},{7,5},{8,10},{9,11},{10,... | collective-permute-start | bytes 1179656 | tf_op jit(solution)/shard_map/ppermute | solution.py:166
  20.8 3.7 %all-to-all-start.1 = ((bf16[256,4,768]{2,0,1:T(8,128)(2,1)}), bf16[256,4,768]{2,0,1:T(8,128)(2,1)S(1)}, u32[]{:S(2)}, u32[]{:S(2)}) async-start(bf16[256,4,768]{2,0,1:T(8,128)(2,1)} %bitcast.63), calls=%async_computation.1 | async-start | bytes 3145728 | tf_op jit(solution)/shard_map/all_to_all | solution.py:175
  34.1 9.0 %collective-permute-done.1 = bf16[256,768]{1,0:T(8,128)(2,1)} collective-permute-done((bf16[256,768]{1,0:T(8,128)(2,1)}, bf16[256,768]{1,0:T(8,128)(2,1)}, u32[]{:S(2)}, u32[]{:S(2)}) %collective-permute-start.1) | collective-permute-done | bytes 393248 | tf_op jit(solution)/shard_map/ppermute | solution.py:166
  43.1 2.6 %pad_maximum_fusion = bf16[4,256,768]{2,1,0:T(8,128)(2,1)} fusion(bf16[1,256,768]{2,1,0:T(8,128)(2,1)} %bitcast.10, bf16[1,256,768]{2,1,0:T(8,128)(2,1)} %bitcast.8, bf16[1,256,768]{2,1,0:T(8,128)(2,1)} %bitcast.6, bf16[1,256,768]{2,1,0:T(8,128)(2,1)S(1)} %bitcast.82), kind=kLoop, calls=%fused_computation.6 | loop fusion | flops 2359296 | bytes 3145728 | tf_op jit(solution)/shard_map/stack | solution.py:168
  49.1 3.6 %convert_reduce_fusion = f32[256,768]{1,0:T(8,128)S(1)} fusion(bf16[256,4,768]{2,1,0:T(4,128)(2,1)} %gather.20, pred[256]{0:T(512)(128)(4,1)S(1)} %copy-done.4), kind=kLoop, calls=%fused_computation.4 | loop fusion | flops 2162688 | bytes 2359552 | tf_op jit(solution)/shard_map/reduce_sum | solution.py:22
  54.8 3.2 %gather_fusion.2 = bf16[8,128,768]{2,1,0:T(8,128)(2,1)} fusion(bf16[8,128,768]{2,1,0:T(8,128)(2,1)} %broadcast_select_fusion.2, s32[1024]{0:T(1024)S(1)} %pad_clamp_fusion), kind=kCustom, calls=%fused_computation.clone | custom fusion | bytes 3145760 | tf_op jit(solution)/shard_map/jit(_take)/gather | solution.py:209
  58.0 26.1 %all-to-all-done.1 = bf16[256,4,768]{2,0,1:T(8,128)(2,1)S(1)} async-done(((bf16[256,4,768]{2,0,1:T(8,128)(2,1)}), bf16[256,4,768]{2,0,1:T(8,128)(2,1)S(1)}, u32[]{:S(2)}, u32[]{:S(2)}) %all-to-all-start.1) | async-done | bytes 1572896 | tf_op jit(solution)/shard_map/all_to_all | solution.py:175
  86.0 3.4 %broadcast_select_fusion = (bf16[8,128,768]{2,1,0:T(8,128)(2,1)}, bf16[8,128,768]{2,1,0:T(8,128)(2,1)S(1)}) fusion(bf16[8,128,768]{2,1,0:T(8,128)(2,1)} %gather_fusion.3, pred[8]{0:T(512)(128)(4,1)S(1)} %copy-done.5, bf16[8,128,768]{2,1,0:T(8,128)(2,1)} %gather_fusion.2), kind=kLoop, calls=%fused_computation.10 | loop fusion | flops 1572864 | bytes 6291464 | tf_op jit(solution)/shard_map/jit(_take)/select_n | solution.py:209
  94.4 8.5 %collective-permute-done.5 = bf16[2,128,768]{2,1,0:T(8,128)(2,1)} collective-permute-done((bf16[2,128,768]{2,1,0:T(8,128)(2,1)}, bf16[2,128,768]{2,1,0:T(8,128)(2,1)}, u32[]{:S(2)}, u32[]{:S(2)}) %collective-permute-start.5) | collective-permute-done | bytes 393248 | tf_op jit(solution)/shard_map/ppermute | solution.py:217
  102.9 10.5 %collective-permute-done.4 = bf16[2,128,768]{2,1,0:T(8,128)(2,1)} collective-permute-done((bf16[2,128,768]{2,1,0:T(8,128)(2,1)}, bf16[2,128,768]{2,1,0:T(8,128)(2,1)}, u32[]{:S(2)}, u32[]{:S(2)}) %collective-permute-start.4) | collective-permute-done | bytes 393248 | tf_op jit(solution)/shard_map/ppermute | solution.py:217
  113.5 4.6 %all-to-all-start = ((bf16[256,4,384]{0,2,1:T(8,128)(2,1)}), bf16[256,4,384]{0,2,1:T(8,128)(2,1)}, u32[]{:S(2)}, u32[]{:S(2)}) async-start(bf16[256,4,384]{0,2,1:T(8,128)(2,1)} %get-tuple-element.33), calls=%async_computation | async-start | bytes 1572864 | tf_op jit(solution)/shard_map/all_to_all | solution.py:187
  121.8 3.1 %reshape.170 = f32[256,4,768]{2,1,0:T(4,128)S(1)} reshape(f32[4,256,768]{2,1,0:T(8,128)} %bitcast_convert_fusion) | data formatting | bytes 6291456 | tf_op jit(solution)/shard_map/convert_element_type | solution.py:21
  124.9 3.0 %reduce_sum.29 = f32[256,768]{1,0:T(8,128)} reduce(f32[256,4,768]{2,1,0:T(4,128)S(1)} %reshape.170, f32[]{:T(128)} %constant.170.clone.1), dimensions={1}, to_apply=%region_5.7 | reduce | flops 589824 | bytes 3932164 | tf_op jit(solution)/shard_map/reduce_sum | solution.py:22
  129.8 7.5 %collective-permute-done.7 = bf16[2,128,768]{2,1,0:T(8,128)(2,1)} collective-permute-done((bf16[2,128,768]{2,1,0:T(8,128)(2,1)}, bf16[2,128,768]{2,1,0:T(8,128)(2,1)}, u32[]{:S(2)}, u32[]{:S(2)}) %collective-permute-start.7) | collective-permute-done | bytes 393248 | tf_op jit(solution)/shard_map/ppermute | solution.py:217
  138.3 5.1 %all-to-all-start.2 = ((bf16[256,4,384]{0,2,1:T(8,128)(2,1)}), bf16[256,4,384]{0,2,1:T(8,128)(2,1)S(1)}, u32[]{:S(2)}, u32[]{:S(2)}) async-start(bf16[256,4,384]{0,2,1:T(8,128)(2,1)} %bitcast.35), calls=%async_computation.2 | async-start | bytes 1572864 | tf_op jit(solution)/shard_map/all_to_all | solution.py:187
  145.7 13.3 %shard_map.61 = bf16[1024,384]{1,0:T(8,128)(2,1)} custom-call(s32[96]{0:T(128)} %reshape.162.tbl_ref, bf16[1024,384]{1,0:T(8,128)(2,1)} %bitcast.73, bf16[1024,768]{1,0:T(8,128)(2,1)} %bitcast_select_fusion.refs_0_, bf16[1024,768]{1,0:T(8,128)(2,1)} %bitcast.67, bf16[256,768]{1,0:T(8,128)(2,1)} %bitcast.15.refs_2_, bf16[256,768]{1,0:T(8,128)(2,1)} %bitcast.17.refs_3_, ...), custom_call_target="tpu_custom_call" | custom-call | flops 2415919104 | bytes 4325376 | tf_op jit(solution)/shard_map/pallas_call | solution.py:88
  159.0 3.8 %all-to-all-done.2 = bf16[256,4,384]{0,2,1:T(8,128)(2,1)S(1)} async-done(((bf16[256,4,384]{0,2,1:T(8,128)(2,1)}), bf16[256,4,384]{0,2,1:T(8,128)(2,1)S(1)}, u32[]{:S(2)}, u32[]{:S(2)}) %all-to-all-start.2) | async-done | bytes 786464 | tf_op jit(solution)/shard_map/all_to_all | solution.py:187
  162.8 3.5 %all-to-all-start.3 = ((bf16[4,256,384]{2,1,0:T(8,128)(2,1)}), bf16[4,256,384]{2,1,0:T(8,128)(2,1)S(1)}, u32[]{:S(2)}, u32[]{:S(2)}) async-start(bf16[4,256,384]{2,1,0:T(8,128)(2,1)} %bitcast.84), calls=%async_computation.3 | async-start | bytes 1572864 | tf_op jit(solution)/shard_map/all_to_all | solution.py:250
  167.4 13.3 %shard_map.59 = bf16[1024,384]{1,0:T(8,128)(2,1)} custom-call(s32[96]{0:T(128)} %reshape.162.tbl_ref, bf16[1024,384]{1,0:T(8,128)(2,1)} %bitcast.75, bf16[1024,768]{1,0:T(8,128)(2,1)} %bitcast_select_fusion.refs_0_, bf16[1024,768]{1,0:T(8,128)(2,1)} %bitcast.68, bf16[256,768]{1,0:T(8,128)(2,1)} %bitcast.15.refs_2_, bf16[256,768]{1,0:T(8,128)(2,1)} %bitcast.17.refs_3_, ...), custom_call_target="tpu_custom_call" | custom-call | flops 2415919104 | bytes 4325376 | tf_op jit(solution)/shard_map/pallas_call | solution.py:88
  180.8 5.0 %all-to-all-done.3 = bf16[4,256,384]{2,1,0:T(8,128)(2,1)S(1)} async-done(((bf16[4,256,384]{2,1,0:T(8,128)(2,1)}), bf16[4,256,384]{2,1,0:T(8,128)(2,1)S(1)}, u32[]{:S(2)}, u32[]{:S(2)}) %all-to-all-start.3) | async-done | bytes 786464 | tf_op jit(solution)/shard_map/all_to_all | solution.py:250
  185.8 3.5 %all-to-all-start.4 = ((bf16[4,256,384]{2,1,0:T(8,128)(2,1)}), bf16[4,256,384]{2,1,0:T(8,128)(2,1)S(1)}, u32[]{:S(2)}, u32[]{:S(2)}) async-start(bf16[4,256,384]{2,1,0:T(8,128)(2,1)} %bitcast.83), calls=%async_computation.4 | async-start | bytes 1572864 | tf_op jit(solution)/shard_map/all_to_all | solution.py:250
  189.3 12.4 %shard_map.60 = bf16[256,768]{1,0:T(8,128)(2,1)} custom-call(bf16[1024,384]{1,0:T(8,128)(2,1)} %bitcast.74, bf16[1024,384]{1,0:T(8,128)(2,1)} %bitcast.76, bf16[1024,768]{1,0:T(8,128)(2,1)} %all-gather.3.cloned.1.call-done.k_ref, bf16[1024,768]{1,0:T(8,128)(2,1)} %all-gather.5.cloned.1.call-done.v_ref), custom_call_target="tpu_custom_call" | custom-call | flops 1006632960 | bytes 6684672 | tf_op jit(solution)/shard_map/pallas_call | solution.py:140
  201.7 7.2 %all-to-all-done.4 = bf16[4,256,384]{2,1,0:T(8,128)(2,1)S(1)} async-done(((bf16[4,256,384]{2,1,0:T(8,128)(2,1)}), bf16[4,256,384]{2,1,0:T(8,128)(2,1)S(1)}, u32[]{:S(2)}, u32[]{:S(2)}) %all-to-all-start.4) | async-done | bytes 786464 | tf_op jit(solution)/shard_map/all_to_all | solution.py:250
  (94 shorter events, 41.3 us)
Async XLA Ops:
  9.8 9.7 %copy-start.2 = (bf16[256,3072]{1,0:T(8,128)(2,1)S(1)}, bf16[256,3072]{1,0:T(8,128)(2,1)}, u32[]{:S(2)}) copy-start(bf16[256,3072]{1,0:T(8,128)(2,1)} %param.8) | copy-start | bytes 4718596
  10.7 23.3 %collective-permute-start = (bf16[256,768]{1,0:T(8,128)(2,1)}, bf16[256,768]{1,0:T(8,128)(2,1)}, u32[]{:S(2)}, u32[]{:S(2)}) collective-permute-start(bf16[256,768]{1,0:T(8,128)(2,1)} %bitcast.5), channel_id=1, source_target_pairs={{0,1},{1,2},{2,3},{3,0},{4,5},{5,6},{6,7},{7,4},{8,9},{9,10},{10,1... | collective-permute-start | bytes 1179656 | tf_op jit(solution)/shard_map/ppermute | solution.py:166
  14.7 28.4 %collective-permute-start.1 = (bf16[256,768]{1,0:T(8,128)(2,1)}, bf16[256,768]{1,0:T(8,128)(2,1)}, u32[]{:S(2)}, u32[]{:S(2)}) collective-permute-start(bf16[256,768]{1,0:T(8,128)(2,1)} %bitcast.7), channel_id=1, source_target_pairs={{0,2},{1,3},{2,0},{3,1},{4,6},{5,7},{6,4},{7,5},{8,10},{9,11},{10,... | collective-permute-start | bytes 1179656 | tf_op jit(solution)/shard_map/ppermute | solution.py:166
  18.2 24.9 %collective-permute-start.2 = (bf16[256,768]{1,0:T(8,128)(2,1)}, bf16[256,768]{1,0:T(8,128)(2,1)}, u32[]{:S(2)}, u32[]{:S(2)}) collective-permute-start(bf16[256,768]{1,0:T(8,128)(2,1)} %bitcast.9), channel_id=1, source_target_pairs={{0,3},{1,0},{2,1},{3,2},{4,7},{5,4},{6,5},{7,6},{8,11},{9,8},{10,9... | collective-permute-start | bytes 1179656 | tf_op jit(solution)/shard_map/ppermute | solution.py:166
  20.8 3.8 %copy-start.3 = (s32[32,12]{0,1:T(8,128)S(1)}, s32[32,12]{0,1:T(8,128)}, u32[]{:S(2)}) copy-start(s32[32,12]{0,1:T(8,128)} %param.9) | copy-start | bytes 4612
  20.8 63.4 %all-to-all-start.1 = ((bf16[256,4,768]{2,0,1:T(8,128)(2,1)}), bf16[256,4,768]{2,0,1:T(8,128)(2,1)S(1)}, u32[]{:S(2)}, u32[]{:S(2)}) async-start(bf16[256,4,768]{2,0,1:T(8,128)(2,1)} %bitcast.63), calls=%async_computation.1 | async-start | bytes 3145728 | tf_op jit(solution)/shard_map/all_to_all | solution.py:175
  24.5 156.3 %all-gather.3.cloned.1.call-start = ((), (), s32[]{:S(2)}) async-start(), calls=%async_computation.5 | async-start | bytes 1966080 | tf_op jit(solution)/shard_map/all_gather | solution.py:189
  47.7 1.4 copy-start.4
  49.1 4.4 %copy-start.6 = (pred[8]{0:T(512)(128)(4,1)S(1)}, pred[8]{0:T(512)(128)(4,1)}, u32[]{:S(2)}) copy-start(pred[8]{0:T(512)(128)(4,1)} %broadcast_in_dim.64) | copy-start | bytes 28
  84.2 35.7 %copy-start = (bf16[256,4,768]{2,0,1:T(8,128)(2,1)}, bf16[256,4,768]{2,0,1:T(8,128)(2,1)S(1)}, u32[]{:S(2)}) copy-start(bf16[256,4,768]{2,0,1:T(8,128)(2,1)S(1)} %all-to-all-done.1) | copy-start | bytes 4718596
  84.2 1.8 copy-start.5
  89.3 2.9 %copy-start.8 = (pred[4]{0:T(512)(128)(4,1)S(1)}, pred[4]{0:T(512)(128)(4,1)}, u32[]{:S(2)}) copy-start(pred[4]{0:T(512)(128)(4,1)} %copy-done.7) | copy-start | bytes 16
  90.4 12.6 %collective-permute-start.5 = (bf16[2,128,768]{2,1,0:T(8,128)(2,1)}, bf16[2,128,768]{2,1,0:T(8,128)(2,1)}, u32[]{:S(2)}, u32[]{:S(2)}) collective-permute-start(bf16[2,128,768]{2,1,0:T(8,128)(2,1)} %get-tuple-element.34), channel_id=1, source_target_pairs={{0,12},{4,0},{8,4},{12,8},{1,13},{5,1},{9,5},{13,9},{2,14},{6,2},{... | collective-permute-start | bytes 1179656 | tf_op jit(solution)/shard_map/ppermute | solution.py:217
  91.7 21.8 %collective-permute-start.4 = (bf16[2,128,768]{2,1,0:T(8,128)(2,1)}, bf16[2,128,768]{2,1,0:T(8,128)(2,1)}, u32[]{:S(2)}, u32[]{:S(2)}) collective-permute-start(bf16[2,128,768]{2,1,0:T(8,128)(2,1)} %get-tuple-element.35), channel_id=1, source_target_pairs={{0,8},{4,12},{8,0},{12,4},{1,9},{5,13},{9,1},{13,5},{2,10},{6,14},... | collective-permute-start | bytes 1179656 | tf_op jit(solution)/shard_map/ppermute | solution.py:217
  92.1 21.4 %collective-permute-start.3 = (bf16[2,128,768]{2,1,0:T(8,128)(2,1)S(1)}, bf16[2,128,768]{2,1,0:T(8,128)(2,1)}, u32[]{:S(2)}, u32[]{:S(2)}) collective-permute-start(bf16[2,128,768]{2,1,0:T(8,128)(2,1)S(1)} %get-tuple-element.36), channel_id=1, source_target_pairs={{0,4},{4,8},{8,12},{12,0},{1,5},{5,9},{9,13},{13,1},{2,6},{6,10},{... | collective-permute-start | bytes 1179656 | tf_op jit(solution)/shard_map/ppermute | solution.py:217
  94.4 23.7 %copy-start.1 = (bf16[8,128,768]{2,1,0:T(8,128)(2,1)S(1)}, bf16[8,128,768]{2,1,0:T(8,128)(2,1)}, u32[]{:S(2)}) copy-start(bf16[8,128,768]{2,1,0:T(8,128)(2,1)} %get-tuple-element.41) | copy-start | bytes 4718596
  113.5 24.9 %all-to-all-start = ((bf16[256,4,384]{0,2,1:T(8,128)(2,1)}), bf16[256,4,384]{0,2,1:T(8,128)(2,1)}, u32[]{:S(2)}, u32[]{:S(2)}) async-start(bf16[256,4,384]{0,2,1:T(8,128)(2,1)} %get-tuple-element.33), calls=%async_computation | async-start | bytes 1572864 | tf_op jit(solution)/shard_map/all_to_all | solution.py:187
  118.1 62.7 %all-gather.5.cloned.1.call-start = ((), (), s32[]{:S(2)}) async-start(), calls=%async_computation.6 | async-start | bytes 1966080 | tf_op jit(solution)/shard_map/all_gather | solution.py:190
  119.1 10.7 %collective-permute-start.8 = (bf16[2,128,768]{2,1,0:T(8,128)(2,1)}, bf16[2,128,768]{2,1,0:T(8,128)(2,1)}, u32[]{:S(2)}, u32[]{:S(2)}) collective-permute-start(bf16[2,128,768]{2,1,0:T(8,128)(2,1)} %get-tuple-element.29), channel_id=1, source_target_pairs={{0,12},{4,0},{8,4},{12,8},{1,13},{5,1},{9,5},{13,9},{2,14},{6,2},{... | collective-permute-start | bytes 1179656 | tf_op jit(solution)/shard_map/ppermute | solution.py:217
  119.1 18.3 %collective-permute-start.7 = (bf16[2,128,768]{2,1,0:T(8,128)(2,1)}, bf16[2,128,768]{2,1,0:T(8,128)(2,1)}, u32[]{:S(2)}, u32[]{:S(2)}) collective-permute-start(bf16[2,128,768]{2,1,0:T(8,128)(2,1)} %get-tuple-element.30), channel_id=1, source_target_pairs={{0,8},{4,12},{8,0},{12,4},{1,9},{5,13},{9,1},{13,5},{2,10},{6,14},... | collective-permute-start | bytes 1179656 | tf_op jit(solution)/shard_map/ppermute | solution.py:217
  119.6 18.7 %collective-permute-start.6 = (bf16[2,128,768]{2,1,0:T(8,128)(2,1)S(1)}, bf16[2,128,768]{2,1,0:T(8,128)(2,1)}, u32[]{:S(2)}, u32[]{:S(2)}) collective-permute-start(bf16[2,128,768]{2,1,0:T(8,128)(2,1)S(1)} %get-tuple-element.31), channel_id=1, source_target_pairs={{0,4},{4,8},{8,12},{12,0},{1,5},{5,9},{9,13},{13,1},{2,6},{6,10},{... | collective-permute-start | bytes 1179656 | tf_op jit(solution)/shard_map/ppermute | solution.py:217
  138.3 24.5 %all-to-all-start.2 = ((bf16[256,4,384]{0,2,1:T(8,128)(2,1)}), bf16[256,4,384]{0,2,1:T(8,128)(2,1)S(1)}, u32[]{:S(2)}, u32[]{:S(2)}) async-start(bf16[256,4,384]{0,2,1:T(8,128)(2,1)} %bitcast.35), calls=%async_computation.2 | async-start | bytes 1572864 | tf_op jit(solution)/shard_map/all_to_all | solution.py:187
  162.8 23.1 %all-to-all-start.3 = ((bf16[4,256,384]{2,1,0:T(8,128)(2,1)}), bf16[4,256,384]{2,1,0:T(8,128)(2,1)S(1)}, u32[]{:S(2)}, u32[]{:S(2)}) async-start(bf16[4,256,384]{2,1,0:T(8,128)(2,1)} %bitcast.84), calls=%async_computation.3 | async-start | bytes 1572864 | tf_op jit(solution)/shard_map/all_to_all | solution.py:250
  185.8 23.1 %all-to-all-start.4 = ((bf16[4,256,384]{2,1,0:T(8,128)(2,1)}), bf16[4,256,384]{2,1,0:T(8,128)(2,1)S(1)}, u32[]{:S(2)}, u32[]{:S(2)}) async-start(bf16[4,256,384]{2,1,0:T(8,128)(2,1)} %bitcast.83), calls=%async_computation.4 | async-start | bytes 1572864 | tf_op jit(solution)/shard_map/all_to_all | solution.py:250
  (1 other events, 0.9 us)
Sparse Core Ops, SparseCore 0:
  53.6 47.3 all-gather.2
  129.9 21.1 all-gather.4
